TPU v7x, 512 devices: a whole 4x4x16 slice. The times are simulated.
512 devices in a mesh: row: 32 (over z_lo, y), col: 16 (over z_hi, x, core).
Axes of the slice: x: 4, y: 4, z: 16 (z_hi: 2, z_lo: 8; z = z_hi * 8 + z_lo), core: 2. Of those that a mesh axis runs over, the one named last changes fastest.
Arguments:
- rhs: bfloat16 [32, 16, 64, 768], P('row', 'col'), may hold values from -6 to 6
- operator_blocks: bfloat16 [32, 16, 768, 768], P('row', 'col'), may hold values from -0.5 to 3.5
- local_solver: bfloat16 [32, 16, 768, 768], P('row', 'col'), may hold values from -0.1 to 0.6
- modes: bfloat16 [32, 16, 48, 768], P('row', 'col'), may hold values from -0.21875 to 0.21875
- coupling: bfloat16 [32, 16, 4, 128, 128], P('row', 'col'), may hold values from -0.25 to 0.25
- coarse_inverse: bfloat16 [16, 1536, 32, 768], P('col', None, 'row'), may hold values from -0.05 to 0.15
- send_block: int32 [32, 16, 8], P('row', 'col'), may hold values from 0 to 5
- slot_dir: int32 [32, 16, 4], P('row', 'col'), may hold values from -1 to 7, as said below
- slot_block: int32 [32, 16, 4], P('row', 'col'), may hold values from 0 to 5
Outputs:
- solution: float32 [32, 16, 64, 768], P('row', 'col')
Inputs may be any that keep to these rules, and one draw needn't show every extreme that they name: `slot_dir`: each subdomain lists 2 to 4 distinct directions toward subdomains inside the grid in its first slots; the remaining slots hold -1.
All inputs are finite; a program needn't handle non-finite values.
Results may differ from a plain program's by a relative error of at most 0.0033.
Values may be sent and summed in bfloat16 or wider, within the bound.
No kernel may reach another device: no remote copies, remote signals or barrier semaphores. Data moves between devices by JAX's collectives and lax.ppermute only.
A program may use at most 64 MiB of HBM per device.

v0:
```python
import jax
import jax.numpy as jnp
from jax import lax
from jax.sharding import PartitionSpec as P

ITERS = 6


OFFSETS = ((-1, -1), (-1, 0), (-1, 1), (0, -1), (0, 1), (1, -1), (1, 0), (1, 1))


def passed_along(block, axis, distance):
    devices = range(lax.axis_size(axis))
    route = [(i - distance, i) for i in devices if i - distance in devices]
    return lax.ppermute(block, axis, route)


def hop_rows(portion, steps):
    return passed_along(portion, "row", steps)


def hop_cols(portion, steps):
    return passed_along(portion, "col", steps)


def neighbour_pieces(outgoing):
    arrived = []
    for direction in range(8):
        shift_a, shift_b = OFFSETS[direction]
        portion = outgoing[7 - direction]
        if shift_a != 0:
            portion = hop_rows(portion, -shift_a)
        if shift_b != 0:
            portion = hop_cols(portion, -shift_b)
        arrived.append(portion)
    return jnp.stack(arrived, 0)


def on_device(
    rhs,
    operator_blocks,
    local_solver,
    modes,
    coupling,
    coarse_inverse,
    send_block,
    slot_dir,
    slot_block,
):
    highest = lax.Precision.HIGHEST
    columns = rhs.shape[2]
    unknowns = rhs.shape[3]
    block_size = coupling.shape[3]
    block_count = unknowns // block_size
    mode_count = modes.shape[2]
    piece_rows = mode_count * columns // 128
    rhs_full = rhs[0, 0].astype(jnp.float32)
    operator_matrix = operator_blocks[0, 0]
    solver_matrix = local_solver[0, 0]
    mode_basis = modes[0, 0]
    couplings = coupling[0, 0]
    coarse_tile = coarse_inverse[0, :, 0, :]
    send_onehot = (send_block[0, 0][:, None] == jnp.arange(block_count)[None, :]).astype(
        jnp.bfloat16
    )
    dir_onehot = (slot_dir[0, 0][:, None] == jnp.arange(8)[None, :]).astype(jnp.bfloat16)
    block_onehot = (slot_block[0, 0][:, None] == jnp.arange(block_count)[None, :]).astype(
        jnp.float32
    )
    col_index = lax.axis_index("col")

    def coarse_solve(rounded):
        restricted = lax.dot_general(
            mode_basis, rounded, (((1,), (1,)), ((), ())), preferred_element_type=jnp.float32
        )
        flat_piece = restricted.astype(jnp.bfloat16).reshape(piece_rows, 128)
        gathered = lax.all_gather(flat_piece, "row", axis=0, tiled=True).reshape(-1, columns)
        partial_sums = lax.dot_general(
            coarse_tile, gathered, (((0,), (0,)), ((), ())), preferred_element_type=jnp.float32
        )
        summed = lax.psum(partial_sums.reshape(-1, 128), "col")
        own_rows = lax.dynamic_slice_in_dim(summed, col_index * piece_rows, piece_rows, 0)
        return own_rows.reshape(mode_count, columns).astype(jnp.bfloat16)

    solution = jnp.zeros((columns, unknowns), jnp.float32)
    pending = None
    for iteration in range(ITERS):
        if iteration == 0:
            residual = rhs_full
        else:
            field_half = solution.astype(jnp.bfloat16)
            blocks = field_half.reshape(columns, block_count, block_size)
            outgoing = jnp.einsum(
                "ckn,ek->ecn", blocks, send_onehot, preferred_element_type=jnp.float32
            ).astype(jnp.bfloat16)
            incoming = neighbour_pieces(outgoing)
            chosen = jnp.einsum(
                "sd,dcn->scn", dir_onehot, incoming, preferred_element_type=jnp.float32
            ).astype(jnp.bfloat16)
            coupled = jnp.einsum(
                "scn,snm->scm", chosen, couplings, preferred_element_type=jnp.float32
            )
            placed = jnp.einsum("scm,sk->ckm", coupled, block_onehot, precision=highest).reshape(
                columns, unknowns
            )
            residual = rhs_full - (
                jnp.dot(field_half, operator_matrix, preferred_element_type=jnp.float32) + placed
            )
        rounded = residual.astype(jnp.bfloat16)
        update = jnp.dot(rounded, solver_matrix, preferred_element_type=jnp.float32)
        fresh = coarse_solve(rounded) if iteration + 1 < ITERS else None
        if pending is not None:
            update = update + lax.dot_general(
                pending, mode_basis, (((0,), (0,)), ((), ())), preferred_element_type=jnp.float32
            )
        solution = solution + update
        pending = fresh
    return solution[None, None]


def solution(mesh):
    in_specs = (
        P("row", "col", None, None),
        P("row", "col", None, None),
        P("row", "col", None, None),
        P("row", "col", None, None),
        P("row", "col", None, None, None),
        P("col", None, "row", None),
        P("row", "col", None),
        P("row", "col", None),
        P("row", "col", None),
    )
    out_specs = P("row", "col", None, None)
    return jax.shard_map(
        on_device, mesh=mesh, in_specs=in_specs, out_specs=out_specs, check_vma=False
    )
```

profile of v0, /device:TPU:6, one launch (start us, length us, event | category | flops | bytes accessed | tf_op | source)
XLA Modules:
  0.0 1449.4 jit_solution(8940192979941187941)
XLA Ops:
  0.0 2.5 fusion.173
  3.6 3.5 collective-permute-start
  7.1 3.5 collective-permute-start.3
  13.3 5.2 collective-permute-start.2
  18.7 124.3 %all_gather.15 = bf16[768,128]{1,0:T(8,128)(2,1)S(1)} all-gather(bf16[24,128]{1,0:T(8,128)(2,1)S(1)} %reshape.90), channel_id=1, replica_groups=mesh['row'=32,'col'=16] {'row'}, dimensions={0}, use_global_device_ids=true | all-gather | bytes 202752 | tf_op jit(solution)/shard_map/all_gather | solution.py:77
  144.0 1.9 collective-permute-start.5
  145.9 3.6 collective-permute-start.6
  149.6 128.0 %all-reduce.5 = bf16[384,128]{1,0:T(8,128)(2,1)S(1)} all-reduce(f32[384,128]{1,0:T(8,128)S(1)} %reshape.92), channel_id=1, replica_groups=mesh['row'=32,'col'=16] {'col'}, use_global_device_ids=true, to_apply=%region_0.0 | all-reduce | flops 49152 | bytes 294912 | tf_op jit(solution)/shard_map/psum | solution.py:81
  278.9 2.6 collective-permute-start.1
  281.5 3.0 collective-permute-start.4
  284.5 13.4 collective-permute-start.8
  297.9 1.9 collective-permute-start.11
  300.2 12.8 collective-permute-done.11
  323.2 5.1 collective-permute-start.12
  328.9 1.9 collective-permute-start.15
  336.3 5.8 collective-permute-start.14
  344.0 14.4 collective-permute-start.17
  358.4 1.9 collective-permute-start.18
  360.3 118.6 %all_gather.16 = bf16[768,128]{1,0:T(8,128)(2,1)} all-gather(bf16[24,128]{1,0:T(8,128)(2,1)} %reshape.95), channel_id=1, replica_groups=mesh['row'=32,'col'=16] {'row'}, dimensions={0}, use_global_device_ids=true | all-gather | bytes 202752 | tf_op jit(solution)/shard_map/all_gather | solution.py:77
  483.4 1.9 collective-permute-start.13
  485.3 3.6 collective-permute-start.16
  489.0 13.8 collective-permute-start.20
  502.8 1.9 collective-permute-start.23
  504.7 2.2 fusion.35
  528.7 120.0 %all_gather.17 = bf16[768,128]{1,0:T(8,128)(2,1)} all-gather(bf16[24,128]{1,0:T(8,128)(2,1)} %reshape.100), channel_id=1, replica_groups=mesh['row'=32,'col'=16] {'row'}, dimensions={0}, use_global_device_ids=true | all-gather | bytes 202752 | tf_op jit(solution)/shard_map/all_gather | solution.py:77
  650.6 2.1 fusion.38
  656.4 139.2 %all-reduce.6 = (bf16[384,128]{1,0:T(8,128)(2,1)}, bf16[384,128]{1,0:T(8,128)(2,1)}) all-reduce(f32[384,128]{1,0:T(8,128)} %reshape.97, f32[384,128]{1,0:T(8,128)} %reshape.102), channel_id=1, replica_groups=mesh['row'=32,'col'=16] {'col'}, use_global_device_ids=true, to_apply=%region_1.0 | all-reduce | flops 98304 | bytes 589824 | tf_op jit(solution)/shard_map/psum | solution.py:81
  797.7 2.0 fusion.175
  802.7 1.9 collective-permute-start.24
  804.6 1.9 collective-permute-start.27
  809.1 5.2 collective-permute-start.26
  814.3 2.0 collective-permute-start.29
  816.4 3.5 collective-permute-start.30
  821.8 13.5 collective-permute-start.25
  835.3 1.9 collective-permute-start.28
  837.3 14.5 collective-permute-start.32
  851.8 2.1 collective-permute-start.35
  881.0 5.1 collective-permute-start.36
  886.7 3.9 collective-permute-start.39
  896.1 5.8 collective-permute-start.38
  903.8 14.1 collective-permute-start.41
  917.8 1.9 collective-permute-start.42
  919.8 119.4 %all_gather.18 = bf16[768,128]{1,0:T(8,128)(2,1)} all-gather(bf16[24,128]{1,0:T(8,128)(2,1)} %reshape.105), channel_id=1, replica_groups=mesh['row'=32,'col'=16] {'row'}, dimensions={0}, use_global_device_ids=true | all-gather | bytes 202752 | tf_op jit(solution)/shard_map/all_gather | solution.py:77
  1043.7 1.9 collective-permute-start.37
  1045.6 3.6 collective-permute-start.40
  1049.3 24.0 %collective-permute-start.44 = (bf16[64,128]{1,0:T(8,128)(2,1)}, bf16[64,128]{1,0:T(8,128)(2,1)}, u32[]{:S(2)}, u32[]{:S(2)}) collective-permute-start(bf16[64,128]{1,0:T(8,128)(2,1)} %collective-permute-done.43), channel_id=1, source_target_pairs={{0,1},{1,2},{2,3},{3,4},{4,5},{5,6},{6,7},{7,8},{8,9},{9,10},{10,1... | collective-permute-start | bytes 49160 | tf_op jit(solution)/shard_map/ppermute | solution.py:15
  1073.2 1.9 collective-permute-start.47
  1075.2 2.2 fusion.41
  1099.2 119.9 %all_gather.19 = bf16[768,128]{1,0:T(8,128)(2,1)} all-gather(bf16[24,128]{1,0:T(8,128)(2,1)} %reshape.110), channel_id=1, replica_groups=mesh['row'=32,'col'=16] {'row'}, dimensions={0}, use_global_device_ids=true | all-gather | bytes 202752 | tf_op jit(solution)/shard_map/all_gather | solution.py:77
  1221.0 2.1 fusion.44
  1226.8 139.8 %all-reduce.7 = (bf16[384,128]{1,0:T(8,128)(2,1)}, bf16[384,128]{1,0:T(8,128)(2,1)}) all-reduce(f32[384,128]{1,0:T(8,128)} %reshape.107, f32[384,128]{1,0:T(8,128)} %reshape.112), channel_id=1, replica_groups=mesh['row'=32,'col'=16] {'col'}, use_global_device_ids=true, to_apply=%region_3.0 | all-reduce | flops 98304 | bytes 589824 | tf_op jit(solution)/shard_map/psum | solution.py:81
  1368.7 2.0 fusion.177
  1373.7 1.9 collective-permute-start.48
  1375.6 1.9 collective-permute-start.51
  1380.1 5.2 collective-permute-start.50
  1385.3 2.1 collective-permute-start.53
  1387.4 3.5 collective-permute-start.54
  1392.8 13.5 collective-permute-start.49
  1406.3 1.9 collective-permute-start.52
  1408.3 14.5 collective-permute-start.56
  1422.8 1.9 collective-permute-start.59
  1435.0 3.3 collective-permute-done.59
  1444.8 2.6 fusion.20
  1447.5 1.9 fusion.48
  (285 shorter events, 159.2 us)
Async XLA Ops:
  0.0 143.2 %copy-start = (bf16[1,1536,1,768]{3,1,2,0:T(8,128)(2,1)S(1)}, bf16[1,1536,1,768]{3,1,2,0:T(8,128)(2,1)}, u32[]{:S(2)}) copy-start(bf16[1,1536,1,768]{3,1,2,0:T(8,128)(2,1)} %param.14) | copy-start | bytes 7077892
  3.6 140.4 %collective-permute-start = (bf16[64,128]{1,0:T(8,128)(2,1)S(1)}, bf16[64,128]{1,0:T(8,128)(2,1)S(1)}, u32[]{:S(2)}, u32[]{:S(2)}) collective-permute-start(bf16[64,128]{1,0:T(8,128)(2,1)S(1)} %bitcast.426), channel_id=1, source_target_pairs={{0,16},{16,32},{32,48},{48,64},{64,80},{80,96},{96,112},{112,128},... | collective-permute-start | bytes 49160 | tf_op jit(solution)/shard_map/ppermute | solution.py:15
  7.1 138.8 %collective-permute-start.3 = (bf16[64,128]{1,0:T(8,128)(2,1)S(1)}, bf16[64,128]{1,0:T(8,128)(2,1)S(1)}, u32[]{:S(2)}, u32[]{:S(2)}) collective-permute-start(bf16[64,128]{1,0:T(8,128)(2,1)S(1)} %bitcast.424), channel_id=1, source_target_pairs={{0,16},{16,32},{32,48},{48,64},{64,80},{80,96},{96,112},{112,128},... | collective-permute-start | bytes 49160 | tf_op jit(solution)/shard_map/ppermute | solution.py:15
  10.6 266.9 %collective-permute-start.7 = (bf16[64,128]{1,0:T(8,128)(2,1)S(1)}, bf16[64,128]{1,0:T(8,128)(2,1)S(1)}, u32[]{:S(2)}, u32[]{:S(2)}) collective-permute-start(bf16[64,128]{1,0:T(8,128)(2,1)S(1)} %bitcast.404), channel_id=1, source_target_pairs={{16,0},{32,16},{48,32},{64,48},{80,64},{96,80},{112,96},{128,112},... | collective-permute-start | bytes 49160 | tf_op jit(solution)/shard_map/ppermute | solution.py:15
  11.9 266.9 %collective-permute-start.10 = (bf16[64,128]{1,0:T(8,128)(2,1)S(1)}, bf16[64,128]{1,0:T(8,128)(2,1)S(1)}, u32[]{:S(2)}, u32[]{:S(2)}) collective-permute-start(bf16[64,128]{1,0:T(8,128)(2,1)S(1)} %bitcast.403), channel_id=1, source_target_pairs={{16,0},{32,16},{48,32},{64,48},{80,64},{96,80},{112,96},{128,112},... | collective-permute-start | bytes 49160 | tf_op jit(solution)/shard_map/ppermute | solution.py:15
  13.3 268.2 %collective-permute-start.2 = (bf16[64,128]{1,0:T(8,128)(2,1)S(1)}, bf16[64,128]{1,0:T(8,128)(2,1)S(1)}, u32[]{:S(2)}, u32[]{:S(2)}) collective-permute-start(bf16[64,128]{1,0:T(8,128)(2,1)S(1)} %bitcast.401), channel_id=1, source_target_pairs={{0,16},{16,32},{32,48},{48,64},{64,80},{80,96},{96,112},{112,128},... | collective-permute-start | bytes 49160 | tf_op jit(solution)/shard_map/ppermute | solution.py:15
  143.7 169.8 %copy-start.22 = (s32[1,1,4]{2,1,0:T(1,128)S(1)}, s32[1,1,4]{2,1,0:T(1,128)}, u32[]{:S(2)}) copy-start(s32[1,1,4]{2,1,0:T(1,128)} %param.16) | copy-start | bytes 52
  144.0 140.5 %collective-permute-start.5 = (bf16[64,128]{1,0:T(8,128)(2,1)S(1)}, bf16[64,128]{1,0:T(8,128)(2,1)S(1)}, u32[]{:S(2)}, u32[]{:S(2)}) collective-permute-start(bf16[64,128]{1,0:T(8,128)(2,1)S(1)} %bitcast.406), channel_id=1, source_target_pairs={{0,1},{1,2},{2,3},{3,4},{4,5},{5,6},{6,7},{7,8},{8,9},{9,10},{10,1... | collective-permute-start | bytes 49160 | tf_op jit(solution)/shard_map/ppermute | solution.py:15
  145.9 152.0 %collective-permute-start.6 = (bf16[64,128]{1,0:T(8,128)(2,1)S(1)}, bf16[64,128]{1,0:T(8,128)(2,1)S(1)}, u32[]{:S(2)}, u32[]{:S(2)}) collective-permute-start(bf16[64,128]{1,0:T(8,128)(2,1)S(1)} %bitcast.402), channel_id=1, source_target_pairs={{1,0},{2,1},{3,2},{4,3},{5,4},{6,5},{7,6},{8,7},{9,8},{10,9},{11,1... | collective-permute-start | bytes 49160 | tf_op jit(solution)/shard_map/ppermute | solution.py:15
  277.6 22.5 %collective-permute-start.9 = (bf16[64,128]{1,0:T(8,128)(2,1)S(1)}, bf16[64,128]{1,0:T(8,128)(2,1)S(1)}, u32[]{:S(2)}, u32[]{:S(2)}) collective-permute-start(bf16[64,128]{1,0:T(8,128)(2,1)S(1)} %bitcast.408), channel_id=1, source_target_pairs={{16,0},{32,16},{48,32},{64,48},{80,64},{96,80},{112,96},{128,112},... | collective-permute-start | bytes 49160 | tf_op jit(solution)/shard_map/ppermute | solution.py:15
  278.9 21.2 %collective-permute-start.1 = (bf16[64,128]{1,0:T(8,128)(2,1)S(1)}, bf16[64,128]{1,0:T(8,128)(2,1)S(1)}, u32[]{:S(2)}, u32[]{:S(2)}) collective-permute-start(bf16[64,128]{1,0:T(8,128)(2,1)S(1)} %collective-permute-done), channel_id=1, source_target_pairs={{0,1},{1,2},{2,3},{3,4},{4,5},{5,6},{6,7},{7,8},{8,9},{9,10},{10,1... | collective-permute-start | bytes 49160 | tf_op jit(solution)/shard_map/ppermute | solution.py:15
  281.5 18.7 %collective-permute-start.4 = (bf16[64,128]{1,0:T(8,128)(2,1)S(1)}, bf16[64,128]{1,0:T(8,128)(2,1)S(1)}, u32[]{:S(2)}, u32[]{:S(2)}) collective-permute-start(bf16[64,128]{1,0:T(8,128)(2,1)S(1)} %collective-permute-done.3), channel_id=1, source_target_pairs={{1,0},{2,1},{3,2},{4,3},{5,4},{6,5},{7,6},{8,7},{9,8},{10,9},{11,1... | collective-permute-start | bytes 49160 | tf_op jit(solution)/shard_map/ppermute | solution.py:15
  284.5 15.7 %collective-permute-start.8 = (bf16[64,128]{1,0:T(8,128)(2,1)S(1)}, bf16[64,128]{1,0:T(8,128)(2,1)S(1)}, u32[]{:S(2)}, u32[]{:S(2)}) collective-permute-start(bf16[64,128]{1,0:T(8,128)(2,1)S(1)} %collective-permute-done.7), channel_id=1, source_target_pairs={{0,1},{1,2},{2,3},{3,4},{4,5},{5,6},{6,7},{7,8},{8,9},{9,10},{10,1... | collective-permute-start | bytes 49160 | tf_op jit(solution)/shard_map/ppermute | solution.py:15
  297.9 15.1 %collective-permute-start.11 = (bf16[64,128]{1,0:T(8,128)(2,1)S(1)}, bf16[64,128]{1,0:T(8,128)(2,1)S(1)}, u32[]{:S(2)}, u32[]{:S(2)}) collective-permute-start(bf16[64,128]{1,0:T(8,128)(2,1)S(1)} %collective-permute-done.10), channel_id=1, source_target_pairs={{1,0},{2,1},{3,2},{4,3},{5,4},{6,5},{7,6},{8,7},{9,8},{10,9},{11,1... | collective-permute-start | bytes 49160 | tf_op jit(solution)/shard_map/ppermute | solution.py:15
  323.2 20.8 %collective-permute-start.12 = (bf16[64,128]{1,0:T(8,128)(2,1)}, bf16[64,128]{1,0:T(8,128)(2,1)}, u32[]{:S(2)}, u32[]{:S(2)}) collective-permute-start(bf16[64,128]{1,0:T(8,128)(2,1)} %bitcast.385), channel_id=1, source_target_pairs={{0,16},{16,32},{32,48},{48,64},{64,80},{80,96},{96,112},{112,128},... | collective-permute-start | bytes 49160 | tf_op jit(solution)/shard_map/ppermute | solution.py:15
  328.9 29.4 %collective-permute-start.15 = (bf16[64,128]{1,0:T(8,128)(2,1)}, bf16[64,128]{1,0:T(8,128)(2,1)}, u32[]{:S(2)}, u32[]{:S(2)}) collective-permute-start(bf16[64,128]{1,0:T(8,128)(2,1)} %bitcast.383), channel_id=1, source_target_pairs={{0,16},{16,32},{32,48},{48,64},{64,80},{80,96},{96,112},{112,128},... | collective-permute-start | bytes 49160 | tf_op jit(solution)/shard_map/ppermute | solution.py:15
  332.5 149.5 %collective-permute-start.19 = (bf16[64,128]{1,0:T(8,128)(2,1)}, bf16[64,128]{1,0:T(8,128)(2,1)}, u32[]{:S(2)}, u32[]{:S(2)}) collective-permute-start(bf16[64,128]{1,0:T(8,128)(2,1)} %bitcast.380), channel_id=1, source_target_pairs={{16,0},{32,16},{48,32},{64,48},{80,64},{96,80},{112,96},{128,112},... | collective-permute-start | bytes 49160 | tf_op jit(solution)/shard_map/ppermute | solution.py:15
  334.4 148.9 %collective-permute-start.22 = (bf16[64,128]{1,0:T(8,128)(2,1)}, bf16[64,128]{1,0:T(8,128)(2,1)}, u32[]{:S(2)}, u32[]{:S(2)}) collective-permute-start(bf16[64,128]{1,0:T(8,128)(2,1)} %bitcast.378), channel_id=1, source_target_pairs={{16,0},{32,16},{48,32},{64,48},{80,64},{96,80},{112,96},{128,112},... | collective-permute-start | bytes 49160 | tf_op jit(solution)/shard_map/ppermute | solution.py:15
  336.3 149.0 %collective-permute-start.14 = (bf16[64,128]{1,0:T(8,128)(2,1)}, bf16[64,128]{1,0:T(8,128)(2,1)}, u32[]{:S(2)}, u32[]{:S(2)}) collective-permute-start(bf16[64,128]{1,0:T(8,128)(2,1)} %bitcast.384), channel_id=1, source_target_pairs={{0,16},{16,32},{32,48},{48,64},{64,80},{80,96},{96,112},{112,128},... | collective-permute-start | bytes 49160 | tf_op jit(solution)/shard_map/ppermute | solution.py:15
  344.0 145.0 %collective-permute-start.17 = (bf16[64,128]{1,0:T(8,128)(2,1)}, bf16[64,128]{1,0:T(8,128)(2,1)S(1)}, u32[]{:S(2)}, u32[]{:S(2)}) collective-permute-start(bf16[64,128]{1,0:T(8,128)(2,1)} %bitcast.419), channel_id=1, source_target_pairs={{0,1},{1,2},{2,3},{3,4},{4,5},{5,6},{6,7},{7,8},{8,9},{9,10},{10,1... | collective-permute-start | bytes 49160 | tf_op jit(solution)/shard_map/ppermute | solution.py:15
  358.4 144.4 %collective-permute-start.18 = (bf16[64,128]{1,0:T(8,128)(2,1)}, bf16[64,128]{1,0:T(8,128)(2,1)}, u32[]{:S(2)}, u32[]{:S(2)}) collective-permute-start(bf16[64,128]{1,0:T(8,128)(2,1)} %bitcast.413), channel_id=1, source_target_pairs={{1,0},{2,1},{3,2},{4,3},{5,4},{6,5},{7,6},{8,7},{9,8},{10,9},{11,1... | collective-permute-start | bytes 49160 | tf_op jit(solution)/shard_map/ppermute | solution.py:15
  482.1 31.8 %collective-permute-start.21 = (bf16[64,128]{1,0:T(8,128)(2,1)}, bf16[64,128]{1,0:T(8,128)(2,1)}, u32[]{:S(2)}, u32[]{:S(2)}) collective-permute-start(bf16[64,128]{1,0:T(8,128)(2,1)} %bitcast.416), channel_id=1, source_target_pairs={{16,0},{32,16},{48,32},{64,48},{80,64},{96,80},{112,96},{128,112},... | collective-permute-start | bytes 49160 | tf_op jit(solution)/shard_map/ppermute | solution.py:15
  483.4 31.8 %collective-permute-start.13 = (bf16[64,128]{1,0:T(8,128)(2,1)}, bf16[64,128]{1,0:T(8,128)(2,1)}, u32[]{:S(2)}, u32[]{:S(2)}) collective-permute-start(bf16[64,128]{1,0:T(8,128)(2,1)} %collective-permute-done.12), channel_id=1, source_target_pairs={{0,1},{1,2},{2,3},{3,4},{4,5},{5,6},{6,7},{7,8},{8,9},{9,10},{10,1... | collective-permute-start | bytes 49160 | tf_op jit(solution)/shard_map/ppermute | solution.py:15
  485.3 31.3 %collective-permute-start.16 = (bf16[64,128]{1,0:T(8,128)(2,1)}, bf16[64,128]{1,0:T(8,128)(2,1)}, u32[]{:S(2)}, u32[]{:S(2)}) collective-permute-start(bf16[64,128]{1,0:T(8,128)(2,1)} %collective-permute-done.15), channel_id=1, source_target_pairs={{1,0},{2,1},{3,2},{4,3},{5,4},{6,5},{7,6},{8,7},{9,8},{10,9},{11,1... | collective-permute-start | bytes 49160 | tf_op jit(solution)/shard_map/ppermute | solution.py:15
  489.0 29.0 %collective-permute-start.20 = (bf16[64,128]{1,0:T(8,128)(2,1)}, bf16[64,128]{1,0:T(8,128)(2,1)}, u32[]{:S(2)}, u32[]{:S(2)}) collective-permute-start(bf16[64,128]{1,0:T(8,128)(2,1)} %collective-permute-done.19), channel_id=1, source_target_pairs={{0,1},{1,2},{2,3},{3,4},{4,5},{5,6},{6,7},{7,8},{8,9},{9,10},{10,1... | collective-permute-start | bytes 49160 | tf_op jit(solution)/shard_map/ppermute | solution.py:15
  502.8 16.5 %collective-permute-start.23 = (bf16[64,128]{1,0:T(8,128)(2,1)}, bf16[64,128]{1,0:T(8,128)(2,1)}, u32[]{:S(2)}, u32[]{:S(2)}) collective-permute-start(bf16[64,128]{1,0:T(8,128)(2,1)} %collective-permute-done.22), channel_id=1, source_target_pairs={{1,0},{2,1},{3,2},{4,3},{5,4},{6,5},{7,6},{8,7},{9,8},{10,9},{11,1... | collective-permute-start | bytes 49160 | tf_op jit(solution)/shard_map/ppermute | solution.py:15
  652.7 148.6 %copy-start.20 = (s32[1,1,8]{2,1,0:T(1,128)S(1)}, s32[1,1,8]{2,1,0:T(1,128)}, u32[]{:S(2)}) copy-start(s32[1,1,8]{2,1,0:T(1,128)} %param.15) | copy-start | bytes 100
  802.7 11.6 collective-permute-start.24
  804.6 11.8 collective-permute-start.27
  806.5 14.0 collective-permute-start.31
  807.8 14.0 collective-permute-start.34
  809.1 26.2 %collective-permute-start.26 = (bf16[64,128]{1,0:T(8,128)(2,1)S(1)}, bf16[64,128]{1,0:T(8,128)(2,1)S(1)}, u32[]{:S(2)}, u32[]{:S(2)}) collective-permute-start(bf16[64,128]{1,0:T(8,128)(2,1)S(1)} %bitcast.430), channel_id=1, source_target_pairs={{0,16},{16,32},{32,48},{48,64},{64,80},{80,96},{96,112},{112,128},... | collective-permute-start | bytes 49160 | tf_op jit(solution)/shard_map/ppermute | solution.py:15
  814.3 22.9 %collective-permute-start.29 = (bf16[64,128]{1,0:T(8,128)(2,1)S(1)}, bf16[64,128]{1,0:T(8,128)(2,1)S(1)}, u32[]{:S(2)}, u32[]{:S(2)}) collective-permute-start(bf16[64,128]{1,0:T(8,128)(2,1)S(1)} %bitcast.427), channel_id=1, source_target_pairs={{0,1},{1,2},{2,3},{3,4},{4,5},{5,6},{6,7},{7,8},{8,9},{9,10},{10,1... | collective-permute-start | bytes 49160 | tf_op jit(solution)/shard_map/ppermute | solution.py:15
  816.4 35.3 %collective-permute-start.30 = (bf16[64,128]{1,0:T(8,128)(2,1)S(1)}, bf16[64,128]{1,0:T(8,128)(2,1)S(1)}, u32[]{:S(2)}, u32[]{:S(2)}) collective-permute-start(bf16[64,128]{1,0:T(8,128)(2,1)S(1)} %bitcast.420), channel_id=1, source_target_pairs={{1,0},{2,1},{3,2},{4,3},{5,4},{6,5},{7,6},{8,7},{9,8},{10,9},{11,1... | collective-permute-start | bytes 49160 | tf_op jit(solution)/shard_map/ppermute | solution.py:15
  820.5 39.5 %collective-permute-start.33 = (bf16[64,128]{1,0:T(8,128)(2,1)}, bf16[64,128]{1,0:T(8,128)(2,1)}, u32[]{:S(2)}, u32[]{:S(2)}) collective-permute-start(bf16[64,128]{1,0:T(8,128)(2,1)} %bitcast.371), channel_id=1, source_target_pairs={{16,0},{32,16},{48,32},{64,48},{80,64},{96,80},{112,96},{128,112},... | collective-permute-start | bytes 49160 | tf_op jit(solution)/shard_map/ppermute | solution.py:15
  821.8 39.6 %collective-permute-start.25 = (bf16[64,128]{1,0:T(8,128)(2,1)}, bf16[64,128]{1,0:T(8,128)(2,1)}, u32[]{:S(2)}, u32[]{:S(2)}) collective-permute-start(bf16[64,128]{1,0:T(8,128)(2,1)} %collective-permute-done.24), channel_id=1, source_target_pairs={{0,1},{1,2},{2,3},{3,4},{4,5},{5,6},{6,7},{7,8},{8,9},{9,10},{10,1... | collective-permute-start | bytes 49160 | tf_op jit(solution)/shard_map/ppermute | solution.py:15
  835.3 27.4 %collective-permute-start.28 = (bf16[64,128]{1,0:T(8,128)(2,1)}, bf16[64,128]{1,0:T(8,128)(2,1)}, u32[]{:S(2)}, u32[]{:S(2)}) collective-permute-start(bf16[64,128]{1,0:T(8,128)(2,1)} %collective-permute-done.27), channel_id=1, source_target_pairs={{1,0},{2,1},{3,2},{4,3},{5,4},{6,5},{7,6},{8,7},{9,8},{10,9},{11,1... | collective-permute-start | bytes 49160 | tf_op jit(solution)/shard_map/ppermute | solution.py:15
  837.3 26.8 %collective-permute-start.32 = (bf16[64,128]{1,0:T(8,128)(2,1)}, bf16[64,128]{1,0:T(8,128)(2,1)}, u32[]{:S(2)}, u32[]{:S(2)}) collective-permute-start(bf16[64,128]{1,0:T(8,128)(2,1)} %collective-permute-done.31), channel_id=1, source_target_pairs={{0,1},{1,2},{2,3},{3,4},{4,5},{5,6},{6,7},{7,8},{8,9},{9,10},{10,1... | collective-permute-start | bytes 49160 | tf_op jit(solution)/shard_map/ppermute | solution.py:15
  851.8 15.5 %collective-permute-start.35 = (bf16[64,128]{1,0:T(8,128)(2,1)}, bf16[64,128]{1,0:T(8,128)(2,1)}, u32[]{:S(2)}, u32[]{:S(2)}) collective-permute-start(bf16[64,128]{1,0:T(8,128)(2,1)} %collective-permute-done.34), channel_id=1, source_target_pairs={{1,0},{2,1},{3,2},{4,3},{5,4},{6,5},{7,6},{8,7},{9,8},{10,9},{11,1... | collective-permute-start | bytes 49160 | tf_op jit(solution)/shard_map/ppermute | solution.py:15
  881.0 22.8 %collective-permute-start.36 = (bf16[64,128]{1,0:T(8,128)(2,1)}, bf16[64,128]{1,0:T(8,128)(2,1)}, u32[]{:S(2)}, u32[]{:S(2)}) collective-permute-start(bf16[64,128]{1,0:T(8,128)(2,1)} %bitcast.369), channel_id=1, source_target_pairs={{0,16},{16,32},{32,48},{48,64},{64,80},{80,96},{96,112},{112,128},... | collective-permute-start | bytes 49160 | tf_op jit(solution)/shard_map/ppermute | solution.py:15
  886.7 31.1 %collective-permute-start.39 = (bf16[64,128]{1,0:T(8,128)(2,1)}, bf16[64,128]{1,0:T(8,128)(2,1)}, u32[]{:S(2)}, u32[]{:S(2)}) collective-permute-start(bf16[64,128]{1,0:T(8,128)(2,1)} %bitcast.367), channel_id=1, source_target_pairs={{0,16},{16,32},{32,48},{48,64},{64,80},{80,96},{96,112},{112,128},... | collective-permute-start | bytes 49160 | tf_op jit(solution)/shard_map/ppermute | solution.py:15
  892.3 150.0 %collective-permute-start.43 = (bf16[64,128]{1,0:T(8,128)(2,1)}, bf16[64,128]{1,0:T(8,128)(2,1)}, u32[]{:S(2)}, u32[]{:S(2)}) collective-permute-start(bf16[64,128]{1,0:T(8,128)(2,1)} %bitcast.364), channel_id=1, source_target_pairs={{16,0},{32,16},{48,32},{64,48},{80,64},{96,80},{112,96},{128,112},... | collective-permute-start | bytes 49160 | tf_op jit(solution)/shard_map/ppermute | solution.py:15
  894.2 149.4 %collective-permute-start.46 = (bf16[64,128]{1,0:T(8,128)(2,1)}, bf16[64,128]{1,0:T(8,128)(2,1)}, u32[]{:S(2)}, u32[]{:S(2)}) collective-permute-start(bf16[64,128]{1,0:T(8,128)(2,1)} %bitcast.362), channel_id=1, source_target_pairs={{16,0},{32,16},{48,32},{64,48},{80,64},{96,80},{112,96},{128,112},... | collective-permute-start | bytes 49160 | tf_op jit(solution)/shard_map/ppermute | solution.py:15
  896.1 149.5 %collective-permute-start.38 = (bf16[64,128]{1,0:T(8,128)(2,1)}, bf16[64,128]{1,0:T(8,128)(2,1)}, u32[]{:S(2)}, u32[]{:S(2)}) collective-permute-start(bf16[64,128]{1,0:T(8,128)(2,1)} %bitcast.368), channel_id=1, source_target_pairs={{0,16},{16,32},{32,48},{48,64},{64,80},{80,96},{96,112},{112,128},... | collective-permute-start | bytes 49160 | tf_op jit(solution)/shard_map/ppermute | solution.py:15
  903.8 145.5 %collective-permute-start.41 = (bf16[64,128]{1,0:T(8,128)(2,1)}, bf16[64,128]{1,0:T(8,128)(2,1)S(1)}, u32[]{:S(2)}, u32[]{:S(2)}) collective-permute-start(bf16[64,128]{1,0:T(8,128)(2,1)} %bitcast.421), channel_id=1, source_target_pairs={{0,1},{1,2},{2,3},{3,4},{4,5},{5,6},{6,7},{7,8},{8,9},{9,10},{10,1... | collective-permute-start | bytes 49160 | tf_op jit(solution)/shard_map/ppermute | solution.py:15
  917.8 155.4 %collective-permute-start.42 = (bf16[64,128]{1,0:T(8,128)(2,1)}, bf16[64,128]{1,0:T(8,128)(2,1)}, u32[]{:S(2)}, u32[]{:S(2)}) collective-permute-start(bf16[64,128]{1,0:T(8,128)(2,1)} %bitcast.414), channel_id=1, source_target_pairs={{1,0},{2,1},{3,2},{4,3},{5,4},{6,5},{7,6},{8,7},{9,8},{10,9},{11,1... | collective-permute-start | bytes 49160 | tf_op jit(solution)/shard_map/ppermute | solution.py:15
  1042.4 42.0 %collective-permute-start.45 = (bf16[64,128]{1,0:T(8,128)(2,1)}, bf16[64,128]{1,0:T(8,128)(2,1)}, u32[]{:S(2)}, u32[]{:S(2)}) collective-permute-start(bf16[64,128]{1,0:T(8,128)(2,1)} %bitcast.417), channel_id=1, source_target_pairs={{16,0},{32,16},{48,32},{64,48},{80,64},{96,80},{112,96},{128,112},... | collective-permute-start | bytes 49160 | tf_op jit(solution)/shard_map/ppermute | solution.py:15
  1043.7 42.0 %collective-permute-start.37 = (bf16[64,128]{1,0:T(8,128)(2,1)}, bf16[64,128]{1,0:T(8,128)(2,1)}, u32[]{:S(2)}, u32[]{:S(2)}) collective-permute-start(bf16[64,128]{1,0:T(8,128)(2,1)} %collective-permute-done.36), channel_id=1, source_target_pairs={{0,1},{1,2},{2,3},{3,4},{4,5},{5,6},{6,7},{7,8},{8,9},{9,10},{10,1... | collective-permute-start | bytes 49160 | tf_op jit(solution)/shard_map/ppermute | solution.py:15
  1045.6 41.4 %collective-permute-start.40 = (bf16[64,128]{1,0:T(8,128)(2,1)}, bf16[64,128]{1,0:T(8,128)(2,1)}, u32[]{:S(2)}, u32[]{:S(2)}) collective-permute-start(bf16[64,128]{1,0:T(8,128)(2,1)} %collective-permute-done.39), channel_id=1, source_target_pairs={{1,0},{2,1},{3,2},{4,3},{5,4},{6,5},{7,6},{8,7},{9,8},{10,9},{11,1... | collective-permute-start | bytes 49160 | tf_op jit(solution)/shard_map/ppermute | solution.py:15
  1049.3 39.1 %collective-permute-start.44 = (bf16[64,128]{1,0:T(8,128)(2,1)}, bf16[64,128]{1,0:T(8,128)(2,1)}, u32[]{:S(2)}, u32[]{:S(2)}) collective-permute-start(bf16[64,128]{1,0:T(8,128)(2,1)} %collective-permute-done.43), channel_id=1, source_target_pairs={{0,1},{1,2},{2,3},{3,4},{4,5},{5,6},{6,7},{7,8},{8,9},{9,10},{10,1... | collective-permute-start | bytes 49160 | tf_op jit(solution)/shard_map/ppermute | solution.py:15
  1073.2 16.5 %collective-permute-start.47 = (bf16[64,128]{1,0:T(8,128)(2,1)}, bf16[64,128]{1,0:T(8,128)(2,1)}, u32[]{:S(2)}, u32[]{:S(2)}) collective-permute-start(bf16[64,128]{1,0:T(8,128)(2,1)} %collective-permute-done.46), channel_id=1, source_target_pairs={{1,0},{2,1},{3,2},{4,3},{5,4},{6,5},{7,6},{8,7},{9,8},{10,9},{11,1... | collective-permute-start | bytes 49160 | tf_op jit(solution)/shard_map/ppermute | solution.py:15
  1223.2 149.2 %copy-start.21 = (s32[1,1,8]{2,1,0:T(1,128)S(1)}, s32[1,1,8]{2,1,0:T(1,128)}, u32[]{:S(2)}) copy-start(s32[1,1,8]{2,1,0:T(1,128)} %param.15) | copy-start | bytes 100
  1373.7 11.6 collective-permute-start.48
  1375.6 11.8 collective-permute-start.51
  1377.5 14.0 collective-permute-start.55
  1378.8 14.0 collective-permute-start.58
  1380.1 26.2 %collective-permute-start.50 = (bf16[64,128]{1,0:T(8,128)(2,1)S(1)}, bf16[64,128]{1,0:T(8,128)(2,1)S(1)}, u32[]{:S(2)}, u32[]{:S(2)}) collective-permute-start(bf16[64,128]{1,0:T(8,128)(2,1)S(1)} %bitcast.431), channel_id=1, source_target_pairs={{0,16},{16,32},{32,48},{48,64},{64,80},{80,96},{96,112},{112,128},... | collective-permute-start | bytes 49160 | tf_op jit(solution)/shard_map/ppermute | solution.py:15
  1385.3 22.9 %collective-permute-start.53 = (bf16[64,128]{1,0:T(8,128)(2,1)S(1)}, bf16[64,128]{1,0:T(8,128)(2,1)S(1)}, u32[]{:S(2)}, u32[]{:S(2)}) collective-permute-start(bf16[64,128]{1,0:T(8,128)(2,1)S(1)} %bitcast.428), channel_id=1, source_target_pairs={{0,1},{1,2},{2,3},{3,4},{4,5},{5,6},{6,7},{7,8},{8,9},{9,10},{10,1... | collective-permute-start | bytes 49160 | tf_op jit(solution)/shard_map/ppermute | solution.py:15
  1387.4 35.3 %collective-permute-start.54 = (bf16[64,128]{1,0:T(8,128)(2,1)S(1)}, bf16[64,128]{1,0:T(8,128)(2,1)S(1)}, u32[]{:S(2)}, u32[]{:S(2)}) collective-permute-start(bf16[64,128]{1,0:T(8,128)(2,1)S(1)} %bitcast.422), channel_id=1, source_target_pairs={{1,0},{2,1},{3,2},{4,3},{5,4},{6,5},{7,6},{8,7},{9,8},{10,9},{11,1... | collective-permute-start | bytes 49160 | tf_op jit(solution)/shard_map/ppermute | solution.py:15
  1391.5 38.0 %collective-permute-start.57 = (bf16[64,128]{1,0:T(8,128)(2,1)}, bf16[64,128]{1,0:T(8,128)(2,1)}, u32[]{:S(2)}, u32[]{:S(2)}) collective-permute-start(bf16[64,128]{1,0:T(8,128)(2,1)} %bitcast.355), channel_id=1, source_target_pairs={{16,0},{32,16},{48,32},{64,48},{80,64},{96,80},{112,96},{128,112},... | collective-permute-start | bytes 49160 | tf_op jit(solution)/shard_map/ppermute | solution.py:15
  1392.8 38.1 %collective-permute-start.49 = (bf16[64,128]{1,0:T(8,128)(2,1)}, bf16[64,128]{1,0:T(8,128)(2,1)}, u32[]{:S(2)}, u32[]{:S(2)}) collective-permute-start(bf16[64,128]{1,0:T(8,128)(2,1)} %collective-permute-done.48), channel_id=1, source_target_pairs={{0,1},{1,2},{2,3},{3,4},{4,5},{5,6},{6,7},{7,8},{8,9},{9,10},{10,1... | collective-permute-start | bytes 49160 | tf_op jit(solution)/shard_map/ppermute | solution.py:15
  1406.3 26.0 %collective-permute-start.52 = (bf16[64,128]{1,0:T(8,128)(2,1)}, bf16[64,128]{1,0:T(8,128)(2,1)}, u32[]{:S(2)}, u32[]{:S(2)}) collective-permute-start(bf16[64,128]{1,0:T(8,128)(2,1)} %collective-permute-done.51), channel_id=1, source_target_pairs={{1,0},{2,1},{3,2},{4,3},{5,4},{6,5},{7,6},{8,7},{9,8},{10,9},{11,1... | collective-permute-start | bytes 49160 | tf_op jit(solution)/shard_map/ppermute | solution.py:15
  1408.3 25.4 %collective-permute-start.56 = (bf16[64,128]{1,0:T(8,128)(2,1)}, bf16[64,128]{1,0:T(8,128)(2,1)}, u32[]{:S(2)}, u32[]{:S(2)}) collective-permute-start(bf16[64,128]{1,0:T(8,128)(2,1)} %collective-permute-done.55), channel_id=1, source_target_pairs={{0,1},{1,2},{2,3},{3,4},{4,5},{5,6},{6,7},{7,8},{8,9},{9,10},{10,1... | collective-permute-start | bytes 49160 | tf_op jit(solution)/shard_map/ppermute | solution.py:15
  1422.8 15.5 %collective-permute-start.59 = (bf16[64,128]{1,0:T(8,128)(2,1)}, bf16[64,128]{1,0:T(8,128)(2,1)}, u32[]{:S(2)}, u32[]{:S(2)}) collective-permute-start(bf16[64,128]{1,0:T(8,128)(2,1)} %collective-permute-done.58), channel_id=1, source_target_pairs={{1,0},{2,1},{3,2},{4,3},{5,4},{6,5},{7,6},{8,7},{9,8},{10,9},{11,1... | collective-permute-start | bytes 49160 | tf_op jit(solution)/shard_map/ppermute | solution.py:15
  (22 other events, 230.6 us)
where the time goes:
time: 1470 us; the launch traced here: 1450 us
  blocking collectives  1010 us (69%)
  starting transfers between devices  263 us (18%)
  local copies, waits for them, and re-layouts  105 us (7%)
  matrix products  52.9 us (4%)
  waiting for transfers between devices  18 us (1%)
    all_gather x5, blocking collectives, coarse_solve(): lax.all_gather(flat_piece, 'row', axis=0, tiled=True).reshape(-1, columns)  602 us
    psum x3, blocking collectives, coarse_solve(): summed = lax.psum(partial_sums.reshape(-1, 128), 'col')  407 us
    ppermute x60, starting transfers between devices, passed_along(): return lax.ppermute(block, axis, route)  263 us
    another operation x45, local copies, waits for them, and re-layouts, neighbour_pieces(): return jnp.stack(arrived, 0)  50 us
  transfers between devices with their start and end apart: 60, of which 3 were waited for; matrix products, arithmetic and copies ran while one was open for 5% of the time, Pallas kernels for 0%

commit v1 on v0

--- a/solution.py
+++ b/solution.py
@@ -9,31 +9,63 @@
 OFFSETS = ((-1, -1), (-1, 0), (-1, 1), (0, -1), (0, 1), (1, -1), (1, 0), (1, 1))
 
 
-def passed_along(block, axis, distance):
-    devices = range(lax.axis_size(axis))
-    route = [(i - distance, i) for i in devices if i - distance in devices]
-    return lax.ppermute(block, axis, route)
-
-
-def hop_rows(portion, steps):
-    return passed_along(portion, "row", steps)
-
-
-def hop_cols(portion, steps):
-    return passed_along(portion, "col", steps)
-
-
 def neighbour_pieces(outgoing):
+    rows = lax.axis_size("row")
+    cols = lax.axis_size("col")
     arrived = []
     for direction in range(8):
         shift_a, shift_b = OFFSETS[direction]
         portion = outgoing[7 - direction]
-        if shift_a != 0:
-            portion = hop_rows(portion, -shift_a)
-        if shift_b != 0:
-            portion = hop_cols(portion, -shift_b)
-        arrived.append(portion)
+        route = []
+        for a in range(rows):
+            for b in range(cols):
+                src_a, src_b = a + shift_a, b + shift_b
+                if 0 <= src_a < rows and 0 <= src_b < cols:
+                    route.append((src_a * cols + src_b, a * cols + b))
+        if shift_a == 0:
+            route = [(s % cols, t % cols) for s, t in route if s // cols == 0]
+            arrived.append(lax.ppermute(portion, "col", route))
+        elif shift_b == 0:
+            route = [(s // cols, t // cols) for s, t in route if s % cols == 0]
+            arrived.append(lax.ppermute(portion, "row", route))
+        else:
+            arrived.append(lax.ppermute(portion, ("row", "col"), route))
     return jnp.stack(arrived, 0)
+
+
+def gather_rows(piece, bits):
+    index = lax.axis_index("row")
+    size = lax.axis_size("row")
+    current = piece
+    for step, bit in enumerate(bits):
+        distance = 1 << bit
+        route = [(i, i ^ distance) for i in range(size)]
+        other = lax.ppermute(current, "row", route)
+        high = ((index >> bit) & 1) == 1
+        low_part = jnp.where(high, other, current)
+        high_part = jnp.where(high, current, other)
+        current = jnp.stack([low_part, high_part], axis=step)
+    return current
+
+
+def scatter_cols(partial, bits):
+    index = lax.axis_index("col")
+    size = lax.axis_size("col")
+    total_bits = len(bits)
+    current = partial
+    remaining = list(range(total_bits - 1, -1, -1))
+    for bit in bits:
+        axis = remaining.index(bit)
+        distance = 1 << bit
+        route = [(i, i ^ distance) for i in range(size)]
+        high = ((index >> bit) & 1) == 1
+        low_part = lax.index_in_dim(current, 0, axis, keepdims=False)
+        high_part = lax.index_in_dim(current, 1, axis, keepdims=False)
+        keep = jnp.where(high, high_part, low_part)
+        send = jnp.where(high, low_part, high_part)
+        current = keep + lax.ppermute(send, "col", route)
+        remaining.pop(axis)
+    return current
 
 
 def on_device(
@@ -53,7 +85,8 @@
     block_size = coupling.shape[3]
     block_count = unknowns // block_size
     mode_count = modes.shape[2]
-    piece_rows = mode_count * columns // 128
+    row_bits = lax.axis_size("row").bit_length() - 1
+    col_bits = lax.axis_size("col").bit_length() - 1
     rhs_full = rhs[0, 0].astype(jnp.float32)
     operator_matrix = operator_blocks[0, 0]
     solver_matrix = local_solver[0, 0]
@@ -67,20 +100,19 @@
     block_onehot = (slot_block[0, 0][:, None] == jnp.arange(block_count)[None, :]).astype(
         jnp.float32
     )
-    col_index = lax.axis_index("col")
 
     def coarse_solve(rounded):
         restricted = lax.dot_general(
             mode_basis, rounded, (((1,), (1,)), ((), ())), preferred_element_type=jnp.float32
-        )
-        flat_piece = restricted.astype(jnp.bfloat16).reshape(piece_rows, 128)
-        gathered = lax.all_gather(flat_piece, "row", axis=0, tiled=True).reshape(-1, columns)
+        ).astype(jnp.bfloat16)
+        gathered = gather_rows(restricted, list(range(row_bits - 1, -1, -1)))
+        gathered = gathered.reshape(-1, columns)
         partial_sums = lax.dot_general(
             coarse_tile, gathered, (((0,), (0,)), ((), ())), preferred_element_type=jnp.float32
         )
-        summed = lax.psum(partial_sums.reshape(-1, 128), "col")
-        own_rows = lax.dynamic_slice_in_dim(summed, col_index * piece_rows, piece_rows, 0)
-        return own_rows.reshape(mode_count, columns).astype(jnp.bfloat16)
+        partial_sums = partial_sums.reshape((2,) * col_bits + (mode_count, columns))
+        own_rows = scatter_cols(partial_sums, list(range(col_bits)))
+        return own_rows.astype(jnp.bfloat16)
 
     solution = jnp.zeros((columns, unknowns), jnp.float32)
     pending = None

time: 1470 us -> 700 us (0.48)
  the two profiles are of different devices: /device:TPU:6 before, /device:TPU:38 now
where the time goes in v1:
time: 700 us; the launch traced here: 695 us
  starting transfers between devices  420 us (60%)
  local copies, waits for them, and re-layouts  106 us (15%)
  waiting for transfers between devices  86.7 us (12%)
  matrix products  51.2 us (7%)
  other arithmetic  29.8 us (4%)
    ppermute x20, starting transfers between devices, neighbour_pieces(): arrived.append(lax.ppermute(portion, ('row', 'col'), route))  143 us
    ppermute x25, starting transfers between devices, gather_rows(): other = lax.ppermute(current, 'row', route)  107 us
    ppermute x20, starting transfers between devices, scatter_cols(): current = keep + lax.ppermute(send, 'col', route)  87.5 us
    ppermute x10, starting transfers between devices, neighbour_pieces(): arrived.append(lax.ppermute(portion, 'col', route))  48 us
    ppermute x20, waiting for transfers between devices, scatter_cols(): current = keep + lax.ppermute(send, 'col', route)  37.5 us
    ppermute x10, starting transfers between devices, neighbour_pieces(): arrived.append(lax.ppermute(portion, 'row', route))  34.5 us
    ppermute x20, waiting for transfers between devices, neighbour_pieces(): arrived.append(lax.ppermute(portion, ('row', 'col'), route))  30.8 us
    another operation x45, local copies, waits for them, and re-layouts, neighbour_pieces(): return jnp.stack(arrived, 0)  28.4 us
  transfers between devices with their start and end apart: 85, of which 29 were waited for; matrix products, arithmetic and copies ran while one was open for 22% of the time, Pallas kernels for 0%

profile of v1, /device:TPU:38, one launch (start us, length us, event | category | flops | bytes accessed | tf_op | source)
XLA Modules:
  0.0 695.4 jit_solution(6328337562070991059)
XLA Ops:
  1.2 9.1 %collective-permute-start.8 = (bf16[48,64]{1,0:T(8,128)(2,1)S(1)}, bf16[48,64]{1,0:T(8,128)(2,1)S(1)}, u32[]{:S(2)}, u32[]{:S(2)}) collective-permute-start(bf16[48,64]{1,0:T(8,128)(2,1)S(1)} %convolution_convert_fusion.14), channel_id=1, source_target_pairs={{0,256},{16,272},{32,288},{48,304},{64,320},{80,336},{96,352},{112... | collective-permute-start | bytes 18440 | tf_op jit(solution)/shard_map/ppermute | solution.py:43
  16.5 3.5 collective-permute-start.1
  20.0 4.4 collective-permute-start.2
  24.4 7.6 %collective-permute-start.3 = (bf16[64,128]{1,0:T(8,128)(2,1)S(1)}, bf16[64,128]{1,0:T(8,128)(2,1)S(1)}, u32[]{:S(2)}, u32[]{:S(2)}) collective-permute-start(bf16[64,128]{1,0:T(8,128)(2,1)S(1)} %bitcast.636), channel_id=1, source_target_pairs={{0,1},{1,2},{2,3},{3,4},{4,5},{5,6},{6,7},{7,8},{8,9},{9,10},{10,1... | collective-permute-start | bytes 49160 | tf_op jit(solution)/shard_map/ppermute | solution.py:27
  34.0 16.7 %collective-permute-start.5 = (bf16[64,128]{1,0:T(8,128)(2,1)S(1)}, bf16[64,128]{1,0:T(8,128)(2,1)S(1)}, u32[]{:S(2)}, u32[]{:S(2)}) collective-permute-start(bf16[64,128]{1,0:T(8,128)(2,1)S(1)} %bitcast.646), channel_id=1, source_target_pairs={{16,1},{17,2},{18,3},{19,4},{20,5},{21,6},{22,7},{23,8},{24,9},{25... | collective-permute-start | bytes 49160 | tf_op jit(solution)/shard_map/ppermute | solution.py:32
  50.8 3.3 collective-permute-start.6
  56.7 3.4 collective-permute-start.9
  60.3 8.6 %collective-permute-done.7 = bf16[64,128]{1,0:T(8,128)(2,1)S(1)} collective-permute-done((bf16[64,128]{1,0:T(8,128)(2,1)S(1)}, bf16[64,128]{1,0:T(8,128)(2,1)S(1)}, u32[]{:S(2)}, u32[]{:S(2)}) %collective-permute-start.7) | collective-permute-done | bytes 16416 | tf_op jit(solution)/shard_map/ppermute | solution.py:32
  74.7 5.5 collective-permute-start.25
  80.9 3.3 collective-permute-done.25
  84.2 3.4 collective-permute-start.26
  93.6 4.6 collective-permute-start.11
  101.7 5.5 collective-permute-start.12
  108.7 5.4 collective-permute-start.29
  132.1 7.7 %collective-permute-start.13 = (f32[2,2,2,48,64]{4,3,0,1,2:T(8,128)}, f32[2,2,2,48,64]{4,3,0,1,2:T(8,128)}, u32[]{:S(2)}, u32[]{:S(2)}) collective-permute-start(f32[2,2,2,48,64]{4,3,0,1,2:T(8,128)} %get-tuple-element.24), channel_id=1, source_target_pairs={{0,1},{1,0},{2,3},{3,2},{4,5},{5,4},{6,7},{7,6},{8,9},{9,8},{10,11... | collective-permute-start | bytes 294920 | tf_op jit(solution)/shard_map/ppermute | solution.py:66
  163.2 3.9 collective-permute-start.31
  170.4 5.5 collective-permute-done.15
  175.9 4.4 collective-permute-start.16
  181.0 5.4 collective-permute-start.32
  186.4 4.0 collective-permute-done.16
  196.3 3.5 collective-permute-start.18
  199.8 3.6 collective-permute-start.19
  203.4 7.0 %collective-permute-start.20 = (bf16[64,128]{1,0:T(8,128)(2,1)S(1)}, bf16[64,128]{1,0:T(8,128)(2,1)S(1)}, u32[]{:S(2)}, u32[]{:S(2)}) collective-permute-start(bf16[64,128]{1,0:T(8,128)(2,1)S(1)} %bitcast.668), channel_id=1, source_target_pairs={{0,1},{1,2},{2,3},{3,4},{4,5},{5,6},{6,7},{7,8},{8,9},{9,10},{10,1... | collective-permute-start | bytes 49160 | tf_op jit(solution)/shard_map/ppermute | solution.py:27
  213.2 16.7 %collective-permute-start.22 = (bf16[64,128]{1,0:T(8,128)(2,1)S(1)}, bf16[64,128]{1,0:T(8,128)(2,1)S(1)}, u32[]{:S(2)}, u32[]{:S(2)}) collective-permute-start(bf16[64,128]{1,0:T(8,128)(2,1)S(1)} %bitcast.651), channel_id=1, source_target_pairs={{16,1},{17,2},{18,3},{19,4},{20,5},{21,6},{22,7},{23,8},{24,9},{25... | collective-permute-start | bytes 49160 | tf_op jit(solution)/shard_map/ppermute | solution.py:32
  242.2 5.9 collective-permute-done.24
  255.4 5.3 collective-permute-start.42
  265.5 15.1 %collective-permute-start.34 = (bf16[64,128]{1,0:T(8,128)(2,1)S(1)}, bf16[64,128]{1,0:T(8,128)(2,1)S(1)}, u32[]{:S(2)}, u32[]{:S(2)}) collective-permute-start(bf16[64,128]{1,0:T(8,128)(2,1)S(1)} %bitcast.689), channel_id=1, source_target_pairs={{0,17},{1,18},{2,19},{3,20},{4,21},{5,22},{6,23},{7,24},{8,25},{9,... | collective-permute-start | bytes 49160 | tf_op jit(solution)/shard_map/ppermute | solution.py:32
  285.2 7.6 %collective-permute-start.37 = (bf16[64,128]{1,0:T(8,128)(2,1)S(1)}, bf16[64,128]{1,0:T(8,128)(2,1)S(1)}, u32[]{:S(2)}, u32[]{:S(2)}) collective-permute-start(bf16[64,128]{1,0:T(8,128)(2,1)S(1)} %bitcast.666), channel_id=1, source_target_pairs={{0,1},{1,2},{2,3},{3,4},{4,5},{5,6},{6,7},{7,8},{8,9},{9,10},{10,1... | collective-permute-start | bytes 49160 | tf_op jit(solution)/shard_map/ppermute | solution.py:27
  295.6 16.7 %collective-permute-start.39 = (bf16[64,128]{1,0:T(8,128)(2,1)S(1)}, bf16[64,128]{1,0:T(8,128)(2,1)S(1)}, u32[]{:S(2)}, u32[]{:S(2)}) collective-permute-start(bf16[64,128]{1,0:T(8,128)(2,1)S(1)} %bitcast.648), channel_id=1, source_target_pairs={{16,1},{17,2},{18,3},{19,4},{20,5},{21,6},{22,7},{23,8},{24,9},{25... | collective-permute-start | bytes 49160 | tf_op jit(solution)/shard_map/ppermute | solution.py:32
  312.4 4.5 collective-permute-start.40
  321.4 4.6 collective-permute-start.43
  339.1 4.5 collective-permute-start.59
  344.4 4.2 collective-permute-done.59
  348.7 4.6 collective-permute-start.60
  355.3 3.8 collective-permute-start.61
  359.3 4.4 collective-permute-start.45
  363.8 3.2 collective-permute-start.62
  367.4 5.3 collective-permute-start.46
  374.1 5.4 collective-permute-start.63
  397.2 9.8 %collective-permute-start.47 = (f32[2,2,2,48,64]{4,3,0,1,2:T(8,128)}, f32[2,2,2,48,64]{4,3,0,1,2:T(8,128)}, u32[]{:S(2)}, u32[]{:S(2)}) collective-permute-start(f32[2,2,2,48,64]{4,3,0,1,2:T(8,128)} %select_bitcast_fusion.6), channel_id=1, source_target_pairs={{0,1},{1,0},{2,3},{3,2},{4,5},{5,4},{6,7},{7,6},{8,9},{9,8},{10,11... | collective-permute-start | bytes 294920 | tf_op jit(solution)/shard_map/ppermute | solution.py:66
  430.5 3.9 collective-permute-start.65
  437.8 5.5 collective-permute-done.49
  443.2 7.9 %collective-permute-start.50 = (f32[48,64]{1,0:T(8,128)S(1)}, f32[48,64]{1,0:T(8,128)S(1)}, u32[]{:S(2)}, u32[]{:S(2)}) collective-permute-start(f32[48,64]{1,0:T(8,128)S(1)} %select_bitcast_fusion.52), channel_id=1, source_target_pairs={{0,8},{1,9},{2,10},{3,11},{4,12},{5,13},{6,14},{7,15},{8,0},{9,1},... | collective-permute-start | bytes 36872 | tf_op jit(solution)/shard_map/ppermute | solution.py:66
  451.8 5.6 collective-permute-start.66
  466.3 4.9 collective-permute-start.53
  471.3 8.7 %collective-permute-start.54 = (bf16[64,128]{1,0:T(8,128)(2,1)S(1)}, bf16[64,128]{1,0:T(8,128)(2,1)S(1)}, u32[]{:S(2)}, u32[]{:S(2)}) collective-permute-start(bf16[64,128]{1,0:T(8,128)(2,1)S(1)} %bitcast.672), channel_id=1, source_target_pairs={{0,1},{1,2},{2,3},{3,4},{4,5},{5,6},{6,7},{7,8},{8,9},{9,10},{10,1... | collective-permute-start | bytes 49160 | tf_op jit(solution)/shard_map/ppermute | solution.py:27
  482.1 16.7 %collective-permute-start.56 = (bf16[64,128]{1,0:T(8,128)(2,1)S(1)}, bf16[64,128]{1,0:T(8,128)(2,1)S(1)}, u32[]{:S(2)}, u32[]{:S(2)}) collective-permute-start(bf16[64,128]{1,0:T(8,128)(2,1)S(1)} %bitcast.663), channel_id=1, source_target_pairs={{16,1},{17,2},{18,3},{19,4},{20,5},{21,6},{22,7},{23,8},{24,9},{25... | collective-permute-start | bytes 49160 | tf_op jit(solution)/shard_map/ppermute | solution.py:32
  498.8 3.1 collective-permute-start.57
  509.8 7.1 %collective-permute-done.58 = bf16[64,128]{1,0:T(8,128)(2,1)S(1)} collective-permute-done((bf16[64,128]{1,0:T(8,128)(2,1)S(1)}, bf16[64,128]{1,0:T(8,128)(2,1)S(1)}, u32[]{:S(2)}, u32[]{:S(2)}) %collective-permute-start.58) | collective-permute-done | bytes 16416 | tf_op jit(solution)/shard_map/ppermute | solution.py:32
  523.9 4.9 collective-permute-start.76
  533.4 4.2 collective-permute-start.77
  548.0 3.4 collective-permute-start.79
  552.6 3.5 collective-permute-done.79
  557.4 4.3 collective-permute-start.80
  561.9 11.0 %collective-permute-start.68 = (bf16[64,128]{1,0:T(8,128)(2,1)S(1)}, bf16[64,128]{1,0:T(8,128)(2,1)S(1)}, u32[]{:S(2)}, u32[]{:S(2)}) collective-permute-start(bf16[64,128]{1,0:T(8,128)(2,1)S(1)} %bitcast.710), channel_id=1, source_target_pairs={{0,17},{1,18},{2,19},{3,20},{4,21},{5,22},{6,23},{7,24},{8,25},{9,... | collective-permute-start | bytes 49160 | tf_op jit(solution)/shard_map/ppermute | solution.py:32
  572.9 3.6 collective-permute-start.69
  578.5 7.5 %collective-permute-start.71 = (bf16[64,128]{1,0:T(8,128)(2,1)S(1)}, bf16[64,128]{1,0:T(8,128)(2,1)S(1)}, u32[]{:S(2)}, u32[]{:S(2)}) collective-permute-start(bf16[64,128]{1,0:T(8,128)(2,1)S(1)} %bitcast.704), channel_id=1, source_target_pairs={{0,1},{1,2},{2,3},{3,4},{4,5},{5,6},{6,7},{7,8},{8,9},{9,10},{10,1... | collective-permute-start | bytes 49160 | tf_op jit(solution)/shard_map/ppermute | solution.py:27
  588.0 16.7 %collective-permute-start.73 = (bf16[64,128]{1,0:T(8,128)(2,1)S(1)}, bf16[64,128]{1,0:T(8,128)(2,1)S(1)}, u32[]{:S(2)}, u32[]{:S(2)}) collective-permute-start(bf16[64,128]{1,0:T(8,128)(2,1)S(1)} %bitcast.678), channel_id=1, source_target_pairs={{16,1},{17,2},{18,3},{19,4},{20,5},{21,6},{22,7},{23,8},{24,9},{25... | collective-permute-start | bytes 49160 | tf_op jit(solution)/shard_map/ppermute | solution.py:32
  604.8 4.5 collective-permute-start.74
  615.7 7.2 %collective-permute-done.75 = bf16[64,128]{1,0:T(8,128)(2,1)S(1)} collective-permute-done((bf16[64,128]{1,0:T(8,128)(2,1)S(1)}, bf16[64,128]{1,0:T(8,128)(2,1)S(1)}, u32[]{:S(2)}, u32[]{:S(2)}) %collective-permute-start.75) | collective-permute-done | bytes 16416 | tf_op jit(solution)/shard_map/ppermute | solution.py:32
  643.6 17.3 %collective-permute-start.81 = (f32[2,2,2,48,64]{4,3,0,1,2:T(8,128)S(1)}, f32[2,2,2,48,64]{4,3,0,1,2:T(8,128)S(1)}, u32[]{:S(2)}, u32[]{:S(2)}) collective-permute-start(f32[2,2,2,48,64]{4,3,0,1,2:T(8,128)S(1)} %select_bitcast_fusion), channel_id=1, source_target_pairs={{0,1},{1,0},{2,3},{3,2},{4,5},{5,4},{6,7},{7,6},{8,9},{9,8},{10,11... | collective-permute-start | bytes 294920 | tf_op jit(solution)/shard_map/ppermute | solution.py:66
  665.1 4.8 collective-permute-done.82
  673.0 4.4 collective-permute-done.83
  683.2 10.2 %collective-permute-done.84 = f32[48,64]{1,0:T(8,128)} collective-permute-done((f32[48,64]{1,0:T(8,128)}, f32[48,64]{1,0:T(8,128)}, u32[]{:S(2)}, u32[]{:S(2)}) %collective-permute-start.84) | collective-permute-done | bytes 12320 | tf_op jit(solution)/shard_map/ppermute | solution.py:66
  (455 shorter events, 271.1 us)
Async XLA Ops:
  1.2 30.8 %collective-permute-start.8 = (bf16[48,64]{1,0:T(8,128)(2,1)S(1)}, bf16[48,64]{1,0:T(8,128)(2,1)S(1)}, u32[]{:S(2)}, u32[]{:S(2)}) collective-permute-start(bf16[48,64]{1,0:T(8,128)(2,1)S(1)} %convolution_convert_fusion.14), channel_id=1, source_target_pairs={{0,256},{16,272},{32,288},{48,304},{64,320},{80,336},{96,352},{112... | collective-permute-start | bytes 18440 | tf_op jit(solution)/shard_map/ppermute | solution.py:43
  13.8 20.2 %collective-permute-start = (bf16[64,128]{1,0:T(8,128)(2,1)S(1)}, bf16[64,128]{1,0:T(8,128)(2,1)S(1)}, u32[]{:S(2)}, u32[]{:S(2)}) collective-permute-start(bf16[64,128]{1,0:T(8,128)(2,1)S(1)} %bitcast.639), channel_id=1, source_target_pairs={{0,17},{1,18},{2,19},{3,20},{4,21},{5,22},{6,23},{7,24},{8,25},{9,... | collective-permute-start | bytes 49160 | tf_op jit(solution)/shard_map/ppermute | solution.py:32
  16.5 34.3 %collective-permute-start.1 = (bf16[64,128]{1,0:T(8,128)(2,1)S(1)}, bf16[64,128]{1,0:T(8,128)(2,1)S(1)}, u32[]{:S(2)}, u32[]{:S(2)}) collective-permute-start(bf16[64,128]{1,0:T(8,128)(2,1)S(1)} %bitcast.638), channel_id=1, source_target_pairs={{0,16},{16,32},{32,48},{48,64},{64,80},{80,96},{96,112},{112,128},... | collective-permute-start | bytes 49160 | tf_op jit(solution)/shard_map/ppermute | solution.py:30
  20.0 34.1 %collective-permute-start.2 = (bf16[64,128]{1,0:T(8,128)(2,1)S(1)}, bf16[64,128]{1,0:T(8,128)(2,1)S(1)}, u32[]{:S(2)}, u32[]{:S(2)}) collective-permute-start(bf16[64,128]{1,0:T(8,128)(2,1)S(1)} %bitcast.637), channel_id=1, source_target_pairs={{1,16},{2,17},{3,18},{4,19},{5,20},{6,21},{7,22},{8,23},{9,24},{10... | collective-permute-start | bytes 49160 | tf_op jit(solution)/shard_map/ppermute | solution.py:32
  24.4 32.3 %collective-permute-start.3 = (bf16[64,128]{1,0:T(8,128)(2,1)S(1)}, bf16[64,128]{1,0:T(8,128)(2,1)S(1)}, u32[]{:S(2)}, u32[]{:S(2)}) collective-permute-start(bf16[64,128]{1,0:T(8,128)(2,1)S(1)} %bitcast.636), channel_id=1, source_target_pairs={{0,1},{1,2},{2,3},{3,4},{4,5},{5,6},{6,7},{7,8},{8,9},{9,10},{10,1... | collective-permute-start | bytes 49160 | tf_op jit(solution)/shard_map/ppermute | solution.py:27
  32.1 28.1 %collective-permute-start.4 = (bf16[64,128]{1,0:T(8,128)(2,1)S(1)}, bf16[64,128]{1,0:T(8,128)(2,1)S(1)}, u32[]{:S(2)}, u32[]{:S(2)}) collective-permute-start(bf16[64,128]{1,0:T(8,128)(2,1)S(1)} %bitcast.654), channel_id=1, source_target_pairs={{1,0},{2,1},{3,2},{4,3},{5,4},{6,5},{7,6},{8,7},{9,8},{10,9},{11,1... | collective-permute-start | bytes 49160 | tf_op jit(solution)/shard_map/ppermute | solution.py:27
  34.0 26.2 %collective-permute-start.5 = (bf16[64,128]{1,0:T(8,128)(2,1)S(1)}, bf16[64,128]{1,0:T(8,128)(2,1)S(1)}, u32[]{:S(2)}, u32[]{:S(2)}) collective-permute-start(bf16[64,128]{1,0:T(8,128)(2,1)S(1)} %bitcast.646), channel_id=1, source_target_pairs={{16,1},{17,2},{18,3},{19,4},{20,5},{21,6},{22,7},{23,8},{24,9},{25... | collective-permute-start | bytes 49160 | tf_op jit(solution)/shard_map/ppermute | solution.py:32
  50.8 9.4 %collective-permute-start.6 = (bf16[64,128]{1,0:T(8,128)(2,1)S(1)}, bf16[64,128]{1,0:T(8,128)(2,1)S(1)}, u32[]{:S(2)}, u32[]{:S(2)}) collective-permute-start(bf16[64,128]{1,0:T(8,128)(2,1)S(1)} %bitcast.643), channel_id=1, source_target_pairs={{16,0},{32,16},{48,32},{64,48},{80,64},{96,80},{112,96},{128,112},... | collective-permute-start | bytes 49160 | tf_op jit(solution)/shard_map/ppermute | solution.py:30
  54.1 14.8 %collective-permute-start.7 = (bf16[64,128]{1,0:T(8,128)(2,1)S(1)}, bf16[64,128]{1,0:T(8,128)(2,1)S(1)}, u32[]{:S(2)}, u32[]{:S(2)}) collective-permute-start(bf16[64,128]{1,0:T(8,128)(2,1)S(1)} %bitcast.640), channel_id=1, source_target_pairs={{17,0},{18,1},{19,2},{20,3},{21,4},{22,5},{23,6},{24,7},{25,8},{26... | collective-permute-start | bytes 49160 | tf_op jit(solution)/shard_map/ppermute | solution.py:32
  56.7 23.4 %collective-permute-start.9 = (bf16[2,48,64]{2,1,0:T(8,128)(2,1)}, bf16[2,48,64]{2,1,0:T(8,128)(2,1)}, u32[]{:S(2)}, u32[]{:S(2)}) collective-permute-start(bf16[2,48,64]{2,1,0:T(8,128)(2,1)} %pad_maximum_fusion.20), channel_id=1, source_target_pairs={{0,128},{16,144},{32,160},{48,176},{64,192},{80,208},{96,224},{112... | collective-permute-start | bytes 36872 | tf_op jit(solution)/shard_map/ppermute | solution.py:43
  74.7 9.5 %collective-permute-start.25 = (bf16[48,64]{1,0:T(8,128)(2,1)S(1)}, bf16[48,64]{1,0:T(8,128)(2,1)S(1)}, u32[]{:S(2)}, u32[]{:S(2)}) collective-permute-start(bf16[48,64]{1,0:T(8,128)(2,1)S(1)} %fusion.100), channel_id=1, source_target_pairs={{0,256},{16,272},{32,288},{48,304},{64,320},{80,336},{96,352},{112... | collective-permute-start | bytes 18440 | tf_op jit(solution)/shard_map/ppermute | solution.py:43
  98.3 9.0 %collective-permute-start.28 = (bf16[2,2,2,48,64]{4,3,0,1,2:T(8,128)(2,1)S(1)}, bf16[2,2,2,48,64]{4,3,0,1,2:T(8,128)(2,1)S(1)}, u32[]{:S(2)}, u32[]{:S(2)}) collective-permute-start(bf16[2,2,2,48,64]{4,3,0,1,2:T(8,128)(2,1)S(1)} %pad_maximum_fusion.11), channel_id=1, source_target_pairs={{0,32},{16,48},{32,0},{48,16},{64,96},{80,112},{96,64},{112,80},{1... | collective-permute-start | bytes 147464 | tf_op jit(solution)/shard_map/ppermute | solution.py:43
  101.7 12.3 %collective-permute-start.12 = (bf16[2,2,2,2,48,64]{5,4,0,1,2,3:T(8,128)(2,1)S(1)}, bf16[2,2,2,2,48,64]{5,4,0,1,2,3:T(8,128)(2,1)S(1)}, u32[]{:S(2)}, u32[]{:S(2)}) collective-permute-start(bf16[2,2,2,2,48,64]{5,4,0,1,2,3:T(8,128)(2,1)S(1)} %pad_maximum_fusion.5), channel_id=1, source_target_pairs={{0,16},{16,0},{32,48},{48,32},{64,80},{80,64},{96,112},{112,96},{1... | collective-permute-start | bytes 294920 | tf_op jit(solution)/shard_map/ppermute | solution.py:43
  108.7 31.1 %collective-permute-start.29 = (bf16[2,2,2,2,48,64]{5,4,0,1,2,3:T(8,128)(2,1)}, bf16[2,2,2,2,48,64]{5,4,0,1,2,3:T(8,128)(2,1)}, u32[]{:S(2)}, u32[]{:S(2)}) collective-permute-start(bf16[2,2,2,2,48,64]{5,4,0,1,2,3:T(8,128)(2,1)} %pad_maximum_fusion.6), channel_id=1, source_target_pairs={{0,16},{16,0},{32,48},{48,32},{64,80},{80,64},{96,112},{112,96},{1... | collective-permute-start | bytes 294920 | tf_op jit(solution)/shard_map/ppermute | solution.py:43
  132.1 27.9 %collective-permute-start.13 = (f32[2,2,2,48,64]{4,3,0,1,2:T(8,128)}, f32[2,2,2,48,64]{4,3,0,1,2:T(8,128)}, u32[]{:S(2)}, u32[]{:S(2)}) collective-permute-start(f32[2,2,2,48,64]{4,3,0,1,2:T(8,128)} %get-tuple-element.24), channel_id=1, source_target_pairs={{0,1},{1,0},{2,3},{3,2},{4,5},{5,4},{6,7},{7,6},{8,9},{9,8},{10,11... | collective-permute-start | bytes 294920 | tf_op jit(solution)/shard_map/ppermute | solution.py:66
  175.9 14.4 %collective-permute-start.16 = (f32[48,64]{1,0:T(8,128)S(1)}, f32[48,64]{1,0:T(8,128)S(1)}, u32[]{:S(2)}, u32[]{:S(2)}) collective-permute-start(f32[48,64]{1,0:T(8,128)S(1)} %select_bitcast_fusion.58), channel_id=1, source_target_pairs={{0,8},{1,9},{2,10},{3,11},{4,12},{5,13},{6,14},{7,15},{8,0},{9,1},... | collective-permute-start | bytes 36872 | tf_op jit(solution)/shard_map/ppermute | solution.py:66
  181.0 29.5 %collective-permute-start.32 = (f32[2,48,64]{2,1,0:T(8,128)}, f32[2,48,64]{2,1,0:T(8,128)}, u32[]{:S(2)}, u32[]{:S(2)}) collective-permute-start(f32[2,48,64]{2,1,0:T(8,128)} %select_bitcast_fusion.40), channel_id=1, source_target_pairs={{0,4},{1,5},{2,6},{3,7},{4,0},{5,1},{6,2},{7,3},{8,12},{9,13},{10,... | collective-permute-start | bytes 73736 | tf_op jit(solution)/shard_map/ppermute | solution.py:66
  194.4 18.9 %collective-permute-start.17 = (bf16[64,128]{1,0:T(8,128)(2,1)S(1)}, bf16[64,128]{1,0:T(8,128)(2,1)S(1)}, u32[]{:S(2)}, u32[]{:S(2)}) collective-permute-start(bf16[64,128]{1,0:T(8,128)(2,1)S(1)} %bitcast.693), channel_id=1, source_target_pairs={{0,17},{1,18},{2,19},{3,20},{4,21},{5,22},{6,23},{7,24},{8,25},{9,... | collective-permute-start | bytes 49160 | tf_op jit(solution)/shard_map/ppermute | solution.py:32
  196.3 33.7 %collective-permute-start.18 = (bf16[64,128]{1,0:T(8,128)(2,1)S(1)}, bf16[64,128]{1,0:T(8,128)(2,1)S(1)}, u32[]{:S(2)}, u32[]{:S(2)}) collective-permute-start(bf16[64,128]{1,0:T(8,128)(2,1)S(1)} %bitcast.686), channel_id=1, source_target_pairs={{0,16},{16,32},{32,48},{48,64},{64,80},{80,96},{96,112},{112,128},... | collective-permute-start | bytes 49160 | tf_op jit(solution)/shard_map/ppermute | solution.py:30
  199.8 33.3 %collective-permute-start.19 = (bf16[64,128]{1,0:T(8,128)(2,1)S(1)}, bf16[64,128]{1,0:T(8,128)(2,1)S(1)}, u32[]{:S(2)}, u32[]{:S(2)}) collective-permute-start(bf16[64,128]{1,0:T(8,128)(2,1)S(1)} %bitcast.683), channel_id=1, source_target_pairs={{1,16},{2,17},{3,18},{4,19},{5,20},{6,21},{7,22},{8,23},{9,24},{10... | collective-permute-start | bytes 49160 | tf_op jit(solution)/shard_map/ppermute | solution.py:32
  203.4 34.1 %collective-permute-start.20 = (bf16[64,128]{1,0:T(8,128)(2,1)S(1)}, bf16[64,128]{1,0:T(8,128)(2,1)S(1)}, u32[]{:S(2)}, u32[]{:S(2)}) collective-permute-start(bf16[64,128]{1,0:T(8,128)(2,1)S(1)} %bitcast.668), channel_id=1, source_target_pairs={{0,1},{1,2},{2,3},{3,4},{4,5},{5,6},{6,7},{7,8},{8,9},{9,10},{10,1... | collective-permute-start | bytes 49160 | tf_op jit(solution)/shard_map/ppermute | solution.py:27
  210.5 29.9 %collective-permute-start.21 = (bf16[64,128]{1,0:T(8,128)(2,1)S(1)}, bf16[64,128]{1,0:T(8,128)(2,1)S(1)}, u32[]{:S(2)}, u32[]{:S(2)}) collective-permute-start(bf16[64,128]{1,0:T(8,128)(2,1)S(1)} %bitcast.660), channel_id=1, source_target_pairs={{1,0},{2,1},{3,2},{4,3},{5,4},{6,5},{7,6},{8,7},{9,8},{10,9},{11,1... | collective-permute-start | bytes 49160 | tf_op jit(solution)/shard_map/ppermute | solution.py:27
  213.2 27.7 %collective-permute-start.22 = (bf16[64,128]{1,0:T(8,128)(2,1)S(1)}, bf16[64,128]{1,0:T(8,128)(2,1)S(1)}, u32[]{:S(2)}, u32[]{:S(2)}) collective-permute-start(bf16[64,128]{1,0:T(8,128)(2,1)S(1)} %bitcast.651), channel_id=1, source_target_pairs={{16,1},{17,2},{18,3},{19,4},{20,5},{21,6},{22,7},{23,8},{24,9},{25... | collective-permute-start | bytes 49160 | tf_op jit(solution)/shard_map/ppermute | solution.py:32
  230.0 11.6 %collective-permute-start.23 = (bf16[64,128]{1,0:T(8,128)(2,1)S(1)}, bf16[64,128]{1,0:T(8,128)(2,1)S(1)}, u32[]{:S(2)}, u32[]{:S(2)}) collective-permute-start(bf16[64,128]{1,0:T(8,128)(2,1)S(1)} %bitcast.645), channel_id=1, source_target_pairs={{16,0},{32,16},{48,32},{64,48},{80,64},{96,80},{112,96},{128,112},... | collective-permute-start | bytes 49160 | tf_op jit(solution)/shard_map/ppermute | solution.py:30
  233.1 15.0 %collective-permute-start.24 = (bf16[64,128]{1,0:T(8,128)(2,1)S(1)}, bf16[64,128]{1,0:T(8,128)(2,1)S(1)}, u32[]{:S(2)}, u32[]{:S(2)}) collective-permute-start(bf16[64,128]{1,0:T(8,128)(2,1)S(1)} %bitcast.642), channel_id=1, source_target_pairs={{17,0},{18,1},{19,2},{20,3},{21,4},{22,5},{23,6},{24,7},{25,8},{26... | collective-permute-start | bytes 49160 | tf_op jit(solution)/shard_map/ppermute | solution.py:32
  237.6 23.2 %collective-permute-start.33 = (f32[48,64]{1,0:T(8,128)}, f32[48,64]{1,0:T(8,128)}, u32[]{:S(2)}, u32[]{:S(2)}) collective-permute-start(f32[48,64]{1,0:T(8,128)} %select_bitcast_fusion.55), channel_id=1, source_target_pairs={{0,8},{1,9},{2,10},{3,11},{4,12},{5,13},{6,14},{7,15},{8,0},{9,1},... | collective-permute-start | bytes 36872 | tf_op jit(solution)/shard_map/ppermute | solution.py:66
  255.4 37.5 %collective-permute-start.42 = (bf16[48,64]{1,0:T(8,128)(2,1)S(1)}, bf16[48,64]{1,0:T(8,128)(2,1)}, u32[]{:S(2)}, u32[]{:S(2)}) collective-permute-start(bf16[48,64]{1,0:T(8,128)(2,1)S(1)} %fusion.101), channel_id=1, source_target_pairs={{0,256},{16,272},{32,288},{48,304},{64,320},{80,336},{96,352},{112... | collective-permute-start | bytes 18440 | tf_op jit(solution)/shard_map/ppermute | solution.py:43
  265.5 30.1 %collective-permute-start.34 = (bf16[64,128]{1,0:T(8,128)(2,1)S(1)}, bf16[64,128]{1,0:T(8,128)(2,1)S(1)}, u32[]{:S(2)}, u32[]{:S(2)}) collective-permute-start(bf16[64,128]{1,0:T(8,128)(2,1)S(1)} %bitcast.689), channel_id=1, source_target_pairs={{0,17},{1,18},{2,19},{3,20},{4,21},{5,22},{6,23},{7,24},{8,25},{9,... | collective-permute-start | bytes 49160 | tf_op jit(solution)/shard_map/ppermute | solution.py:32
  280.6 31.8 %collective-permute-start.35 = (bf16[64,128]{1,0:T(8,128)(2,1)S(1)}, bf16[64,128]{1,0:T(8,128)(2,1)S(1)}, u32[]{:S(2)}, u32[]{:S(2)}) collective-permute-start(bf16[64,128]{1,0:T(8,128)(2,1)S(1)} %bitcast.684), channel_id=1, source_target_pairs={{0,16},{16,32},{32,48},{48,64},{64,80},{80,96},{96,112},{112,128},... | collective-permute-start | bytes 49160 | tf_op jit(solution)/shard_map/ppermute | solution.py:30
  283.3 33.6 %collective-permute-start.36 = (bf16[64,128]{1,0:T(8,128)(2,1)S(1)}, bf16[64,128]{1,0:T(8,128)(2,1)S(1)}, u32[]{:S(2)}, u32[]{:S(2)}) collective-permute-start(bf16[64,128]{1,0:T(8,128)(2,1)S(1)} %bitcast.680), channel_id=1, source_target_pairs={{1,16},{2,17},{3,18},{4,19},{5,20},{6,21},{7,22},{8,23},{9,24},{10... | collective-permute-start | bytes 49160 | tf_op jit(solution)/shard_map/ppermute | solution.py:32
  285.2 36.1 %collective-permute-start.37 = (bf16[64,128]{1,0:T(8,128)(2,1)S(1)}, bf16[64,128]{1,0:T(8,128)(2,1)S(1)}, u32[]{:S(2)}, u32[]{:S(2)}) collective-permute-start(bf16[64,128]{1,0:T(8,128)(2,1)S(1)} %bitcast.666), channel_id=1, source_target_pairs={{0,1},{1,2},{2,3},{3,4},{4,5},{5,6},{6,7},{7,8},{8,9},{9,10},{10,1... | collective-permute-start | bytes 49160 | tf_op jit(solution)/shard_map/ppermute | solution.py:27
  293.0 33.6 %collective-permute-start.38 = (bf16[64,128]{1,0:T(8,128)(2,1)S(1)}, bf16[64,128]{1,0:T(8,128)(2,1)S(1)}, u32[]{:S(2)}, u32[]{:S(2)}) collective-permute-start(bf16[64,128]{1,0:T(8,128)(2,1)S(1)} %bitcast.657), channel_id=1, source_target_pairs={{1,0},{2,1},{3,2},{4,3},{5,4},{6,5},{7,6},{8,7},{9,8},{10,9},{11,1... | collective-permute-start | bytes 49160 | tf_op jit(solution)/shard_map/ppermute | solution.py:27
  295.6 31.6 %collective-permute-start.39 = (bf16[64,128]{1,0:T(8,128)(2,1)S(1)}, bf16[64,128]{1,0:T(8,128)(2,1)S(1)}, u32[]{:S(2)}, u32[]{:S(2)}) collective-permute-start(bf16[64,128]{1,0:T(8,128)(2,1)S(1)} %bitcast.648), channel_id=1, source_target_pairs={{16,1},{17,2},{18,3},{19,4},{20,5},{21,6},{22,7},{23,8},{24,9},{25... | collective-permute-start | bytes 49160 | tf_op jit(solution)/shard_map/ppermute | solution.py:32
  312.4 15.5 %collective-permute-start.40 = (bf16[64,128]{1,0:T(8,128)(2,1)S(1)}, bf16[64,128]{1,0:T(8,128)(2,1)S(1)}, u32[]{:S(2)}, u32[]{:S(2)}) collective-permute-start(bf16[64,128]{1,0:T(8,128)(2,1)S(1)} %bitcast.644), channel_id=1, source_target_pairs={{16,0},{32,16},{48,32},{64,48},{80,64},{96,80},{112,96},{128,112},... | collective-permute-start | bytes 49160 | tf_op jit(solution)/shard_map/ppermute | solution.py:30
  316.9 13.5 %collective-permute-start.41 = (bf16[64,128]{1,0:T(8,128)(2,1)S(1)}, bf16[64,128]{1,0:T(8,128)(2,1)S(1)}, u32[]{:S(2)}, u32[]{:S(2)}) collective-permute-start(bf16[64,128]{1,0:T(8,128)(2,1)S(1)} %bitcast.641), channel_id=1, source_target_pairs={{17,0},{18,1},{19,2},{20,3},{21,4},{22,5},{23,6},{24,7},{25,8},{26... | collective-permute-start | bytes 49160 | tf_op jit(solution)/shard_map/ppermute | solution.py:32
  321.4 22.3 %collective-permute-start.43 = (bf16[2,48,64]{2,1,0:T(8,128)(2,1)}, bf16[2,48,64]{2,1,0:T(8,128)(2,1)}, u32[]{:S(2)}, u32[]{:S(2)}) collective-permute-start(bf16[2,48,64]{2,1,0:T(8,128)(2,1)} %pad_maximum_fusion.22), channel_id=1, source_target_pairs={{0,128},{16,144},{32,160},{48,176},{64,192},{80,208},{96,224},{112... | collective-permute-start | bytes 36872 | tf_op jit(solution)/shard_map/ppermute | solution.py:43
  339.1 9.5 %collective-permute-start.59 = (bf16[48,64]{1,0:T(8,128)(2,1)S(1)}, bf16[48,64]{1,0:T(8,128)(2,1)S(1)}, u32[]{:S(2)}, u32[]{:S(2)}) collective-permute-start(bf16[48,64]{1,0:T(8,128)(2,1)S(1)} %fusion.102), channel_id=1, source_target_pairs={{0,256},{16,272},{32,288},{48,304},{64,320},{80,336},{96,352},{112... | collective-permute-start | bytes 18440 | tf_op jit(solution)/shard_map/ppermute | solution.py:43
  363.8 8.9 %collective-permute-start.62 = (bf16[2,2,2,48,64]{4,3,0,1,2:T(8,128)(2,1)S(1)}, bf16[2,2,2,48,64]{4,3,0,1,2:T(8,128)(2,1)S(1)}, u32[]{:S(2)}, u32[]{:S(2)}) collective-permute-start(bf16[2,2,2,48,64]{4,3,0,1,2:T(8,128)(2,1)S(1)} %pad_maximum_fusion.13), channel_id=1, source_target_pairs={{0,32},{16,48},{32,0},{48,16},{64,96},{80,112},{96,64},{112,80},{1... | collective-permute-start | bytes 147464 | tf_op jit(solution)/shard_map/ppermute | solution.py:43
  367.4 12.1 %collective-permute-start.46 = (bf16[2,2,2,2,48,64]{5,4,0,1,2,3:T(8,128)(2,1)S(1)}, bf16[2,2,2,2,48,64]{5,4,0,1,2,3:T(8,128)(2,1)S(1)}, u32[]{:S(2)}, u32[]{:S(2)}) collective-permute-start(bf16[2,2,2,2,48,64]{5,4,0,1,2,3:T(8,128)(2,1)S(1)} %pad_maximum_fusion.7), channel_id=1, source_target_pairs={{0,16},{16,0},{32,48},{48,32},{64,80},{80,64},{96,112},{112,96},{1... | collective-permute-start | bytes 294920 | tf_op jit(solution)/shard_map/ppermute | solution.py:43
  374.1 33.0 %collective-permute-start.63 = (bf16[2,2,2,2,48,64]{5,4,0,1,2,3:T(8,128)(2,1)}, bf16[2,2,2,2,48,64]{5,4,0,1,2,3:T(8,128)(2,1)}, u32[]{:S(2)}, u32[]{:S(2)}) collective-permute-start(bf16[2,2,2,2,48,64]{5,4,0,1,2,3:T(8,128)(2,1)} %pad_maximum_fusion.8), channel_id=1, source_target_pairs={{0,16},{16,0},{32,48},{48,32},{64,80},{80,64},{96,112},{112,96},{1... | collective-permute-start | bytes 294920 | tf_op jit(solution)/shard_map/ppermute | solution.py:43
  397.2 30.0 %collective-permute-start.47 = (f32[2,2,2,48,64]{4,3,0,1,2:T(8,128)}, f32[2,2,2,48,64]{4,3,0,1,2:T(8,128)}, u32[]{:S(2)}, u32[]{:S(2)}) collective-permute-start(f32[2,2,2,48,64]{4,3,0,1,2:T(8,128)} %select_bitcast_fusion.6), channel_id=1, source_target_pairs={{0,1},{1,0},{2,3},{3,2},{4,5},{5,4},{6,7},{7,6},{8,9},{9,8},{10,11... | collective-permute-start | bytes 294920 | tf_op jit(solution)/shard_map/ppermute | solution.py:66
  443.2 14.5 %collective-permute-start.50 = (f32[48,64]{1,0:T(8,128)S(1)}, f32[48,64]{1,0:T(8,128)S(1)}, u32[]{:S(2)}, u32[]{:S(2)}) collective-permute-start(f32[48,64]{1,0:T(8,128)S(1)} %select_bitcast_fusion.52), channel_id=1, source_target_pairs={{0,8},{1,9},{2,10},{3,11},{4,12},{5,13},{6,14},{7,15},{8,0},{9,1},... | collective-permute-start | bytes 36872 | tf_op jit(solution)/shard_map/ppermute | solution.py:66
  451.8 28.3 %collective-permute-start.66 = (f32[2,48,64]{2,1,0:T(8,128)}, f32[2,48,64]{2,1,0:T(8,128)}, u32[]{:S(2)}, u32[]{:S(2)}) collective-permute-start(f32[2,48,64]{2,1,0:T(8,128)} %select_bitcast_fusion.34), channel_id=1, source_target_pairs={{0,4},{1,5},{2,6},{3,7},{4,0},{5,1},{6,2},{7,3},{8,12},{9,13},{10,... | collective-permute-start | bytes 73736 | tf_op jit(solution)/shard_map/ppermute | solution.py:66
  461.8 20.3 %collective-permute-start.51 = (bf16[64,128]{1,0:T(8,128)(2,1)S(1)}, bf16[64,128]{1,0:T(8,128)(2,1)S(1)}, u32[]{:S(2)}, u32[]{:S(2)}) collective-permute-start(bf16[64,128]{1,0:T(8,128)(2,1)S(1)} %bitcast.701), channel_id=1, source_target_pairs={{0,17},{1,18},{2,19},{3,20},{4,21},{5,22},{6,23},{7,24},{8,25},{9,... | collective-permute-start | bytes 49160 | tf_op jit(solution)/shard_map/ppermute | solution.py:32
  463.7 35.1 %collective-permute-start.52 = (bf16[64,128]{1,0:T(8,128)(2,1)S(1)}, bf16[64,128]{1,0:T(8,128)(2,1)S(1)}, u32[]{:S(2)}, u32[]{:S(2)}) collective-permute-start(bf16[64,128]{1,0:T(8,128)(2,1)S(1)} %bitcast.696), channel_id=1, source_target_pairs={{0,16},{16,32},{32,48},{48,64},{64,80},{80,96},{96,112},{112,128},... | collective-permute-start | bytes 49160 | tf_op jit(solution)/shard_map/ppermute | solution.py:30
  466.3 35.6 %collective-permute-start.53 = (bf16[64,128]{1,0:T(8,128)(2,1)S(1)}, bf16[64,128]{1,0:T(8,128)(2,1)S(1)}, u32[]{:S(2)}, u32[]{:S(2)}) collective-permute-start(bf16[64,128]{1,0:T(8,128)(2,1)S(1)} %bitcast.690), channel_id=1, source_target_pairs={{1,16},{2,17},{3,18},{4,19},{5,20},{6,21},{7,22},{8,23},{9,24},{10... | collective-permute-start | bytes 49160 | tf_op jit(solution)/shard_map/ppermute | solution.py:32
  471.3 35.9 %collective-permute-start.54 = (bf16[64,128]{1,0:T(8,128)(2,1)S(1)}, bf16[64,128]{1,0:T(8,128)(2,1)S(1)}, u32[]{:S(2)}, u32[]{:S(2)}) collective-permute-start(bf16[64,128]{1,0:T(8,128)(2,1)S(1)} %bitcast.672), channel_id=1, source_target_pairs={{0,1},{1,2},{2,3},{3,4},{4,5},{5,6},{6,7},{7,8},{8,9},{9,10},{10,1... | collective-permute-start | bytes 49160 | tf_op jit(solution)/shard_map/ppermute | solution.py:27
  480.1 27.7 %collective-permute-start.55 = (bf16[64,128]{1,0:T(8,128)(2,1)S(1)}, bf16[64,128]{1,0:T(8,128)(2,1)S(1)}, u32[]{:S(2)}, u32[]{:S(2)}) collective-permute-start(bf16[64,128]{1,0:T(8,128)(2,1)S(1)} %bitcast.674), channel_id=1, source_target_pairs={{1,0},{2,1},{3,2},{4,3},{5,4},{6,5},{7,6},{8,7},{9,8},{10,9},{11,1... | collective-permute-start | bytes 49160 | tf_op jit(solution)/shard_map/ppermute | solution.py:27
  482.1 26.4 %collective-permute-start.56 = (bf16[64,128]{1,0:T(8,128)(2,1)S(1)}, bf16[64,128]{1,0:T(8,128)(2,1)S(1)}, u32[]{:S(2)}, u32[]{:S(2)}) collective-permute-start(bf16[64,128]{1,0:T(8,128)(2,1)S(1)} %bitcast.663), channel_id=1, source_target_pairs={{16,1},{17,2},{18,3},{19,4},{20,5},{21,6},{22,7},{23,8},{24,9},{25... | collective-permute-start | bytes 49160 | tf_op jit(solution)/shard_map/ppermute | solution.py:32
  498.8 10.3 %collective-permute-start.57 = (bf16[64,128]{1,0:T(8,128)(2,1)S(1)}, bf16[64,128]{1,0:T(8,128)(2,1)S(1)}, u32[]{:S(2)}, u32[]{:S(2)}) collective-permute-start(bf16[64,128]{1,0:T(8,128)(2,1)S(1)} %bitcast.653), channel_id=1, source_target_pairs={{16,0},{32,16},{48,32},{64,48},{80,64},{96,80},{112,96},{128,112},... | collective-permute-start | bytes 49160 | tf_op jit(solution)/shard_map/ppermute | solution.py:30
  502.0 15.0 %collective-permute-start.58 = (bf16[64,128]{1,0:T(8,128)(2,1)S(1)}, bf16[64,128]{1,0:T(8,128)(2,1)S(1)}, u32[]{:S(2)}, u32[]{:S(2)}) collective-permute-start(bf16[64,128]{1,0:T(8,128)(2,1)S(1)} %bitcast.649), channel_id=1, source_target_pairs={{17,0},{18,1},{19,2},{20,3},{21,4},{22,5},{23,6},{24,7},{25,8},{26... | collective-permute-start | bytes 49160 | tf_op jit(solution)/shard_map/ppermute | solution.py:32
  523.9 9.5 %collective-permute-start.76 = (bf16[48,64]{1,0:T(8,128)(2,1)S(1)}, bf16[48,64]{1,0:T(8,128)(2,1)S(1)}, u32[]{:S(2)}, u32[]{:S(2)}) collective-permute-start(bf16[48,64]{1,0:T(8,128)(2,1)S(1)} %fusion.103), channel_id=1, source_target_pairs={{0,256},{16,272},{32,288},{48,304},{64,320},{80,336},{96,352},{112... | collective-permute-start | bytes 18440 | tf_op jit(solution)/shard_map/ppermute | solution.py:43
  528.9 14.4 %collective-permute-start.67 = (f32[48,64]{1,0:T(8,128)S(1)}, f32[48,64]{1,0:T(8,128)S(1)}, u32[]{:S(2)}, u32[]{:S(2)}) collective-permute-start(f32[48,64]{1,0:T(8,128)S(1)} %select_bitcast_fusion.49), channel_id=1, source_target_pairs={{0,8},{1,9},{2,10},{3,11},{4,12},{5,13},{6,14},{7,15},{8,0},{9,1},... | collective-permute-start | bytes 36872 | tf_op jit(solution)/shard_map/ppermute | solution.py:66
  557.4 68.0 %collective-permute-start.80 = (bf16[2,2,2,2,48,64]{5,4,0,1,2,3:T(8,128)(2,1)}, bf16[2,2,2,2,48,64]{5,4,0,1,2,3:T(8,128)(2,1)}, u32[]{:S(2)}, u32[]{:S(2)}) collective-permute-start(bf16[2,2,2,2,48,64]{5,4,0,1,2,3:T(8,128)(2,1)} %pad_maximum_fusion.9), channel_id=1, source_target_pairs={{0,16},{16,0},{32,48},{48,32},{64,80},{80,64},{96,112},{112,96},{1... | collective-permute-start | bytes 294920 | tf_op jit(solution)/shard_map/ppermute | solution.py:43
  561.9 24.1 %collective-permute-start.68 = (bf16[64,128]{1,0:T(8,128)(2,1)S(1)}, bf16[64,128]{1,0:T(8,128)(2,1)S(1)}, u32[]{:S(2)}, u32[]{:S(2)}) collective-permute-start(bf16[64,128]{1,0:T(8,128)(2,1)S(1)} %bitcast.710), channel_id=1, source_target_pairs={{0,17},{1,18},{2,19},{3,20},{4,21},{5,22},{6,23},{7,24},{8,25},{9,... | collective-permute-start | bytes 49160 | tf_op jit(solution)/shard_map/ppermute | solution.py:32
  572.9 15.1 %collective-permute-start.69 = (bf16[64,128]{1,0:T(8,128)(2,1)S(1)}, bf16[64,128]{1,0:T(8,128)(2,1)S(1)}, u32[]{:S(2)}, u32[]{:S(2)}) collective-permute-start(bf16[64,128]{1,0:T(8,128)(2,1)S(1)} %bitcast.708), channel_id=1, source_target_pairs={{0,16},{16,32},{32,48},{48,64},{64,80},{80,96},{96,112},{112,128},... | collective-permute-start | bytes 49160 | tf_op jit(solution)/shard_map/ppermute | solution.py:30
  576.6 28.2 %collective-permute-start.70 = (bf16[64,128]{1,0:T(8,128)(2,1)S(1)}, bf16[64,128]{1,0:T(8,128)(2,1)S(1)}, u32[]{:S(2)}, u32[]{:S(2)}) collective-permute-start(bf16[64,128]{1,0:T(8,128)(2,1)S(1)} %bitcast.706), channel_id=1, source_target_pairs={{1,16},{2,17},{3,18},{4,19},{5,20},{6,21},{7,22},{8,23},{9,24},{10... | collective-permute-start | bytes 49160 | tf_op jit(solution)/shard_map/ppermute | solution.py:32
  578.5 30.8 %collective-permute-start.71 = (bf16[64,128]{1,0:T(8,128)(2,1)S(1)}, bf16[64,128]{1,0:T(8,128)(2,1)S(1)}, u32[]{:S(2)}, u32[]{:S(2)}) collective-permute-start(bf16[64,128]{1,0:T(8,128)(2,1)S(1)} %bitcast.704), channel_id=1, source_target_pairs={{0,1},{1,2},{2,3},{3,4},{4,5},{5,6},{6,7},{7,8},{8,9},{9,10},{10,1... | collective-permute-start | bytes 49160 | tf_op jit(solution)/shard_map/ppermute | solution.py:27
  586.1 27.7 %collective-permute-start.72 = (bf16[64,128]{1,0:T(8,128)(2,1)S(1)}, bf16[64,128]{1,0:T(8,128)(2,1)S(1)}, u32[]{:S(2)}, u32[]{:S(2)}) collective-permute-start(bf16[64,128]{1,0:T(8,128)(2,1)S(1)} %bitcast.682), channel_id=1, source_target_pairs={{1,0},{2,1},{3,2},{4,3},{5,4},{6,5},{7,6},{8,7},{9,8},{10,9},{11,1... | collective-permute-start | bytes 49160 | tf_op jit(solution)/shard_map/ppermute | solution.py:27
  588.0 26.4 %collective-permute-start.73 = (bf16[64,128]{1,0:T(8,128)(2,1)S(1)}, bf16[64,128]{1,0:T(8,128)(2,1)S(1)}, u32[]{:S(2)}, u32[]{:S(2)}) collective-permute-start(bf16[64,128]{1,0:T(8,128)(2,1)S(1)} %bitcast.678), channel_id=1, source_target_pairs={{16,1},{17,2},{18,3},{19,4},{20,5},{21,6},{22,7},{23,8},{24,9},{25... | collective-permute-start | bytes 49160 | tf_op jit(solution)/shard_map/ppermute | solution.py:32
  604.8 10.3 %collective-permute-start.74 = (bf16[64,128]{1,0:T(8,128)(2,1)S(1)}, bf16[64,128]{1,0:T(8,128)(2,1)S(1)}, u32[]{:S(2)}, u32[]{:S(2)}) collective-permute-start(bf16[64,128]{1,0:T(8,128)(2,1)S(1)} %bitcast.670), channel_id=1, source_target_pairs={{16,0},{32,16},{48,32},{64,48},{80,64},{96,80},{112,96},{128,112},... | collective-permute-start | bytes 49160 | tf_op jit(solution)/shard_map/ppermute | solution.py:30
  609.3 13.5 %collective-permute-start.75 = (bf16[64,128]{1,0:T(8,128)(2,1)S(1)}, bf16[64,128]{1,0:T(8,128)(2,1)S(1)}, u32[]{:S(2)}, u32[]{:S(2)}) collective-permute-start(bf16[64,128]{1,0:T(8,128)(2,1)S(1)} %bitcast.664), channel_id=1, source_target_pairs={{17,0},{18,1},{19,2},{20,3},{21,4},{22,5},{23,6},{24,7},{25,8},{26... | collective-permute-start | bytes 49160 | tf_op jit(solution)/shard_map/ppermute | solution.py:32
  643.6 18.4 %collective-permute-start.81 = (f32[2,2,2,48,64]{4,3,0,1,2:T(8,128)S(1)}, f32[2,2,2,48,64]{4,3,0,1,2:T(8,128)S(1)}, u32[]{:S(2)}, u32[]{:S(2)}) collective-permute-start(f32[2,2,2,48,64]{4,3,0,1,2:T(8,128)S(1)} %select_bitcast_fusion), channel_id=1, source_target_pairs={{0,1},{1,0},{2,3},{3,2},{4,5},{5,4},{6,7},{7,6},{8,9},{9,8},{10,11... | collective-permute-start | bytes 294920 | tf_op jit(solution)/shard_map/ppermute | solution.py:66
  678.6 14.7 %collective-permute-start.84 = (f32[48,64]{1,0:T(8,128)}, f32[48,64]{1,0:T(8,128)}, u32[]{:S(2)}, u32[]{:S(2)}) collective-permute-start(f32[48,64]{1,0:T(8,128)} %select_bitcast_fusion.46), channel_id=1, source_target_pairs={{0,8},{1,9},{2,10},{3,11},{4,12},{5,13},{6,14},{7,15},{8,0},{9,1},... | collective-permute-start | bytes 36872 | tf_op jit(solution)/shard_map/ppermute | solution.py:66
  (68 other events, 1099.3 us)

commit v2 on v0

--- a/solution.py
+++ b/solution.py
@@ -9,31 +9,47 @@
 OFFSETS = ((-1, -1), (-1, 0), (-1, 1), (0, -1), (0, 1), (1, -1), (1, 0), (1, 1))
 
 
-def passed_along(block, axis, distance):
-    devices = range(lax.axis_size(axis))
-    route = [(i - distance, i) for i in devices if i - distance in devices]
+def shifted(block, axis, distance):
+    size = lax.axis_size(axis)
+    route = [(i + distance, i) for i in range(size) if 0 <= i + distance < size]
     return lax.ppermute(block, axis, route)
 
 
-def hop_rows(portion, steps):
-    return passed_along(portion, "row", steps)
+def neighbour_pieces(outgoing):
+    from_above = shifted(outgoing[jnp.array([7, 6, 5])], "row", -1)
+    from_below = shifted(outgoing[jnp.array([2, 1, 0])], "row", 1)
+    to_right = jnp.stack([from_above[0], outgoing[4], from_below[0]], 0)
+    to_left = jnp.stack([from_above[2], outgoing[3], from_below[2]], 0)
+    from_left = shifted(to_right, "col", -1)
+    from_right = shifted(to_left, "col", 1)
+    return jnp.stack(
+        [
+            from_left[0],
+            from_above[1],
+            from_right[0],
+            from_left[1],
+            from_right[1],
+            from_left[2],
+            from_below[1],
+            from_right[2],
+        ],
+        0,
+    )
 
 
-def hop_cols(portion, steps):
-    return passed_along(portion, "col", steps)
-
-
-def neighbour_pieces(outgoing):
-    arrived = []
-    for direction in range(8):
-        shift_a, shift_b = OFFSETS[direction]
-        portion = outgoing[7 - direction]
-        if shift_a != 0:
-            portion = hop_rows(portion, -shift_a)
-        if shift_b != 0:
-            portion = hop_cols(portion, -shift_b)
-        arrived.append(portion)
-    return jnp.stack(arrived, 0)
+def gather_rows(piece, bits):
+    index = lax.axis_index("row")
+    size = lax.axis_size("row")
+    current = piece
+    for step, bit in enumerate(bits):
+        distance = 1 << bit
+        route = [(i, i ^ distance) for i in range(size)]
+        other = lax.ppermute(current, "row", route)
+        high = ((index >> bit) & 1) == 1
+        low_part = jnp.where(high, other, current)
+        high_part = jnp.where(high, current, other)
+        current = jnp.stack([low_part, high_part], axis=step)
+    return current
 
 
 def on_device(
@@ -53,7 +69,7 @@
     block_size = coupling.shape[3]
     block_count = unknowns // block_size
     mode_count = modes.shape[2]
-    piece_rows = mode_count * columns // 128
+    row_bits = lax.axis_size("row").bit_length() - 1
     rhs_full = rhs[0, 0].astype(jnp.float32)
     operator_matrix = operator_blocks[0, 0]
     solver_matrix = local_solver[0, 0]
@@ -67,19 +83,19 @@
     block_onehot = (slot_block[0, 0][:, None] == jnp.arange(block_count)[None, :]).astype(
         jnp.float32
     )
-    col_index = lax.axis_index("col")
 
     def coarse_solve(rounded):
         restricted = lax.dot_general(
             mode_basis, rounded, (((1,), (1,)), ((), ())), preferred_element_type=jnp.float32
-        )
-        flat_piece = restricted.astype(jnp.bfloat16).reshape(piece_rows, 128)
-        gathered = lax.all_gather(flat_piece, "row", axis=0, tiled=True).reshape(-1, columns)
+        ).astype(jnp.bfloat16)
+        gathered = gather_rows(restricted, list(range(row_bits - 1, -1, -1)))
+        gathered = gathered.reshape(-1, columns)
         partial_sums = lax.dot_general(
             coarse_tile, gathered, (((0,), (0,)), ((), ())), preferred_element_type=jnp.float32
         )
-        summed = lax.psum(partial_sums.reshape(-1, 128), "col")
-        own_rows = lax.dynamic_slice_in_dim(summed, col_index * piece_rows, piece_rows, 0)
+        own_rows = lax.psum_scatter(
+            partial_sums.reshape(-1, 128), "col", scatter_dimension=0, tiled=True
+        )
         return own_rows.reshape(mode_count, columns).astype(jnp.bfloat16)
 
     solution = jnp.zeros((columns, unknowns), jnp.float32)

time: 1470 us -> 821 us (0.56)
  blocking collectives: 1010 us -> 0 us
  waiting for transfers between devices: 18 us -> 439 us
  starting transfers between devices: 263 us -> 142 us
  other arithmetic: 0 us -> 29 us
  local copies, waits for them, and re-layouts: 105 us -> 123 us
    all_gather x5 -> x0, blocking collectives: 602 us -> none  [coarse_solve(): lax.all_gather(flat_piece, 'row', axis=0, tiled=True).reshape(-1, columns)]
    psum x3 -> x0, blocking collectives: 407 us -> none  [coarse_solve(): summed = lax.psum(partial_sums.reshape(-1, 128), 'col')]
    unnamed x0 -> x10, waiting for transfers between devices: none -> 394 us
    ppermute x60 -> x45, starting transfers between devices: 263 us -> 142 us  [the longest x25 94.7 us: gather_rows(): other = lax.ppermute(current, 'row', route)]
    another operation x45 -> x10, local copies, waits for them, and re-layouts: 50 us -> 20.3 us  [the longest x5 10.8 us: gather_rows(): current = jnp.stack([low_part, high_part], axis=step)]
    gather x0 -> x20, local copies, waits for them, and re-layouts: none -> 28 us  [the longest x10 14.6 us: neighbour_pieces(): from_above = shifted(outgoing[jnp.array([7, 6, 5])], 'row', -1)]
    ppermute x60 -> x45, waiting for transfers between devices: 18 us -> 44.5 us  [the longest x25 25.1 us: gather_rows(): other = lax.ppermute(current, 'row', route)]
    another operation x0 -> x59, other arithmetic: none -> 22.5 us  [the longest x49 14.4 us: gather_rows(): current = jnp.stack([low_part, high_part], axis=step)]
  transfers between devices with their start and end apart: 60 -> 50, of which waited for: 3 -> 25; matrix products, arithmetic and copies ran while one was open for 5% -> 19% of each run, Pallas kernels for 0% -> 0%
where the time goes in v2:
time: 821 us; the launch traced here: 806 us
  waiting for transfers between devices  439 us (53%)
  starting transfers between devices  142 us (17%)
  local copies, waits for them, and re-layouts  123 us (15%)
  matrix products  58.4 us (7%)
  other arithmetic  29 us (4%)
  between operations  14.5 us (2%)
    unnamed x10, waiting for transfers between devices  394 us
    ppermute x25, starting transfers between devices, gather_rows(): other = lax.ppermute(current, 'row', route)  94.7 us
    ppermute x20, starting transfers between devices, shifted(): return lax.ppermute(block, axis, route)  47.1 us
    ppermute x25, waiting for transfers between devices, gather_rows(): other = lax.ppermute(current, 'row', route)  25.1 us
    ppermute x20, waiting for transfers between devices, shifted(): return lax.ppermute(block, axis, route)  19.4 us
  transfers between devices with their start and end apart: 50, of which 25 were waited for; matrix products, arithmetic and copies ran while one was open for 19% of the time, Pallas kernels for 0%

profile of v2, /device:TPU:6, one launch (start us, length us, event | category | flops | bytes accessed | tf_op | source)
XLA Modules:
  0.0 805.8 jit_solution(15832193438941708385)
XLA Ops:
  7.8 9.2 %collective-permute-start.4 = (bf16[48,64]{1,0:T(8,128)(2,1)S(1)}, bf16[48,64]{1,0:T(8,128)(2,1)S(1)}, u32[]{:S(2)}, u32[]{:S(2)}) collective-permute-start(bf16[48,64]{1,0:T(8,128)(2,1)S(1)} %convolution_convert_fusion.14), channel_id=1, source_target_pairs={{0,256},{16,272},{32,288},{48,304},{64,320},{80,336},{96,352},{112... | collective-permute-start | bytes 18440 | tf_op jit(solution)/shard_map/ppermute | solution.py:47
  17.1 2.3 fusion.193
  20.5 3.5 collective-permute-start
  24.0 5.2 collective-permute-start.5
  31.8 7.0 collective-permute-start.6
  47.7 2.4 collective-permute-start.2
  50.8 2.4 collective-permute-done.2
  60.0 5.7 collective-permute-start.13
  69.6 3.7 collective-permute-start.14
  73.8 2.5 collective-permute-done.14
  76.3 3.9 collective-permute-start.15
  82.4 4.2 collective-permute-start.16
  87.6 2.8 collective-permute-done.16
  91.8 4.0 collective-permute-start.17
  98.9 2.5 reshape.75
  111.3 2.5 reshape.79
  119.7 90.8 %reduce-scatter.16.cloned.1.call-done = f32[24,128]{1,0:T(8,128)} async-done(((f32[384,128]{1,0:T(8,128)}), f32[24,128]{1,0:T(8,128)}) %reduce-scatter.16.cloned.1.call-update) | async-done | bytes 12304
  218.7 2.2 gather_fusion.2
  222.3 4.1 collective-permute-start.9
  228.1 2.2 gather_fusion.3
  234.1 3.2 collective-permute-done.10
  241.7 2.4 collective-permute-start.11
  244.8 2.4 collective-permute-done.11
  255.4 47.0 %reduce-scatter.18.cloned.1.call-done = f32[24,128]{1,0:T(8,128)} async-done(((f32[384,128]{1,0:T(8,128)}), f32[24,128]{1,0:T(8,128)}) %reduce-scatter.18.cloned.1.call-update) | async-done | bytes 12304
  305.1 2.8 collective-permute-start.22
  311.6 3.1 collective-permute-done.22
  315.4 2.7 collective-permute-start.23
  319.3 3.0 collective-permute-done.23
  323.6 2.4 collective-permute-start.24
  327.4 2.2 gather_fusion.4
  329.6 2.2 gather_fusion.5
  332.6 3.4 collective-permute-start.18
  339.0 6.3 collective-permute-start.25
  349.6 2.4 collective-permute-start.20
  353.5 2.5 collective-permute-start.26
  364.2 3.8 collective-permute-start.31
  372.0 2.5 reshape.83
  383.6 97.6 %reduce-scatter.20.cloned.1.call-done = f32[24,128]{1,0:T(8,128)} async-done(((f32[384,128]{1,0:T(8,128)}), f32[24,128]{1,0:T(8,128)}) %reduce-scatter.20.cloned.1.call-update) | async-done | bytes 12304
  490.0 2.2 gather_fusion.6
  493.7 4.0 collective-permute-start.27
  499.4 2.2 gather_fusion.7
  505.4 3.2 collective-permute-done.28
  513.0 2.4 collective-permute-start.29
  516.1 2.4 collective-permute-done.29
  526.3 3.7 collective-permute-start.40
  532.0 4.0 collective-permute-done.40
  536.0 2.3 collective-permute-start.41
  539.4 3.8 collective-permute-done.41
  545.1 3.9 collective-permute-start.42
  549.2 3.8 collective-permute-start.34
  553.1 3.6 collective-permute-start.43
  557.3 2.7 collective-permute-start.35
  562.9 3.6 collective-permute-start.44
  569.6 2.5 reshape.87
  582.1 2.5 reshape.91
  590.4 88.2 %reduce-scatter.22.cloned.1.call-done = f32[24,128]{1,0:T(8,128)} async-done(((f32[384,128]{1,0:T(8,128)}), f32[24,128]{1,0:T(8,128)}) %reduce-scatter.22.cloned.1.call-update) | async-done | bytes 12304
  686.9 2.2 gather_fusion.8
  690.5 4.0 collective-permute-start.36
  696.2 2.2 gather_fusion.9
  698.4 70.7 %reduce-scatter.24.cloned.1.call-done = f32[24,128]{1,0:T(8,128)} async-done(((f32[384,128]{1,0:T(8,128)}), f32[24,128]{1,0:T(8,128)}) %reduce-scatter.24.cloned.1.call-update) | async-done | bytes 12304
  775.0 3.2 collective-permute-done.37
  782.6 2.4 collective-permute-start.38
  785.7 2.4 collective-permute-done.38
  794.7 2.7 fusion.20
  (315 shorter events, 205.3 us)
Async XLA Ops:
  6.5 94.8 %copy-start = (bf16[1,1536,1,768]{3,1,2,0:T(8,128)(2,1)S(1)}, bf16[1,1536,1,768]{3,1,2,0:T(8,128)(2,1)}, u32[]{:S(2)}) copy-start(bf16[1,1536,1,768]{3,1,2,0:T(8,128)(2,1)} %param.24) | copy-start | bytes 7077892
  6.5 13.2 %copy-start.38 = (s32[3]{0:T(128)S(1)}, s32[3]{0:T(128)}, u32[]{:S(2)}) copy-start(s32[3]{0:T(128)} %constant.42) | copy-start | bytes 40
  6.5 203.9 %reduce-scatter.16.cloned.1.call-start = ((), (), s32[]{:S(2)}) async-start(), calls=%async_computation.5 | async-start | bytes 208896
  7.8 21.4 %copy-start.37 = (s32[3]{0:T(128)S(1)}, s32[3]{0:T(128)}, u32[]{:S(2)}) copy-start(s32[3]{0:T(128)} %constant.43) | copy-start | bytes 40
  7.8 16.1 %collective-permute-start.4 = (bf16[48,64]{1,0:T(8,128)(2,1)S(1)}, bf16[48,64]{1,0:T(8,128)(2,1)S(1)}, u32[]{:S(2)}, u32[]{:S(2)}) collective-permute-start(bf16[48,64]{1,0:T(8,128)(2,1)S(1)} %convolution_convert_fusion.14), channel_id=1, source_target_pairs={{0,256},{16,272},{32,288},{48,304},{64,320},{80,336},{96,352},{112... | collective-permute-start | bytes 18440 | tf_op jit(solution)/shard_map/ppermute | solution.py:47
  19.4 22.2 %copy-start.7 = (bf16[64,768]{1,0:T(8,128)(2,1)}, bf16[64,768]{1,0:T(8,128)(2,1)S(1)}, u32[]{:S(2)}) copy-start(bf16[64,768]{1,0:T(8,128)(2,1)S(1)} %get-tuple-element.125) | copy-start | bytes 294916
  20.5 21.1 %collective-permute-start = (bf16[3,64,128]{2,0,1:T(4,128)(2,1)S(1)}, bf16[3,64,128]{2,0,1:T(4,128)(2,1)S(1)}, u32[]{:S(2)}, u32[]{:S(2)}) collective-permute-start(bf16[3,64,128]{2,0,1:T(4,128)(2,1)S(1)} %copy.51), channel_id=1, source_target_pairs={{0,16},{16,32},{32,48},{48,64},{64,80},{80,96},{96,112},{112,128},... | collective-permute-start | bytes 147464 | tf_op jit(solution)/shard_map/ppermute | solution.py:15
  24.0 31.9 %copy-start.28 = (s32[1,1,4]{2,1,0:T(1,128)S(1)}, s32[1,1,4]{2,1,0:T(1,128)}, u32[]{:S(2)}) copy-start(s32[1,1,4]{2,1,0:T(1,128)} %param.26) | copy-start | bytes 52
  24.0 7.8 collective-permute-start.5
  30.5 11.8 %collective-permute-start.1 = (bf16[3,64,128]{2,0,1:T(4,128)(2,1)}, bf16[3,64,128]{2,0,1:T(4,128)(2,1)}, u32[]{:S(2)}, u32[]{:S(2)}) collective-permute-start(bf16[3,64,128]{2,0,1:T(4,128)(2,1)} %copy.53), channel_id=1, source_target_pairs={{16,0},{32,16},{48,32},{64,48},{80,64},{96,80},{112,96},{128,112},... | collective-permute-start | bytes 147464 | tf_op jit(solution)/shard_map/ppermute | solution.py:15
  31.8 26.3 %copy-start.32 = (s32[1,1,4]{2,1,0:T(1,128)S(1)}, s32[1,1,4]{2,1,0:T(1,128)}, u32[]{:S(2)}) copy-start(s32[1,1,4]{2,1,0:T(1,128)} %param.27) | copy-start | bytes 52
  31.8 9.1 %collective-permute-start.6 = (bf16[2,2,48,64]{3,2,0,1:T(8,128)(2,1)S(1)}, bf16[2,2,48,64]{3,2,0,1:T(8,128)(2,1)S(1)}, u32[]{:S(2)}, u32[]{:S(2)}) collective-permute-start(bf16[2,2,48,64]{3,2,0,1:T(8,128)(2,1)S(1)} %pad_maximum_fusion.25), channel_id=1, source_target_pairs={{0,64},{16,80},{32,96},{48,112},{64,0},{80,16},{96,32},{112,48},{1... | collective-permute-start | bytes 73736 | tf_op jit(solution)/shard_map/ppermute | solution.py:47
  42.3 16.3 %copy-start.2 = (bf16[1,1,768,768]{3,2,1,0:T(8,128)(2,1)S(1)}, bf16[1,1,768,768]{3,2,1,0:T(8,128)(2,1)}, u32[]{:S(2)}) copy-start(bf16[1,1,768,768]{3,2,1,0:T(8,128)(2,1)} %param.20) | copy-start | bytes 3538948
  44.8 5.2 collective-permute-start.3
  47.7 5.6 collective-permute-start.2
  59.8 26.7 %copy-start.1 = (bf16[1,1,768,768]{3,2,1,0:T(8,128)(2,1)S(1)}, bf16[1,1,768,768]{3,2,1,0:T(8,128)(2,1)}, u32[]{:S(2)}) copy-start(bf16[1,1,768,768]{3,2,1,0:T(8,128)(2,1)} %param.21) | copy-start | bytes 3538948
  60.0 9.6 %collective-permute-start.13 = (bf16[48,64]{1,0:T(8,128)(2,1)S(1)}, bf16[48,64]{1,0:T(8,128)(2,1)S(1)}, u32[]{:S(2)}, u32[]{:S(2)}) collective-permute-start(bf16[48,64]{1,0:T(8,128)(2,1)S(1)} %fusion.100), channel_id=1, source_target_pairs={{0,256},{16,272},{32,288},{48,304},{64,320},{80,336},{96,352},{112... | collective-permute-start | bytes 18440 | tf_op jit(solution)/shard_map/ppermute | solution.py:47
  65.8 8.0 collective-permute-start.7
  69.6 6.6 collective-permute-start.14
  76.3 6.0 collective-permute-start.15
  80.3 15.5 %collective-permute-start.8 = (bf16[2,2,2,2,48,64]{5,4,0,1,2,3:T(8,128)(2,1)S(1)}, bf16[2,2,2,2,48,64]{5,4,0,1,2,3:T(8,128)(2,1)S(1)}, u32[]{:S(2)}, u32[]{:S(2)}) collective-permute-start(bf16[2,2,2,2,48,64]{5,4,0,1,2,3:T(8,128)(2,1)S(1)} %pad_maximum_fusion.5), channel_id=1, source_target_pairs={{0,16},{16,0},{32,48},{48,32},{64,80},{80,64},{96,112},{112,96},{1... | collective-permute-start | bytes 294920 | tf_op jit(solution)/shard_map/ppermute | solution.py:47
  82.4 8.0 collective-permute-start.16
  91.8 15.4 %collective-permute-start.17 = (bf16[2,2,2,2,48,64]{5,4,0,1,2,3:T(8,128)(2,1)}, bf16[2,2,2,2,48,64]{5,4,0,1,2,3:T(8,128)(2,1)}, u32[]{:S(2)}, u32[]{:S(2)}) collective-permute-start(bf16[2,2,2,2,48,64]{5,4,0,1,2,3:T(8,128)(2,1)} %pad_maximum_fusion.6), channel_id=1, source_target_pairs={{0,16},{16,0},{32,48},{48,32},{64,80},{80,64},{96,112},{112,96},{1... | collective-permute-start | bytes 294920 | tf_op jit(solution)/shard_map/ppermute | solution.py:47
  107.2 195.3 %reduce-scatter.18.cloned.1.call-start = ((), (), s32[]{:S(2)}) async-start(), calls=%async_computation.6 | async-start | bytes 208896
  119.7 361.6 %reduce-scatter.20.cloned.1.call-start = ((), (), s32[]{:S(2)}) async-start(), calls=%async_computation.7 | async-start | bytes 208896
  218.0 31.9 %copy-start.29 = (s32[1,1,4]{2,1,0:T(1,128)S(1)}, s32[1,1,4]{2,1,0:T(1,128)}, u32[]{:S(2)}) copy-start(s32[1,1,4]{2,1,0:T(1,128)} %param.26) | copy-start | bytes 52
  222.3 29.8 %copy-start.33 = (s32[1,1,4]{2,1,0:T(1,128)S(1)}, s32[1,1,4]{2,1,0:T(1,128)}, u32[]{:S(2)}) copy-start(s32[1,1,4]{2,1,0:T(1,128)} %param.27) | copy-start | bytes 52
  222.3 10.1 %collective-permute-start.9 = (bf16[3,64,128]{2,0,1:T(4,128)(2,1)}, bf16[3,64,128]{2,0,1:T(4,128)(2,1)}, u32[]{:S(2)}, u32[]{:S(2)}) collective-permute-start(bf16[3,64,128]{2,0,1:T(4,128)(2,1)} %copy.59), channel_id=1, source_target_pairs={{0,16},{16,32},{32,48},{48,64},{64,80},{80,96},{96,112},{112,128},... | collective-permute-start | bytes 147464 | tf_op jit(solution)/shard_map/ppermute | solution.py:15
  231.2 6.2 collective-permute-start.10
  238.9 5.2 collective-permute-start.12
  241.7 5.6 collective-permute-start.11
  305.1 9.6 %collective-permute-start.22 = (bf16[48,64]{1,0:T(8,128)(2,1)S(1)}, bf16[48,64]{1,0:T(8,128)(2,1)}, u32[]{:S(2)}, u32[]{:S(2)}) collective-permute-start(bf16[48,64]{1,0:T(8,128)(2,1)S(1)} %fusion.101), channel_id=1, source_target_pairs={{0,256},{16,272},{32,288},{48,304},{64,320},{80,336},{96,352},{112... | collective-permute-start | bytes 18440 | tf_op jit(solution)/shard_map/ppermute | solution.py:47
  315.4 6.9 collective-permute-start.23
  323.6 14.5 %collective-permute-start.24 = (bf16[2,2,48,64]{3,2,0,1:T(8,128)(2,1)}, bf16[2,2,48,64]{3,2,0,1:T(8,128)(2,1)}, u32[]{:S(2)}, u32[]{:S(2)}) collective-permute-start(bf16[2,2,48,64]{3,2,0,1:T(8,128)(2,1)} %pad_maximum_fusion.27), channel_id=1, source_target_pairs={{0,64},{16,80},{32,96},{48,112},{64,0},{80,16},{96,32},{112,48},{1... | collective-permute-start | bytes 73736 | tf_op jit(solution)/shard_map/ppermute | solution.py:47
  331.7 17.8 %copy-start.24 = (bf16[1,64,128]{2,0,1:T(2,128)(2,1)S(1)}, bf16[1,64,128]{2,0,1:T(2,128)(2,1)}, u32[]{:S(2)}) copy-start(bf16[1,64,128]{2,0,1:T(2,128)(2,1)} %get-tuple-element.30) | copy-start | bytes 49156
  332.6 12.7 %collective-permute-start.18 = (bf16[3,64,128]{2,0,1:T(4,128)(2,1)S(1)}, bf16[3,64,128]{2,0,1:T(4,128)(2,1)S(1)}, u32[]{:S(2)}, u32[]{:S(2)}) collective-permute-start(bf16[3,64,128]{2,0,1:T(4,128)(2,1)S(1)} %copy.67), channel_id=1, source_target_pairs={{0,16},{16,32},{32,48},{48,64},{64,80},{80,96},{96,112},{112,128},... | collective-permute-start | bytes 147464 | tf_op jit(solution)/shard_map/ppermute | solution.py:15
  336.8 9.2 %collective-permute-start.19 = (bf16[3,64,128]{2,0,1:T(4,128)(2,1)S(1)}, bf16[3,64,128]{2,0,1:T(4,128)(2,1)S(1)}, u32[]{:S(2)}, u32[]{:S(2)}) collective-permute-start(bf16[3,64,128]{2,0,1:T(4,128)(2,1)S(1)} %copy.69), channel_id=1, source_target_pairs={{16,0},{32,16},{48,32},{64,48},{80,64},{96,80},{112,96},{128,112},... | collective-permute-start | bytes 147464 | tf_op jit(solution)/shard_map/ppermute | solution.py:15
  339.0 20.3 %copy-start.30 = (s32[1,1,4]{2,1,0:T(1,128)S(1)}, s32[1,1,4]{2,1,0:T(1,128)}, u32[]{:S(2)}) copy-start(s32[1,1,4]{2,1,0:T(1,128)} %param.26) | copy-start | bytes 52
  339.0 13.1 %collective-permute-start.25 = (bf16[2,2,2,48,64]{4,3,0,1,2:T(8,128)(2,1)S(1)}, bf16[2,2,2,48,64]{4,3,0,1,2:T(8,128)(2,1)S(1)}, u32[]{:S(2)}, u32[]{:S(2)}) collective-permute-start(bf16[2,2,2,48,64]{4,3,0,1,2:T(8,128)(2,1)S(1)} %pad_maximum_fusion.12), channel_id=1, source_target_pairs={{0,32},{16,48},{32,0},{48,16},{64,96},{80,112},{96,64},{112,80},{1... | collective-permute-start | bytes 147464 | tf_op jit(solution)/shard_map/ppermute | solution.py:47
  347.6 13.9 %copy-start.34 = (s32[1,1,4]{2,1,0:T(1,128)S(1)}, s32[1,1,4]{2,1,0:T(1,128)}, u32[]{:S(2)}) copy-start(s32[1,1,4]{2,1,0:T(1,128)} %param.27) | copy-start | bytes 52
  347.6 8.4 %collective-permute-start.21 = (bf16[3,64,128]{2,0,1:T(4,128)(2,1)S(1)}, bf16[3,64,128]{2,0,1:T(4,128)(2,1)S(1)}, u32[]{:S(2)}, u32[]{:S(2)}) collective-permute-start(bf16[3,64,128]{2,0,1:T(4,128)(2,1)S(1)} %pad_maximum_fusion.20), channel_id=1, source_target_pairs={{1,0},{2,1},{3,2},{4,3},{5,4},{6,5},{7,6},{8,7},{9,8},{10,9},{11,1... | collective-permute-start | bytes 147464 | tf_op jit(solution)/shard_map/ppermute | solution.py:15
  349.6 7.0 collective-permute-start.20
  353.5 14.5 %collective-permute-start.26 = (bf16[2,2,2,2,48,64]{5,4,0,1,2,3:T(8,128)(2,1)}, bf16[2,2,2,2,48,64]{5,4,0,1,2,3:T(8,128)(2,1)}, u32[]{:S(2)}, u32[]{:S(2)}) collective-permute-start(bf16[2,2,2,2,48,64]{5,4,0,1,2,3:T(8,128)(2,1)} %pad_maximum_fusion.7), channel_id=1, source_target_pairs={{0,16},{16,0},{32,48},{48,32},{64,80},{80,64},{96,112},{112,96},{1... | collective-permute-start | bytes 294920 | tf_op jit(solution)/shard_map/ppermute | solution.py:47
  364.2 18.1 %collective-permute-start.31 = (bf16[48,64]{1,0:T(8,128)(2,1)S(1)}, bf16[48,64]{1,0:T(8,128)(2,1)}, u32[]{:S(2)}, u32[]{:S(2)}) collective-permute-start(bf16[48,64]{1,0:T(8,128)(2,1)S(1)} %fusion.102), channel_id=1, source_target_pairs={{0,256},{16,272},{32,288},{48,304},{64,320},{80,336},{96,352},{112... | collective-permute-start | bytes 18440 | tf_op jit(solution)/shard_map/ppermute | solution.py:47
  380.4 298.3 %reduce-scatter.22.cloned.1.call-start = ((), (), s32[]{:S(2)}) async-start(), calls=%async_computation.8 | async-start | bytes 208896
  493.7 10.1 %collective-permute-start.27 = (bf16[3,64,128]{2,0,1:T(4,128)(2,1)}, bf16[3,64,128]{2,0,1:T(4,128)(2,1)}, u32[]{:S(2)}, u32[]{:S(2)}) collective-permute-start(bf16[3,64,128]{2,0,1:T(4,128)(2,1)} %copy.75), channel_id=1, source_target_pairs={{0,16},{16,32},{32,48},{48,64},{64,80},{80,96},{96,112},{112,128},... | collective-permute-start | bytes 147464 | tf_op jit(solution)/shard_map/ppermute | solution.py:15
  502.5 6.2 collective-permute-start.28
  510.2 5.2 collective-permute-start.30
  513.0 5.6 collective-permute-start.29
  526.3 9.7 %collective-permute-start.40 = (bf16[48,64]{1,0:T(8,128)(2,1)S(1)}, bf16[48,64]{1,0:T(8,128)(2,1)S(1)}, u32[]{:S(2)}, u32[]{:S(2)}) collective-permute-start(bf16[48,64]{1,0:T(8,128)(2,1)S(1)} %fusion.103), channel_id=1, source_target_pairs={{0,256},{16,272},{32,288},{48,304},{64,320},{80,336},{96,352},{112... | collective-permute-start | bytes 18440 | tf_op jit(solution)/shard_map/ppermute | solution.py:47
  530.1 9.3 %collective-permute-start.32 = (bf16[2,48,64]{2,1,0:T(8,128)(2,1)S(1)}, bf16[2,48,64]{2,1,0:T(8,128)(2,1)S(1)}, u32[]{:S(2)}, u32[]{:S(2)}) collective-permute-start(bf16[2,48,64]{2,1,0:T(8,128)(2,1)S(1)} %pad_maximum_fusion.33), channel_id=1, source_target_pairs={{0,128},{16,144},{32,160},{48,176},{64,192},{80,208},{96,224},{112... | collective-permute-start | bytes 36872 | tf_op jit(solution)/shard_map/ppermute | solution.py:47
  536.0 7.1 collective-permute-start.41
  543.2 6.0 collective-permute-start.33
  545.1 7.9 collective-permute-start.42
  549.2 8.0 collective-permute-start.34
  553.1 8.4 %collective-permute-start.43 = (bf16[2,2,2,48,64]{4,3,0,1,2:T(8,128)(2,1)S(1)}, bf16[2,2,2,48,64]{4,3,0,1,2:T(8,128)(2,1)S(1)}, u32[]{:S(2)}, u32[]{:S(2)}) collective-permute-start(bf16[2,2,2,48,64]{4,3,0,1,2:T(8,128)(2,1)S(1)} %pad_maximum_fusion.14), channel_id=1, source_target_pairs={{0,32},{16,48},{32,0},{48,16},{64,96},{80,112},{96,64},{112,80},{1... | collective-permute-start | bytes 147464 | tf_op jit(solution)/shard_map/ppermute | solution.py:47
  557.3 9.2 %collective-permute-start.35 = (bf16[2,2,2,2,48,64]{5,4,0,1,2,3:T(8,128)(2,1)S(1)}, bf16[2,2,2,2,48,64]{5,4,0,1,2,3:T(8,128)(2,1)S(1)}, u32[]{:S(2)}, u32[]{:S(2)}) collective-permute-start(bf16[2,2,2,2,48,64]{5,4,0,1,2,3:T(8,128)(2,1)S(1)} %pad_maximum_fusion.8), channel_id=1, source_target_pairs={{0,16},{16,0},{32,48},{48,32},{64,80},{80,64},{96,112},{112,96},{1... | collective-permute-start | bytes 294920 | tf_op jit(solution)/shard_map/ppermute | solution.py:47
  562.9 15.1 %collective-permute-start.44 = (bf16[2,2,2,2,48,64]{5,4,0,1,2,3:T(8,128)(2,1)}, bf16[2,2,2,2,48,64]{5,4,0,1,2,3:T(8,128)(2,1)}, u32[]{:S(2)}, u32[]{:S(2)}) collective-permute-start(bf16[2,2,2,2,48,64]{5,4,0,1,2,3:T(8,128)(2,1)} %pad_maximum_fusion.9), channel_id=1, source_target_pairs={{0,16},{16,0},{32,48},{48,32},{64,80},{80,64},{96,112},{112,96},{1... | collective-permute-start | bytes 294920 | tf_op jit(solution)/shard_map/ppermute | solution.py:47
  578.0 191.2 %reduce-scatter.24.cloned.1.call-start = ((), (), s32[]{:S(2)}) async-start(), calls=%async_computation.9 | async-start | bytes 208896
  686.2 104.6 %copy-start.31 = (s32[1,1,4]{2,1,0:T(1,128)S(1)}, s32[1,1,4]{2,1,0:T(1,128)}, u32[]{:S(2)}) copy-start(s32[1,1,4]{2,1,0:T(1,128)} %param.26) | copy-start | bytes 52
  690.5 82.8 %collective-permute-start.36 = (bf16[3,64,128]{2,0,1:T(4,128)(2,1)}, bf16[3,64,128]{2,0,1:T(4,128)(2,1)}, u32[]{:S(2)}, u32[]{:S(2)}) collective-permute-start(bf16[3,64,128]{2,0,1:T(4,128)(2,1)} %copy.83), channel_id=1, source_target_pairs={{0,16},{16,32},{32,48},{48,64},{64,80},{80,96},{96,112},{112,128},... | collective-permute-start | bytes 147464 | tf_op jit(solution)/shard_map/ppermute | solution.py:15
  772.0 6.2 collective-permute-start.37
  779.8 5.2 collective-permute-start.39
  782.6 5.6 collective-permute-start.38
  (25 other events, 82.4 us)
Sparse Core Ops, SparseCore 0:
  107.3 103.1 reduce-scatter.15
  215.1 87.3 reduce-scatter.17
  380.5 100.7 reduce-scatter.19
  578.1 100.5 reduce-scatter.21
  683.1 85.9 reduce-scatter.23

commit v3 on v1

--- a/solution.py
+++ b/solution.py
@@ -5,32 +5,31 @@
 
 ITERS = 6
 
-
-OFFSETS = ((-1, -1), (-1, 0), (-1, 1), (0, -1), (0, 1), (1, -1), (1, 0), (1, 1))
+SEND_ORDER = (7, 6, 5, 2, 1, 0, 4, 3)
+RECV_DIRS = (0, 3, 5, 2, 4, 7, 1, 6)
 
 
-def neighbour_pieces(outgoing):
-    rows = lax.axis_size("row")
-    cols = lax.axis_size("col")
-    arrived = []
-    for direction in range(8):
-        shift_a, shift_b = OFFSETS[direction]
-        portion = outgoing[7 - direction]
-        route = []
-        for a in range(rows):
-            for b in range(cols):
-                src_a, src_b = a + shift_a, b + shift_b
-                if 0 <= src_a < rows and 0 <= src_b < cols:
-                    route.append((src_a * cols + src_b, a * cols + b))
-        if shift_a == 0:
-            route = [(s % cols, t % cols) for s, t in route if s // cols == 0]
-            arrived.append(lax.ppermute(portion, "col", route))
-        elif shift_b == 0:
-            route = [(s // cols, t // cols) for s, t in route if s % cols == 0]
-            arrived.append(lax.ppermute(portion, "row", route))
-        else:
-            arrived.append(lax.ppermute(portion, ("row", "col"), route))
-    return jnp.stack(arrived, 0)
+def shifted(block, axis, distance):
+    size = lax.axis_size(axis)
+    route = [(i + distance, i) for i in range(size) if 0 <= i + distance < size]
+    return lax.ppermute(block, axis, route)
+
+
+def neighbour_pieces(outgoing, width):
+    from_above = shifted(outgoing[:, 0 : 3 * width], "row", -1)
+    from_below = shifted(outgoing[:, 3 * width : 6 * width], "row", 1)
+    to_right = jnp.concatenate(
+        [from_above[:, :width], outgoing[:, 6 * width : 7 * width], from_below[:, :width]], 1
+    )
+    to_left = jnp.concatenate(
+        [from_above[:, 2 * width :], outgoing[:, 7 * width :], from_below[:, 2 * width :]], 1
+    )
+    from_left = shifted(to_right, "col", -1)
+    from_right = shifted(to_left, "col", 1)
+    return jnp.concatenate(
+        [from_left, from_right, from_above[:, width : 2 * width], from_below[:, width : 2 * width]],
+        1,
+    )
 
 
 def gather_rows(piece, bits):
@@ -51,9 +50,8 @@
 def scatter_cols(partial, bits):
     index = lax.axis_index("col")
     size = lax.axis_size("col")
-    total_bits = len(bits)
     current = partial
-    remaining = list(range(total_bits - 1, -1, -1))
+    remaining = list(range(len(bits) - 1, -1, -1))
     for bit in bits:
         axis = remaining.index(bit)
         distance = 1 << bit
@@ -79,7 +77,6 @@
     slot_dir,
     slot_block,
 ):
-    highest = lax.Precision.HIGHEST
     columns = rhs.shape[2]
     unknowns = rhs.shape[3]
     block_size = coupling.shape[3]
@@ -88,17 +85,23 @@
     row_bits = lax.axis_size("row").bit_length() - 1
     col_bits = lax.axis_size("col").bit_length() - 1
     rhs_full = rhs[0, 0].astype(jnp.float32)
-    operator_matrix = operator_blocks[0, 0]
     solver_matrix = local_solver[0, 0]
     mode_basis = modes[0, 0]
-    couplings = coupling[0, 0]
     coarse_tile = coarse_inverse[0, :, 0, :]
-    send_onehot = (send_block[0, 0][:, None] == jnp.arange(block_count)[None, :]).astype(
-        jnp.bfloat16
-    )
-    dir_onehot = (slot_dir[0, 0][:, None] == jnp.arange(8)[None, :]).astype(jnp.bfloat16)
-    block_onehot = (slot_block[0, 0][:, None] == jnp.arange(block_count)[None, :]).astype(
-        jnp.float32
+    eye = jnp.eye(block_size, dtype=jnp.float32)
+
+    send_onehot = (
+        send_block[0, 0][jnp.array(SEND_ORDER)][:, None] == jnp.arange(block_count)[None, :]
+    ).astype(jnp.float32)
+    select = jnp.einsum("jk,nm->knjm", send_onehot, eye).reshape(unknowns, -1).astype(jnp.bfloat16)
+
+    slot_of = (slot_dir[0, 0][:, None] == jnp.array(RECV_DIRS)[None, :]).astype(jnp.float32)
+    block_of = (slot_block[0, 0][:, None] == jnp.arange(block_count)[None, :]).astype(jnp.float32)
+    placed_matrix = jnp.einsum(
+        "sj,sk,snm->jnkm", slot_of, block_of, coupling[0, 0].astype(jnp.float32)
+    ).reshape(-1, unknowns)
+    operator_matrix = jnp.concatenate(
+        [operator_blocks[0, 0], placed_matrix.astype(jnp.bfloat16)], 0
     )
 
     def coarse_solve(rounded):
@@ -121,22 +124,13 @@
             residual = rhs_full
         else:
             field_half = solution.astype(jnp.bfloat16)
-            blocks = field_half.reshape(columns, block_count, block_size)
-            outgoing = jnp.einsum(
-                "ckn,ek->ecn", blocks, send_onehot, preferred_element_type=jnp.float32
-            ).astype(jnp.bfloat16)
-            incoming = neighbour_pieces(outgoing)
-            chosen = jnp.einsum(
-                "sd,dcn->scn", dir_onehot, incoming, preferred_element_type=jnp.float32
-            ).astype(jnp.bfloat16)
-            coupled = jnp.einsum(
-                "scn,snm->scm", chosen, couplings, preferred_element_type=jnp.float32
+            outgoing = jnp.dot(field_half, select, preferred_element_type=jnp.float32).astype(
+                jnp.bfloat16
             )
-            placed = jnp.einsum("scm,sk->ckm", coupled, block_onehot, precision=highest).reshape(
-                columns, unknowns
-            )
-            residual = rhs_full - (
-                jnp.dot(field_half, operator_matrix, preferred_element_type=jnp.float32) + placed
+            incoming = neighbour_pieces(outgoing, block_size)
+            stacked = jnp.concatenate([field_half, incoming], 1)
+            residual = rhs_full - jnp.dot(
+                stacked, operator_matrix, preferred_element_type=jnp.float32
             )
         rounded = residual.astype(jnp.bfloat16)
         update = jnp.dot(rounded, solver_matrix, preferred_element_type=jnp.float32)

time: 700 us -> 502 us (0.72)
  the two profiles are of different devices: /device:TPU:38 before, /device:TPU:6 now
where the time goes in v3:
time: 502 us; the launch traced here: 497 us
  starting transfers between devices  262 us (52%)
  local copies, waits for them, and re-layouts  90.2 us (18%)
  waiting for transfers between devices  79.9 us (16%)
  matrix products  36.2 us (7%)
  other arithmetic  26.8 us (5%)
    ppermute x25, starting transfers between devices, gather_rows(): other = lax.ppermute(current, 'row', route)  123 us
    ppermute x20, starting transfers between devices, scatter_cols(): current = keep + lax.ppermute(send, 'col', route)  96.3 us
    ppermute x20, starting transfers between devices, shifted(): return lax.ppermute(block, axis, route)  42.8 us
    unnamed x105, local copies, waits for them, and re-layouts  31.4 us
    ppermute x25, waiting for transfers between devices, gather_rows(): other = lax.ppermute(current, 'row', route)  30.6 us
    ppermute x20, waiting for transfers between devices, scatter_cols(): current = keep + lax.ppermute(send, 'col', route)  25.6 us
    ppermute x20, waiting for transfers between devices, shifted(): return lax.ppermute(block, axis, route)  23.7 us
    reshape x5, local copies, waits for them, and re-layouts, coarse_solve(): partial_sums = partial_sums.reshape((2,) * col_bits + (mode_count, columns))  12.9 us
  transfers between devices with their start and end apart: 65, of which 27 were waited for; matrix products, arithmetic and copies ran while one was open for 23% of the time, Pallas kernels for 0%

profile of v3, /device:TPU:6, one launch (start us, length us, event | category | flops | bytes accessed | tf_op | source)
XLA Modules:
  0.0 497.0 jit_solution(4931614750053973959)
XLA Ops:
  1.2 9.1 %collective-permute-start.4 = (bf16[48,64]{1,0:T(8,128)(2,1)S(1)}, bf16[48,64]{1,0:T(8,128)(2,1)S(1)}, u32[]{:S(2)}, u32[]{:S(2)}) collective-permute-start(bf16[48,64]{1,0:T(8,128)(2,1)S(1)} %convolution_convert_fusion.5), channel_id=1, source_target_pairs={{0,256},{16,272},{32,288},{48,304},{64,320},{80,336},{96,352},{112... | collective-permute-start | bytes 18440 | tf_op jit(solution)/shard_map/ppermute | solution.py:42
  17.2 4.1 collective-permute-start
  22.7 7.8 %collective-permute-start.5 = (bf16[2,48,64]{2,1,0:T(8,128)(2,1)S(1)}, bf16[2,48,64]{2,1,0:T(8,128)(2,1)S(1)}, u32[]{:S(2)}, u32[]{:S(2)}) collective-permute-start(bf16[2,48,64]{2,1,0:T(8,128)(2,1)S(1)} %pad_maximum_fusion.31), channel_id=1, source_target_pairs={{0,128},{16,144},{32,160},{48,176},{64,192},{80,208},{96,224},{112... | collective-permute-start | bytes 36872 | tf_op jit(solution)/shard_map/ppermute | solution.py:42
  33.2 3.8 collective-permute-start.6
  37.6 3.2 copy.77
  40.9 3.1 copy.153
  50.4 3.6 collective-permute-start.3
  54.7 5.9 %collective-permute-done.3 = bf16[64,384]{1,0:T(8,128)(2,1)S(1)} collective-permute-done((bf16[64,384]{1,0:T(8,128)(2,1)S(1)}, bf16[64,384]{1,0:T(8,128)(2,1)S(1)}, u32[]{:S(2)}, u32[]{:S(2)}) %collective-permute-start.3) | collective-permute-done | bytes 49184 | tf_op jit(solution)/shard_map/ppermute | solution.py:15
  63.9 2.9 fusion.69
  66.9 5.8 %collective-permute-start.17 = (bf16[48,64]{1,0:T(8,128)(2,1)S(1)}, bf16[48,64]{1,0:T(8,128)(2,1)S(1)}, u32[]{:S(2)}, u32[]{:S(2)}) collective-permute-start(bf16[48,64]{1,0:T(8,128)(2,1)S(1)} %fusion.74), channel_id=1, source_target_pairs={{0,256},{16,272},{32,288},{48,304},{64,320},{80,336},{96,352},{112... | collective-permute-start | bytes 18440 | tf_op jit(solution)/shard_map/ppermute | solution.py:42
  72.7 2.8 collective-permute-start.7
  76.6 3.4 collective-permute-start.18
  85.4 2.9 collective-permute-start.8
  89.3 3.6 collective-permute-start.20
  93.9 3.4 collective-permute-done.20
  105.7 2.6 reshape.119
  108.3 2.5 fusion.133
  115.4 11.2 %collective-permute-start.9 = (f32[2,2,2,48,64]{4,3,0,1,2:T(8,128)S(1)}, f32[2,2,2,48,64]{4,3,0,1,2:T(8,128)S(1)}, u32[]{:S(2)}, u32[]{:S(2)}) collective-permute-start(f32[2,2,2,48,64]{4,3,0,1,2:T(8,128)S(1)} %get-tuple-element.24), channel_id=1, source_target_pairs={{0,1},{1,0},{2,3},{3,2},{4,5},{5,4},{6,7},{7,6},{8,9},{9,8},{10,11... | collective-permute-start | bytes 294920 | tf_op jit(solution)/shard_map/ppermute | solution.py:64
  127.6 3.6 collective-permute-start.21
  144.0 2.6 reshape.121
  150.8 2.5 fusion.132
  157.8 4.8 collective-permute-start.12
  165.7 6.9 %collective-permute-done.12 = f32[48,64]{1,0:T(8,128)S(1)} collective-permute-done((f32[48,64]{1,0:T(8,128)S(1)}, f32[48,64]{1,0:T(8,128)S(1)}, u32[]{:S(2)}, u32[]{:S(2)}) %collective-permute-start.12) | collective-permute-done | bytes 12320 | tf_op jit(solution)/shard_map/ppermute | solution.py:64
  174.4 3.4 collective-permute-start.13
  181.1 2.6 collective-permute-done.14
  185.8 5.4 %collective-permute-start.24 = (f32[2,48,64]{2,1,0:T(8,128)S(1)}, f32[2,48,64]{2,1,0:T(8,128)S(1)}, u32[]{:S(2)}, u32[]{:S(2)}) collective-permute-start(f32[2,48,64]{2,1,0:T(8,128)S(1)} %select_bitcast_fusion.40), channel_id=1, source_target_pairs={{0,4},{1,5},{2,6},{3,7},{4,0},{5,1},{6,2},{7,3},{8,12},{9,13},{10,... | collective-permute-start | bytes 73736 | tf_op jit(solution)/shard_map/ppermute | solution.py:64
  193.6 4.7 collective-permute-start.25
  199.9 11.3 %collective-permute-start.30 = (bf16[48,64]{1,0:T(8,128)(2,1)S(1)}, bf16[48,64]{1,0:T(8,128)(2,1)S(1)}, u32[]{:S(2)}, u32[]{:S(2)}) collective-permute-start(bf16[48,64]{1,0:T(8,128)(2,1)S(1)} %fusion.75), channel_id=1, source_target_pairs={{0,256},{16,272},{32,288},{48,304},{64,320},{80,336},{96,352},{112... | collective-permute-start | bytes 18440 | tf_op jit(solution)/shard_map/ppermute | solution.py:42
  213.3 3.6 collective-permute-start.31
  216.8 3.0 collective-permute-done.31
  219.9 2.9 collective-permute-start.32
  226.0 6.9 %collective-permute-start.33 = (bf16[2,2,2,48,64]{4,3,0,1,2:T(8,128)(2,1)S(1)}, bf16[2,2,2,48,64]{4,3,0,1,2:T(8,128)(2,1)S(1)}, u32[]{:S(2)}, u32[]{:S(2)}) collective-permute-start(bf16[2,2,2,48,64]{4,3,0,1,2:T(8,128)(2,1)S(1)} %pad_maximum_fusion.13), channel_id=1, source_target_pairs={{0,32},{16,48},{32,0},{48,16},{64,96},{80,112},{96,64},{112,80},{1... | collective-permute-start | bytes 147464 | tf_op jit(solution)/shard_map/ppermute | solution.py:42
  232.9 3.6 collective-permute-start.28
  238.6 13.4 %collective-permute-done.29 = bf16[64,384]{1,0:T(8,128)(2,1)S(1)} collective-permute-done((bf16[64,384]{1,0:T(8,128)(2,1)S(1)}, bf16[64,384]{1,0:T(8,128)(2,1)S(1)}, u32[]{:S(2)}, u32[]{:S(2)}) %collective-permute-start.29) | collective-permute-done | bytes 49184 | tf_op jit(solution)/shard_map/ppermute | solution.py:15
  253.1 6.8 %collective-permute-start.43 = (bf16[48,64]{1,0:T(8,128)(2,1)S(1)}, bf16[48,64]{1,0:T(8,128)(2,1)S(1)}, u32[]{:S(2)}, u32[]{:S(2)}) collective-permute-start(bf16[48,64]{1,0:T(8,128)(2,1)S(1)} %fusion.76), channel_id=1, source_target_pairs={{0,256},{16,272},{32,288},{48,304},{64,320},{80,336},{96,352},{112... | collective-permute-start | bytes 18440 | tf_op jit(solution)/shard_map/ppermute | solution.py:42
  260.0 2.7 collective-permute-done.43
  262.7 4.8 collective-permute-start.44
  267.5 3.3 collective-permute-start.34
  273.9 3.0 collective-permute-done.45
  277.6 5.9 %collective-permute-start.46 = (bf16[2,2,2,48,64]{4,3,0,1,2:T(8,128)(2,1)}, bf16[2,2,2,48,64]{4,3,0,1,2:T(8,128)(2,1)}, u32[]{:S(2)}, u32[]{:S(2)}) collective-permute-start(bf16[2,2,2,48,64]{4,3,0,1,2:T(8,128)(2,1)} %pad_maximum_fusion.14), channel_id=1, source_target_pairs={{0,32},{16,48},{32,0},{48,16},{64,96},{80,112},{96,64},{112,80},{1... | collective-permute-start | bytes 147464 | tf_op jit(solution)/shard_map/ppermute | solution.py:42
  291.2 2.6 reshape.123
  293.8 2.5 fusion.131
  300.8 13.0 %collective-permute-start.35 = (f32[2,2,2,48,64]{4,3,0,1,2:T(8,128)S(1)}, f32[2,2,2,48,64]{4,3,0,1,2:T(8,128)S(1)}, u32[]{:S(2)}, u32[]{:S(2)}) collective-permute-start(f32[2,2,2,48,64]{4,3,0,1,2:T(8,128)S(1)} %select_bitcast_fusion.6), channel_id=1, source_target_pairs={{0,1},{1,0},{2,3},{3,2},{4,5},{5,4},{6,7},{7,6},{8,9},{9,8},{10,11... | collective-permute-start | bytes 294920 | tf_op jit(solution)/shard_map/ppermute | solution.py:64
  331.2 2.6 reshape.125
  338.0 2.5 fusion.130
  345.0 3.8 collective-permute-start.38
  351.9 7.6 %collective-permute-done.38 = f32[48,64]{1,0:T(8,128)S(1)} collective-permute-done((f32[48,64]{1,0:T(8,128)S(1)}, f32[48,64]{1,0:T(8,128)S(1)}, u32[]{:S(2)}, u32[]{:S(2)}) %collective-permute-start.38) | collective-permute-done | bytes 12320 | tf_op jit(solution)/shard_map/ppermute | solution.py:64
  365.0 3.6 collective-permute-start.49
  371.6 5.4 %collective-permute-start.50 = (f32[2,48,64]{2,1,0:T(8,128)S(1)}, f32[2,48,64]{2,1,0:T(8,128)S(1)}, u32[]{:S(2)}, u32[]{:S(2)}) collective-permute-start(f32[2,48,64]{2,1,0:T(8,128)S(1)} %select_bitcast_fusion.34), channel_id=1, source_target_pairs={{0,4},{1,5},{2,6},{3,7},{4,0},{5,1},{6,2},{7,3},{8,12},{9,13},{10,... | collective-permute-start | bytes 73736 | tf_op jit(solution)/shard_map/ppermute | solution.py:64
  379.4 5.3 %collective-permute-start.51 = (f32[48,64]{1,0:T(8,128)S(1)}, f32[48,64]{1,0:T(8,128)S(1)}, u32[]{:S(2)}, u32[]{:S(2)}) collective-permute-start(f32[48,64]{1,0:T(8,128)S(1)} %select_bitcast_fusion.49), channel_id=1, source_target_pairs={{0,8},{1,9},{2,10},{3,11},{4,12},{5,13},{6,14},{7,15},{8,0},{9,1},... | collective-permute-start | bytes 36872 | tf_op jit(solution)/shard_map/ppermute | solution.py:64
  386.2 10.4 %collective-permute-start.56 = (bf16[48,64]{1,0:T(8,128)(2,1)S(1)}, bf16[48,64]{1,0:T(8,128)(2,1)S(1)}, u32[]{:S(2)}, u32[]{:S(2)}) collective-permute-start(bf16[48,64]{1,0:T(8,128)(2,1)S(1)} %fusion.77), channel_id=1, source_target_pairs={{0,256},{16,272},{32,288},{48,304},{64,320},{80,336},{96,352},{112... | collective-permute-start | bytes 18440 | tf_op jit(solution)/shard_map/ppermute | solution.py:42
  398.3 4.4 collective-permute-start.57
  404.9 4.6 collective-permute-start.58
  412.4 6.0 %collective-permute-start.59 = (bf16[2,2,2,48,64]{4,3,0,1,2:T(8,128)(2,1)S(1)}, bf16[2,2,2,48,64]{4,3,0,1,2:T(8,128)(2,1)S(1)}, u32[]{:S(2)}, u32[]{:S(2)}) collective-permute-start(bf16[2,2,2,48,64]{4,3,0,1,2:T(8,128)(2,1)S(1)} %pad_maximum_fusion.15), channel_id=1, source_target_pairs={{0,32},{16,48},{32,0},{48,16},{64,96},{80,112},{96,64},{112,80},{1... | collective-permute-start | bytes 147464 | tf_op jit(solution)/shard_map/ppermute | solution.py:42
  423.6 3.3 collective-permute-start.60
  427.8 3.4 collective-permute-done.60
  434.2 2.5 reshape.126
  438.8 2.6 reshape.127
  448.4 14.0 %collective-permute-start.61 = (f32[2,2,2,48,64]{4,3,0,1,2:T(8,128)S(1)}, f32[2,2,2,48,64]{4,3,0,1,2:T(8,128)S(1)}, u32[]{:S(2)}, u32[]{:S(2)}) collective-permute-start(f32[2,2,2,48,64]{4,3,0,1,2:T(8,128)S(1)} %select_bitcast_fusion), channel_id=1, source_target_pairs={{0,1},{1,0},{2,3},{3,2},{4,5},{5,4},{6,7},{7,6},{8,9},{9,8},{10,11... | collective-permute-start | bytes 294920 | tf_op jit(solution)/shard_map/ppermute | solution.py:64
  468.1 3.4 collective-permute-done.62
  474.8 4.2 collective-permute-done.63
  480.2 7.6 %collective-permute-start.64 = (f32[48,64]{1,0:T(8,128)}, f32[48,64]{1,0:T(8,128)}, u32[]{:S(2)}, u32[]{:S(2)}) collective-permute-start(f32[48,64]{1,0:T(8,128)} %select_bitcast_fusion.46), channel_id=1, source_target_pairs={{0,8},{1,9},{2,10},{3,11},{4,12},{5,13},{6,14},{7,15},{8,0},{9,1},... | collective-permute-start | bytes 36872 | tf_op jit(solution)/shard_map/ppermute | solution.py:64
  487.8 4.0 fusion.21
  491.8 3.1 collective-permute-done.64
  (350 shorter events, 183.0 us)
Async XLA Ops:
  1.2 21.5 %collective-permute-start.4 = (bf16[48,64]{1,0:T(8,128)(2,1)S(1)}, bf16[48,64]{1,0:T(8,128)(2,1)S(1)}, u32[]{:S(2)}, u32[]{:S(2)}) collective-permute-start(bf16[48,64]{1,0:T(8,128)(2,1)S(1)} %convolution_convert_fusion.5), channel_id=1, source_target_pairs={{0,256},{16,272},{32,288},{48,304},{64,320},{80,336},{96,352},{112... | collective-permute-start | bytes 18440 | tf_op jit(solution)/shard_map/ppermute | solution.py:42
  17.2 29.1 %collective-permute-start = (bf16[64,384]{1,0:T(8,128)(2,1)}, bf16[64,384]{1,0:T(8,128)(2,1)}, u32[]{:S(2)}, u32[]{:S(2)}) collective-permute-start(bf16[64,384]{1,0:T(8,128)(2,1)} %get-tuple-element.58), channel_id=1, source_target_pairs={{0,16},{16,32},{32,48},{48,64},{64,80},{80,96},{96,112},{112,128},... | collective-permute-start | bytes 147464 | tf_op jit(solution)/shard_map/ppermute | solution.py:15
  21.3 25.7 %collective-permute-start.1 = (bf16[64,384]{1,0:T(8,128)(2,1)}, bf16[64,384]{1,0:T(8,128)(2,1)}, u32[]{:S(2)}, u32[]{:S(2)}) collective-permute-start(bf16[64,384]{1,0:T(8,128)(2,1)} %get-tuple-element.59), channel_id=1, source_target_pairs={{16,0},{32,16},{48,32},{64,48},{80,64},{96,80},{112,96},{128,112},... | collective-permute-start | bytes 147464 | tf_op jit(solution)/shard_map/ppermute | solution.py:15
  22.7 9.8 %collective-permute-start.5 = (bf16[2,48,64]{2,1,0:T(8,128)(2,1)S(1)}, bf16[2,48,64]{2,1,0:T(8,128)(2,1)S(1)}, u32[]{:S(2)}, u32[]{:S(2)}) collective-permute-start(bf16[2,48,64]{2,1,0:T(8,128)(2,1)S(1)} %pad_maximum_fusion.31), channel_id=1, source_target_pairs={{0,128},{16,144},{32,160},{48,176},{64,192},{80,208},{96,224},{112... | collective-permute-start | bytes 36872 | tf_op jit(solution)/shard_map/ppermute | solution.py:42
  33.2 12.3 %collective-permute-start.6 = (bf16[2,2,48,64]{3,2,0,1:T(8,128)(2,1)}, bf16[2,2,48,64]{3,2,0,1:T(8,128)(2,1)}, u32[]{:S(2)}, u32[]{:S(2)}) collective-permute-start(bf16[2,2,48,64]{3,2,0,1:T(8,128)(2,1)} %pad_maximum_fusion.18), channel_id=1, source_target_pairs={{0,64},{16,80},{32,96},{48,112},{64,0},{80,16},{96,32},{112,48},{1... | collective-permute-start | bytes 73736 | tf_op jit(solution)/shard_map/ppermute | solution.py:42
  50.4 10.2 %collective-permute-start.3 = (bf16[64,384]{1,0:T(8,128)(2,1)S(1)}, bf16[64,384]{1,0:T(8,128)(2,1)S(1)}, u32[]{:S(2)}, u32[]{:S(2)}) collective-permute-start(bf16[64,384]{1,0:T(8,128)(2,1)S(1)} %pad_maximum_fusion.17), channel_id=1, source_target_pairs={{1,0},{2,1},{3,2},{4,3},{5,4},{6,5},{7,6},{8,7},{9,8},{10,9},{11,1... | collective-permute-start | bytes 147464 | tf_op jit(solution)/shard_map/ppermute | solution.py:15
  66.9 9.6 %collective-permute-start.17 = (bf16[48,64]{1,0:T(8,128)(2,1)S(1)}, bf16[48,64]{1,0:T(8,128)(2,1)S(1)}, u32[]{:S(2)}, u32[]{:S(2)}) collective-permute-start(bf16[48,64]{1,0:T(8,128)(2,1)S(1)} %fusion.74), channel_id=1, source_target_pairs={{0,256},{16,272},{32,288},{48,304},{64,320},{80,336},{96,352},{112... | collective-permute-start | bytes 18440 | tf_op jit(solution)/shard_map/ppermute | solution.py:42
  72.7 8.0 %collective-permute-start.7 = (bf16[2,2,2,48,64]{4,3,0,1,2:T(8,128)(2,1)S(1)}, bf16[2,2,2,48,64]{4,3,0,1,2:T(8,128)(2,1)S(1)}, u32[]{:S(2)}, u32[]{:S(2)}) collective-permute-start(bf16[2,2,2,48,64]{4,3,0,1,2:T(8,128)(2,1)S(1)} %pad_maximum_fusion.11), channel_id=1, source_target_pairs={{0,32},{16,48},{32,0},{48,16},{64,96},{80,112},{96,64},{112,80},{1... | collective-permute-start | bytes 147464 | tf_op jit(solution)/shard_map/ppermute | solution.py:42
  76.6 6.6 %collective-permute-start.18 = (bf16[2,48,64]{2,1,0:T(8,128)(2,1)S(1)}, bf16[2,48,64]{2,1,0:T(8,128)(2,1)S(1)}, u32[]{:S(2)}, u32[]{:S(2)}) collective-permute-start(bf16[2,48,64]{2,1,0:T(8,128)(2,1)S(1)} %pad_maximum_fusion.32), channel_id=1, source_target_pairs={{0,128},{16,144},{32,160},{48,176},{64,192},{80,208},{96,224},{112... | collective-permute-start | bytes 36872 | tf_op jit(solution)/shard_map/ppermute | solution.py:42
  83.2 6.0 %collective-permute-start.19 = (bf16[2,2,48,64]{3,2,0,1:T(8,128)(2,1)S(1)}, bf16[2,2,48,64]{3,2,0,1:T(8,128)(2,1)S(1)}, u32[]{:S(2)}, u32[]{:S(2)}) collective-permute-start(bf16[2,2,48,64]{3,2,0,1:T(8,128)(2,1)S(1)} %pad_maximum_fusion.21), channel_id=1, source_target_pairs={{0,64},{16,80},{32,96},{48,112},{64,0},{80,16},{96,32},{112,48},{1... | collective-permute-start | bytes 73736 | tf_op jit(solution)/shard_map/ppermute | solution.py:42
  85.4 12.7 %collective-permute-start.8 = (bf16[2,2,2,2,48,64]{5,4,0,1,2,3:T(8,128)(2,1)S(1)}, bf16[2,2,2,2,48,64]{5,4,0,1,2,3:T(8,128)(2,1)S(1)}, u32[]{:S(2)}, u32[]{:S(2)}) collective-permute-start(bf16[2,2,2,2,48,64]{5,4,0,1,2,3:T(8,128)(2,1)S(1)} %pad_maximum_fusion.6), channel_id=1, source_target_pairs={{0,16},{16,0},{32,48},{48,32},{64,80},{80,64},{96,112},{112,96},{1... | collective-permute-start | bytes 294920 | tf_op jit(solution)/shard_map/ppermute | solution.py:42
  89.3 8.0 %collective-permute-start.20 = (bf16[2,2,2,48,64]{4,3,0,1,2:T(8,128)(2,1)S(1)}, bf16[2,2,2,48,64]{4,3,0,1,2:T(8,128)(2,1)S(1)}, u32[]{:S(2)}, u32[]{:S(2)}) collective-permute-start(bf16[2,2,2,48,64]{4,3,0,1,2:T(8,128)(2,1)S(1)} %pad_maximum_fusion.12), channel_id=1, source_target_pairs={{0,32},{16,48},{32,0},{48,16},{64,96},{80,112},{96,64},{112,80},{1... | collective-permute-start | bytes 147464 | tf_op jit(solution)/shard_map/ppermute | solution.py:42
  115.4 15.9 %collective-permute-start.9 = (f32[2,2,2,48,64]{4,3,0,1,2:T(8,128)S(1)}, f32[2,2,2,48,64]{4,3,0,1,2:T(8,128)S(1)}, u32[]{:S(2)}, u32[]{:S(2)}) collective-permute-start(f32[2,2,2,48,64]{4,3,0,1,2:T(8,128)S(1)} %get-tuple-element.24), channel_id=1, source_target_pairs={{0,1},{1,0},{2,3},{3,2},{4,5},{5,4},{6,7},{7,6},{8,9},{9,8},{10,11... | collective-permute-start | bytes 294920 | tf_op jit(solution)/shard_map/ppermute | solution.py:64
  127.6 8.7 %collective-permute-start.21 = (bf16[2,2,2,2,48,64]{5,4,0,1,2,3:T(8,128)(2,1)S(1)}, bf16[2,2,2,2,48,64]{5,4,0,1,2,3:T(8,128)(2,1)S(1)}, u32[]{:S(2)}, u32[]{:S(2)}) collective-permute-start(bf16[2,2,2,2,48,64]{5,4,0,1,2,3:T(8,128)(2,1)S(1)} %pad_maximum_fusion.7), channel_id=1, source_target_pairs={{0,16},{16,0},{32,48},{48,32},{64,80},{80,64},{96,112},{112,96},{1... | collective-permute-start | bytes 294920 | tf_op jit(solution)/shard_map/ppermute | solution.py:42
  132.1 14.5 %collective-permute-start.10 = (f32[2,2,48,64]{3,2,1,0:T(8,128)}, f32[2,2,48,64]{3,2,1,0:T(8,128)}, u32[]{:S(2)}, u32[]{:S(2)}) collective-permute-start(f32[2,2,48,64]{3,2,1,0:T(8,128)} %get-tuple-element.36), channel_id=1, source_target_pairs={{0,2},{1,3},{2,0},{3,1},{4,6},{5,7},{6,4},{7,5},{8,10},{9,11},{10,... | collective-permute-start | bytes 147464 | tf_op jit(solution)/shard_map/ppermute | solution.py:64
  148.9 8.0 %collective-permute-start.11 = (f32[2,48,64]{2,1,0:T(8,128)}, f32[2,48,64]{2,1,0:T(8,128)}, u32[]{:S(2)}, u32[]{:S(2)}) collective-permute-start(f32[2,48,64]{2,1,0:T(8,128)} %select_bitcast_fusion.43), channel_id=1, source_target_pairs={{0,4},{1,5},{2,6},{3,7},{4,0},{5,1},{6,2},{7,3},{8,12},{9,13},{10,... | collective-permute-start | bytes 73736 | tf_op jit(solution)/shard_map/ppermute | solution.py:64
  157.8 14.8 %collective-permute-start.12 = (f32[48,64]{1,0:T(8,128)S(1)}, f32[48,64]{1,0:T(8,128)S(1)}, u32[]{:S(2)}, u32[]{:S(2)}) collective-permute-start(f32[48,64]{1,0:T(8,128)S(1)} %select_bitcast_fusion.58), channel_id=1, source_target_pairs={{0,8},{1,9},{2,10},{3,11},{4,12},{5,13},{6,14},{7,15},{8,0},{9,1},... | collective-permute-start | bytes 36872 | tf_op jit(solution)/shard_map/ppermute | solution.py:64
  163.6 15.4 %collective-permute-start.22 = (f32[2,2,2,48,64]{4,3,0,1,2:T(8,128)S(1)}, f32[2,2,2,48,64]{4,3,0,1,2:T(8,128)S(1)}, u32[]{:S(2)}, u32[]{:S(2)}) collective-permute-start(f32[2,2,2,48,64]{4,3,0,1,2:T(8,128)S(1)} %select_bitcast_fusion.9), channel_id=1, source_target_pairs={{0,1},{1,0},{2,3},{3,2},{4,5},{5,4},{6,7},{7,6},{8,9},{9,8},{10,11... | collective-permute-start | bytes 294920 | tf_op jit(solution)/shard_map/ppermute | solution.py:64
  174.4 6.7 %collective-permute-start.13 = (bf16[64,384]{1,0:T(8,128)(2,1)S(1)}, bf16[64,384]{1,0:T(8,128)(2,1)S(1)}, u32[]{:S(2)}, u32[]{:S(2)}) collective-permute-start(bf16[64,384]{1,0:T(8,128)(2,1)S(1)} %get-tuple-element.54), channel_id=1, source_target_pairs={{0,16},{16,32},{32,48},{48,64},{64,80},{80,96},{96,112},{112,128},... | collective-permute-start | bytes 147464 | tf_op jit(solution)/shard_map/ppermute | solution.py:15
  177.8 6.0 %collective-permute-start.14 = (bf16[64,384]{1,0:T(8,128)(2,1)S(1)}, bf16[64,384]{1,0:T(8,128)(2,1)S(1)}, u32[]{:S(2)}, u32[]{:S(2)}) collective-permute-start(bf16[64,384]{1,0:T(8,128)(2,1)S(1)} %get-tuple-element.55), channel_id=1, source_target_pairs={{16,0},{32,16},{48,32},{64,48},{80,64},{96,80},{112,96},{128,112},... | collective-permute-start | bytes 147464 | tf_op jit(solution)/shard_map/ppermute | solution.py:15
  179.2 6.5 %collective-permute-start.23 = (f32[2,2,48,64]{3,2,0,1:T(8,128)S(1)}, f32[2,2,48,64]{3,2,0,1:T(8,128)S(1)}, u32[]{:S(2)}, u32[]{:S(2)}) collective-permute-start(f32[2,2,48,64]{3,2,0,1:T(8,128)S(1)} %select_bitcast_fusion.25), channel_id=1, source_target_pairs={{0,2},{1,3},{2,0},{3,1},{4,6},{5,7},{6,4},{7,5},{8,10},{9,11},{10,... | collective-permute-start | bytes 147464 | tf_op jit(solution)/shard_map/ppermute | solution.py:64
  183.8 14.5 %collective-permute-start.16 = (bf16[64,384]{1,0:T(8,128)(2,1)S(1)}, bf16[64,384]{1,0:T(8,128)(2,1)S(1)}, u32[]{:S(2)}, u32[]{:S(2)}) collective-permute-start(bf16[64,384]{1,0:T(8,128)(2,1)S(1)} %pad_maximum_fusion.20), channel_id=1, source_target_pairs={{1,0},{2,1},{3,2},{4,3},{5,4},{6,5},{7,6},{8,7},{9,8},{10,9},{11,1... | collective-permute-start | bytes 147464 | tf_op jit(solution)/shard_map/ppermute | solution.py:15
  185.8 7.8 %collective-permute-start.24 = (f32[2,48,64]{2,1,0:T(8,128)S(1)}, f32[2,48,64]{2,1,0:T(8,128)S(1)}, u32[]{:S(2)}, u32[]{:S(2)}) collective-permute-start(f32[2,48,64]{2,1,0:T(8,128)S(1)} %select_bitcast_fusion.40), channel_id=1, source_target_pairs={{0,4},{1,5},{2,6},{3,7},{4,0},{5,1},{6,2},{7,3},{8,12},{9,13},{10,... | collective-permute-start | bytes 73736 | tf_op jit(solution)/shard_map/ppermute | solution.py:64
  191.2 7.1 %collective-permute-start.15 = (bf16[64,384]{1,0:T(8,128)(2,1)S(1)}, bf16[64,384]{1,0:T(8,128)(2,1)S(1)}, u32[]{:S(2)}, u32[]{:S(2)}) collective-permute-start(bf16[64,384]{1,0:T(8,128)(2,1)S(1)} %pad_maximum_fusion.19), channel_id=1, source_target_pairs={{0,1},{1,2},{2,3},{3,4},{4,5},{5,6},{6,7},{7,8},{8,9},{9,10},{10,1... | collective-permute-start | bytes 147464 | tf_op jit(solution)/shard_map/ppermute | solution.py:15
  193.6 17.6 %collective-permute-start.25 = (f32[48,64]{1,0:T(8,128)S(1)}, f32[48,64]{1,0:T(8,128)S(1)}, u32[]{:S(2)}, u32[]{:S(2)}) collective-permute-start(f32[48,64]{1,0:T(8,128)S(1)} %select_bitcast_fusion.55), channel_id=1, source_target_pairs={{0,8},{1,9},{2,10},{3,11},{4,12},{5,13},{6,14},{7,15},{8,0},{9,1},... | collective-permute-start | bytes 36872 | tf_op jit(solution)/shard_map/ppermute | solution.py:64
  199.9 13.3 %collective-permute-start.30 = (bf16[48,64]{1,0:T(8,128)(2,1)S(1)}, bf16[48,64]{1,0:T(8,128)(2,1)S(1)}, u32[]{:S(2)}, u32[]{:S(2)}) collective-permute-start(bf16[48,64]{1,0:T(8,128)(2,1)S(1)} %fusion.75), channel_id=1, source_target_pairs={{0,256},{16,272},{32,288},{48,304},{64,320},{80,336},{96,352},{112... | collective-permute-start | bytes 18440 | tf_op jit(solution)/shard_map/ppermute | solution.py:42
  213.3 6.6 %collective-permute-start.31 = (bf16[2,48,64]{2,1,0:T(8,128)(2,1)S(1)}, bf16[2,48,64]{2,1,0:T(8,128)(2,1)S(1)}, u32[]{:S(2)}, u32[]{:S(2)}) collective-permute-start(bf16[2,48,64]{2,1,0:T(8,128)(2,1)S(1)} %pad_maximum_fusion.33), channel_id=1, source_target_pairs={{0,128},{16,144},{32,160},{48,176},{64,192},{80,208},{96,224},{112... | collective-permute-start | bytes 36872 | tf_op jit(solution)/shard_map/ppermute | solution.py:42
  219.9 6.0 %collective-permute-start.32 = (bf16[2,2,48,64]{3,2,0,1:T(8,128)(2,1)S(1)}, bf16[2,2,48,64]{3,2,0,1:T(8,128)(2,1)S(1)}, u32[]{:S(2)}, u32[]{:S(2)}) collective-permute-start(bf16[2,2,48,64]{3,2,0,1:T(8,128)(2,1)S(1)} %pad_maximum_fusion.24), channel_id=1, source_target_pairs={{0,64},{16,80},{32,96},{48,112},{64,0},{80,16},{96,32},{112,48},{1... | collective-permute-start | bytes 73736 | tf_op jit(solution)/shard_map/ppermute | solution.py:42
  222.8 10.0 %collective-permute-start.26 = (bf16[64,384]{1,0:T(8,128)(2,1)S(1)}, bf16[64,384]{1,0:T(8,128)(2,1)S(1)}, u32[]{:S(2)}, u32[]{:S(2)}) collective-permute-start(bf16[64,384]{1,0:T(8,128)(2,1)S(1)} %get-tuple-element.50), channel_id=1, source_target_pairs={{0,16},{16,32},{32,48},{48,64},{64,80},{80,96},{96,112},{112,128},... | collective-permute-start | bytes 147464 | tf_op jit(solution)/shard_map/ppermute | solution.py:15
  224.1 8.8 %collective-permute-start.27 = (bf16[64,384]{1,0:T(8,128)(2,1)S(1)}, bf16[64,384]{1,0:T(8,128)(2,1)S(1)}, u32[]{:S(2)}, u32[]{:S(2)}) collective-permute-start(bf16[64,384]{1,0:T(8,128)(2,1)S(1)} %get-tuple-element.51), channel_id=1, source_target_pairs={{16,0},{32,16},{48,32},{64,48},{80,64},{96,80},{112,96},{128,112},... | collective-permute-start | bytes 147464 | tf_op jit(solution)/shard_map/ppermute | solution.py:15
  226.0 34.0 %collective-permute-start.33 = (bf16[2,2,2,48,64]{4,3,0,1,2:T(8,128)(2,1)S(1)}, bf16[2,2,2,48,64]{4,3,0,1,2:T(8,128)(2,1)S(1)}, u32[]{:S(2)}, u32[]{:S(2)}) collective-permute-start(bf16[2,2,2,48,64]{4,3,0,1,2:T(8,128)(2,1)S(1)} %pad_maximum_fusion.13), channel_id=1, source_target_pairs={{0,32},{16,48},{32,0},{48,16},{64,96},{80,112},{96,64},{112,80},{1... | collective-permute-start | bytes 147464 | tf_op jit(solution)/shard_map/ppermute | solution.py:42
  232.9 5.6 %collective-permute-start.28 = (bf16[64,384]{1,0:T(8,128)(2,1)S(1)}, bf16[64,384]{1,0:T(8,128)(2,1)S(1)}, u32[]{:S(2)}, u32[]{:S(2)}) collective-permute-start(bf16[64,384]{1,0:T(8,128)(2,1)S(1)} %pad_maximum_fusion.22), channel_id=1, source_target_pairs={{0,1},{1,2},{2,3},{3,4},{4,5},{5,6},{6,7},{7,8},{8,9},{9,10},{10,1... | collective-permute-start | bytes 147464 | tf_op jit(solution)/shard_map/ppermute | solution.py:15
  236.6 15.4 %collective-permute-start.29 = (bf16[64,384]{1,0:T(8,128)(2,1)S(1)}, bf16[64,384]{1,0:T(8,128)(2,1)S(1)}, u32[]{:S(2)}, u32[]{:S(2)}) collective-permute-start(bf16[64,384]{1,0:T(8,128)(2,1)S(1)} %pad_maximum_fusion.23), channel_id=1, source_target_pairs={{1,0},{2,1},{3,2},{4,3},{5,4},{6,5},{7,6},{8,7},{9,8},{10,9},{11,1... | collective-permute-start | bytes 147464 | tf_op jit(solution)/shard_map/ppermute | solution.py:15
  253.1 9.5 %collective-permute-start.43 = (bf16[48,64]{1,0:T(8,128)(2,1)S(1)}, bf16[48,64]{1,0:T(8,128)(2,1)S(1)}, u32[]{:S(2)}, u32[]{:S(2)}) collective-permute-start(bf16[48,64]{1,0:T(8,128)(2,1)S(1)} %fusion.76), channel_id=1, source_target_pairs={{0,256},{16,272},{32,288},{48,304},{64,320},{80,336},{96,352},{112... | collective-permute-start | bytes 18440 | tf_op jit(solution)/shard_map/ppermute | solution.py:42
  262.7 8.2 %collective-permute-start.44 = (bf16[2,48,64]{2,1,0:T(8,128)(2,1)S(1)}, bf16[2,48,64]{2,1,0:T(8,128)(2,1)S(1)}, u32[]{:S(2)}, u32[]{:S(2)}) collective-permute-start(bf16[2,48,64]{2,1,0:T(8,128)(2,1)S(1)} %pad_maximum_fusion.34), channel_id=1, source_target_pairs={{0,128},{16,144},{32,160},{48,176},{64,192},{80,208},{96,224},{112... | collective-permute-start | bytes 36872 | tf_op jit(solution)/shard_map/ppermute | solution.py:42
  267.5 16.0 %collective-permute-start.34 = (bf16[2,2,2,2,48,64]{5,4,0,1,2,3:T(8,128)(2,1)S(1)}, bf16[2,2,2,2,48,64]{5,4,0,1,2,3:T(8,128)(2,1)S(1)}, u32[]{:S(2)}, u32[]{:S(2)}) collective-permute-start(bf16[2,2,2,2,48,64]{5,4,0,1,2,3:T(8,128)(2,1)S(1)} %pad_maximum_fusion.8), channel_id=1, source_target_pairs={{0,16},{16,0},{32,48},{48,32},{64,80},{80,64},{96,112},{112,96},{1... | collective-permute-start | bytes 294920 | tf_op jit(solution)/shard_map/ppermute | solution.py:42
  270.9 6.0 %collective-permute-start.45 = (bf16[2,2,48,64]{3,2,0,1:T(8,128)(2,1)S(1)}, bf16[2,2,48,64]{3,2,0,1:T(8,128)(2,1)S(1)}, u32[]{:S(2)}, u32[]{:S(2)}) collective-permute-start(bf16[2,2,48,64]{3,2,0,1:T(8,128)(2,1)S(1)} %pad_maximum_fusion.27), channel_id=1, source_target_pairs={{0,64},{16,80},{32,96},{48,112},{64,0},{80,16},{96,32},{112,48},{1... | collective-permute-start | bytes 73736 | tf_op jit(solution)/shard_map/ppermute | solution.py:42
  277.6 36.2 %collective-permute-start.46 = (bf16[2,2,2,48,64]{4,3,0,1,2:T(8,128)(2,1)}, bf16[2,2,2,48,64]{4,3,0,1,2:T(8,128)(2,1)}, u32[]{:S(2)}, u32[]{:S(2)}) collective-permute-start(bf16[2,2,2,48,64]{4,3,0,1,2:T(8,128)(2,1)} %pad_maximum_fusion.14), channel_id=1, source_target_pairs={{0,32},{16,48},{32,0},{48,16},{64,96},{80,112},{96,64},{112,80},{1... | collective-permute-start | bytes 147464 | tf_op jit(solution)/shard_map/ppermute | solution.py:42
  300.8 16.0 %collective-permute-start.35 = (f32[2,2,2,48,64]{4,3,0,1,2:T(8,128)S(1)}, f32[2,2,2,48,64]{4,3,0,1,2:T(8,128)S(1)}, u32[]{:S(2)}, u32[]{:S(2)}) collective-permute-start(f32[2,2,2,48,64]{4,3,0,1,2:T(8,128)S(1)} %select_bitcast_fusion.6), channel_id=1, source_target_pairs={{0,1},{1,0},{2,3},{3,2},{4,5},{5,4},{6,7},{7,6},{8,9},{9,8},{10,11... | collective-permute-start | bytes 294920 | tf_op jit(solution)/shard_map/ppermute | solution.py:64
  314.8 8.7 %collective-permute-start.47 = (bf16[2,2,2,2,48,64]{5,4,0,1,2,3:T(8,128)(2,1)S(1)}, bf16[2,2,2,2,48,64]{5,4,0,1,2,3:T(8,128)(2,1)S(1)}, u32[]{:S(2)}, u32[]{:S(2)}) collective-permute-start(bf16[2,2,2,2,48,64]{5,4,0,1,2,3:T(8,128)(2,1)S(1)} %pad_maximum_fusion.9), channel_id=1, source_target_pairs={{0,16},{16,0},{32,48},{48,32},{64,80},{80,64},{96,112},{112,96},{1... | collective-permute-start | bytes 294920 | tf_op jit(solution)/shard_map/ppermute | solution.py:42
  319.1 14.6 %collective-permute-start.36 = (f32[2,2,48,64]{3,2,0,1:T(8,128)}, f32[2,2,48,64]{3,2,0,1:T(8,128)}, u32[]{:S(2)}, u32[]{:S(2)}) collective-permute-start(f32[2,2,48,64]{3,2,0,1:T(8,128)} %select_bitcast_fusion.22), channel_id=1, source_target_pairs={{0,2},{1,3},{2,0},{3,1},{4,6},{5,7},{6,4},{7,5},{8,10},{9,11},{10,... | collective-permute-start | bytes 147464 | tf_op jit(solution)/shard_map/ppermute | solution.py:64
  336.1 8.0 %collective-permute-start.37 = (f32[2,48,64]{2,1,0:T(8,128)}, f32[2,48,64]{2,1,0:T(8,128)}, u32[]{:S(2)}, u32[]{:S(2)}) collective-permute-start(f32[2,48,64]{2,1,0:T(8,128)} %select_bitcast_fusion.37), channel_id=1, source_target_pairs={{0,4},{1,5},{2,6},{3,7},{4,0},{5,1},{6,2},{7,3},{8,12},{9,13},{10,... | collective-permute-start | bytes 73736 | tf_op jit(solution)/shard_map/ppermute | solution.py:64
  345.0 14.5 %collective-permute-start.38 = (f32[48,64]{1,0:T(8,128)S(1)}, f32[48,64]{1,0:T(8,128)S(1)}, u32[]{:S(2)}, u32[]{:S(2)}) collective-permute-start(f32[48,64]{1,0:T(8,128)S(1)} %select_bitcast_fusion.52), channel_id=1, source_target_pairs={{0,8},{1,9},{2,10},{3,11},{4,12},{5,13},{6,14},{7,15},{8,0},{9,1},... | collective-permute-start | bytes 36872 | tf_op jit(solution)/shard_map/ppermute | solution.py:64
  349.8 15.1 %collective-permute-start.48 = (f32[2,2,2,48,64]{4,3,0,1,2:T(8,128)S(1)}, f32[2,2,2,48,64]{4,3,0,1,2:T(8,128)S(1)}, u32[]{:S(2)}, u32[]{:S(2)}) collective-permute-start(f32[2,2,2,48,64]{4,3,0,1,2:T(8,128)S(1)} %select_bitcast_fusion.3), channel_id=1, source_target_pairs={{0,1},{1,0},{2,3},{3,2},{4,5},{5,4},{6,7},{7,6},{8,9},{9,8},{10,11... | collective-permute-start | bytes 294920 | tf_op jit(solution)/shard_map/ppermute | solution.py:64
  361.2 7.4 %collective-permute-start.39 = (bf16[64,384]{1,0:T(8,128)(2,1)S(1)}, bf16[64,384]{1,0:T(8,128)(2,1)S(1)}, u32[]{:S(2)}, u32[]{:S(2)}) collective-permute-start(bf16[64,384]{1,0:T(8,128)(2,1)S(1)} %get-tuple-element.46), channel_id=1, source_target_pairs={{0,16},{16,32},{32,48},{48,64},{64,80},{80,96},{96,112},{112,128},... | collective-permute-start | bytes 147464 | tf_op jit(solution)/shard_map/ppermute | solution.py:15
  363.6 6.0 %collective-permute-start.40 = (bf16[64,384]{1,0:T(8,128)(2,1)S(1)}, bf16[64,384]{1,0:T(8,128)(2,1)S(1)}, u32[]{:S(2)}, u32[]{:S(2)}) collective-permute-start(bf16[64,384]{1,0:T(8,128)(2,1)S(1)} %get-tuple-element.47), channel_id=1, source_target_pairs={{16,0},{32,16},{48,32},{64,48},{80,64},{96,80},{112,96},{128,112},... | collective-permute-start | bytes 147464 | tf_op jit(solution)/shard_map/ppermute | solution.py:15
  365.0 6.5 %collective-permute-start.49 = (f32[2,2,48,64]{3,2,0,1:T(8,128)S(1)}, f32[2,2,48,64]{3,2,0,1:T(8,128)S(1)}, u32[]{:S(2)}, u32[]{:S(2)}) collective-permute-start(f32[2,2,48,64]{3,2,0,1:T(8,128)S(1)} %select_bitcast_fusion.19), channel_id=1, source_target_pairs={{0,2},{1,3},{2,0},{3,1},{4,6},{5,7},{6,4},{7,5},{8,10},{9,11},{10,... | collective-permute-start | bytes 147464 | tf_op jit(solution)/shard_map/ppermute | solution.py:64
  369.6 15.1 %collective-permute-start.42 = (bf16[64,384]{1,0:T(8,128)(2,1)S(1)}, bf16[64,384]{1,0:T(8,128)(2,1)S(1)}, u32[]{:S(2)}, u32[]{:S(2)}) collective-permute-start(bf16[64,384]{1,0:T(8,128)(2,1)S(1)} %pad_maximum_fusion.26), channel_id=1, source_target_pairs={{1,0},{2,1},{3,2},{4,3},{5,4},{6,5},{7,6},{8,7},{9,8},{10,9},{11,1... | collective-permute-start | bytes 147464 | tf_op jit(solution)/shard_map/ppermute | solution.py:15
  371.6 7.8 %collective-permute-start.50 = (f32[2,48,64]{2,1,0:T(8,128)S(1)}, f32[2,48,64]{2,1,0:T(8,128)S(1)}, u32[]{:S(2)}, u32[]{:S(2)}) collective-permute-start(f32[2,48,64]{2,1,0:T(8,128)S(1)} %select_bitcast_fusion.34), channel_id=1, source_target_pairs={{0,4},{1,5},{2,6},{3,7},{4,0},{5,1},{6,2},{7,3},{8,12},{9,13},{10,... | collective-permute-start | bytes 73736 | tf_op jit(solution)/shard_map/ppermute | solution.py:64
  377.0 7.7 %collective-permute-start.41 = (bf16[64,384]{1,0:T(8,128)(2,1)S(1)}, bf16[64,384]{1,0:T(8,128)(2,1)S(1)}, u32[]{:S(2)}, u32[]{:S(2)}) collective-permute-start(bf16[64,384]{1,0:T(8,128)(2,1)S(1)} %pad_maximum_fusion.25), channel_id=1, source_target_pairs={{0,1},{1,2},{2,3},{3,4},{4,5},{5,6},{6,7},{7,8},{8,9},{9,10},{10,1... | collective-permute-start | bytes 147464 | tf_op jit(solution)/shard_map/ppermute | solution.py:15
  379.4 17.2 %collective-permute-start.51 = (f32[48,64]{1,0:T(8,128)S(1)}, f32[48,64]{1,0:T(8,128)S(1)}, u32[]{:S(2)}, u32[]{:S(2)}) collective-permute-start(f32[48,64]{1,0:T(8,128)S(1)} %select_bitcast_fusion.49), channel_id=1, source_target_pairs={{0,8},{1,9},{2,10},{3,11},{4,12},{5,13},{6,14},{7,15},{8,0},{9,1},... | collective-permute-start | bytes 36872 | tf_op jit(solution)/shard_map/ppermute | solution.py:64
  386.2 12.0 %collective-permute-start.56 = (bf16[48,64]{1,0:T(8,128)(2,1)S(1)}, bf16[48,64]{1,0:T(8,128)(2,1)S(1)}, u32[]{:S(2)}, u32[]{:S(2)}) collective-permute-start(bf16[48,64]{1,0:T(8,128)(2,1)S(1)} %fusion.77), channel_id=1, source_target_pairs={{0,256},{16,272},{32,288},{48,304},{64,320},{80,336},{96,352},{112... | collective-permute-start | bytes 18440 | tf_op jit(solution)/shard_map/ppermute | solution.py:42
  398.3 6.6 %collective-permute-start.57 = (bf16[2,48,64]{2,1,0:T(8,128)(2,1)S(1)}, bf16[2,48,64]{2,1,0:T(8,128)(2,1)S(1)}, u32[]{:S(2)}, u32[]{:S(2)}) collective-permute-start(bf16[2,48,64]{2,1,0:T(8,128)(2,1)S(1)} %pad_maximum_fusion.35), channel_id=1, source_target_pairs={{0,128},{16,144},{32,160},{48,176},{64,192},{80,208},{96,224},{112... | collective-permute-start | bytes 36872 | tf_op jit(solution)/shard_map/ppermute | solution.py:42
  404.9 7.4 %collective-permute-start.58 = (bf16[2,2,48,64]{3,2,0,1:T(8,128)(2,1)S(1)}, bf16[2,2,48,64]{3,2,0,1:T(8,128)(2,1)S(1)}, u32[]{:S(2)}, u32[]{:S(2)}) collective-permute-start(bf16[2,2,48,64]{3,2,0,1:T(8,128)(2,1)S(1)} %pad_maximum_fusion.30), channel_id=1, source_target_pairs={{0,64},{16,80},{32,96},{48,112},{64,0},{80,16},{96,32},{112,48},{1... | collective-permute-start | bytes 73736 | tf_op jit(solution)/shard_map/ppermute | solution.py:42
  409.6 8.9 %collective-permute-start.52 = (bf16[64,384]{1,0:T(8,128)(2,1)S(1)}, bf16[64,384]{1,0:T(8,128)(2,1)S(1)}, u32[]{:S(2)}, u32[]{:S(2)}) collective-permute-start(bf16[64,384]{1,0:T(8,128)(2,1)S(1)} %get-tuple-element.42), channel_id=1, source_target_pairs={{0,16},{16,32},{32,48},{48,64},{64,80},{80,96},{96,112},{112,128},... | collective-permute-start | bytes 147464 | tf_op jit(solution)/shard_map/ppermute | solution.py:15
  411.0 7.4 %collective-permute-start.53 = (bf16[64,384]{1,0:T(8,128)(2,1)S(1)}, bf16[64,384]{1,0:T(8,128)(2,1)S(1)}, u32[]{:S(2)}, u32[]{:S(2)}) collective-permute-start(bf16[64,384]{1,0:T(8,128)(2,1)S(1)} %get-tuple-element.43), channel_id=1, source_target_pairs={{16,0},{32,16},{48,32},{64,48},{80,64},{96,80},{112,96},{128,112},... | collective-permute-start | bytes 147464 | tf_op jit(solution)/shard_map/ppermute | solution.py:15
  412.4 11.1 %collective-permute-start.59 = (bf16[2,2,2,48,64]{4,3,0,1,2:T(8,128)(2,1)S(1)}, bf16[2,2,2,48,64]{4,3,0,1,2:T(8,128)(2,1)S(1)}, u32[]{:S(2)}, u32[]{:S(2)}) collective-permute-start(bf16[2,2,2,48,64]{4,3,0,1,2:T(8,128)(2,1)S(1)} %pad_maximum_fusion.15), channel_id=1, source_target_pairs={{0,32},{16,48},{32,0},{48,16},{64,96},{80,112},{96,64},{112,80},{1... | collective-permute-start | bytes 147464 | tf_op jit(solution)/shard_map/ppermute | solution.py:42
  419.1 43.3 %collective-permute-start.55 = (bf16[64,384]{1,0:T(8,128)(2,1)}, bf16[64,384]{1,0:T(8,128)(2,1)}, u32[]{:S(2)}, u32[]{:S(2)}) collective-permute-start(bf16[64,384]{1,0:T(8,128)(2,1)} %pad_maximum_fusion.29), channel_id=1, source_target_pairs={{1,0},{2,1},{3,2},{4,3},{5,4},{6,5},{7,6},{8,7},{9,8},{10,9},{11,1... | collective-permute-start | bytes 147464 | tf_op jit(solution)/shard_map/ppermute | solution.py:15
  421.1 6.7 %collective-permute-start.54 = (bf16[64,384]{1,0:T(8,128)(2,1)S(1)}, bf16[64,384]{1,0:T(8,128)(2,1)S(1)}, u32[]{:S(2)}, u32[]{:S(2)}) collective-permute-start(bf16[64,384]{1,0:T(8,128)(2,1)S(1)} %pad_maximum_fusion.28), channel_id=1, source_target_pairs={{0,1},{1,2},{2,3},{3,4},{4,5},{5,6},{6,7},{7,8},{8,9},{9,10},{10,1... | collective-permute-start | bytes 147464 | tf_op jit(solution)/shard_map/ppermute | solution.py:15
  423.6 7.6 %collective-permute-start.60 = (bf16[2,2,2,2,48,64]{5,4,0,1,2,3:T(8,128)(2,1)S(1)}, bf16[2,2,2,2,48,64]{5,4,0,1,2,3:T(8,128)(2,1)S(1)}, u32[]{:S(2)}, u32[]{:S(2)}) collective-permute-start(bf16[2,2,2,2,48,64]{5,4,0,1,2,3:T(8,128)(2,1)S(1)} %pad_maximum_fusion.10), channel_id=1, source_target_pairs={{0,16},{16,0},{32,48},{48,32},{64,80},{80,64},{96,112},{112,96},{1... | collective-permute-start | bytes 294920 | tf_op jit(solution)/shard_map/ppermute | solution.py:42
  448.4 15.5 %collective-permute-start.61 = (f32[2,2,2,48,64]{4,3,0,1,2:T(8,128)S(1)}, f32[2,2,2,48,64]{4,3,0,1,2:T(8,128)S(1)}, u32[]{:S(2)}, u32[]{:S(2)}) collective-permute-start(f32[2,2,2,48,64]{4,3,0,1,2:T(8,128)S(1)} %select_bitcast_fusion), channel_id=1, source_target_pairs={{0,1},{1,0},{2,3},{3,2},{4,5},{5,4},{6,7},{7,6},{8,9},{9,8},{10,11... | collective-permute-start | bytes 294920 | tf_op jit(solution)/shard_map/ppermute | solution.py:64
  464.9 6.6 %collective-permute-start.62 = (f32[2,2,48,64]{3,2,0,1:T(8,128)S(1)}, f32[2,2,48,64]{3,2,0,1:T(8,128)S(1)}, u32[]{:S(2)}, u32[]{:S(2)}) collective-permute-start(f32[2,2,48,64]{3,2,0,1:T(8,128)S(1)} %select_bitcast_fusion.16), channel_id=1, source_target_pairs={{0,2},{1,3},{2,0},{3,1},{4,6},{5,7},{6,4},{7,5},{8,10},{9,11},{10,... | collective-permute-start | bytes 147464 | tf_op jit(solution)/shard_map/ppermute | solution.py:64
  471.5 7.5 %collective-permute-start.63 = (f32[2,48,64]{2,1,0:T(8,128)S(1)}, f32[2,48,64]{2,1,0:T(8,128)S(1)}, u32[]{:S(2)}, u32[]{:S(2)}) collective-permute-start(f32[2,48,64]{2,1,0:T(8,128)S(1)} %select_bitcast_fusion.31), channel_id=1, source_target_pairs={{0,4},{1,5},{2,6},{3,7},{4,0},{5,1},{6,2},{7,3},{8,12},{9,13},{10,... | collective-permute-start | bytes 73736 | tf_op jit(solution)/shard_map/ppermute | solution.py:64
  480.2 14.7 %collective-permute-start.64 = (f32[48,64]{1,0:T(8,128)}, f32[48,64]{1,0:T(8,128)}, u32[]{:S(2)}, u32[]{:S(2)}) collective-permute-start(f32[48,64]{1,0:T(8,128)} %select_bitcast_fusion.46), channel_id=1, source_target_pairs={{0,8},{1,9},{2,10},{3,11},{4,12},{5,13},{6,14},{7,15},{8,0},{9,1},... | collective-permute-start | bytes 36872 | tf_op jit(solution)/shard_map/ppermute | solution.py:64
  (40 other events, 564.8 us)

commit v4 on v3

--- a/solution.py
+++ b/solution.py
@@ -32,37 +32,35 @@
     )
 
 
-def gather_rows(piece, bits):
+def bit_reversed(bits):
+    return [int(format(i, f"0{bits}b")[::-1], 2) if bits else 0 for i in range(1 << bits)]
+
+
+def gather_rows(piece):
     index = lax.axis_index("row")
     size = lax.axis_size("row")
     current = piece
-    for step, bit in enumerate(bits):
-        distance = 1 << bit
-        route = [(i, i ^ distance) for i in range(size)]
+    for bit in range(size.bit_length() - 2, -1, -1):
+        route = [(i, i ^ (1 << bit)) for i in range(size)]
         other = lax.ppermute(current, "row", route)
         high = ((index >> bit) & 1) == 1
-        low_part = jnp.where(high, other, current)
-        high_part = jnp.where(high, current, other)
-        current = jnp.stack([low_part, high_part], axis=step)
+        current = jnp.where(
+            high, jnp.concatenate([other, current], 0), jnp.concatenate([current, other], 0)
+        )
     return current
 
 
-def scatter_cols(partial, bits):
+def scatter_cols(partial):
     index = lax.axis_index("col")
     size = lax.axis_size("col")
     current = partial
-    remaining = list(range(len(bits) - 1, -1, -1))
-    for bit in bits:
-        axis = remaining.index(bit)
-        distance = 1 << bit
-        route = [(i, i ^ distance) for i in range(size)]
+    for bit in range(size.bit_length() - 1):
+        route = [(i, i ^ (1 << bit)) for i in range(size)]
+        half = current.shape[0] // 2
         high = ((index >> bit) & 1) == 1
-        low_part = lax.index_in_dim(current, 0, axis, keepdims=False)
-        high_part = lax.index_in_dim(current, 1, axis, keepdims=False)
-        keep = jnp.where(high, high_part, low_part)
-        send = jnp.where(high, low_part, high_part)
+        keep = jnp.where(high, current[half:], current[:half])
+        send = jnp.where(high, current[:half], current[half:])
         current = keep + lax.ppermute(send, "col", route)
-        remaining.pop(axis)
     return current
 
 
@@ -87,7 +85,6 @@
     rhs_full = rhs[0, 0].astype(jnp.float32)
     solver_matrix = local_solver[0, 0]
     mode_basis = modes[0, 0]
-    coarse_tile = coarse_inverse[0, :, 0, :]
     eye = jnp.eye(block_size, dtype=jnp.float32)
 
     send_onehot = (
@@ -95,27 +92,31 @@
     ).astype(jnp.float32)
     select = jnp.einsum("jk,nm->knjm", send_onehot, eye).reshape(unknowns, -1).astype(jnp.bfloat16)
 
-    slot_of = (slot_dir[0, 0][:, None] == jnp.array(RECV_DIRS)[None, :]).astype(jnp.float32)
-    block_of = (slot_block[0, 0][:, None] == jnp.arange(block_count)[None, :]).astype(jnp.float32)
-    placed_matrix = jnp.einsum(
-        "sj,sk,snm->jnkm", slot_of, block_of, coupling[0, 0].astype(jnp.float32)
-    ).reshape(-1, unknowns)
+    slot_of = (slot_dir[0, 0][:, None] == jnp.array(RECV_DIRS)[None, :]).astype(jnp.bfloat16)
+    block_of = (slot_block[0, 0][:, None] == jnp.arange(block_count)[None, :]).astype(jnp.bfloat16)
+    placed_matrix = jnp.zeros((len(RECV_DIRS), block_size, unknowns), jnp.bfloat16)
+    for slot in range(coupling.shape[2]):
+        spread = jnp.tile(coupling[0, 0, slot], (1, block_count)) * jnp.repeat(
+            block_of[slot], block_size
+        )[None, :]
+        placed_matrix = placed_matrix + slot_of[slot][:, None, None] * spread[None]
     operator_matrix = jnp.concatenate(
-        [operator_blocks[0, 0], placed_matrix.astype(jnp.bfloat16)], 0
+        [operator_blocks[0, 0], placed_matrix.reshape(-1, unknowns)], 0
     )
+
+    rows = lax.axis_size("row")
+    cols = lax.axis_size("col")
+    tile = coarse_inverse[0, :, 0, :].reshape(rows, mode_count, cols, mode_count)
+    tile = tile[jnp.array(bit_reversed(row_bits))][:, :, jnp.array(bit_reversed(col_bits))]
+    coarse_matrix = tile.reshape(rows * mode_count, cols * mode_count).T
 
     def coarse_solve(rounded):
         restricted = lax.dot_general(
             mode_basis, rounded, (((1,), (1,)), ((), ())), preferred_element_type=jnp.float32
         ).astype(jnp.bfloat16)
-        gathered = gather_rows(restricted, list(range(row_bits - 1, -1, -1)))
-        gathered = gathered.reshape(-1, columns)
-        partial_sums = lax.dot_general(
-            coarse_tile, gathered, (((0,), (0,)), ((), ())), preferred_element_type=jnp.float32
-        )
-        partial_sums = partial_sums.reshape((2,) * col_bits + (mode_count, columns))
-        own_rows = scatter_cols(partial_sums, list(range(col_bits)))
-        return own_rows.astype(jnp.bfloat16)
+        gathered = gather_rows(restricted)
+        partial_sums = jnp.dot(coarse_matrix, gathered, preferred_element_type=jnp.float32)
+        return scatter_cols(partial_sums).astype(jnp.bfloat16)
 
     solution = jnp.zeros((columns, unknowns), jnp.float32)
     pending = None

time: 502 us -> 452 us (0.900)
  local copies, waits for them, and re-layouts: 90.2 us -> 65.8 us
  waiting for transfers between devices: 79.9 us -> 101 us
  matrix products: 36.2 us -> 16.5 us
  other arithmetic: 26.8 us -> 9.92 us
  starting transfers between devices: 262 us -> 254 us
    gather x0 -> x4, local copies, waits for them, and re-layouts: none -> 33.3 us  [on_device(): tile[jnp.array(bit_reversed(row_bits))]]
    unnamed x105 -> x55, local copies, waits for them, and re-layouts: 31.4 us -> 1.24 us
    ppermute x20, waiting for transfers between devices: 25.6 us -> 50.2 us  [scatter_cols(): current = keep + lax.ppermute(send, 'col', route)]
    reshape x10 -> x1, local copies, waits for them, and re-layouts: 25.4 us -> 9.72 us  [on_device(): coarse_matrix = tile.reshape(rows * mode_count, cols * mode_count).T]
    ppermute x20, starting transfers between devices: 96.3 us -> 81.9 us  [scatter_cols(): current = keep + lax.ppermute(send, 'col', route)]
    slice x5 -> x0, local copies, waits for them, and re-layouts: 12.7 us -> none  [scatter_cols(): high_part = lax.index_in_dim(current, 1, axis, keepdims=False)]
    another operation x54 -> x2, other arithmetic: 10 us -> 0.02 us  [the longest x50 9.9 us: gather_rows(): current = jnp.stack([low_part, high_part], axis=step)]
    dot_general x6 -> x5, matrix products: 12.7 us -> 2.94 us  [coarse_solve(): jnp.dot(coarse_matrix, gathered, preferred_element_type=jnp.float32)]
  transfers between devices with their start and end apart: 65 -> 65, of which waited for: 27 -> 31; matrix products, arithmetic and copies ran while one was open for 23% -> 20% of each run, Pallas kernels for 0% -> 0%
where the time goes in v4:
time: 452 us; the launch traced here: 449 us
  starting transfers between devices  254 us (56%)
  waiting for transfers between devices  101 us (22%)
  local copies, waits for them, and re-layouts  65.8 us (15%)
  matrix products  16.5 us (4%)
  other arithmetic  9.92 us (2%)
    ppermute x25, starting transfers between devices, gather_rows(): other = lax.ppermute(current, 'row', route)  127 us
    ppermute x20, starting transfers between devices, scatter_cols(): current = keep + lax.ppermute(send, 'col', route)  81.9 us
    ppermute x20, waiting for transfers between devices, scatter_cols(): current = keep + lax.ppermute(send, 'col', route)  50.2 us
    ppermute x20, starting transfers between devices, shifted(): return lax.ppermute(block, axis, route)  45 us
    gather x4, local copies, waits for them, and re-layouts, on_device(): tile[jnp.array(bit_reversed(row_bits))]  33.3 us
    ppermute x25, waiting for transfers between devices, gather_rows(): other = lax.ppermute(current, 'row', route)  26.1 us
    ppermute x20, waiting for transfers between devices, shifted(): return lax.ppermute(block, axis, route)  25.2 us
    another operation x1, local copies, waits for them, and re-layouts, on_device(): coarse_inverse[0, :, 0, :].reshape(rows, mode_count, cols, mode_count)  10 us
  transfers between devices with their start and end apart: 65, of which 31 were waited for; matrix products, arithmetic and copies ran while one was open for 20% of the time, Pallas kernels for 0%

profile of v4, /device:TPU:6, one launch (start us, length us, event | category | flops | bytes accessed | tf_op | source)
XLA Modules:
  0.0 449.0 jit_solution(18411614617009512773)
XLA Ops:
  1.2 9.1 %collective-permute-start.4 = (bf16[48,64]{1,0:T(8,128)(2,1)S(1)}, bf16[48,64]{1,0:T(8,128)(2,1)S(1)}, u32[]{:S(2)}, u32[]{:S(2)}) collective-permute-start(bf16[48,64]{1,0:T(8,128)(2,1)S(1)} %convolution_convert_fusion.4), channel_id=1, source_target_pairs={{0,256},{16,272},{32,288},{48,304},{64,320},{80,336},{96,352},{112... | collective-permute-start | bytes 18440 | tf_op jit(solution)/shard_map/ppermute | solution.py:45
  15.6 4.1 collective-permute-start
  22.6 7.8 %collective-permute-start.5 = (bf16[96,64]{1,0:T(8,128)(2,1)S(1)}, bf16[96,64]{1,0:T(8,128)(2,1)S(1)}, u32[]{:S(2)}, u32[]{:S(2)}) collective-permute-start(bf16[96,64]{1,0:T(8,128)(2,1)S(1)} %maximum_select_fusion.25), channel_id=1, source_target_pairs={{0,128},{16,144},{32,160},{48,176},{64,192},{80,208},{96,224},{112... | collective-permute-start | bytes 36872 | tf_op jit(solution)/shard_map/ppermute | solution.py:45
  32.2 3.8 collective-permute-start.6
  36.0 10.0 %reshape_squeeze.3 = bf16[32,48,16,48]{3,2,1,0:T(8,128)(2,1)} reshape(bf16[1,1536,1,768]{3,1,2,0:T(8,128)(2,1)} %param.18) | data formatting | bytes 4718592 | tf_op jit(solution)/shard_map/reshape;squeeze | solution.py:109
  46.0 6.7 %gather_fusion.1 = bf16[32,48,16,48]{3,2,1,0:T(8,128)(2,1)} fusion(bf16[32,48,16,48]{3,2,1,0:T(8,128)(2,1)} %reshape_squeeze.3, s32[1024]{0:T(1024)S(1)} %get-tuple-element.68), kind=kCustom, calls=%fused_computation.1 | custom fusion | bytes 4718720 | tf_op jit(solution)/shard_map/gather | solution.py:110
  52.8 7.1 %copy.30 = bf16[32,48,16,48]{3,1,2,0:T(8,128)(2,1)} copy(bf16[32,48,16,48]{3,2,1,0:T(8,128)(2,1)} %gather_fusion.1) | data formatting | bytes 4718592 | tf_op jit(solution)/shard_map/gather | solution.py:110
  59.9 6.7 %gather_fusion.2 = bf16[16,32,48,48]{3,2,1,0:T(8,128)(2,1)} fusion(bf16[32,48,16,48]{3,1,2,0:T(8,128)(2,1)} %copy.30, s32[1024]{0:T(1024)S(1)} %get-tuple-element.67), kind=kCustom, calls=%fused_computation.2 | custom fusion | bytes 4718656 | tf_op jit(solution)/shard_map/gather | solution.py:110
  66.6 12.8 %copy.31 = bf16[32,48,16,48]{3,2,1,0:T(8,128)(2,1)} copy(bf16[32,48,16,48]{3,1,0,2:T(8,128)(2,1)} %bitcast.196) | data formatting | bytes 4718592 | tf_op jit(solution)/shard_map/gather | solution.py:110
  79.4 9.7 %reshape.138 = bf16[1536,768]{1,0:T(8,128)(2,1)} reshape(bf16[32,48,16,48]{3,2,1,0:T(8,128)(2,1)} %copy.31) | data formatting | bytes 4718592 | tf_op jit(solution)/shard_map/reshape | solution.py:111
  97.0 2.3 fusion.10
  100.3 3.0 collective-permute-start.7
  106.8 3.6 collective-permute-start.3
  110.5 6.7 %collective-permute-done.3 = bf16[64,384]{1,0:T(8,128)(2,1)S(1)} collective-permute-done((bf16[64,384]{1,0:T(8,128)(2,1)S(1)}, bf16[64,384]{1,0:T(8,128)(2,1)S(1)}, u32[]{:S(2)}, u32[]{:S(2)}) %collective-permute-start.3) | collective-permute-done | bytes 49184 | tf_op jit(solution)/shard_map/ppermute | solution.py:15
  119.7 5.5 %collective-permute-start.17 = (bf16[48,64]{1,0:T(8,128)(2,1)S(1)}, bf16[48,64]{1,0:T(8,128)(2,1)S(1)}, u32[]{:S(2)}, u32[]{:S(2)}) collective-permute-start(bf16[48,64]{1,0:T(8,128)(2,1)S(1)} %fusion.51), channel_id=1, source_target_pairs={{0,256},{16,272},{32,288},{48,304},{64,320},{80,336},{96,352},{112... | collective-permute-start | bytes 18440 | tf_op jit(solution)/shard_map/ppermute | solution.py:45
  125.2 2.6 collective-permute-start.8
  129.2 3.4 collective-permute-start.18
  132.9 2.9 collective-permute-done.18
  135.8 2.9 collective-permute-start.19
  139.4 13.0 %collective-permute-start.9 = (f32[384,64]{0,1:T(8,128)S(1)}, f32[384,64]{0,1:T(8,128)S(1)}, u32[]{:S(2)}, u32[]{:S(2)}) collective-permute-start(f32[384,64]{0,1:T(8,128)S(1)} %slice_select_fusion.4), channel_id=1, source_target_pairs={{0,1},{1,0},{2,3},{3,2},{4,5},{5,4},{6,7},{7,6},{8,9},{9,8},{10,11... | collective-permute-start | bytes 294920 | tf_op jit(solution)/shard_map/ppermute | solution.py:63
  152.4 4.6 %collective-permute-start.20 = (bf16[384,64]{1,0:T(8,128)(2,1)S(1)}, bf16[384,64]{1,0:T(8,128)(2,1)S(1)}, u32[]{:S(2)}, u32[]{:S(2)}) collective-permute-start(bf16[384,64]{1,0:T(8,128)(2,1)S(1)} %maximum_select_fusion.16), channel_id=1, source_target_pairs={{0,32},{16,48},{32,0},{48,16},{64,96},{80,112},{96,64},{112,80},{1... | collective-permute-start | bytes 147464 | tf_op jit(solution)/shard_map/ppermute | solution.py:45
  160.6 2.6 collective-permute-start.21
  165.4 3.0 collective-permute-done.21
  174.8 10.6 %collective-permute-done.12 = f32[48,64]{0,1:T(8,128)S(1)} collective-permute-done((f32[48,64]{0,1:T(8,128)S(1)}, f32[48,64]{0,1:T(8,128)S(1)}, u32[]{:S(2)}, u32[]{:S(2)}) %collective-permute-start.12) | collective-permute-done | bytes 12320 | tf_op jit(solution)/shard_map/ppermute | solution.py:63
  186.2 3.1 collective-permute-start.13
  190.7 2.5 collective-permute-start.23
  193.2 2.4 collective-permute-done.14
  197.8 2.3 collective-permute-start.24
  200.0 2.1 collective-permute-start.15
  202.2 2.9 collective-permute-done.24
  208.5 11.5 %collective-permute-start.30 = (bf16[48,64]{1,0:T(8,128)(2,1)S(1)}, bf16[48,64]{1,0:T(8,128)(2,1)S(1)}, u32[]{:S(2)}, u32[]{:S(2)}) collective-permute-start(bf16[48,64]{1,0:T(8,128)(2,1)S(1)} %fusion.52), channel_id=1, source_target_pairs={{0,256},{16,272},{32,288},{48,304},{64,320},{80,336},{96,352},{112... | collective-permute-start | bytes 18440 | tf_op jit(solution)/shard_map/ppermute | solution.py:45
  221.7 5.5 %collective-permute-start.31 = (bf16[96,64]{1,0:T(8,128)(2,1)S(1)}, bf16[96,64]{1,0:T(8,128)(2,1)S(1)}, u32[]{:S(2)}, u32[]{:S(2)}) collective-permute-start(bf16[96,64]{1,0:T(8,128)(2,1)S(1)} %maximum_select_fusion.27), channel_id=1, source_target_pairs={{0,128},{16,144},{32,160},{48,176},{64,192},{80,208},{96,224},{112... | collective-permute-start | bytes 36872 | tf_op jit(solution)/shard_map/ppermute | solution.py:45
  228.9 4.2 collective-permute-start.32
  236.1 8.4 %collective-permute-start.33 = (bf16[384,64]{1,0:T(8,128)(2,1)S(1)}, bf16[384,64]{1,0:T(8,128)(2,1)S(1)}, u32[]{:S(2)}, u32[]{:S(2)}) collective-permute-start(bf16[384,64]{1,0:T(8,128)(2,1)S(1)} %maximum_select_fusion.17), channel_id=1, source_target_pairs={{0,32},{16,48},{32,0},{48,16},{64,96},{80,112},{96,64},{112,80},{1... | collective-permute-start | bytes 147464 | tf_op jit(solution)/shard_map/ppermute | solution.py:45
  244.5 2.5 collective-permute-start.28
  247.0 3.1 collective-permute-start.29
  250.2 12.6 %collective-permute-done.29 = bf16[64,384]{1,0:T(8,128)(2,1)S(1)} collective-permute-done((bf16[64,384]{1,0:T(8,128)(2,1)S(1)}, bf16[64,384]{1,0:T(8,128)(2,1)S(1)}, u32[]{:S(2)}, u32[]{:S(2)}) %collective-permute-start.29) | collective-permute-done | bytes 49184 | tf_op jit(solution)/shard_map/ppermute | solution.py:15
  263.6 5.8 %collective-permute-start.43 = (bf16[48,64]{1,0:T(8,128)(2,1)S(1)}, bf16[48,64]{1,0:T(8,128)(2,1)S(1)}, u32[]{:S(2)}, u32[]{:S(2)}) collective-permute-start(bf16[48,64]{1,0:T(8,128)(2,1)S(1)} %fusion.53), channel_id=1, source_target_pairs={{0,256},{16,272},{32,288},{48,304},{64,320},{80,336},{96,352},{112... | collective-permute-start | bytes 18440 | tf_op jit(solution)/shard_map/ppermute | solution.py:45
  269.5 2.1 collective-permute-start.34
  273.1 4.8 %collective-permute-start.44 = (bf16[96,64]{1,0:T(8,128)(2,1)S(1)}, bf16[96,64]{1,0:T(8,128)(2,1)S(1)}, u32[]{:S(2)}, u32[]{:S(2)}) collective-permute-start(bf16[96,64]{1,0:T(8,128)(2,1)S(1)} %maximum_select_fusion.28), channel_id=1, source_target_pairs={{0,128},{16,144},{32,160},{48,176},{64,192},{80,208},{96,224},{112... | collective-permute-start | bytes 36872 | tf_op jit(solution)/shard_map/ppermute | solution.py:45
  282.4 13.8 %collective-permute-start.35 = (f32[384,64]{0,1:T(8,128)S(1)}, f32[384,64]{0,1:T(8,128)S(1)}, u32[]{:S(2)}, u32[]{:S(2)}) collective-permute-start(f32[384,64]{0,1:T(8,128)S(1)} %slice_select_fusion.2), channel_id=1, source_target_pairs={{0,1},{1,0},{2,3},{3,2},{4,5},{5,4},{6,7},{7,6},{8,9},{9,8},{10,11... | collective-permute-start | bytes 294920 | tf_op jit(solution)/shard_map/ppermute | solution.py:63
  296.2 5.4 %collective-permute-start.46 = (bf16[384,64]{1,0:T(8,128)(2,1)S(1)}, bf16[384,64]{1,0:T(8,128)(2,1)S(1)}, u32[]{:S(2)}, u32[]{:S(2)}) collective-permute-start(bf16[384,64]{1,0:T(8,128)(2,1)S(1)} %maximum_select_fusion.18), channel_id=1, source_target_pairs={{0,32},{16,48},{32,0},{48,16},{64,96},{80,112},{96,64},{112,80},{1... | collective-permute-start | bytes 147464 | tf_op jit(solution)/shard_map/ppermute | solution.py:45
  305.0 3.8 collective-permute-start.47
  310.9 2.5 collective-permute-done.47
  314.0 2.3 collective-permute-done.37
  320.3 10.8 %collective-permute-done.38 = f32[48,64]{0,1:T(8,128)S(1)} collective-permute-done((f32[48,64]{0,1:T(8,128)S(1)}, f32[48,64]{0,1:T(8,128)S(1)}, u32[]{:S(2)}, u32[]{:S(2)}) %collective-permute-start.38) | collective-permute-done | bytes 12320 | tf_op jit(solution)/shard_map/ppermute | solution.py:63
  331.8 3.2 collective-permute-start.39
  336.5 2.1 collective-permute-start.49
  338.6 2.9 collective-permute-done.40
  345.7 2.2 collective-permute-start.41
  348.0 3.0 collective-permute-done.50
  354.2 9.5 %collective-permute-start.56 = (bf16[48,64]{1,0:T(8,128)(2,1)S(1)}, bf16[48,64]{1,0:T(8,128)(2,1)S(1)}, u32[]{:S(2)}, u32[]{:S(2)}) collective-permute-start(bf16[48,64]{1,0:T(8,128)(2,1)S(1)} %fusion.54), channel_id=1, source_target_pairs={{0,256},{16,272},{32,288},{48,304},{64,320},{80,336},{96,352},{112... | collective-permute-start | bytes 18440 | tf_op jit(solution)/shard_map/ppermute | solution.py:45
  363.7 2.7 collective-permute-done.51
  367.0 7.3 %collective-permute-start.57 = (bf16[96,64]{1,0:T(8,128)(2,1)S(1)}, bf16[96,64]{1,0:T(8,128)(2,1)S(1)}, u32[]{:S(2)}, u32[]{:S(2)}) collective-permute-start(bf16[96,64]{1,0:T(8,128)(2,1)S(1)} %maximum_select_fusion.29), channel_id=1, source_target_pairs={{0,128},{16,144},{32,160},{48,176},{64,192},{80,208},{96,224},{112... | collective-permute-start | bytes 36872 | tf_op jit(solution)/shard_map/ppermute | solution.py:45
  382.1 6.2 %collective-permute-start.59 = (bf16[384,64]{1,0:T(8,128)(2,1)S(1)}, bf16[384,64]{1,0:T(8,128)(2,1)S(1)}, u32[]{:S(2)}, u32[]{:S(2)}) collective-permute-start(bf16[384,64]{1,0:T(8,128)(2,1)S(1)} %maximum_select_fusion.19), channel_id=1, source_target_pairs={{0,32},{16,48},{32,0},{48,16},{64,96},{80,112},{96,64},{112,80},{1... | collective-permute-start | bytes 147464 | tf_op jit(solution)/shard_map/ppermute | solution.py:45
  390.4 3.5 collective-permute-start.54
  394.0 3.0 collective-permute-start.60
  397.6 4.0 collective-permute-done.60
  402.2 16.4 %collective-permute-start.61 = (f32[384,64]{0,1:T(8,128)S(1)}, f32[384,64]{0,1:T(8,128)S(1)}, u32[]{:S(2)}, u32[]{:S(2)}) collective-permute-start(f32[384,64]{0,1:T(8,128)S(1)} %slice_select_fusion), channel_id=1, source_target_pairs={{0,1},{1,0},{2,3},{3,2},{4,5},{5,4},{6,7},{7,6},{8,9},{9,8},{10,11... | collective-permute-start | bytes 294920 | tf_op jit(solution)/shard_map/ppermute | solution.py:63
  421.6 4.3 collective-permute-done.62
  428.0 5.4 %collective-permute-done.63 = f32[96,64]{0,1:T(8,128)S(1)} collective-permute-done((f32[96,64]{0,1:T(8,128)S(1)}, f32[96,64]{0,1:T(8,128)S(1)}, u32[]{:S(2)}, u32[]{:S(2)}) %collective-permute-start.63) | collective-permute-done | bytes 24608 | tf_op jit(solution)/shard_map/ppermute | solution.py:63
  433.6 6.6 %collective-permute-start.64 = (f32[48,64]{0,1:T(8,128)S(1)}, f32[48,64]{0,1:T(8,128)S(1)}, u32[]{:S(2)}, u32[]{:S(2)}) collective-permute-start(f32[48,64]{0,1:T(8,128)S(1)} %slice_select_fusion.10), channel_id=1, source_target_pairs={{0,8},{1,9},{2,10},{3,11},{4,12},{5,13},{6,14},{7,15},{8,0},{9,1},... | collective-permute-start | bytes 36872 | tf_op jit(solution)/shard_map/ppermute | solution.py:63
  440.1 2.4 fusion.13
  442.6 5.5 %collective-permute-done.64 = f32[48,64]{0,1:T(8,128)S(1)} collective-permute-done((f32[48,64]{0,1:T(8,128)S(1)}, f32[48,64]{0,1:T(8,128)S(1)}, u32[]{:S(2)}, u32[]{:S(2)}) %collective-permute-start.64) | collective-permute-done | bytes 12320 | tf_op jit(solution)/shard_map/ppermute | solution.py:63
  (275 shorter events, 98.1 us)
Async XLA Ops:
  1.2 21.4 %collective-permute-start.4 = (bf16[48,64]{1,0:T(8,128)(2,1)S(1)}, bf16[48,64]{1,0:T(8,128)(2,1)S(1)}, u32[]{:S(2)}, u32[]{:S(2)}) collective-permute-start(bf16[48,64]{1,0:T(8,128)(2,1)S(1)} %convolution_convert_fusion.4), channel_id=1, source_target_pairs={{0,256},{16,272},{32,288},{48,304},{64,320},{80,336},{96,352},{112... | collective-permute-start | bytes 18440 | tf_op jit(solution)/shard_map/ppermute | solution.py:45
  15.6 87.8 %collective-permute-start = (bf16[64,384]{1,0:T(8,128)(2,1)}, bf16[64,384]{1,0:T(8,128)(2,1)}, u32[]{:S(2)}, u32[]{:S(2)}) collective-permute-start(bf16[64,384]{1,0:T(8,128)(2,1)} %get-tuple-element.27), channel_id=1, source_target_pairs={{0,16},{16,32},{32,48},{48,64},{64,80},{80,96},{96,112},{112,128},... | collective-permute-start | bytes 147464 | tf_op jit(solution)/shard_map/ppermute | solution.py:15
  19.7 84.4 %collective-permute-start.1 = (bf16[64,384]{1,0:T(8,128)(2,1)}, bf16[64,384]{1,0:T(8,128)(2,1)}, u32[]{:S(2)}, u32[]{:S(2)}) collective-permute-start(bf16[64,384]{1,0:T(8,128)(2,1)} %get-tuple-element.28), channel_id=1, source_target_pairs={{16,0},{32,16},{48,32},{64,48},{80,64},{96,80},{112,96},{128,112},... | collective-permute-start | bytes 147464 | tf_op jit(solution)/shard_map/ppermute | solution.py:15
  22.6 9.6 %collective-permute-start.5 = (bf16[96,64]{1,0:T(8,128)(2,1)S(1)}, bf16[96,64]{1,0:T(8,128)(2,1)S(1)}, u32[]{:S(2)}, u32[]{:S(2)}) collective-permute-start(bf16[96,64]{1,0:T(8,128)(2,1)S(1)} %maximum_select_fusion.25), channel_id=1, source_target_pairs={{0,128},{16,144},{32,160},{48,176},{64,192},{80,208},{96,224},{112... | collective-permute-start | bytes 36872 | tf_op jit(solution)/shard_map/ppermute | solution.py:45
  32.2 67.2 %collective-permute-start.6 = (bf16[192,64]{1,0:T(8,128)(2,1)S(1)}, bf16[192,64]{1,0:T(8,128)(2,1)}, u32[]{:S(2)}, u32[]{:S(2)}) collective-permute-start(bf16[192,64]{1,0:T(8,128)(2,1)S(1)} %maximum_select_fusion.20), channel_id=1, source_target_pairs={{0,64},{16,80},{32,96},{48,112},{64,0},{80,16},{96,32},{112,48},{1... | collective-permute-start | bytes 73736 | tf_op jit(solution)/shard_map/ppermute | solution.py:45
  100.3 24.8 %collective-permute-start.7 = (bf16[384,64]{1,0:T(8,128)(2,1)S(1)}, bf16[384,64]{1,0:T(8,128)(2,1)S(1)}, u32[]{:S(2)}, u32[]{:S(2)}) collective-permute-start(bf16[384,64]{1,0:T(8,128)(2,1)S(1)} %maximum_select_fusion.15), channel_id=1, source_target_pairs={{0,32},{16,48},{32,0},{48,16},{64,96},{80,112},{96,64},{112,80},{1... | collective-permute-start | bytes 147464 | tf_op jit(solution)/shard_map/ppermute | solution.py:45
  104.8 5.6 %collective-permute-start.2 = (bf16[64,384]{1,0:T(8,128)(2,1)S(1)}, bf16[64,384]{1,0:T(8,128)(2,1)S(1)}, u32[]{:S(2)}, u32[]{:S(2)}) collective-permute-start(bf16[64,384]{1,0:T(8,128)(2,1)S(1)} %pad_maximum_fusion.1), channel_id=1, source_target_pairs={{0,1},{1,2},{2,3},{3,4},{4,5},{5,6},{6,7},{7,8},{8,9},{9,10},{10,1... | collective-permute-start | bytes 147464 | tf_op jit(solution)/shard_map/ppermute | solution.py:15
  106.8 10.4 %collective-permute-start.3 = (bf16[64,384]{1,0:T(8,128)(2,1)S(1)}, bf16[64,384]{1,0:T(8,128)(2,1)S(1)}, u32[]{:S(2)}, u32[]{:S(2)}) collective-permute-start(bf16[64,384]{1,0:T(8,128)(2,1)S(1)} %pad_maximum_fusion.2), channel_id=1, source_target_pairs={{1,0},{2,1},{3,2},{4,3},{5,4},{6,5},{7,6},{8,7},{9,8},{10,9},{11,1... | collective-permute-start | bytes 147464 | tf_op jit(solution)/shard_map/ppermute | solution.py:15
  119.7 9.5 %collective-permute-start.17 = (bf16[48,64]{1,0:T(8,128)(2,1)S(1)}, bf16[48,64]{1,0:T(8,128)(2,1)S(1)}, u32[]{:S(2)}, u32[]{:S(2)}) collective-permute-start(bf16[48,64]{1,0:T(8,128)(2,1)S(1)} %fusion.51), channel_id=1, source_target_pairs={{0,256},{16,272},{32,288},{48,304},{64,320},{80,336},{96,352},{112... | collective-permute-start | bytes 18440 | tf_op jit(solution)/shard_map/ppermute | solution.py:45
  125.2 13.5 %collective-permute-start.8 = (bf16[768,64]{1,0:T(8,128)(2,1)S(1)}, bf16[768,64]{1,0:T(8,128)(2,1)S(1)}, u32[]{:S(2)}, u32[]{:S(2)}) collective-permute-start(bf16[768,64]{1,0:T(8,128)(2,1)S(1)} %maximum_select_fusion.10), channel_id=1, source_target_pairs={{0,16},{16,0},{32,48},{48,32},{64,80},{80,64},{96,112},{112,96},{1... | collective-permute-start | bytes 294920 | tf_op jit(solution)/shard_map/ppermute | solution.py:45
  129.2 6.6 %collective-permute-start.18 = (bf16[96,64]{1,0:T(8,128)(2,1)S(1)}, bf16[96,64]{1,0:T(8,128)(2,1)S(1)}, u32[]{:S(2)}, u32[]{:S(2)}) collective-permute-start(bf16[96,64]{1,0:T(8,128)(2,1)S(1)} %maximum_select_fusion.26), channel_id=1, source_target_pairs={{0,128},{16,144},{32,160},{48,176},{64,192},{80,208},{96,224},{112... | collective-permute-start | bytes 36872 | tf_op jit(solution)/shard_map/ppermute | solution.py:45
  135.8 16.6 %collective-permute-start.19 = (bf16[192,64]{1,0:T(8,128)(2,1)S(1)}, bf16[192,64]{1,0:T(8,128)(2,1)S(1)}, u32[]{:S(2)}, u32[]{:S(2)}) collective-permute-start(bf16[192,64]{1,0:T(8,128)(2,1)S(1)} %maximum_select_fusion.21), channel_id=1, source_target_pairs={{0,64},{16,80},{32,96},{48,112},{64,0},{80,16},{96,32},{112,48},{1... | collective-permute-start | bytes 73736 | tf_op jit(solution)/shard_map/ppermute | solution.py:45
  139.4 17.7 %collective-permute-start.9 = (f32[384,64]{0,1:T(8,128)S(1)}, f32[384,64]{0,1:T(8,128)S(1)}, u32[]{:S(2)}, u32[]{:S(2)}) collective-permute-start(f32[384,64]{0,1:T(8,128)S(1)} %slice_select_fusion.4), channel_id=1, source_target_pairs={{0,1},{1,0},{2,3},{3,2},{4,5},{5,4},{6,7},{7,6},{8,9},{9,8},{10,11... | collective-permute-start | bytes 294920 | tf_op jit(solution)/shard_map/ppermute | solution.py:63
  152.4 8.1 %collective-permute-start.20 = (bf16[384,64]{1,0:T(8,128)(2,1)S(1)}, bf16[384,64]{1,0:T(8,128)(2,1)S(1)}, u32[]{:S(2)}, u32[]{:S(2)}) collective-permute-start(bf16[384,64]{1,0:T(8,128)(2,1)S(1)} %maximum_select_fusion.16), channel_id=1, source_target_pairs={{0,32},{16,48},{32,0},{48,16},{64,96},{80,112},{96,64},{112,80},{1... | collective-permute-start | bytes 147464 | tf_op jit(solution)/shard_map/ppermute | solution.py:45
  157.2 6.2 %collective-permute-start.10 = (f32[192,64]{0,1:T(8,128)S(1)}, f32[192,64]{0,1:T(8,128)S(1)}, u32[]{:S(2)}, u32[]{:S(2)}) collective-permute-start(f32[192,64]{0,1:T(8,128)S(1)} %slice_select_fusion.9), channel_id=1, source_target_pairs={{0,2},{1,3},{2,0},{3,1},{4,6},{5,7},{6,4},{7,5},{8,10},{9,11},{10,... | collective-permute-start | bytes 147464 | tf_op jit(solution)/shard_map/ppermute | solution.py:63
  160.6 7.9 %collective-permute-start.21 = (bf16[768,64]{1,0:T(8,128)(2,1)S(1)}, bf16[768,64]{1,0:T(8,128)(2,1)S(1)}, u32[]{:S(2)}, u32[]{:S(2)}) collective-permute-start(bf16[768,64]{1,0:T(8,128)(2,1)S(1)} %maximum_select_fusion.11), channel_id=1, source_target_pairs={{0,16},{16,0},{32,48},{48,32},{64,80},{80,64},{96,112},{112,96},{1... | collective-permute-start | bytes 294920 | tf_op jit(solution)/shard_map/ppermute | solution.py:45
  163.5 7.3 %collective-permute-start.11 = (f32[96,64]{0,1:T(8,128)S(1)}, f32[96,64]{0,1:T(8,128)S(1)}, u32[]{:S(2)}, u32[]{:S(2)}) collective-permute-start(f32[96,64]{0,1:T(8,128)S(1)} %slice_select_fusion.19), channel_id=1, source_target_pairs={{0,4},{1,5},{2,6},{3,7},{4,0},{5,1},{6,2},{7,3},{8,12},{9,13},{10,... | collective-permute-start | bytes 73736 | tf_op jit(solution)/shard_map/ppermute | solution.py:63
  171.0 14.5 %collective-permute-start.12 = (f32[48,64]{0,1:T(8,128)S(1)}, f32[48,64]{0,1:T(8,128)S(1)}, u32[]{:S(2)}, u32[]{:S(2)}) collective-permute-start(f32[48,64]{0,1:T(8,128)S(1)} %slice_select_fusion.18), channel_id=1, source_target_pairs={{0,8},{1,9},{2,10},{3,11},{4,12},{5,13},{6,14},{7,15},{8,0},{9,1},... | collective-permute-start | bytes 36872 | tf_op jit(solution)/shard_map/ppermute | solution.py:63
  172.9 17.7 %collective-permute-start.22 = (f32[384,64]{0,1:T(8,128)S(1)}, f32[384,64]{0,1:T(8,128)S(1)}, u32[]{:S(2)}, u32[]{:S(2)}) collective-permute-start(f32[384,64]{0,1:T(8,128)S(1)} %slice_select_fusion.3), channel_id=1, source_target_pairs={{0,1},{1,0},{2,3},{3,2},{4,5},{5,4},{6,7},{7,6},{8,9},{9,8},{10,11... | collective-permute-start | bytes 294920 | tf_op jit(solution)/shard_map/ppermute | solution.py:63
  186.2 7.1 %collective-permute-start.13 = (bf16[64,384]{1,0:T(8,128)(2,1)S(1)}, bf16[64,384]{1,0:T(8,128)(2,1)S(1)}, u32[]{:S(2)}, u32[]{:S(2)}) collective-permute-start(bf16[64,384]{1,0:T(8,128)(2,1)S(1)} %get-tuple-element.19), channel_id=1, source_target_pairs={{0,16},{16,32},{32,48},{48,64},{64,80},{80,96},{96,112},{112,128},... | collective-permute-start | bytes 147464 | tf_op jit(solution)/shard_map/ppermute | solution.py:15
  189.3 6.3 %collective-permute-start.14 = (bf16[64,384]{1,0:T(8,128)(2,1)S(1)}, bf16[64,384]{1,0:T(8,128)(2,1)S(1)}, u32[]{:S(2)}, u32[]{:S(2)}) collective-permute-start(bf16[64,384]{1,0:T(8,128)(2,1)S(1)} %get-tuple-element.20), channel_id=1, source_target_pairs={{16,0},{32,16},{48,32},{64,48},{80,64},{96,80},{112,96},{128,112},... | collective-permute-start | bytes 147464 | tf_op jit(solution)/shard_map/ppermute | solution.py:15
  190.7 6.9 %collective-permute-start.23 = (f32[192,64]{0,1:T(8,128)S(1)}, f32[192,64]{0,1:T(8,128)S(1)}, u32[]{:S(2)}, u32[]{:S(2)}) collective-permute-start(f32[192,64]{0,1:T(8,128)S(1)} %slice_select_fusion.8), channel_id=1, source_target_pairs={{0,2},{1,3},{2,0},{3,1},{4,6},{5,7},{6,4},{7,5},{8,10},{9,11},{10,... | collective-permute-start | bytes 147464 | tf_op jit(solution)/shard_map/ppermute | solution.py:63
  195.6 11.7 %collective-permute-start.16 = (bf16[64,384]{1,0:T(8,128)(2,1)S(1)}, bf16[64,384]{1,0:T(8,128)(2,1)S(1)}, u32[]{:S(2)}, u32[]{:S(2)}) collective-permute-start(bf16[64,384]{1,0:T(8,128)(2,1)S(1)} %pad_maximum_fusion.4), channel_id=1, source_target_pairs={{1,0},{2,1},{3,2},{4,3},{5,4},{6,5},{7,6},{8,7},{9,8},{10,9},{11,1... | collective-permute-start | bytes 147464 | tf_op jit(solution)/shard_map/ppermute | solution.py:15
  197.8 7.3 %collective-permute-start.24 = (f32[96,64]{0,1:T(8,128)S(1)}, f32[96,64]{0,1:T(8,128)S(1)}, u32[]{:S(2)}, u32[]{:S(2)}) collective-permute-start(f32[96,64]{0,1:T(8,128)S(1)} %slice_select_fusion.17), channel_id=1, source_target_pairs={{0,4},{1,5},{2,6},{3,7},{4,0},{5,1},{6,2},{7,3},{8,12},{9,13},{10,... | collective-permute-start | bytes 73736 | tf_op jit(solution)/shard_map/ppermute | solution.py:63
  200.0 7.2 %collective-permute-start.15 = (bf16[64,384]{1,0:T(8,128)(2,1)S(1)}, bf16[64,384]{1,0:T(8,128)(2,1)S(1)}, u32[]{:S(2)}, u32[]{:S(2)}) collective-permute-start(bf16[64,384]{1,0:T(8,128)(2,1)S(1)} %pad_maximum_fusion.3), channel_id=1, source_target_pairs={{0,1},{1,2},{2,3},{3,4},{4,5},{5,6},{6,7},{7,8},{8,9},{9,10},{10,1... | collective-permute-start | bytes 147464 | tf_op jit(solution)/shard_map/ppermute | solution.py:15
  205.2 14.8 %collective-permute-start.25 = (f32[48,64]{0,1:T(8,128)S(1)}, f32[48,64]{0,1:T(8,128)S(1)}, u32[]{:S(2)}, u32[]{:S(2)}) collective-permute-start(f32[48,64]{0,1:T(8,128)S(1)} %slice_select_fusion.16), channel_id=1, source_target_pairs={{0,8},{1,9},{2,10},{3,11},{4,12},{5,13},{6,14},{7,15},{8,0},{9,1},... | collective-permute-start | bytes 36872 | tf_op jit(solution)/shard_map/ppermute | solution.py:63
  208.5 13.2 %collective-permute-start.30 = (bf16[48,64]{1,0:T(8,128)(2,1)S(1)}, bf16[48,64]{1,0:T(8,128)(2,1)S(1)}, u32[]{:S(2)}, u32[]{:S(2)}) collective-permute-start(bf16[48,64]{1,0:T(8,128)(2,1)S(1)} %fusion.52), channel_id=1, source_target_pairs={{0,256},{16,272},{32,288},{48,304},{64,320},{80,336},{96,352},{112... | collective-permute-start | bytes 18440 | tf_op jit(solution)/shard_map/ppermute | solution.py:45
  221.7 7.2 %collective-permute-start.31 = (bf16[96,64]{1,0:T(8,128)(2,1)S(1)}, bf16[96,64]{1,0:T(8,128)(2,1)S(1)}, u32[]{:S(2)}, u32[]{:S(2)}) collective-permute-start(bf16[96,64]{1,0:T(8,128)(2,1)S(1)} %maximum_select_fusion.27), channel_id=1, source_target_pairs={{0,128},{16,144},{32,160},{48,176},{64,192},{80,208},{96,224},{112... | collective-permute-start | bytes 36872 | tf_op jit(solution)/shard_map/ppermute | solution.py:45
  228.9 7.1 %collective-permute-start.32 = (bf16[192,64]{1,0:T(8,128)(2,1)S(1)}, bf16[192,64]{1,0:T(8,128)(2,1)S(1)}, u32[]{:S(2)}, u32[]{:S(2)}) collective-permute-start(bf16[192,64]{1,0:T(8,128)(2,1)S(1)} %maximum_select_fusion.22), channel_id=1, source_target_pairs={{0,64},{16,80},{32,96},{48,112},{64,0},{80,16},{96,32},{112,48},{1... | collective-permute-start | bytes 73736 | tf_op jit(solution)/shard_map/ppermute | solution.py:45
  233.2 11.3 %collective-permute-start.26 = (bf16[64,384]{1,0:T(8,128)(2,1)S(1)}, bf16[64,384]{1,0:T(8,128)(2,1)S(1)}, u32[]{:S(2)}, u32[]{:S(2)}) collective-permute-start(bf16[64,384]{1,0:T(8,128)(2,1)S(1)} %get-tuple-element.15), channel_id=1, source_target_pairs={{0,16},{16,32},{32,48},{48,64},{64,80},{80,96},{96,112},{112,128},... | collective-permute-start | bytes 147464 | tf_op jit(solution)/shard_map/ppermute | solution.py:15
  234.7 9.8 %collective-permute-start.27 = (bf16[64,384]{1,0:T(8,128)(2,1)S(1)}, bf16[64,384]{1,0:T(8,128)(2,1)S(1)}, u32[]{:S(2)}, u32[]{:S(2)}) collective-permute-start(bf16[64,384]{1,0:T(8,128)(2,1)S(1)} %get-tuple-element.16), channel_id=1, source_target_pairs={{16,0},{32,16},{48,32},{64,48},{80,64},{96,80},{112,96},{128,112},... | collective-permute-start | bytes 147464 | tf_op jit(solution)/shard_map/ppermute | solution.py:15
  236.1 33.3 %collective-permute-start.33 = (bf16[384,64]{1,0:T(8,128)(2,1)S(1)}, bf16[384,64]{1,0:T(8,128)(2,1)S(1)}, u32[]{:S(2)}, u32[]{:S(2)}) collective-permute-start(bf16[384,64]{1,0:T(8,128)(2,1)S(1)} %maximum_select_fusion.17), channel_id=1, source_target_pairs={{0,32},{16,48},{32,0},{48,16},{64,96},{80,112},{96,64},{112,80},{1... | collective-permute-start | bytes 147464 | tf_op jit(solution)/shard_map/ppermute | solution.py:45
  247.0 15.8 %collective-permute-start.29 = (bf16[64,384]{1,0:T(8,128)(2,1)S(1)}, bf16[64,384]{1,0:T(8,128)(2,1)S(1)}, u32[]{:S(2)}, u32[]{:S(2)}) collective-permute-start(bf16[64,384]{1,0:T(8,128)(2,1)S(1)} %pad_maximum_fusion.6), channel_id=1, source_target_pairs={{1,0},{2,1},{3,2},{4,3},{5,4},{6,5},{7,6},{8,7},{9,8},{10,9},{11,1... | collective-permute-start | bytes 147464 | tf_op jit(solution)/shard_map/ppermute | solution.py:15
  263.6 9.5 %collective-permute-start.43 = (bf16[48,64]{1,0:T(8,128)(2,1)S(1)}, bf16[48,64]{1,0:T(8,128)(2,1)S(1)}, u32[]{:S(2)}, u32[]{:S(2)}) collective-permute-start(bf16[48,64]{1,0:T(8,128)(2,1)S(1)} %fusion.53), channel_id=1, source_target_pairs={{0,256},{16,272},{32,288},{48,304},{64,320},{80,336},{96,352},{112... | collective-permute-start | bytes 18440 | tf_op jit(solution)/shard_map/ppermute | solution.py:45
  269.5 12.3 %collective-permute-start.34 = (bf16[768,64]{1,0:T(8,128)(2,1)S(1)}, bf16[768,64]{1,0:T(8,128)(2,1)S(1)}, u32[]{:S(2)}, u32[]{:S(2)}) collective-permute-start(bf16[768,64]{1,0:T(8,128)(2,1)S(1)} %maximum_select_fusion.12), channel_id=1, source_target_pairs={{0,16},{16,0},{32,48},{48,32},{64,80},{80,64},{96,112},{112,96},{1... | collective-permute-start | bytes 294920 | tf_op jit(solution)/shard_map/ppermute | solution.py:45
  273.1 6.6 %collective-permute-start.44 = (bf16[96,64]{1,0:T(8,128)(2,1)S(1)}, bf16[96,64]{1,0:T(8,128)(2,1)S(1)}, u32[]{:S(2)}, u32[]{:S(2)}) collective-permute-start(bf16[96,64]{1,0:T(8,128)(2,1)S(1)} %maximum_select_fusion.28), channel_id=1, source_target_pairs={{0,128},{16,144},{32,160},{48,176},{64,192},{80,208},{96,224},{112... | collective-permute-start | bytes 36872 | tf_op jit(solution)/shard_map/ppermute | solution.py:45
  279.8 16.4 %collective-permute-start.45 = (bf16[192,64]{1,0:T(8,128)(2,1)S(1)}, bf16[192,64]{1,0:T(8,128)(2,1)S(1)}, u32[]{:S(2)}, u32[]{:S(2)}) collective-permute-start(bf16[192,64]{1,0:T(8,128)(2,1)S(1)} %maximum_select_fusion.23), channel_id=1, source_target_pairs={{0,64},{16,80},{32,96},{48,112},{64,0},{80,16},{96,32},{112,48},{1... | collective-permute-start | bytes 73736 | tf_op jit(solution)/shard_map/ppermute | solution.py:45
  282.4 19.3 %collective-permute-start.35 = (f32[384,64]{0,1:T(8,128)S(1)}, f32[384,64]{0,1:T(8,128)S(1)}, u32[]{:S(2)}, u32[]{:S(2)}) collective-permute-start(f32[384,64]{0,1:T(8,128)S(1)} %slice_select_fusion.2), channel_id=1, source_target_pairs={{0,1},{1,0},{2,3},{3,2},{4,5},{5,4},{6,7},{7,6},{8,9},{9,8},{10,11... | collective-permute-start | bytes 294920 | tf_op jit(solution)/shard_map/ppermute | solution.py:63
  296.2 8.7 %collective-permute-start.46 = (bf16[384,64]{1,0:T(8,128)(2,1)S(1)}, bf16[384,64]{1,0:T(8,128)(2,1)S(1)}, u32[]{:S(2)}, u32[]{:S(2)}) collective-permute-start(bf16[384,64]{1,0:T(8,128)(2,1)S(1)} %maximum_select_fusion.18), channel_id=1, source_target_pairs={{0,32},{16,48},{32,0},{48,16},{64,96},{80,112},{96,64},{112,80},{1... | collective-permute-start | bytes 147464 | tf_op jit(solution)/shard_map/ppermute | solution.py:45
  301.8 7.1 %collective-permute-start.36 = (f32[192,64]{0,1:T(8,128)S(1)}, f32[192,64]{0,1:T(8,128)S(1)}, u32[]{:S(2)}, u32[]{:S(2)}) collective-permute-start(f32[192,64]{0,1:T(8,128)S(1)} %slice_select_fusion.7), channel_id=1, source_target_pairs={{0,2},{1,3},{2,0},{3,1},{4,6},{5,7},{6,4},{7,5},{8,10},{9,11},{10,... | collective-permute-start | bytes 147464 | tf_op jit(solution)/shard_map/ppermute | solution.py:63
  305.0 8.4 %collective-permute-start.47 = (bf16[768,64]{1,0:T(8,128)(2,1)S(1)}, bf16[768,64]{1,0:T(8,128)(2,1)S(1)}, u32[]{:S(2)}, u32[]{:S(2)}) collective-permute-start(bf16[768,64]{1,0:T(8,128)(2,1)S(1)} %maximum_select_fusion.13), channel_id=1, source_target_pairs={{0,16},{16,0},{32,48},{48,32},{64,80},{80,64},{96,112},{112,96},{1... | collective-permute-start | bytes 294920 | tf_op jit(solution)/shard_map/ppermute | solution.py:45
  309.0 7.3 %collective-permute-start.37 = (f32[96,64]{0,1:T(8,128)S(1)}, f32[96,64]{0,1:T(8,128)S(1)}, u32[]{:S(2)}, u32[]{:S(2)}) collective-permute-start(f32[96,64]{0,1:T(8,128)S(1)} %slice_select_fusion.15), channel_id=1, source_target_pairs={{0,4},{1,5},{2,6},{3,7},{4,0},{5,1},{6,2},{7,3},{8,12},{9,13},{10,... | collective-permute-start | bytes 73736 | tf_op jit(solution)/shard_map/ppermute | solution.py:63
  316.5 14.7 %collective-permute-start.38 = (f32[48,64]{0,1:T(8,128)S(1)}, f32[48,64]{0,1:T(8,128)S(1)}, u32[]{:S(2)}, u32[]{:S(2)}) collective-permute-start(f32[48,64]{0,1:T(8,128)S(1)} %slice_select_fusion.14), channel_id=1, source_target_pairs={{0,8},{1,9},{2,10},{3,11},{4,12},{5,13},{6,14},{7,15},{8,0},{9,1},... | collective-permute-start | bytes 36872 | tf_op jit(solution)/shard_map/ppermute | solution.py:63
  318.4 18.0 %collective-permute-start.48 = (f32[384,64]{0,1:T(8,128)S(1)}, f32[384,64]{0,1:T(8,128)S(1)}, u32[]{:S(2)}, u32[]{:S(2)}) collective-permute-start(f32[384,64]{0,1:T(8,128)S(1)} %slice_select_fusion.1), channel_id=1, source_target_pairs={{0,1},{1,0},{2,3},{3,2},{4,5},{5,4},{6,7},{7,6},{8,9},{9,8},{10,11... | collective-permute-start | bytes 294920 | tf_op jit(solution)/shard_map/ppermute | solution.py:63
  331.8 6.8 %collective-permute-start.39 = (bf16[64,384]{1,0:T(8,128)(2,1)S(1)}, bf16[64,384]{1,0:T(8,128)(2,1)S(1)}, u32[]{:S(2)}, u32[]{:S(2)}) collective-permute-start(bf16[64,384]{1,0:T(8,128)(2,1)S(1)} %get-tuple-element.11), channel_id=1, source_target_pairs={{0,16},{16,32},{32,48},{48,64},{64,80},{80,96},{96,112},{112,128},... | collective-permute-start | bytes 147464 | tf_op jit(solution)/shard_map/ppermute | solution.py:15
  335.1 6.4 %collective-permute-start.40 = (bf16[64,384]{1,0:T(8,128)(2,1)S(1)}, bf16[64,384]{1,0:T(8,128)(2,1)S(1)}, u32[]{:S(2)}, u32[]{:S(2)}) collective-permute-start(bf16[64,384]{1,0:T(8,128)(2,1)S(1)} %get-tuple-element.12), channel_id=1, source_target_pairs={{16,0},{32,16},{48,32},{64,48},{80,64},{96,80},{112,96},{128,112},... | collective-permute-start | bytes 147464 | tf_op jit(solution)/shard_map/ppermute | solution.py:15
  336.5 7.0 %collective-permute-start.49 = (f32[192,64]{0,1:T(8,128)S(1)}, f32[192,64]{0,1:T(8,128)S(1)}, u32[]{:S(2)}, u32[]{:S(2)}) collective-permute-start(f32[192,64]{0,1:T(8,128)S(1)} %slice_select_fusion.6), channel_id=1, source_target_pairs={{0,2},{1,3},{2,0},{3,1},{4,6},{5,7},{6,4},{7,5},{8,10},{9,11},{10,... | collective-permute-start | bytes 147464 | tf_op jit(solution)/shard_map/ppermute | solution.py:63
  341.5 11.5 %collective-permute-start.42 = (bf16[64,384]{1,0:T(8,128)(2,1)S(1)}, bf16[64,384]{1,0:T(8,128)(2,1)S(1)}, u32[]{:S(2)}, u32[]{:S(2)}) collective-permute-start(bf16[64,384]{1,0:T(8,128)(2,1)S(1)} %pad_maximum_fusion.8), channel_id=1, source_target_pairs={{1,0},{2,1},{3,2},{4,3},{5,4},{6,5},{7,6},{8,7},{9,8},{10,9},{11,1... | collective-permute-start | bytes 147464 | tf_op jit(solution)/shard_map/ppermute | solution.py:15
  343.6 7.3 %collective-permute-start.50 = (f32[96,64]{0,1:T(8,128)S(1)}, f32[96,64]{0,1:T(8,128)S(1)}, u32[]{:S(2)}, u32[]{:S(2)}) collective-permute-start(f32[96,64]{0,1:T(8,128)S(1)} %slice_select_fusion.13), channel_id=1, source_target_pairs={{0,4},{1,5},{2,6},{3,7},{4,0},{5,1},{6,2},{7,3},{8,12},{9,13},{10,... | collective-permute-start | bytes 73736 | tf_op jit(solution)/shard_map/ppermute | solution.py:63
  345.7 7.3 %collective-permute-start.41 = (bf16[64,384]{1,0:T(8,128)(2,1)S(1)}, bf16[64,384]{1,0:T(8,128)(2,1)S(1)}, u32[]{:S(2)}, u32[]{:S(2)}) collective-permute-start(bf16[64,384]{1,0:T(8,128)(2,1)S(1)} %pad_maximum_fusion.7), channel_id=1, source_target_pairs={{0,1},{1,2},{2,3},{3,4},{4,5},{5,6},{6,7},{7,8},{8,9},{9,10},{10,1... | collective-permute-start | bytes 147464 | tf_op jit(solution)/shard_map/ppermute | solution.py:15
  351.1 15.3 %collective-permute-start.51 = (f32[48,64]{0,1:T(8,128)S(1)}, f32[48,64]{0,1:T(8,128)S(1)}, u32[]{:S(2)}, u32[]{:S(2)}) collective-permute-start(f32[48,64]{0,1:T(8,128)S(1)} %slice_select_fusion.12), channel_id=1, source_target_pairs={{0,8},{1,9},{2,10},{3,11},{4,12},{5,13},{6,14},{7,15},{8,0},{9,1},... | collective-permute-start | bytes 36872 | tf_op jit(solution)/shard_map/ppermute | solution.py:63
  354.2 12.8 %collective-permute-start.56 = (bf16[48,64]{1,0:T(8,128)(2,1)S(1)}, bf16[48,64]{1,0:T(8,128)(2,1)S(1)}, u32[]{:S(2)}, u32[]{:S(2)}) collective-permute-start(bf16[48,64]{1,0:T(8,128)(2,1)S(1)} %fusion.54), channel_id=1, source_target_pairs={{0,256},{16,272},{32,288},{48,304},{64,320},{80,336},{96,352},{112... | collective-permute-start | bytes 18440 | tf_op jit(solution)/shard_map/ppermute | solution.py:45
  367.0 9.1 %collective-permute-start.57 = (bf16[96,64]{1,0:T(8,128)(2,1)S(1)}, bf16[96,64]{1,0:T(8,128)(2,1)S(1)}, u32[]{:S(2)}, u32[]{:S(2)}) collective-permute-start(bf16[96,64]{1,0:T(8,128)(2,1)S(1)} %maximum_select_fusion.29), channel_id=1, source_target_pairs={{0,128},{16,144},{32,160},{48,176},{64,192},{80,208},{96,224},{112... | collective-permute-start | bytes 36872 | tf_op jit(solution)/shard_map/ppermute | solution.py:45
  376.1 6.0 %collective-permute-start.58 = (bf16[192,64]{1,0:T(8,128)(2,1)S(1)}, bf16[192,64]{1,0:T(8,128)(2,1)S(1)}, u32[]{:S(2)}, u32[]{:S(2)}) collective-permute-start(bf16[192,64]{1,0:T(8,128)(2,1)S(1)} %maximum_select_fusion.24), channel_id=1, source_target_pairs={{0,64},{16,80},{32,96},{48,112},{64,0},{80,16},{96,32},{112,48},{1... | collective-permute-start | bytes 73736 | tf_op jit(solution)/shard_map/ppermute | solution.py:45
  378.1 10.3 %collective-permute-start.52 = (bf16[64,384]{1,0:T(8,128)(2,1)S(1)}, bf16[64,384]{1,0:T(8,128)(2,1)S(1)}, u32[]{:S(2)}, u32[]{:S(2)}) collective-permute-start(bf16[64,384]{1,0:T(8,128)(2,1)S(1)} %get-tuple-element.7), channel_id=1, source_target_pairs={{0,16},{16,32},{32,48},{48,64},{64,80},{80,96},{96,112},{112,128},... | collective-permute-start | bytes 147464 | tf_op jit(solution)/shard_map/ppermute | solution.py:15
  379.8 8.6 %collective-permute-start.53 = (bf16[64,384]{1,0:T(8,128)(2,1)S(1)}, bf16[64,384]{1,0:T(8,128)(2,1)S(1)}, u32[]{:S(2)}, u32[]{:S(2)}) collective-permute-start(bf16[64,384]{1,0:T(8,128)(2,1)S(1)} %get-tuple-element.8), channel_id=1, source_target_pairs={{16,0},{32,16},{48,32},{64,48},{80,64},{96,80},{112,96},{128,112},... | collective-permute-start | bytes 147464 | tf_op jit(solution)/shard_map/ppermute | solution.py:15
  382.1 11.8 %collective-permute-start.59 = (bf16[384,64]{1,0:T(8,128)(2,1)S(1)}, bf16[384,64]{1,0:T(8,128)(2,1)S(1)}, u32[]{:S(2)}, u32[]{:S(2)}) collective-permute-start(bf16[384,64]{1,0:T(8,128)(2,1)S(1)} %maximum_select_fusion.19), channel_id=1, source_target_pairs={{0,32},{16,48},{32,0},{48,16},{64,96},{80,112},{96,64},{112,80},{1... | collective-permute-start | bytes 147464 | tf_op jit(solution)/shard_map/ppermute | solution.py:45
  388.4 30.2 %collective-permute-start.55 = (bf16[64,384]{1,0:T(8,128)(2,1)S(1)}, bf16[64,384]{1,0:T(8,128)(2,1)S(1)}, u32[]{:S(2)}, u32[]{:S(2)}) collective-permute-start(bf16[64,384]{1,0:T(8,128)(2,1)S(1)} %pad_maximum_fusion.10), channel_id=1, source_target_pairs={{1,0},{2,1},{3,2},{4,3},{5,4},{6,5},{7,6},{8,7},{9,8},{10,9},{11,1... | collective-permute-start | bytes 147464 | tf_op jit(solution)/shard_map/ppermute | solution.py:15
  390.4 7.2 %collective-permute-start.54 = (bf16[64,384]{1,0:T(8,128)(2,1)S(1)}, bf16[64,384]{1,0:T(8,128)(2,1)S(1)}, u32[]{:S(2)}, u32[]{:S(2)}) collective-permute-start(bf16[64,384]{1,0:T(8,128)(2,1)S(1)} %pad_maximum_fusion.9), channel_id=1, source_target_pairs={{0,1},{1,2},{2,3},{3,4},{4,5},{5,6},{6,7},{7,8},{8,9},{9,10},{10,1... | collective-permute-start | bytes 147464 | tf_op jit(solution)/shard_map/ppermute | solution.py:15
  394.0 7.6 %collective-permute-start.60 = (bf16[768,64]{1,0:T(8,128)(2,1)S(1)}, bf16[768,64]{1,0:T(8,128)(2,1)S(1)}, u32[]{:S(2)}, u32[]{:S(2)}) collective-permute-start(bf16[768,64]{1,0:T(8,128)(2,1)S(1)} %maximum_select_fusion.14), channel_id=1, source_target_pairs={{0,16},{16,0},{32,48},{48,32},{64,80},{80,64},{96,112},{112,96},{1... | collective-permute-start | bytes 294920 | tf_op jit(solution)/shard_map/ppermute | solution.py:45
  402.2 17.4 %collective-permute-start.61 = (f32[384,64]{0,1:T(8,128)S(1)}, f32[384,64]{0,1:T(8,128)S(1)}, u32[]{:S(2)}, u32[]{:S(2)}) collective-permute-start(f32[384,64]{0,1:T(8,128)S(1)} %slice_select_fusion), channel_id=1, source_target_pairs={{0,1},{1,0},{2,3},{3,2},{4,5},{5,4},{6,7},{7,6},{8,9},{9,8},{10,11... | collective-permute-start | bytes 294920 | tf_op jit(solution)/shard_map/ppermute | solution.py:63
  419.7 6.2 %collective-permute-start.62 = (f32[192,64]{0,1:T(8,128)S(1)}, f32[192,64]{0,1:T(8,128)S(1)}, u32[]{:S(2)}, u32[]{:S(2)}) collective-permute-start(f32[192,64]{0,1:T(8,128)S(1)} %slice_select_fusion.5), channel_id=1, source_target_pairs={{0,2},{1,3},{2,0},{3,1},{4,6},{5,7},{6,4},{7,5},{8,10},{9,11},{10,... | collective-permute-start | bytes 147464 | tf_op jit(solution)/shard_map/ppermute | solution.py:63
  426.1 7.3 %collective-permute-start.63 = (f32[96,64]{0,1:T(8,128)S(1)}, f32[96,64]{0,1:T(8,128)S(1)}, u32[]{:S(2)}, u32[]{:S(2)}) collective-permute-start(f32[96,64]{0,1:T(8,128)S(1)} %slice_select_fusion.11), channel_id=1, source_target_pairs={{0,4},{1,5},{2,6},{3,7},{4,0},{5,1},{6,2},{7,3},{8,12},{9,13},{10,... | collective-permute-start | bytes 73736 | tf_op jit(solution)/shard_map/ppermute | solution.py:63
  433.6 14.5 %collective-permute-start.64 = (f32[48,64]{0,1:T(8,128)S(1)}, f32[48,64]{0,1:T(8,128)S(1)}, u32[]{:S(2)}, u32[]{:S(2)}) collective-permute-start(f32[48,64]{0,1:T(8,128)S(1)} %slice_select_fusion.10), channel_id=1, source_target_pairs={{0,8},{1,9},{2,10},{3,11},{4,12},{5,13},{6,14},{7,15},{8,0},{9,1},... | collective-permute-start | bytes 36872 | tf_op jit(solution)/shard_map/ppermute | solution.py:63
  (21 other events, 506.6 us)

commit v5 on v4

--- a/solution.py
+++ b/solution.py
@@ -32,15 +32,11 @@
     )
 
 
-def bit_reversed(bits):
-    return [int(format(i, f"0{bits}b")[::-1], 2) if bits else 0 for i in range(1 << bits)]
-
-
 def gather_rows(piece):
     index = lax.axis_index("row")
     size = lax.axis_size("row")
     current = piece
-    for bit in range(size.bit_length() - 2, -1, -1):
+    for bit in range(size.bit_length() - 1):
         route = [(i, i ^ (1 << bit)) for i in range(size)]
         other = lax.ppermute(current, "row", route)
         high = ((index >> bit) & 1) == 1
@@ -54,7 +50,7 @@
     index = lax.axis_index("col")
     size = lax.axis_size("col")
     current = partial
-    for bit in range(size.bit_length() - 1):
+    for bit in range(size.bit_length() - 2, -1, -1):
         route = [(i, i ^ (1 << bit)) for i in range(size)]
         half = current.shape[0] // 2
         high = ((index >> bit) & 1) == 1
@@ -80,8 +76,6 @@
     block_size = coupling.shape[3]
     block_count = unknowns // block_size
     mode_count = modes.shape[2]
-    row_bits = lax.axis_size("row").bit_length() - 1
-    col_bits = lax.axis_size("col").bit_length() - 1
     rhs_full = rhs[0, 0].astype(jnp.float32)
     solver_matrix = local_solver[0, 0]
     mode_basis = modes[0, 0]
@@ -104,11 +98,7 @@
         [operator_blocks[0, 0], placed_matrix.reshape(-1, unknowns)], 0
     )
 
-    rows = lax.axis_size("row")
-    cols = lax.axis_size("col")
-    tile = coarse_inverse[0, :, 0, :].reshape(rows, mode_count, cols, mode_count)
-    tile = tile[jnp.array(bit_reversed(row_bits))][:, :, jnp.array(bit_reversed(col_bits))]
-    coarse_matrix = tile.reshape(rows * mode_count, cols * mode_count).T
+    coarse_matrix = coarse_inverse[0, :, 0, :].T
 
     def coarse_solve(rounded):
         restricted = lax.dot_general(

time: 452 us -> 433 us (0.958)
  local copies, waits for them, and re-layouts: 65.8 us -> 9.86 us
  waiting for transfers between devices: 101 us -> 135 us
    ppermute x25, waiting for transfers between devices: 26.1 us -> 64.1 us  [gather_rows(): other = lax.ppermute(current, 'row', route)]
    gather x4 -> x0, local copies, waits for them, and re-layouts: 33.3 us -> none  [on_device(): tile[jnp.array(bit_reversed(row_bits))]]
    ppermute x25, starting transfers between devices: 127 us -> 94.9 us  [gather_rows(): other = lax.ppermute(current, 'row', route)]
    ppermute x20, starting transfers between devices: 45 us -> 70.5 us  [shifted(): return lax.ppermute(block, axis, route)]
    ppermute x20, waiting for transfers between devices: 25.2 us -> 14 us  [shifted(): return lax.ppermute(block, axis, route)]
    another operation x1 -> x0, local copies, waits for them, and re-layouts: 10 us -> none  [on_device(): coarse_inverse[0, :, 0, :].reshape(rows, mode_count, cols, mode_count)]
    reshape x1 -> x0, local copies, waits for them, and re-layouts: 9.72 us -> none  [on_device(): coarse_matrix = tile.reshape(rows * mode_count, cols * mode_count).T]
    ppermute x20, waiting for transfers between devices: 50.2 us -> 57.1 us  [scatter_cols(): current = keep + lax.ppermute(send, 'col', route)]
  transfers between devices with their start and end apart: 65 -> 65, of which waited for: 31 -> 23; matrix products, arithmetic and copies ran while one was open for 20% -> 7% of each run, Pallas kernels for 0% -> 0%
where the time goes in v5:
time: 433 us; the launch traced here: 428 us
  starting transfers between devices  253 us (58%)
  waiting for transfers between devices  135 us (31%)
  matrix products  18.9 us (4%)
  local copies, waits for them, and re-layouts  9.86 us (2%)
  other arithmetic  8.73 us (2%)
    ppermute x25, starting transfers between devices, gather_rows(): other = lax.ppermute(current, 'row', route)  94.9 us
    ppermute x20, starting transfers between devices, scatter_cols(): current = keep + lax.ppermute(send, 'col', route)  87.9 us
    ppermute x20, starting transfers between devices, shifted(): return lax.ppermute(block, axis, route)  70.5 us
    ppermute x25, waiting for transfers between devices, gather_rows(): other = lax.ppermute(current, 'row', route)  64.1 us
    ppermute x20, waiting for transfers between devices, scatter_cols(): current = keep + lax.ppermute(send, 'col', route)  57.1 us
    ppermute x20, waiting for transfers between devices, shifted(): return lax.ppermute(block, axis, route)  14 us
  transfers between devices with their start and end apart: 65, of which 23 were waited for; matrix products, arithmetic and copies ran while one was open for 7% of the time, Pallas kernels for 0%

profile of v5, /device:TPU:6, one launch (start us, length us, event | category | flops | bytes accessed | tf_op | source)
XLA Modules:
  0.0 427.9 jit_solution(10676532141736269355)
XLA Ops:
  1.2 3.5 collective-permute-start.4
  6.7 2.3 constant_dynamic-update-slice_fusion.4
  11.6 3.0 collective-permute-start
  17.4 6.4 %collective-permute-start.5 = (bf16[96,64]{1,0:T(8,128)(2,1)S(1)}, bf16[96,64]{1,0:T(8,128)(2,1)S(1)}, u32[]{:S(2)}, u32[]{:S(2)}) collective-permute-start(bf16[96,64]{1,0:T(8,128)(2,1)S(1)} %maximum_select_fusion.25), channel_id=1, source_target_pairs={{0,32},{16,48},{32,0},{48,16},{64,96},{80,112},{96,64},{112,80},{1... | collective-permute-start | bytes 36872 | tf_op jit(solution)/shard_map/ppermute | solution.py:41
  25.6 6.6 %collective-permute-start.6 = (bf16[192,64]{1,0:T(8,128)(2,1)S(1)}, bf16[192,64]{1,0:T(8,128)(2,1)}, u32[]{:S(2)}, u32[]{:S(2)}) collective-permute-start(bf16[192,64]{1,0:T(8,128)(2,1)S(1)} %maximum_select_fusion.20), channel_id=1, source_target_pairs={{0,64},{16,80},{32,96},{48,112},{64,0},{80,16},{96,32},{112,48},{1... | collective-permute-start | bytes 73736 | tf_op jit(solution)/shard_map/ppermute | solution.py:41
  36.3 5.2 %collective-permute-start.7 = (bf16[384,64]{1,0:T(8,128)(2,1)S(1)}, bf16[384,64]{1,0:T(8,128)(2,1)S(1)}, u32[]{:S(2)}, u32[]{:S(2)}) collective-permute-start(bf16[384,64]{1,0:T(8,128)(2,1)S(1)} %maximum_select_fusion.15), channel_id=1, source_target_pairs={{0,128},{16,144},{32,160},{48,176},{64,192},{80,208},{96,224},{112... | collective-permute-start | bytes 147464 | tf_op jit(solution)/shard_map/ppermute | solution.py:41
  43.0 1.9 collective-permute-start.2
  45.0 3.6 collective-permute-start.3
  48.7 10.1 %collective-permute-done.3 = bf16[64,384]{1,0:T(8,128)(2,1)S(1)} collective-permute-done((bf16[64,384]{1,0:T(8,128)(2,1)S(1)}, bf16[64,384]{1,0:T(8,128)(2,1)S(1)}, u32[]{:S(2)}, u32[]{:S(2)}) %collective-permute-start.3) | collective-permute-done | bytes 49184 | tf_op jit(solution)/shard_map/ppermute | solution.py:15
  61.2 1.9 collective-permute-start.17
  63.2 4.3 %collective-permute-start.8 = (bf16[768,64]{1,0:T(8,128)(2,1)S(1)}, bf16[768,64]{1,0:T(8,128)(2,1)S(1)}, u32[]{:S(2)}, u32[]{:S(2)}) collective-permute-start(bf16[768,64]{1,0:T(8,128)(2,1)S(1)} %maximum_select_fusion.10), channel_id=1, source_target_pairs={{0,256},{16,272},{32,288},{48,304},{64,320},{80,336},{96,352},{112... | collective-permute-start | bytes 294920 | tf_op jit(solution)/shard_map/ppermute | solution.py:41
  67.6 4.0 collective-permute-start.18
  71.9 2.9 collective-permute-done.18
  74.8 2.9 collective-permute-start.19
  77.7 3.4 collective-permute-done.8
  81.7 10.0 %collective-permute-start.9 = (f32[384,64]{0,1:T(8,128)S(1)}, f32[384,64]{0,1:T(8,128)S(1)}, u32[]{:S(2)}, u32[]{:S(2)}) collective-permute-start(f32[384,64]{0,1:T(8,128)S(1)} %slice_select_fusion.4), channel_id=1, source_target_pairs={{0,8},{1,9},{2,10},{3,11},{4,12},{5,13},{6,14},{7,15},{8,0},{9,1},... | collective-permute-start | bytes 294920 | tf_op jit(solution)/shard_map/ppermute | solution.py:59
  93.7 5.5 %collective-permute-done.9 = f32[384,64]{0,1:T(8,128)S(1)} collective-permute-done((f32[384,64]{0,1:T(8,128)S(1)}, f32[384,64]{0,1:T(8,128)S(1)}, u32[]{:S(2)}, u32[]{:S(2)}) %collective-permute-start.9) | collective-permute-done | bytes 98336 | tf_op jit(solution)/shard_map/ppermute | solution.py:59
  99.3 8.9 %collective-permute-start.10 = (f32[192,64]{0,1:T(8,128)S(1)}, f32[192,64]{0,1:T(8,128)S(1)}, u32[]{:S(2)}, u32[]{:S(2)}) collective-permute-start(f32[192,64]{0,1:T(8,128)S(1)} %slice_select_fusion.9), channel_id=1, source_target_pairs={{0,4},{1,5},{2,6},{3,7},{4,0},{5,1},{6,2},{7,3},{8,12},{9,13},{10,... | collective-permute-start | bytes 147464 | tf_op jit(solution)/shard_map/ppermute | solution.py:59
  110.6 5.1 %collective-permute-start.11 = (f32[96,64]{0,1:T(8,128)S(1)}, f32[96,64]{0,1:T(8,128)S(1)}, u32[]{:S(2)}, u32[]{:S(2)}) collective-permute-start(f32[96,64]{0,1:T(8,128)S(1)} %slice_select_fusion.19), channel_id=1, source_target_pairs={{0,2},{1,3},{2,0},{3,1},{4,6},{5,7},{6,4},{7,5},{8,10},{9,11},{10,... | collective-permute-start | bytes 73736 | tf_op jit(solution)/shard_map/ppermute | solution.py:59
  115.7 14.0 %collective-permute-done.21 = bf16[768,64]{1,0:T(8,128)(2,1)S(1)} collective-permute-done((bf16[768,64]{1,0:T(8,128)(2,1)S(1)}, bf16[768,64]{1,0:T(8,128)(2,1)S(1)}, u32[]{:S(2)}, u32[]{:S(2)}) %collective-permute-start.21) | collective-permute-done | bytes 98336 | tf_op jit(solution)/shard_map/ppermute | solution.py:41
  130.4 2.0 collective-permute-start.12
  132.4 7.4 %collective-permute-start.22 = (f32[384,64]{0,1:T(8,128)S(1)}, f32[384,64]{0,1:T(8,128)S(1)}, u32[]{:S(2)}, u32[]{:S(2)}) collective-permute-start(f32[384,64]{0,1:T(8,128)S(1)} %slice_select_fusion.3), channel_id=1, source_target_pairs={{0,8},{1,9},{2,10},{3,11},{4,12},{5,13},{6,14},{7,15},{8,0},{9,1},... | collective-permute-start | bytes 294920 | tf_op jit(solution)/shard_map/ppermute | solution.py:59
  140.5 3.9 collective-permute-start.13
  145.7 4.9 %collective-permute-done.22 = f32[384,64]{0,1:T(8,128)S(1)} collective-permute-done((f32[384,64]{0,1:T(8,128)S(1)}, f32[384,64]{0,1:T(8,128)S(1)}, u32[]{:S(2)}, u32[]{:S(2)}) %collective-permute-start.22) | collective-permute-done | bytes 98336 | tf_op jit(solution)/shard_map/ppermute | solution.py:59
  150.7 4.0 collective-permute-start.23
  160.4 6.5 %collective-permute-start.16 = (bf16[64,384]{1,0:T(8,128)(2,1)S(1)}, bf16[64,384]{1,0:T(8,128)(2,1)S(1)}, u32[]{:S(2)}, u32[]{:S(2)}) collective-permute-start(bf16[64,384]{1,0:T(8,128)(2,1)S(1)} %pad_maximum_fusion.4), channel_id=1, source_target_pairs={{1,0},{2,1},{3,2},{4,3},{5,4},{6,5},{7,6},{8,7},{9,8},{10,9},{11,1... | collective-permute-start | bytes 147464 | tf_op jit(solution)/shard_map/ppermute | solution.py:15
  170.2 4.0 collective-permute-start.30
  175.9 3.6 collective-permute-start.31
  179.5 3.6 collective-permute-done.31
  185.1 3.9 collective-permute-start.26
  190.4 4.6 %collective-permute-start.33 = (bf16[384,64]{1,0:T(8,128)(2,1)S(1)}, bf16[384,64]{1,0:T(8,128)(2,1)S(1)}, u32[]{:S(2)}, u32[]{:S(2)}) collective-permute-start(bf16[384,64]{1,0:T(8,128)(2,1)S(1)} %maximum_select_fusion.17), channel_id=1, source_target_pairs={{0,128},{16,144},{32,160},{48,176},{64,192},{80,208},{96,224},{112... | collective-permute-start | bytes 147464 | tf_op jit(solution)/shard_map/ppermute | solution.py:41
  195.1 9.9 %collective-permute-start.28 = (bf16[64,384]{1,0:T(8,128)(2,1)S(1)}, bf16[64,384]{1,0:T(8,128)(2,1)S(1)}, u32[]{:S(2)}, u32[]{:S(2)}) collective-permute-start(bf16[64,384]{1,0:T(8,128)(2,1)S(1)} %pad_maximum_fusion.5), channel_id=1, source_target_pairs={{0,1},{1,2},{2,3},{3,4},{4,5},{5,6},{6,7},{7,8},{8,9},{9,10},{10,1... | collective-permute-start | bytes 147464 | tf_op jit(solution)/shard_map/ppermute | solution.py:15
  206.9 3.9 collective-permute-done.29
  211.7 1.9 collective-permute-start.43
  213.7 6.8 %collective-permute-start.34 = (bf16[768,64]{1,0:T(8,128)(2,1)S(1)}, bf16[768,64]{1,0:T(8,128)(2,1)S(1)}, u32[]{:S(2)}, u32[]{:S(2)}) collective-permute-start(bf16[768,64]{1,0:T(8,128)(2,1)S(1)} %maximum_select_fusion.12), channel_id=1, source_target_pairs={{0,256},{16,272},{32,288},{48,304},{64,320},{80,336},{96,352},{112... | collective-permute-start | bytes 294920 | tf_op jit(solution)/shard_map/ppermute | solution.py:41
  220.5 4.2 collective-permute-start.44
  225.0 2.7 collective-permute-done.44
  227.7 3.6 collective-permute-start.45
  231.9 2.6 collective-permute-start.35
  236.5 10.7 %collective-permute-done.35 = f32[384,64]{0,1:T(8,128)S(1)} collective-permute-done((f32[384,64]{0,1:T(8,128)S(1)}, f32[384,64]{0,1:T(8,128)S(1)}, u32[]{:S(2)}, u32[]{:S(2)}) %collective-permute-start.35) | collective-permute-done | bytes 98336 | tf_op jit(solution)/shard_map/ppermute | solution.py:59
  247.3 3.6 collective-permute-start.36
  251.0 6.3 %collective-permute-start.47 = (bf16[768,64]{1,0:T(8,128)(2,1)S(1)}, bf16[768,64]{1,0:T(8,128)(2,1)S(1)}, u32[]{:S(2)}, u32[]{:S(2)}) collective-permute-start(bf16[768,64]{1,0:T(8,128)(2,1)S(1)} %maximum_select_fusion.13), channel_id=1, source_target_pairs={{0,256},{16,272},{32,288},{48,304},{64,320},{80,336},{96,352},{112... | collective-permute-start | bytes 294920 | tf_op jit(solution)/shard_map/ppermute | solution.py:41
  257.4 5.4 %collective-permute-start.37 = (f32[96,64]{0,1:T(8,128)S(1)}, f32[96,64]{0,1:T(8,128)S(1)}, u32[]{:S(2)}, u32[]{:S(2)}) collective-permute-start(f32[96,64]{0,1:T(8,128)S(1)} %slice_select_fusion.15), channel_id=1, source_target_pairs={{0,2},{1,3},{2,0},{3,1},{4,6},{5,7},{6,4},{7,5},{8,10},{9,11},{10,... | collective-permute-start | bytes 73736 | tf_op jit(solution)/shard_map/ppermute | solution.py:59
  262.8 6.2 %collective-permute-done.47 = bf16[768,64]{1,0:T(8,128)(2,1)S(1)} collective-permute-done((bf16[768,64]{1,0:T(8,128)(2,1)S(1)}, bf16[768,64]{1,0:T(8,128)(2,1)S(1)}, u32[]{:S(2)}, u32[]{:S(2)}) %collective-permute-start.47) | collective-permute-done | bytes 98336 | tf_op jit(solution)/shard_map/ppermute | solution.py:41
  269.7 11.7 %collective-permute-start.38 = (f32[48,64]{0,1:T(8,128)S(1)}, f32[48,64]{0,1:T(8,128)S(1)}, u32[]{:S(2)}, u32[]{:S(2)}) collective-permute-start(f32[48,64]{0,1:T(8,128)S(1)} %slice_select_fusion.14), channel_id=1, source_target_pairs={{0,1},{1,0},{2,3},{3,2},{4,5},{5,4},{6,7},{7,6},{8,9},{9,8},{10,11... | collective-permute-start | bytes 36872 | tf_op jit(solution)/shard_map/ppermute | solution.py:59
  281.3 9.5 %collective-permute-start.48 = (f32[384,64]{0,1:T(8,128)S(1)}, f32[384,64]{0,1:T(8,128)S(1)}, u32[]{:S(2)}, u32[]{:S(2)}) collective-permute-start(f32[384,64]{0,1:T(8,128)S(1)} %slice_select_fusion.1), channel_id=1, source_target_pairs={{0,8},{1,9},{2,10},{3,11},{4,12},{5,13},{6,14},{7,15},{8,0},{9,1},... | collective-permute-start | bytes 294920 | tf_op jit(solution)/shard_map/ppermute | solution.py:59
  291.5 2.4 collective-permute-start.39
  295.2 7.8 %collective-permute-done.48 = f32[384,64]{0,1:T(8,128)S(1)} collective-permute-done((f32[384,64]{0,1:T(8,128)S(1)}, f32[384,64]{0,1:T(8,128)S(1)}, u32[]{:S(2)}, u32[]{:S(2)}) %collective-permute-start.48) | collective-permute-done | bytes 98336 | tf_op jit(solution)/shard_map/ppermute | solution.py:59
  303.1 2.5 collective-permute-start.49
  307.7 3.3 collective-permute-done.49
  313.1 7.4 %collective-permute-start.42 = (bf16[64,384]{1,0:T(8,128)(2,1)S(1)}, bf16[64,384]{1,0:T(8,128)(2,1)S(1)}, u32[]{:S(2)}, u32[]{:S(2)}) collective-permute-start(bf16[64,384]{1,0:T(8,128)(2,1)S(1)} %pad_maximum_fusion.8), channel_id=1, source_target_pairs={{1,0},{2,1},{3,2},{4,3},{5,4},{6,5},{7,6},{8,7},{9,8},{10,9},{11,1... | collective-permute-start | bytes 147464 | tf_op jit(solution)/shard_map/ppermute | solution.py:15
  323.8 4.0 collective-permute-start.56
  329.5 2.1 collective-permute-start.57
  331.6 5.1 %collective-permute-done.57 = bf16[96,64]{1,0:T(8,128)(2,1)S(1)} collective-permute-done((bf16[96,64]{1,0:T(8,128)(2,1)S(1)}, bf16[96,64]{1,0:T(8,128)(2,1)S(1)}, u32[]{:S(2)}, u32[]{:S(2)}) %collective-permute-start.57) | collective-permute-done | bytes 12320 | tf_op jit(solution)/shard_map/ppermute | solution.py:41
  338.7 3.9 collective-permute-start.52
  343.9 4.6 %collective-permute-start.59 = (bf16[384,64]{1,0:T(8,128)(2,1)S(1)}, bf16[384,64]{1,0:T(8,128)(2,1)S(1)}, u32[]{:S(2)}, u32[]{:S(2)}) collective-permute-start(bf16[384,64]{1,0:T(8,128)(2,1)S(1)} %maximum_select_fusion.19), channel_id=1, source_target_pairs={{0,128},{16,144},{32,160},{48,176},{64,192},{80,208},{96,224},{112... | collective-permute-start | bytes 147464 | tf_op jit(solution)/shard_map/ppermute | solution.py:41
  348.6 9.9 %collective-permute-start.54 = (bf16[64,384]{1,0:T(8,128)(2,1)S(1)}, bf16[64,384]{1,0:T(8,128)(2,1)S(1)}, u32[]{:S(2)}, u32[]{:S(2)}) collective-permute-start(bf16[64,384]{1,0:T(8,128)(2,1)S(1)} %pad_maximum_fusion.9), channel_id=1, source_target_pairs={{0,1},{1,2},{2,3},{3,4},{4,5},{5,6},{6,7},{7,8},{8,9},{9,10},{10,1... | collective-permute-start | bytes 147464 | tf_op jit(solution)/shard_map/ppermute | solution.py:15
  360.5 4.9 %collective-permute-start.60 = (bf16[768,64]{1,0:T(8,128)(2,1)S(1)}, bf16[768,64]{1,0:T(8,128)(2,1)S(1)}, u32[]{:S(2)}, u32[]{:S(2)}) collective-permute-start(bf16[768,64]{1,0:T(8,128)(2,1)S(1)} %maximum_select_fusion.14), channel_id=1, source_target_pairs={{0,256},{16,272},{32,288},{48,304},{64,320},{80,336},{96,352},{112... | collective-permute-start | bytes 294920 | tf_op jit(solution)/shard_map/ppermute | solution.py:41
  365.5 23.1 %collective-permute-done.60 = bf16[768,64]{1,0:T(8,128)(2,1)S(1)} collective-permute-done((bf16[768,64]{1,0:T(8,128)(2,1)S(1)}, bf16[768,64]{1,0:T(8,128)(2,1)S(1)}, u32[]{:S(2)}, u32[]{:S(2)}) %collective-permute-start.60) | collective-permute-done | bytes 98336 | tf_op jit(solution)/shard_map/ppermute | solution.py:41
  391.1 13.4 %collective-permute-done.61 = f32[384,64]{0,1:T(8,128)S(1)} collective-permute-done((f32[384,64]{0,1:T(8,128)S(1)}, f32[384,64]{0,1:T(8,128)S(1)}, u32[]{:S(2)}, u32[]{:S(2)}) %collective-permute-start.61) | collective-permute-done | bytes 98336 | tf_op jit(solution)/shard_map/ppermute | solution.py:59
  406.5 5.7 %collective-permute-done.62 = f32[192,64]{0,1:T(8,128)S(1)} collective-permute-done((f32[192,64]{0,1:T(8,128)S(1)}, f32[192,64]{0,1:T(8,128)S(1)}, u32[]{:S(2)}, u32[]{:S(2)}) %collective-permute-start.62) | collective-permute-done | bytes 49184 | tf_op jit(solution)/shard_map/ppermute | solution.py:59
  414.3 3.9 collective-permute-done.63
  422.3 3.6 fusion.23
  425.9 2.0 fusion.51
  (272 shorter events, 73.8 us)
Async XLA Ops:
  1.2 16.1 %collective-permute-start.4 = (bf16[48,64]{1,0:T(8,128)(2,1)S(1)}, bf16[48,64]{1,0:T(8,128)(2,1)S(1)}, u32[]{:S(2)}, u32[]{:S(2)}) collective-permute-start(bf16[48,64]{1,0:T(8,128)(2,1)S(1)} %convolution_convert_fusion.4), channel_id=1, source_target_pairs={{0,16},{16,0},{32,48},{48,32},{64,80},{80,64},{96,112},{112,96},{1... | collective-permute-start | bytes 18440 | tf_op jit(solution)/shard_map/ppermute | solution.py:41
  11.6 29.9 %collective-permute-start = (bf16[64,384]{1,0:T(8,128)(2,1)}, bf16[64,384]{1,0:T(8,128)(2,1)}, u32[]{:S(2)}, u32[]{:S(2)}) collective-permute-start(bf16[64,384]{1,0:T(8,128)(2,1)} %get-tuple-element.27), channel_id=1, source_target_pairs={{0,16},{16,32},{32,48},{48,64},{64,80},{80,96},{96,112},{112,128},... | collective-permute-start | bytes 147464 | tf_op jit(solution)/shard_map/ppermute | solution.py:15
  14.5 27.7 %collective-permute-start.1 = (bf16[64,384]{1,0:T(8,128)(2,1)}, bf16[64,384]{1,0:T(8,128)(2,1)}, u32[]{:S(2)}, u32[]{:S(2)}) collective-permute-start(bf16[64,384]{1,0:T(8,128)(2,1)} %get-tuple-element.28), channel_id=1, source_target_pairs={{16,0},{32,16},{48,32},{64,48},{80,64},{96,80},{112,96},{128,112},... | collective-permute-start | bytes 147464 | tf_op jit(solution)/shard_map/ppermute | solution.py:15
  17.4 8.2 %collective-permute-start.5 = (bf16[96,64]{1,0:T(8,128)(2,1)S(1)}, bf16[96,64]{1,0:T(8,128)(2,1)S(1)}, u32[]{:S(2)}, u32[]{:S(2)}) collective-permute-start(bf16[96,64]{1,0:T(8,128)(2,1)S(1)} %maximum_select_fusion.25), channel_id=1, source_target_pairs={{0,32},{16,48},{32,0},{48,16},{64,96},{80,112},{96,64},{112,80},{1... | collective-permute-start | bytes 36872 | tf_op jit(solution)/shard_map/ppermute | solution.py:41
  25.6 9.7 %collective-permute-start.6 = (bf16[192,64]{1,0:T(8,128)(2,1)S(1)}, bf16[192,64]{1,0:T(8,128)(2,1)}, u32[]{:S(2)}, u32[]{:S(2)}) collective-permute-start(bf16[192,64]{1,0:T(8,128)(2,1)S(1)} %maximum_select_fusion.20), channel_id=1, source_target_pairs={{0,64},{16,80},{32,96},{48,112},{64,0},{80,16},{96,32},{112,48},{1... | collective-permute-start | bytes 73736 | tf_op jit(solution)/shard_map/ppermute | solution.py:41
  36.3 26.8 %collective-permute-start.7 = (bf16[384,64]{1,0:T(8,128)(2,1)S(1)}, bf16[384,64]{1,0:T(8,128)(2,1)S(1)}, u32[]{:S(2)}, u32[]{:S(2)}) collective-permute-start(bf16[384,64]{1,0:T(8,128)(2,1)S(1)} %maximum_select_fusion.15), channel_id=1, source_target_pairs={{0,128},{16,144},{32,160},{48,176},{64,192},{80,208},{96,224},{112... | collective-permute-start | bytes 147464 | tf_op jit(solution)/shard_map/ppermute | solution.py:41
  43.0 5.6 %collective-permute-start.2 = (bf16[64,384]{1,0:T(8,128)(2,1)S(1)}, bf16[64,384]{1,0:T(8,128)(2,1)S(1)}, u32[]{:S(2)}, u32[]{:S(2)}) collective-permute-start(bf16[64,384]{1,0:T(8,128)(2,1)S(1)} %pad_maximum_fusion.1), channel_id=1, source_target_pairs={{0,1},{1,2},{2,3},{3,4},{4,5},{5,6},{6,7},{7,8},{8,9},{9,10},{10,1... | collective-permute-start | bytes 147464 | tf_op jit(solution)/shard_map/ppermute | solution.py:15
  45.0 13.8 %collective-permute-start.3 = (bf16[64,384]{1,0:T(8,128)(2,1)S(1)}, bf16[64,384]{1,0:T(8,128)(2,1)S(1)}, u32[]{:S(2)}, u32[]{:S(2)}) collective-permute-start(bf16[64,384]{1,0:T(8,128)(2,1)S(1)} %pad_maximum_fusion.2), channel_id=1, source_target_pairs={{1,0},{2,1},{3,2},{4,3},{5,4},{6,5},{7,6},{8,7},{9,8},{10,9},{11,1... | collective-permute-start | bytes 147464 | tf_op jit(solution)/shard_map/ppermute | solution.py:15
  61.2 6.3 %collective-permute-start.17 = (bf16[48,64]{1,0:T(8,128)(2,1)S(1)}, bf16[48,64]{1,0:T(8,128)(2,1)S(1)}, u32[]{:S(2)}, u32[]{:S(2)}) collective-permute-start(bf16[48,64]{1,0:T(8,128)(2,1)S(1)} %fusion.76), channel_id=1, source_target_pairs={{0,16},{16,0},{32,48},{48,32},{64,80},{80,64},{96,112},{112,96},{1... | collective-permute-start | bytes 18440 | tf_op jit(solution)/shard_map/ppermute | solution.py:41
  63.2 17.9 %collective-permute-start.8 = (bf16[768,64]{1,0:T(8,128)(2,1)S(1)}, bf16[768,64]{1,0:T(8,128)(2,1)S(1)}, u32[]{:S(2)}, u32[]{:S(2)}) collective-permute-start(bf16[768,64]{1,0:T(8,128)(2,1)S(1)} %maximum_select_fusion.10), channel_id=1, source_target_pairs={{0,256},{16,272},{32,288},{48,304},{64,320},{80,336},{96,352},{112... | collective-permute-start | bytes 294920 | tf_op jit(solution)/shard_map/ppermute | solution.py:41
  67.6 7.2 %collective-permute-start.18 = (bf16[96,64]{1,0:T(8,128)(2,1)S(1)}, bf16[96,64]{1,0:T(8,128)(2,1)S(1)}, u32[]{:S(2)}, u32[]{:S(2)}) collective-permute-start(bf16[96,64]{1,0:T(8,128)(2,1)S(1)} %maximum_select_fusion.26), channel_id=1, source_target_pairs={{0,32},{16,48},{32,0},{48,16},{64,96},{80,112},{96,64},{112,80},{1... | collective-permute-start | bytes 36872 | tf_op jit(solution)/shard_map/ppermute | solution.py:41
  74.8 16.9 %collective-permute-start.19 = (bf16[192,64]{1,0:T(8,128)(2,1)S(1)}, bf16[192,64]{1,0:T(8,128)(2,1)S(1)}, u32[]{:S(2)}, u32[]{:S(2)}) collective-permute-start(bf16[192,64]{1,0:T(8,128)(2,1)S(1)} %maximum_select_fusion.21), channel_id=1, source_target_pairs={{0,64},{16,80},{32,96},{48,112},{64,0},{80,16},{96,32},{112,48},{1... | collective-permute-start | bytes 73736 | tf_op jit(solution)/shard_map/ppermute | solution.py:41
  81.7 17.5 %collective-permute-start.9 = (f32[384,64]{0,1:T(8,128)S(1)}, f32[384,64]{0,1:T(8,128)S(1)}, u32[]{:S(2)}, u32[]{:S(2)}) collective-permute-start(f32[384,64]{0,1:T(8,128)S(1)} %slice_select_fusion.4), channel_id=1, source_target_pairs={{0,8},{1,9},{2,10},{3,11},{4,12},{5,13},{6,14},{7,15},{8,0},{9,1},... | collective-permute-start | bytes 294920 | tf_op jit(solution)/shard_map/ppermute | solution.py:59
  91.7 16.5 %collective-permute-start.20 = (bf16[384,64]{1,0:T(8,128)(2,1)S(1)}, bf16[384,64]{1,0:T(8,128)(2,1)S(1)}, u32[]{:S(2)}, u32[]{:S(2)}) collective-permute-start(bf16[384,64]{1,0:T(8,128)(2,1)S(1)} %maximum_select_fusion.16), channel_id=1, source_target_pairs={{0,128},{16,144},{32,160},{48,176},{64,192},{80,208},{96,224},{112... | collective-permute-start | bytes 147464 | tf_op jit(solution)/shard_map/ppermute | solution.py:41
  99.3 11.1 %collective-permute-start.10 = (f32[192,64]{0,1:T(8,128)S(1)}, f32[192,64]{0,1:T(8,128)S(1)}, u32[]{:S(2)}, u32[]{:S(2)}) collective-permute-start(f32[192,64]{0,1:T(8,128)S(1)} %slice_select_fusion.9), channel_id=1, source_target_pairs={{0,4},{1,5},{2,6},{3,7},{4,0},{5,1},{6,2},{7,3},{8,12},{9,13},{10,... | collective-permute-start | bytes 147464 | tf_op jit(solution)/shard_map/ppermute | solution.py:59
  108.3 21.4 %collective-permute-start.21 = (bf16[768,64]{1,0:T(8,128)(2,1)S(1)}, bf16[768,64]{1,0:T(8,128)(2,1)S(1)}, u32[]{:S(2)}, u32[]{:S(2)}) collective-permute-start(bf16[768,64]{1,0:T(8,128)(2,1)S(1)} %maximum_select_fusion.11), channel_id=1, source_target_pairs={{0,256},{16,272},{32,288},{48,304},{64,320},{80,336},{96,352},{112... | collective-permute-start | bytes 294920 | tf_op jit(solution)/shard_map/ppermute | solution.py:41
  110.6 19.6 %collective-permute-start.11 = (f32[96,64]{0,1:T(8,128)S(1)}, f32[96,64]{0,1:T(8,128)S(1)}, u32[]{:S(2)}, u32[]{:S(2)}) collective-permute-start(f32[96,64]{0,1:T(8,128)S(1)} %slice_select_fusion.19), channel_id=1, source_target_pairs={{0,2},{1,3},{2,0},{3,1},{4,6},{5,7},{6,4},{7,5},{8,10},{9,11},{10,... | collective-permute-start | bytes 73736 | tf_op jit(solution)/shard_map/ppermute | solution.py:59
  130.4 9.4 %collective-permute-start.12 = (f32[48,64]{0,1:T(8,128)S(1)}, f32[48,64]{0,1:T(8,128)S(1)}, u32[]{:S(2)}, u32[]{:S(2)}) collective-permute-start(f32[48,64]{0,1:T(8,128)S(1)} %slice_select_fusion.18), channel_id=1, source_target_pairs={{0,1},{1,0},{2,3},{3,2},{4,5},{5,4},{6,7},{7,6},{8,9},{9,8},{10,11... | collective-permute-start | bytes 36872 | tf_op jit(solution)/shard_map/ppermute | solution.py:59
  132.4 18.1 %collective-permute-start.22 = (f32[384,64]{0,1:T(8,128)S(1)}, f32[384,64]{0,1:T(8,128)S(1)}, u32[]{:S(2)}, u32[]{:S(2)}) collective-permute-start(f32[384,64]{0,1:T(8,128)S(1)} %slice_select_fusion.3), channel_id=1, source_target_pairs={{0,8},{1,9},{2,10},{3,11},{4,12},{5,13},{6,14},{7,15},{8,0},{9,1},... | collective-permute-start | bytes 294920 | tf_op jit(solution)/shard_map/ppermute | solution.py:59
  140.5 14.2 %collective-permute-start.13 = (bf16[64,384]{1,0:T(8,128)(2,1)S(1)}, bf16[64,384]{1,0:T(8,128)(2,1)S(1)}, u32[]{:S(2)}, u32[]{:S(2)}) collective-permute-start(bf16[64,384]{1,0:T(8,128)(2,1)S(1)} %get-tuple-element.19), channel_id=1, source_target_pairs={{0,16},{16,32},{32,48},{48,64},{64,80},{80,96},{96,112},{112,128},... | collective-permute-start | bytes 147464 | tf_op jit(solution)/shard_map/ppermute | solution.py:15
  144.4 10.3 %collective-permute-start.14 = (bf16[64,384]{1,0:T(8,128)(2,1)S(1)}, bf16[64,384]{1,0:T(8,128)(2,1)S(1)}, u32[]{:S(2)}, u32[]{:S(2)}) collective-permute-start(bf16[64,384]{1,0:T(8,128)(2,1)S(1)} %get-tuple-element.20), channel_id=1, source_target_pairs={{16,0},{32,16},{48,32},{64,48},{80,64},{96,80},{112,96},{128,112},... | collective-permute-start | bytes 147464 | tf_op jit(solution)/shard_map/ppermute | solution.py:15
  150.7 7.7 %collective-permute-start.23 = (f32[192,64]{0,1:T(8,128)S(1)}, f32[192,64]{0,1:T(8,128)S(1)}, u32[]{:S(2)}, u32[]{:S(2)}) collective-permute-start(f32[192,64]{0,1:T(8,128)S(1)} %slice_select_fusion.8), channel_id=1, source_target_pairs={{0,4},{1,5},{2,6},{3,7},{4,0},{5,1},{6,2},{7,3},{8,12},{9,13},{10,... | collective-permute-start | bytes 147464 | tf_op jit(solution)/shard_map/ppermute | solution.py:59
  154.7 14.3 %collective-permute-start.15 = (bf16[64,384]{1,0:T(8,128)(2,1)S(1)}, bf16[64,384]{1,0:T(8,128)(2,1)S(1)}, u32[]{:S(2)}, u32[]{:S(2)}) collective-permute-start(bf16[64,384]{1,0:T(8,128)(2,1)S(1)} %pad_maximum_fusion.3), channel_id=1, source_target_pairs={{0,1},{1,2},{2,3},{3,4},{4,5},{5,6},{6,7},{7,8},{8,9},{9,10},{10,1... | collective-permute-start | bytes 147464 | tf_op jit(solution)/shard_map/ppermute | solution.py:15
  158.5 8.4 %collective-permute-start.24 = (f32[96,64]{0,1:T(8,128)S(1)}, f32[96,64]{0,1:T(8,128)S(1)}, u32[]{:S(2)}, u32[]{:S(2)}) collective-permute-start(f32[96,64]{0,1:T(8,128)S(1)} %slice_select_fusion.17), channel_id=1, source_target_pairs={{0,2},{1,3},{2,0},{3,1},{4,6},{5,7},{6,4},{7,5},{8,10},{9,11},{10,... | collective-permute-start | bytes 73736 | tf_op jit(solution)/shard_map/ppermute | solution.py:59
  160.4 8.6 %collective-permute-start.16 = (bf16[64,384]{1,0:T(8,128)(2,1)S(1)}, bf16[64,384]{1,0:T(8,128)(2,1)S(1)}, u32[]{:S(2)}, u32[]{:S(2)}) collective-permute-start(bf16[64,384]{1,0:T(8,128)(2,1)S(1)} %pad_maximum_fusion.4), channel_id=1, source_target_pairs={{1,0},{2,1},{3,2},{4,3},{5,4},{6,5},{7,6},{8,7},{9,8},{10,9},{11,1... | collective-permute-start | bytes 147464 | tf_op jit(solution)/shard_map/ppermute | solution.py:15
  167.1 7.1 %collective-permute-start.25 = (f32[48,64]{0,1:T(8,128)S(1)}, f32[48,64]{0,1:T(8,128)S(1)}, u32[]{:S(2)}, u32[]{:S(2)}) collective-permute-start(f32[48,64]{0,1:T(8,128)S(1)} %slice_select_fusion.16), channel_id=1, source_target_pairs={{0,1},{1,0},{2,3},{3,2},{4,5},{5,4},{6,7},{7,6},{8,9},{9,8},{10,11... | collective-permute-start | bytes 36872 | tf_op jit(solution)/shard_map/ppermute | solution.py:59
  170.2 5.7 %collective-permute-start.30 = (bf16[48,64]{1,0:T(8,128)(2,1)S(1)}, bf16[48,64]{1,0:T(8,128)(2,1)S(1)}, u32[]{:S(2)}, u32[]{:S(2)}) collective-permute-start(bf16[48,64]{1,0:T(8,128)(2,1)S(1)} %fusion.77), channel_id=1, source_target_pairs={{0,16},{16,0},{32,48},{48,32},{64,80},{80,64},{96,112},{112,96},{1... | collective-permute-start | bytes 18440 | tf_op jit(solution)/shard_map/ppermute | solution.py:41
  175.9 7.2 %collective-permute-start.31 = (bf16[96,64]{1,0:T(8,128)(2,1)S(1)}, bf16[96,64]{1,0:T(8,128)(2,1)S(1)}, u32[]{:S(2)}, u32[]{:S(2)}) collective-permute-start(bf16[96,64]{1,0:T(8,128)(2,1)S(1)} %maximum_select_fusion.27), channel_id=1, source_target_pairs={{0,32},{16,48},{32,0},{48,16},{64,96},{80,112},{96,64},{112,80},{1... | collective-permute-start | bytes 36872 | tf_op jit(solution)/shard_map/ppermute | solution.py:41
  183.2 7.2 %collective-permute-start.32 = (bf16[192,64]{1,0:T(8,128)(2,1)S(1)}, bf16[192,64]{1,0:T(8,128)(2,1)S(1)}, u32[]{:S(2)}, u32[]{:S(2)}) collective-permute-start(bf16[192,64]{1,0:T(8,128)(2,1)S(1)} %maximum_select_fusion.22), channel_id=1, source_target_pairs={{0,64},{16,80},{32,96},{48,112},{64,0},{80,16},{96,32},{112,48},{1... | collective-permute-start | bytes 73736 | tf_op jit(solution)/shard_map/ppermute | solution.py:41
  185.1 9.9 %collective-permute-start.26 = (bf16[64,384]{1,0:T(8,128)(2,1)S(1)}, bf16[64,384]{1,0:T(8,128)(2,1)S(1)}, u32[]{:S(2)}, u32[]{:S(2)}) collective-permute-start(bf16[64,384]{1,0:T(8,128)(2,1)S(1)} %get-tuple-element.15), channel_id=1, source_target_pairs={{0,16},{16,32},{32,48},{48,64},{64,80},{80,96},{96,112},{112,128},... | collective-permute-start | bytes 147464 | tf_op jit(solution)/shard_map/ppermute | solution.py:15
  189.0 6.0 %collective-permute-start.27 = (bf16[64,384]{1,0:T(8,128)(2,1)S(1)}, bf16[64,384]{1,0:T(8,128)(2,1)S(1)}, u32[]{:S(2)}, u32[]{:S(2)}) collective-permute-start(bf16[64,384]{1,0:T(8,128)(2,1)S(1)} %get-tuple-element.16), channel_id=1, source_target_pairs={{16,0},{32,16},{48,32},{64,48},{80,64},{96,80},{112,96},{128,112},... | collective-permute-start | bytes 147464 | tf_op jit(solution)/shard_map/ppermute | solution.py:15
  190.4 23.2 %collective-permute-start.33 = (bf16[384,64]{1,0:T(8,128)(2,1)S(1)}, bf16[384,64]{1,0:T(8,128)(2,1)S(1)}, u32[]{:S(2)}, u32[]{:S(2)}) collective-permute-start(bf16[384,64]{1,0:T(8,128)(2,1)S(1)} %maximum_select_fusion.17), channel_id=1, source_target_pairs={{0,128},{16,144},{32,160},{48,176},{64,192},{80,208},{96,224},{112... | collective-permute-start | bytes 147464 | tf_op jit(solution)/shard_map/ppermute | solution.py:41
  195.1 11.8 %collective-permute-start.28 = (bf16[64,384]{1,0:T(8,128)(2,1)S(1)}, bf16[64,384]{1,0:T(8,128)(2,1)S(1)}, u32[]{:S(2)}, u32[]{:S(2)}) collective-permute-start(bf16[64,384]{1,0:T(8,128)(2,1)S(1)} %pad_maximum_fusion.5), channel_id=1, source_target_pairs={{0,1},{1,2},{2,3},{3,4},{4,5},{5,6},{6,7},{7,8},{8,9},{9,10},{10,1... | collective-permute-start | bytes 147464 | tf_op jit(solution)/shard_map/ppermute | solution.py:15
  205.0 5.9 %collective-permute-start.29 = (bf16[64,384]{1,0:T(8,128)(2,1)S(1)}, bf16[64,384]{1,0:T(8,128)(2,1)S(1)}, u32[]{:S(2)}, u32[]{:S(2)}) collective-permute-start(bf16[64,384]{1,0:T(8,128)(2,1)S(1)} %pad_maximum_fusion.6), channel_id=1, source_target_pairs={{1,0},{2,1},{3,2},{4,3},{5,4},{6,5},{7,6},{8,7},{9,8},{10,9},{11,1... | collective-permute-start | bytes 147464 | tf_op jit(solution)/shard_map/ppermute | solution.py:15
  211.7 8.8 %collective-permute-start.43 = (bf16[48,64]{1,0:T(8,128)(2,1)S(1)}, bf16[48,64]{1,0:T(8,128)(2,1)S(1)}, u32[]{:S(2)}, u32[]{:S(2)}) collective-permute-start(bf16[48,64]{1,0:T(8,128)(2,1)S(1)} %fusion.78), channel_id=1, source_target_pairs={{0,16},{16,0},{32,48},{48,32},{64,80},{80,64},{96,112},{112,96},{1... | collective-permute-start | bytes 18440 | tf_op jit(solution)/shard_map/ppermute | solution.py:41
  213.7 17.7 %collective-permute-start.34 = (bf16[768,64]{1,0:T(8,128)(2,1)S(1)}, bf16[768,64]{1,0:T(8,128)(2,1)S(1)}, u32[]{:S(2)}, u32[]{:S(2)}) collective-permute-start(bf16[768,64]{1,0:T(8,128)(2,1)S(1)} %maximum_select_fusion.12), channel_id=1, source_target_pairs={{0,256},{16,272},{32,288},{48,304},{64,320},{80,336},{96,352},{112... | collective-permute-start | bytes 294920 | tf_op jit(solution)/shard_map/ppermute | solution.py:41
  220.5 7.2 %collective-permute-start.44 = (bf16[96,64]{1,0:T(8,128)(2,1)S(1)}, bf16[96,64]{1,0:T(8,128)(2,1)S(1)}, u32[]{:S(2)}, u32[]{:S(2)}) collective-permute-start(bf16[96,64]{1,0:T(8,128)(2,1)S(1)} %maximum_select_fusion.28), channel_id=1, source_target_pairs={{0,32},{16,48},{32,0},{48,16},{64,96},{80,112},{96,64},{112,80},{1... | collective-permute-start | bytes 36872 | tf_op jit(solution)/shard_map/ppermute | solution.py:41
  227.7 6.8 %collective-permute-start.45 = (bf16[192,64]{1,0:T(8,128)(2,1)S(1)}, bf16[192,64]{1,0:T(8,128)(2,1)S(1)}, u32[]{:S(2)}, u32[]{:S(2)}) collective-permute-start(bf16[192,64]{1,0:T(8,128)(2,1)S(1)} %maximum_select_fusion.23), channel_id=1, source_target_pairs={{0,64},{16,80},{32,96},{48,112},{64,0},{80,16},{96,32},{112,48},{1... | collective-permute-start | bytes 73736 | tf_op jit(solution)/shard_map/ppermute | solution.py:41
  231.9 15.3 %collective-permute-start.35 = (f32[384,64]{0,1:T(8,128)S(1)}, f32[384,64]{0,1:T(8,128)S(1)}, u32[]{:S(2)}, u32[]{:S(2)}) collective-permute-start(f32[384,64]{0,1:T(8,128)S(1)} %slice_select_fusion.2), channel_id=1, source_target_pairs={{0,8},{1,9},{2,10},{3,11},{4,12},{5,13},{6,14},{7,15},{8,0},{9,1},... | collective-permute-start | bytes 294920 | tf_op jit(solution)/shard_map/ppermute | solution.py:59
  234.5 16.3 %collective-permute-start.46 = (bf16[384,64]{1,0:T(8,128)(2,1)S(1)}, bf16[384,64]{1,0:T(8,128)(2,1)S(1)}, u32[]{:S(2)}, u32[]{:S(2)}) collective-permute-start(bf16[384,64]{1,0:T(8,128)(2,1)S(1)} %maximum_select_fusion.18), channel_id=1, source_target_pairs={{0,128},{16,144},{32,160},{48,176},{64,192},{80,208},{96,224},{112... | collective-permute-start | bytes 147464 | tf_op jit(solution)/shard_map/ppermute | solution.py:41
  247.3 10.0 %collective-permute-start.36 = (f32[192,64]{0,1:T(8,128)S(1)}, f32[192,64]{0,1:T(8,128)S(1)}, u32[]{:S(2)}, u32[]{:S(2)}) collective-permute-start(f32[192,64]{0,1:T(8,128)S(1)} %slice_select_fusion.7), channel_id=1, source_target_pairs={{0,4},{1,5},{2,6},{3,7},{4,0},{5,1},{6,2},{7,3},{8,12},{9,13},{10,... | collective-permute-start | bytes 147464 | tf_op jit(solution)/shard_map/ppermute | solution.py:59
  251.0 18.0 %collective-permute-start.47 = (bf16[768,64]{1,0:T(8,128)(2,1)S(1)}, bf16[768,64]{1,0:T(8,128)(2,1)S(1)}, u32[]{:S(2)}, u32[]{:S(2)}) collective-permute-start(bf16[768,64]{1,0:T(8,128)(2,1)S(1)} %maximum_select_fusion.13), channel_id=1, source_target_pairs={{0,256},{16,272},{32,288},{48,304},{64,320},{80,336},{96,352},{112... | collective-permute-start | bytes 294920 | tf_op jit(solution)/shard_map/ppermute | solution.py:41
  257.4 12.1 %collective-permute-start.37 = (f32[96,64]{0,1:T(8,128)S(1)}, f32[96,64]{0,1:T(8,128)S(1)}, u32[]{:S(2)}, u32[]{:S(2)}) collective-permute-start(f32[96,64]{0,1:T(8,128)S(1)} %slice_select_fusion.15), channel_id=1, source_target_pairs={{0,2},{1,3},{2,0},{3,1},{4,6},{5,7},{6,4},{7,5},{8,10},{9,11},{10,... | collective-permute-start | bytes 73736 | tf_op jit(solution)/shard_map/ppermute | solution.py:59
  269.7 21.2 %collective-permute-start.38 = (f32[48,64]{0,1:T(8,128)S(1)}, f32[48,64]{0,1:T(8,128)S(1)}, u32[]{:S(2)}, u32[]{:S(2)}) collective-permute-start(f32[48,64]{0,1:T(8,128)S(1)} %slice_select_fusion.14), channel_id=1, source_target_pairs={{0,1},{1,0},{2,3},{3,2},{4,5},{5,4},{6,7},{7,6},{8,9},{9,8},{10,11... | collective-permute-start | bytes 36872 | tf_op jit(solution)/shard_map/ppermute | solution.py:59
  281.3 21.7 %collective-permute-start.48 = (f32[384,64]{0,1:T(8,128)S(1)}, f32[384,64]{0,1:T(8,128)S(1)}, u32[]{:S(2)}, u32[]{:S(2)}) collective-permute-start(f32[384,64]{0,1:T(8,128)S(1)} %slice_select_fusion.1), channel_id=1, source_target_pairs={{0,8},{1,9},{2,10},{3,11},{4,12},{5,13},{6,14},{7,15},{8,0},{9,1},... | collective-permute-start | bytes 294920 | tf_op jit(solution)/shard_map/ppermute | solution.py:59
  291.5 14.2 %collective-permute-start.39 = (bf16[64,384]{1,0:T(8,128)(2,1)S(1)}, bf16[64,384]{1,0:T(8,128)(2,1)S(1)}, u32[]{:S(2)}, u32[]{:S(2)}) collective-permute-start(bf16[64,384]{1,0:T(8,128)(2,1)S(1)} %get-tuple-element.11), channel_id=1, source_target_pairs={{0,16},{16,32},{32,48},{48,64},{64,80},{80,96},{96,112},{112,128},... | collective-permute-start | bytes 147464 | tf_op jit(solution)/shard_map/ppermute | solution.py:15
  293.9 11.8 %collective-permute-start.40 = (bf16[64,384]{1,0:T(8,128)(2,1)S(1)}, bf16[64,384]{1,0:T(8,128)(2,1)S(1)}, u32[]{:S(2)}, u32[]{:S(2)}) collective-permute-start(bf16[64,384]{1,0:T(8,128)(2,1)S(1)} %get-tuple-element.12), channel_id=1, source_target_pairs={{16,0},{32,16},{48,32},{64,48},{80,64},{96,80},{112,96},{128,112},... | collective-permute-start | bytes 147464 | tf_op jit(solution)/shard_map/ppermute | solution.py:15
  303.1 7.8 %collective-permute-start.49 = (f32[192,64]{0,1:T(8,128)S(1)}, f32[192,64]{0,1:T(8,128)S(1)}, u32[]{:S(2)}, u32[]{:S(2)}) collective-permute-start(f32[192,64]{0,1:T(8,128)S(1)} %slice_select_fusion.6), channel_id=1, source_target_pairs={{0,4},{1,5},{2,6},{3,7},{4,0},{5,1},{6,2},{7,3},{8,12},{9,13},{10,... | collective-permute-start | bytes 147464 | tf_op jit(solution)/shard_map/ppermute | solution.py:59
  305.8 16.9 %collective-permute-start.41 = (bf16[64,384]{1,0:T(8,128)(2,1)S(1)}, bf16[64,384]{1,0:T(8,128)(2,1)S(1)}, u32[]{:S(2)}, u32[]{:S(2)}) collective-permute-start(bf16[64,384]{1,0:T(8,128)(2,1)S(1)} %pad_maximum_fusion.7), channel_id=1, source_target_pairs={{0,1},{1,2},{2,3},{3,4},{4,5},{5,6},{6,7},{7,8},{8,9},{9,10},{10,1... | collective-permute-start | bytes 147464 | tf_op jit(solution)/shard_map/ppermute | solution.py:15
  311.1 9.4 %collective-permute-start.50 = (f32[96,64]{0,1:T(8,128)S(1)}, f32[96,64]{0,1:T(8,128)S(1)}, u32[]{:S(2)}, u32[]{:S(2)}) collective-permute-start(f32[96,64]{0,1:T(8,128)S(1)} %slice_select_fusion.13), channel_id=1, source_target_pairs={{0,2},{1,3},{2,0},{3,1},{4,6},{5,7},{6,4},{7,5},{8,10},{9,11},{10,... | collective-permute-start | bytes 73736 | tf_op jit(solution)/shard_map/ppermute | solution.py:59
  313.1 9.6 %collective-permute-start.42 = (bf16[64,384]{1,0:T(8,128)(2,1)S(1)}, bf16[64,384]{1,0:T(8,128)(2,1)S(1)}, u32[]{:S(2)}, u32[]{:S(2)}) collective-permute-start(bf16[64,384]{1,0:T(8,128)(2,1)S(1)} %pad_maximum_fusion.8), channel_id=1, source_target_pairs={{1,0},{2,1},{3,2},{4,3},{5,4},{6,5},{7,6},{8,7},{9,8},{10,9},{11,1... | collective-permute-start | bytes 147464 | tf_op jit(solution)/shard_map/ppermute | solution.py:15
  320.7 7.1 %collective-permute-start.51 = (f32[48,64]{0,1:T(8,128)S(1)}, f32[48,64]{0,1:T(8,128)S(1)}, u32[]{:S(2)}, u32[]{:S(2)}) collective-permute-start(f32[48,64]{0,1:T(8,128)S(1)} %slice_select_fusion.12), channel_id=1, source_target_pairs={{0,1},{1,0},{2,3},{3,2},{4,5},{5,4},{6,7},{7,6},{8,9},{9,8},{10,11... | collective-permute-start | bytes 36872 | tf_op jit(solution)/shard_map/ppermute | solution.py:59
  323.8 5.6 %collective-permute-start.56 = (bf16[48,64]{1,0:T(8,128)(2,1)S(1)}, bf16[48,64]{1,0:T(8,128)(2,1)S(1)}, u32[]{:S(2)}, u32[]{:S(2)}) collective-permute-start(bf16[48,64]{1,0:T(8,128)(2,1)S(1)} %fusion.79), channel_id=1, source_target_pairs={{0,16},{16,0},{32,48},{48,32},{64,80},{80,64},{96,112},{112,96},{1... | collective-permute-start | bytes 18440 | tf_op jit(solution)/shard_map/ppermute | solution.py:41
  329.5 7.2 %collective-permute-start.57 = (bf16[96,64]{1,0:T(8,128)(2,1)S(1)}, bf16[96,64]{1,0:T(8,128)(2,1)S(1)}, u32[]{:S(2)}, u32[]{:S(2)}) collective-permute-start(bf16[96,64]{1,0:T(8,128)(2,1)S(1)} %maximum_select_fusion.29), channel_id=1, source_target_pairs={{0,32},{16,48},{32,0},{48,16},{64,96},{80,112},{96,64},{112,80},{1... | collective-permute-start | bytes 36872 | tf_op jit(solution)/shard_map/ppermute | solution.py:41
  336.7 7.2 %collective-permute-start.58 = (bf16[192,64]{1,0:T(8,128)(2,1)S(1)}, bf16[192,64]{1,0:T(8,128)(2,1)S(1)}, u32[]{:S(2)}, u32[]{:S(2)}) collective-permute-start(bf16[192,64]{1,0:T(8,128)(2,1)S(1)} %maximum_select_fusion.24), channel_id=1, source_target_pairs={{0,64},{16,80},{32,96},{48,112},{64,0},{80,16},{96,32},{112,48},{1... | collective-permute-start | bytes 73736 | tf_op jit(solution)/shard_map/ppermute | solution.py:41
  338.7 9.9 %collective-permute-start.52 = (bf16[64,384]{1,0:T(8,128)(2,1)S(1)}, bf16[64,384]{1,0:T(8,128)(2,1)S(1)}, u32[]{:S(2)}, u32[]{:S(2)}) collective-permute-start(bf16[64,384]{1,0:T(8,128)(2,1)S(1)} %get-tuple-element.7), channel_id=1, source_target_pairs={{0,16},{16,32},{32,48},{48,64},{64,80},{80,96},{96,112},{112,128},... | collective-permute-start | bytes 147464 | tf_op jit(solution)/shard_map/ppermute | solution.py:15
  342.6 6.0 %collective-permute-start.53 = (bf16[64,384]{1,0:T(8,128)(2,1)S(1)}, bf16[64,384]{1,0:T(8,128)(2,1)S(1)}, u32[]{:S(2)}, u32[]{:S(2)}) collective-permute-start(bf16[64,384]{1,0:T(8,128)(2,1)S(1)} %get-tuple-element.8), channel_id=1, source_target_pairs={{16,0},{32,16},{48,32},{64,48},{80,64},{96,80},{112,96},{128,112},... | collective-permute-start | bytes 147464 | tf_op jit(solution)/shard_map/ppermute | solution.py:15
  343.9 16.5 %collective-permute-start.59 = (bf16[384,64]{1,0:T(8,128)(2,1)S(1)}, bf16[384,64]{1,0:T(8,128)(2,1)S(1)}, u32[]{:S(2)}, u32[]{:S(2)}) collective-permute-start(bf16[384,64]{1,0:T(8,128)(2,1)S(1)} %maximum_select_fusion.19), channel_id=1, source_target_pairs={{0,128},{16,144},{32,160},{48,176},{64,192},{80,208},{96,224},{112... | collective-permute-start | bytes 147464 | tf_op jit(solution)/shard_map/ppermute | solution.py:41
  348.6 16.8 %collective-permute-start.54 = (bf16[64,384]{1,0:T(8,128)(2,1)S(1)}, bf16[64,384]{1,0:T(8,128)(2,1)S(1)}, u32[]{:S(2)}, u32[]{:S(2)}) collective-permute-start(bf16[64,384]{1,0:T(8,128)(2,1)S(1)} %pad_maximum_fusion.9), channel_id=1, source_target_pairs={{0,1},{1,2},{2,3},{3,4},{4,5},{5,6},{6,7},{7,8},{8,9},{9,10},{10,1... | collective-permute-start | bytes 147464 | tf_op jit(solution)/shard_map/ppermute | solution.py:15
  358.5 32.5 %collective-permute-start.55 = (bf16[64,384]{1,0:T(8,128)(2,1)S(1)}, bf16[64,384]{1,0:T(8,128)(2,1)S(1)}, u32[]{:S(2)}, u32[]{:S(2)}) collective-permute-start(bf16[64,384]{1,0:T(8,128)(2,1)S(1)} %pad_maximum_fusion.10), channel_id=1, source_target_pairs={{1,0},{2,1},{3,2},{4,3},{5,4},{6,5},{7,6},{8,7},{9,8},{10,9},{11,1... | collective-permute-start | bytes 147464 | tf_op jit(solution)/shard_map/ppermute | solution.py:15
  360.5 28.1 %collective-permute-start.60 = (bf16[768,64]{1,0:T(8,128)(2,1)S(1)}, bf16[768,64]{1,0:T(8,128)(2,1)S(1)}, u32[]{:S(2)}, u32[]{:S(2)}) collective-permute-start(bf16[768,64]{1,0:T(8,128)(2,1)S(1)} %maximum_select_fusion.14), channel_id=1, source_target_pairs={{0,256},{16,272},{32,288},{48,304},{64,320},{80,336},{96,352},{112... | collective-permute-start | bytes 294920 | tf_op jit(solution)/shard_map/ppermute | solution.py:41
  389.1 15.3 %collective-permute-start.61 = (f32[384,64]{0,1:T(8,128)S(1)}, f32[384,64]{0,1:T(8,128)S(1)}, u32[]{:S(2)}, u32[]{:S(2)}) collective-permute-start(f32[384,64]{0,1:T(8,128)S(1)} %slice_select_fusion), channel_id=1, source_target_pairs={{0,8},{1,9},{2,10},{3,11},{4,12},{5,13},{6,14},{7,15},{8,0},{9,1},... | collective-permute-start | bytes 294920 | tf_op jit(solution)/shard_map/ppermute | solution.py:59
  404.6 7.7 %collective-permute-start.62 = (f32[192,64]{0,1:T(8,128)S(1)}, f32[192,64]{0,1:T(8,128)S(1)}, u32[]{:S(2)}, u32[]{:S(2)}) collective-permute-start(f32[192,64]{0,1:T(8,128)S(1)} %slice_select_fusion.5), channel_id=1, source_target_pairs={{0,4},{1,5},{2,6},{3,7},{4,0},{5,1},{6,2},{7,3},{8,12},{9,13},{10,... | collective-permute-start | bytes 147464 | tf_op jit(solution)/shard_map/ppermute | solution.py:59
  412.4 5.8 %collective-permute-start.63 = (f32[96,64]{0,1:T(8,128)S(1)}, f32[96,64]{0,1:T(8,128)S(1)}, u32[]{:S(2)}, u32[]{:S(2)}) collective-permute-start(f32[96,64]{0,1:T(8,128)S(1)} %slice_select_fusion.11), channel_id=1, source_target_pairs={{0,2},{1,3},{2,0},{3,1},{4,6},{5,7},{6,4},{7,5},{8,10},{9,11},{10,... | collective-permute-start | bytes 73736 | tf_op jit(solution)/shard_map/ppermute | solution.py:59
  (23 other events, 589.7 us)

commit v6 on v5

--- a/solution.py
+++ b/solution.py
@@ -36,7 +36,7 @@
     index = lax.axis_index("row")
     size = lax.axis_size("row")
     current = piece
-    for bit in range(size.bit_length() - 1):
+    for bit in range(size.bit_length() - 2, -1, -1):
         route = [(i, i ^ (1 << bit)) for i in range(size)]
         other = lax.ppermute(current, "row", route)
         high = ((index >> bit) & 1) == 1
@@ -46,16 +46,18 @@
     return current
 
 
-def scatter_cols(partial):
+def scatter_cols(partial, block):
     index = lax.axis_index("col")
     size = lax.axis_size("col")
     current = partial
-    for bit in range(size.bit_length() - 2, -1, -1):
+    for bit in range(size.bit_length() - 1):
         route = [(i, i ^ (1 << bit)) for i in range(size)]
-        half = current.shape[0] // 2
+        pairs = current.reshape(-1, 2, block, current.shape[1])
+        low_part = pairs[:, 0].reshape(-1, current.shape[1])
+        high_part = pairs[:, 1].reshape(-1, current.shape[1])
         high = ((index >> bit) & 1) == 1
-        keep = jnp.where(high, current[half:], current[:half])
-        send = jnp.where(high, current[:half], current[half:])
+        keep = jnp.where(high, high_part, low_part)
+        send = jnp.where(high, low_part, high_part)
         current = keep + lax.ppermute(send, "col", route)
     return current
 
@@ -98,7 +100,11 @@
         [operator_blocks[0, 0], placed_matrix.reshape(-1, unknowns)], 0
     )
 
-    coarse_matrix = coarse_inverse[0, :, 0, :].T
+    rows = lax.axis_size("row")
+    row_bits = rows.bit_length() - 1
+    tile = coarse_inverse[0, :, 0, :].reshape((2,) * row_bits + (mode_count, -1))
+    tile = jnp.transpose(tile, tuple(range(row_bits - 1, -1, -1)) + (row_bits, row_bits + 1))
+    coarse_matrix = tile.reshape(rows * mode_count, -1).T
 
     def coarse_solve(rounded):
         restricted = lax.dot_general(
@@ -106,7 +112,7 @@
         ).astype(jnp.bfloat16)
         gathered = gather_rows(restricted)
         partial_sums = jnp.dot(coarse_matrix, gathered, preferred_element_type=jnp.float32)
-        return scatter_cols(partial_sums).astype(jnp.bfloat16)
+        return scatter_cols(partial_sums, mode_count).astype(jnp.bfloat16)
 
     solution = jnp.zeros((columns, unknowns), jnp.float32)
     pending = None

time: 433 us -> 527 us (1.22)
  local copies, waits for them, and re-layouts: 9.86 us -> 93.1 us
  waiting for transfers between devices: 135 us -> 56.2 us
  other arithmetic: 8.73 us -> 61 us
  starting transfers between devices: 253 us -> 277 us
  matrix products: 18.9 us -> 33.4 us
    ppermute x25, waiting for transfers between devices: 64.1 us -> 21.3 us  [gather_rows(): other = lax.ppermute(current, 'row', route)]
    ppermute x20, waiting for transfers between devices: 57.1 us -> 15.3 us  [scatter_cols(): current = keep + lax.ppermute(send, 'col', route)]
    select_n x0 -> x20, local copies, waits for them, and re-layouts: none -> 28.3 us  [the longest x10 14.7 us: scatter_cols(): send = jnp.where(high, low_part, high_part)]
    ppermute x20, starting transfers between devices: 70.5 us -> 44.1 us  [shifted(): return lax.ppermute(block, axis, route)]
    ppermute x25, starting transfers between devices: 94.9 us -> 121 us  [gather_rows(): other = lax.ppermute(current, 'row', route)]
    select_n x20, other arithmetic: 2.68 us -> 27 us  [the longest x10 17.7 us: scatter_cols(): send = jnp.where(high, low_part, high_part)]
    ppermute x20, starting transfers between devices: 87.9 us -> 112 us  [scatter_cols(): current = keep + lax.ppermute(send, 'col', route)]
    reshape x0 -> x10, local copies, waits for them, and re-layouts: none -> 20.5 us  [scatter_cols(): pairs = current.reshape(-1, 2, block, current.shape[1])]
  transfers between devices with their start and end apart: 65 -> 65, of which waited for: 23 -> 24; matrix products, arithmetic and copies ran while one was open for 7% -> 34% of each run, Pallas kernels for 0% -> 0%
where the time goes in v6:
time: 527 us; the launch traced here: 522 us
  starting transfers between devices  277 us (53%)
  local copies, waits for them, and re-layouts  93.1 us (18%)
  other arithmetic  61 us (12%)
  waiting for transfers between devices  56.2 us (11%)
  matrix products  33.4 us (6%)
    ppermute x25, starting transfers between devices, gather_rows(): other = lax.ppermute(current, 'row', route)  121 us
    ppermute x20, starting transfers between devices, scatter_cols(): current = keep + lax.ppermute(send, 'col', route)  112 us
    ppermute x20, starting transfers between devices, shifted(): return lax.ppermute(block, axis, route)  44.1 us
    ppermute x25, waiting for transfers between devices, gather_rows(): other = lax.ppermute(current, 'row', route)  21.3 us
    reshape x10, local copies, waits for them, and re-layouts, scatter_cols(): pairs = current.reshape(-1, 2, block, current.shape[1])  20.5 us
    ppermute x20, waiting for transfers between devices, shifted(): return lax.ppermute(block, axis, route)  19.6 us
    select_n x10, other arithmetic, scatter_cols(): send = jnp.where(high, low_part, high_part)  17.7 us
    ppermute x20, waiting for transfers between devices, scatter_cols(): current = keep + lax.ppermute(send, 'col', route)  15.3 us
  transfers between devices with their start and end apart: 65, of which 24 were waited for; matrix products, arithmetic and copies ran while one was open for 34% of the time, Pallas kernels for 0%

profile of v6, /device:TPU:6, one launch (start us, length us, event | category | flops | bytes accessed | tf_op | source)
XLA Modules:
  0.0 522.1 jit_solution(13199021288453568662)
XLA Ops:
  1.2 9.1 %collective-permute-start.4 = (bf16[48,64]{1,0:T(8,128)(2,1)S(1)}, bf16[48,64]{1,0:T(8,128)(2,1)S(1)}, u32[]{:S(2)}, u32[]{:S(2)}) collective-permute-start(bf16[48,64]{1,0:T(8,128)(2,1)S(1)} %convolution_convert_fusion.4), channel_id=1, source_target_pairs={{0,256},{16,272},{32,288},{48,304},{64,320},{80,336},{96,352},{112... | collective-permute-start | bytes 18440 | tf_op jit(solution)/shard_map/ppermute | solution.py:41
  15.6 4.1 collective-permute-start
  23.8 7.8 %collective-permute-start.5 = (bf16[96,64]{1,0:T(8,128)(2,1)S(1)}, bf16[96,64]{1,0:T(8,128)(2,1)S(1)}, u32[]{:S(2)}, u32[]{:S(2)}) collective-permute-start(bf16[96,64]{1,0:T(8,128)(2,1)S(1)} %maximum_select_fusion.25), channel_id=1, source_target_pairs={{0,128},{16,144},{32,160},{48,176},{64,192},{80,208},{96,224},{112... | collective-permute-start | bytes 36872 | tf_op jit(solution)/shard_map/ppermute | solution.py:41
  34.0 3.8 collective-permute-start.6
  59.6 2.5 fusion.10
  63.3 3.0 collective-permute-start.7
  69.7 3.6 collective-permute-start.3
  73.4 6.7 %collective-permute-done.3 = bf16[64,384]{1,0:T(8,128)(2,1)S(1)} collective-permute-done((bf16[64,384]{1,0:T(8,128)(2,1)S(1)}, bf16[64,384]{1,0:T(8,128)(2,1)S(1)}, u32[]{:S(2)}, u32[]{:S(2)}) %collective-permute-start.3) | collective-permute-done | bytes 49184 | tf_op jit(solution)/shard_map/ppermute | solution.py:15
  82.7 5.5 %collective-permute-start.17 = (bf16[48,64]{1,0:T(8,128)(2,1)S(1)}, bf16[48,64]{1,0:T(8,128)(2,1)S(1)}, u32[]{:S(2)}, u32[]{:S(2)}) collective-permute-start(bf16[48,64]{1,0:T(8,128)(2,1)S(1)} %fusion.51), channel_id=1, source_target_pairs={{0,256},{16,272},{32,288},{48,304},{64,320},{80,336},{96,352},{112... | collective-permute-start | bytes 18440 | tf_op jit(solution)/shard_map/ppermute | solution.py:41
  88.2 2.6 collective-permute-start.8
  92.2 3.4 collective-permute-start.18
  96.6 2.2 collective-permute-done.18
  99.4 2.9 collective-permute-start.19
  103.5 2.6 reshape.279
  106.1 3.7 fusion.92
  111.5 13.0 %collective-permute-start.9 = (f32[384,64]{0,1:T(8,128)}, f32[384,64]{0,1:T(8,128)}, u32[]{:S(2)}, u32[]{:S(2)}) collective-permute-start(f32[384,64]{0,1:T(8,128)} %select_n.437), channel_id=1, source_target_pairs={{0,1},{1,0},{2,3},{3,2},{4,5},{5,4},{6,7},{7,6},{8,9},{9,8},{10,11... | collective-permute-start | bytes 294920 | tf_op jit(solution)/shard_map/ppermute | solution.py:61
  126.0 4.6 collective-permute-start.20
  143.3 3.0 collective-permute-start.21
  152.0 2.4 convolution_bitcast_fusion.3
  154.4 2.6 reshape.283
  159.4 5.0 collective-permute-start.12
  164.4 3.7 fusion.94
  179.9 3.9 collective-permute-start.13
  192.2 3.4 collective-permute-start.23
  202.4 5.1 collective-permute-start.24
  210.0 9.0 %collective-permute-start.25 = (f32[48,64]{1,0:T(8,128)S(1)}, f32[48,64]{1,0:T(8,128)S(1)}, u32[]{:S(2)}, u32[]{:S(2)}) collective-permute-start(f32[48,64]{1,0:T(8,128)S(1)} %select_bitcast_fusion.3), channel_id=1, source_target_pairs={{0,8},{1,9},{2,10},{3,11},{4,12},{5,13},{6,14},{7,15},{8,0},{9,1},... | collective-permute-start | bytes 36872 | tf_op jit(solution)/shard_map/ppermute | solution.py:61
  222.9 2.5 fusion.47
  225.9 10.5 %collective-permute-start.30 = (bf16[48,64]{1,0:T(8,128)(2,1)S(1)}, bf16[48,64]{1,0:T(8,128)(2,1)S(1)}, u32[]{:S(2)}, u32[]{:S(2)}) collective-permute-start(bf16[48,64]{1,0:T(8,128)(2,1)S(1)} %fusion.52), channel_id=1, source_target_pairs={{0,256},{16,272},{32,288},{48,304},{64,320},{80,336},{96,352},{112... | collective-permute-start | bytes 18440 | tf_op jit(solution)/shard_map/ppermute | solution.py:41
  238.2 3.2 collective-permute-start.31
  241.4 3.6 collective-permute-done.31
  245.0 3.1 collective-permute-start.32
  251.0 4.5 collective-permute-start.33
  257.5 3.6 collective-permute-start.29
  261.2 12.7 %collective-permute-done.29 = bf16[64,384]{1,0:T(8,128)(2,1)S(1)} collective-permute-done((bf16[64,384]{1,0:T(8,128)(2,1)S(1)}, bf16[64,384]{1,0:T(8,128)(2,1)S(1)}, u32[]{:S(2)}, u32[]{:S(2)}) %collective-permute-start.29) | collective-permute-done | bytes 49184 | tf_op jit(solution)/shard_map/ppermute | solution.py:15
  274.7 10.0 %collective-permute-start.43 = (bf16[48,64]{1,0:T(8,128)(2,1)S(1)}, bf16[48,64]{1,0:T(8,128)(2,1)S(1)}, u32[]{:S(2)}, u32[]{:S(2)}) collective-permute-start(bf16[48,64]{1,0:T(8,128)(2,1)S(1)} %fusion.53), channel_id=1, source_target_pairs={{0,256},{16,272},{32,288},{48,304},{64,320},{80,336},{96,352},{112... | collective-permute-start | bytes 18440 | tf_op jit(solution)/shard_map/ppermute | solution.py:41
  290.1 3.7 collective-permute-done.44
  294.4 2.4 collective-permute-start.45
  298.0 2.6 reshape.287
  300.6 3.7 fusion.96
  305.9 13.7 %collective-permute-start.35 = (f32[384,64]{0,1:T(8,128)}, f32[384,64]{0,1:T(8,128)}, u32[]{:S(2)}, u32[]{:S(2)}) collective-permute-start(f32[384,64]{0,1:T(8,128)} %select_n.479), channel_id=1, source_target_pairs={{0,1},{1,0},{2,3},{3,2},{4,5},{5,4},{6,7},{7,6},{8,9},{9,8},{10,11... | collective-permute-start | bytes 294920 | tf_op jit(solution)/shard_map/ppermute | solution.py:61
  321.2 6.5 %collective-permute-start.46 = (bf16[384,64]{1,0:T(8,128)(2,1)}, bf16[384,64]{1,0:T(8,128)(2,1)}, u32[]{:S(2)}, u32[]{:S(2)}) collective-permute-start(bf16[384,64]{1,0:T(8,128)(2,1)} %maximum_select_fusion.18), channel_id=1, source_target_pairs={{0,32},{16,48},{32,0},{48,16},{64,96},{80,112},{96,64},{112,80},{1... | collective-permute-start | bytes 147464 | tf_op jit(solution)/shard_map/ppermute | solution.py:41
  340.4 3.7 collective-permute-start.47
  349.3 2.4 convolution_bitcast_fusion.1
  351.7 2.6 reshape.291
  357.2 5.3 %collective-permute-start.38 = (f32[48,64]{1,0:T(8,128)}, f32[48,64]{1,0:T(8,128)}, u32[]{:S(2)}, u32[]{:S(2)}) collective-permute-start(f32[48,64]{1,0:T(8,128)} %select_bitcast_fusion.2), channel_id=1, source_target_pairs={{0,8},{1,9},{2,10},{3,11},{4,12},{5,13},{6,14},{7,15},{8,0},{9,1},... | collective-permute-start | bytes 36872 | tf_op jit(solution)/shard_map/ppermute | solution.py:61
  362.5 3.7 fusion.98
  377.6 3.6 collective-permute-start.39
  389.6 3.7 collective-permute-start.49
  400.1 4.7 collective-permute-start.50
  407.7 8.7 %collective-permute-start.51 = (f32[48,64]{1,0:T(8,128)S(1)}, f32[48,64]{1,0:T(8,128)S(1)}, u32[]{:S(2)}, u32[]{:S(2)}) collective-permute-start(f32[48,64]{1,0:T(8,128)S(1)} %select_bitcast_fusion.1), channel_id=1, source_target_pairs={{0,8},{1,9},{2,10},{3,11},{4,12},{5,13},{6,14},{7,15},{8,0},{9,1},... | collective-permute-start | bytes 36872 | tf_op jit(solution)/shard_map/ppermute | solution.py:61
  420.3 2.5 fusion.49
  423.4 9.4 %collective-permute-start.56 = (bf16[48,64]{1,0:T(8,128)(2,1)S(1)}, bf16[48,64]{1,0:T(8,128)(2,1)S(1)}, u32[]{:S(2)}, u32[]{:S(2)}) collective-permute-start(bf16[48,64]{1,0:T(8,128)(2,1)S(1)} %fusion.54), channel_id=1, source_target_pairs={{0,256},{16,272},{32,288},{48,304},{64,320},{80,336},{96,352},{112... | collective-permute-start | bytes 18440 | tf_op jit(solution)/shard_map/ppermute | solution.py:41
  434.6 6.6 %collective-permute-start.57 = (bf16[96,64]{1,0:T(8,128)(2,1)S(1)}, bf16[96,64]{1,0:T(8,128)(2,1)S(1)}, u32[]{:S(2)}, u32[]{:S(2)}) collective-permute-start(bf16[96,64]{1,0:T(8,128)(2,1)S(1)} %maximum_select_fusion.29), channel_id=1, source_target_pairs={{0,128},{16,144},{32,160},{48,176},{64,192},{80,208},{96,224},{112... | collective-permute-start | bytes 36872 | tf_op jit(solution)/shard_map/ppermute | solution.py:41
  443.3 2.4 collective-permute-start.58
  449.3 5.2 collective-permute-start.59
  457.1 2.4 collective-permute-start.54
  459.6 4.0 collective-permute-start.60
  463.8 3.5 collective-permute-done.60
  473.2 16.9 %collective-permute-start.61 = (f32[384,64]{0,1:T(8,128)S(1)}, f32[384,64]{0,1:T(8,128)S(1)}, u32[]{:S(2)}, u32[]{:S(2)}) collective-permute-start(f32[384,64]{0,1:T(8,128)S(1)} %select_n.521), channel_id=1, source_target_pairs={{0,1},{1,0},{2,3},{3,2},{4,5},{5,4},{6,7},{7,6},{8,9},{9,8},{10,11... | collective-permute-start | bytes 294920 | tf_op jit(solution)/shard_map/ppermute | solution.py:61
  495.8 3.3 collective-permute-done.62
  502.4 4.2 collective-permute-done.63
  506.7 7.7 %collective-permute-start.64 = (f32[48,64]{1,0:T(8,128)S(1)}, f32[48,64]{1,0:T(8,128)S(1)}, u32[]{:S(2)}, u32[]{:S(2)}) collective-permute-start(f32[48,64]{1,0:T(8,128)S(1)} %select_bitcast_fusion), channel_id=1, source_target_pairs={{0,8},{1,9},{2,10},{3,11},{4,12},{5,13},{6,14},{7,15},{8,0},{9,1},... | collective-permute-start | bytes 36872 | tf_op jit(solution)/shard_map/ppermute | solution.py:61
  514.4 2.4 fusion.13
  516.8 4.4 collective-permute-done.64
  (333 shorter events, 202.1 us)
Async XLA Ops:
  1.2 22.6 %collective-permute-start.4 = (bf16[48,64]{1,0:T(8,128)(2,1)S(1)}, bf16[48,64]{1,0:T(8,128)(2,1)S(1)}, u32[]{:S(2)}, u32[]{:S(2)}) collective-permute-start(bf16[48,64]{1,0:T(8,128)(2,1)S(1)} %convolution_convert_fusion.4), channel_id=1, source_target_pairs={{0,256},{16,272},{32,288},{48,304},{64,320},{80,336},{96,352},{112... | collective-permute-start | bytes 18440 | tf_op jit(solution)/shard_map/ppermute | solution.py:41
  15.6 50.7 %collective-permute-start = (bf16[64,384]{1,0:T(8,128)(2,1)}, bf16[64,384]{1,0:T(8,128)(2,1)}, u32[]{:S(2)}, u32[]{:S(2)}) collective-permute-start(bf16[64,384]{1,0:T(8,128)(2,1)} %get-tuple-element.47), channel_id=1, source_target_pairs={{0,16},{16,32},{32,48},{48,64},{64,80},{80,96},{96,112},{112,128},... | collective-permute-start | bytes 147464 | tf_op jit(solution)/shard_map/ppermute | solution.py:15
  19.7 47.3 %collective-permute-start.1 = (bf16[64,384]{1,0:T(8,128)(2,1)}, bf16[64,384]{1,0:T(8,128)(2,1)}, u32[]{:S(2)}, u32[]{:S(2)}) collective-permute-start(bf16[64,384]{1,0:T(8,128)(2,1)} %get-tuple-element.48), channel_id=1, source_target_pairs={{16,0},{32,16},{48,32},{64,48},{80,64},{96,80},{112,96},{128,112},... | collective-permute-start | bytes 147464 | tf_op jit(solution)/shard_map/ppermute | solution.py:15
  23.8 9.6 %collective-permute-start.5 = (bf16[96,64]{1,0:T(8,128)(2,1)S(1)}, bf16[96,64]{1,0:T(8,128)(2,1)S(1)}, u32[]{:S(2)}, u32[]{:S(2)}) collective-permute-start(bf16[96,64]{1,0:T(8,128)(2,1)S(1)} %maximum_select_fusion.25), channel_id=1, source_target_pairs={{0,128},{16,144},{32,160},{48,176},{64,192},{80,208},{96,224},{112... | collective-permute-start | bytes 36872 | tf_op jit(solution)/shard_map/ppermute | solution.py:41
  34.0 28.1 %collective-permute-start.6 = (bf16[192,64]{1,0:T(8,128)(2,1)}, bf16[192,64]{1,0:T(8,128)(2,1)}, u32[]{:S(2)}, u32[]{:S(2)}) collective-permute-start(bf16[192,64]{1,0:T(8,128)(2,1)} %maximum_select_fusion.20), channel_id=1, source_target_pairs={{0,64},{16,80},{32,96},{48,112},{64,0},{80,16},{96,32},{112,48},{1... | collective-permute-start | bytes 73736 | tf_op jit(solution)/shard_map/ppermute | solution.py:41
  63.3 24.8 %collective-permute-start.7 = (bf16[384,64]{1,0:T(8,128)(2,1)S(1)}, bf16[384,64]{1,0:T(8,128)(2,1)S(1)}, u32[]{:S(2)}, u32[]{:S(2)}) collective-permute-start(bf16[384,64]{1,0:T(8,128)(2,1)S(1)} %maximum_select_fusion.15), channel_id=1, source_target_pairs={{0,32},{16,48},{32,0},{48,16},{64,96},{80,112},{96,64},{112,80},{1... | collective-permute-start | bytes 147464 | tf_op jit(solution)/shard_map/ppermute | solution.py:41
  67.8 5.6 %collective-permute-start.2 = (bf16[64,384]{1,0:T(8,128)(2,1)S(1)}, bf16[64,384]{1,0:T(8,128)(2,1)S(1)}, u32[]{:S(2)}, u32[]{:S(2)}) collective-permute-start(bf16[64,384]{1,0:T(8,128)(2,1)S(1)} %pad_maximum_fusion.1), channel_id=1, source_target_pairs={{0,1},{1,2},{2,3},{3,4},{4,5},{5,6},{6,7},{7,8},{8,9},{9,10},{10,1... | collective-permute-start | bytes 147464 | tf_op jit(solution)/shard_map/ppermute | solution.py:15
  69.7 10.4 %collective-permute-start.3 = (bf16[64,384]{1,0:T(8,128)(2,1)S(1)}, bf16[64,384]{1,0:T(8,128)(2,1)S(1)}, u32[]{:S(2)}, u32[]{:S(2)}) collective-permute-start(bf16[64,384]{1,0:T(8,128)(2,1)S(1)} %pad_maximum_fusion.2), channel_id=1, source_target_pairs={{1,0},{2,1},{3,2},{4,3},{5,4},{6,5},{7,6},{8,7},{9,8},{10,9},{11,1... | collective-permute-start | bytes 147464 | tf_op jit(solution)/shard_map/ppermute | solution.py:15
  82.7 9.5 %collective-permute-start.17 = (bf16[48,64]{1,0:T(8,128)(2,1)S(1)}, bf16[48,64]{1,0:T(8,128)(2,1)S(1)}, u32[]{:S(2)}, u32[]{:S(2)}) collective-permute-start(bf16[48,64]{1,0:T(8,128)(2,1)S(1)} %fusion.51), channel_id=1, source_target_pairs={{0,256},{16,272},{32,288},{48,304},{64,320},{80,336},{96,352},{112... | collective-permute-start | bytes 18440 | tf_op jit(solution)/shard_map/ppermute | solution.py:41
  88.2 14.1 %collective-permute-start.8 = (bf16[768,64]{1,0:T(8,128)(2,1)S(1)}, bf16[768,64]{1,0:T(8,128)(2,1)S(1)}, u32[]{:S(2)}, u32[]{:S(2)}) collective-permute-start(bf16[768,64]{1,0:T(8,128)(2,1)S(1)} %maximum_select_fusion.10), channel_id=1, source_target_pairs={{0,16},{16,0},{32,48},{48,32},{64,80},{80,64},{96,112},{112,96},{1... | collective-permute-start | bytes 294920 | tf_op jit(solution)/shard_map/ppermute | solution.py:41
  92.2 6.6 %collective-permute-start.18 = (bf16[96,64]{1,0:T(8,128)(2,1)S(1)}, bf16[96,64]{1,0:T(8,128)(2,1)S(1)}, u32[]{:S(2)}, u32[]{:S(2)}) collective-permute-start(bf16[96,64]{1,0:T(8,128)(2,1)S(1)} %maximum_select_fusion.26), channel_id=1, source_target_pairs={{0,128},{16,144},{32,160},{48,176},{64,192},{80,208},{96,224},{112... | collective-permute-start | bytes 36872 | tf_op jit(solution)/shard_map/ppermute | solution.py:41
  99.4 25.0 %collective-permute-start.19 = (bf16[192,64]{1,0:T(8,128)(2,1)}, bf16[192,64]{1,0:T(8,128)(2,1)}, u32[]{:S(2)}, u32[]{:S(2)}) collective-permute-start(bf16[192,64]{1,0:T(8,128)(2,1)} %maximum_select_fusion.21), channel_id=1, source_target_pairs={{0,64},{16,80},{32,96},{48,112},{64,0},{80,16},{96,32},{112,48},{1... | collective-permute-start | bytes 73736 | tf_op jit(solution)/shard_map/ppermute | solution.py:41
  111.5 20.9 %collective-permute-start.9 = (f32[384,64]{0,1:T(8,128)}, f32[384,64]{0,1:T(8,128)}, u32[]{:S(2)}, u32[]{:S(2)}) collective-permute-start(f32[384,64]{0,1:T(8,128)} %select_n.437), channel_id=1, source_target_pairs={{0,1},{1,0},{2,3},{3,2},{4,5},{5,4},{6,7},{7,6},{8,9},{9,8},{10,11... | collective-permute-start | bytes 294920 | tf_op jit(solution)/shard_map/ppermute | solution.py:61
  126.0 15.4 %collective-permute-start.20 = (bf16[384,64]{1,0:T(8,128)(2,1)}, bf16[384,64]{1,0:T(8,128)(2,1)}, u32[]{:S(2)}, u32[]{:S(2)}) collective-permute-start(bf16[384,64]{1,0:T(8,128)(2,1)} %maximum_select_fusion.16), channel_id=1, source_target_pairs={{0,32},{16,48},{32,0},{48,16},{64,96},{80,112},{96,64},{112,80},{1... | collective-permute-start | bytes 147464 | tf_op jit(solution)/shard_map/ppermute | solution.py:41
  139.5 8.4 %collective-permute-start.10 = (f32[192,64]{1,0:T(8,128)}, f32[192,64]{1,0:T(8,128)}, u32[]{:S(2)}, u32[]{:S(2)}) collective-permute-start(f32[192,64]{1,0:T(8,128)} %bitcast.349), channel_id=1, source_target_pairs={{0,2},{1,3},{2,0},{3,1},{4,6},{5,7},{6,4},{7,5},{8,10},{9,11},{10,... | collective-permute-start | bytes 147464 | tf_op jit(solution)/shard_map/ppermute | solution.py:61
  143.3 8.7 %collective-permute-start.21 = (bf16[768,64]{1,0:T(8,128)(2,1)}, bf16[768,64]{1,0:T(8,128)(2,1)}, u32[]{:S(2)}, u32[]{:S(2)}) collective-permute-start(bf16[768,64]{1,0:T(8,128)(2,1)} %maximum_select_fusion.11), channel_id=1, source_target_pairs={{0,16},{16,0},{32,48},{48,32},{64,80},{80,64},{96,112},{112,96},{1... | collective-permute-start | bytes 294920 | tf_op jit(solution)/shard_map/ppermute | solution.py:41
  149.6 7.8 %collective-permute-start.11 = (f32[96,64]{1,0:T(8,128)}, f32[96,64]{1,0:T(8,128)}, u32[]{:S(2)}, u32[]{:S(2)}) collective-permute-start(f32[96,64]{1,0:T(8,128)} %bitcast.44), channel_id=1, source_target_pairs={{0,4},{1,5},{2,6},{3,7},{4,0},{5,1},{6,2},{7,3},{8,12},{9,13},{10,... | collective-permute-start | bytes 73736 | tf_op jit(solution)/shard_map/ppermute | solution.py:61
  159.4 14.8 %collective-permute-start.12 = (f32[48,64]{1,0:T(8,128)}, f32[48,64]{1,0:T(8,128)}, u32[]{:S(2)}, u32[]{:S(2)}) collective-permute-start(f32[48,64]{1,0:T(8,128)} %select_bitcast_fusion.4), channel_id=1, source_target_pairs={{0,8},{1,9},{2,10},{3,11},{4,12},{5,13},{6,14},{7,15},{8,0},{9,1},... | collective-permute-start | bytes 36872 | tf_op jit(solution)/shard_map/ppermute | solution.py:61
  169.8 15.3 %collective-permute-start.22 = (f32[384,64]{0,1:T(8,128)}, f32[384,64]{0,1:T(8,128)}, u32[]{:S(2)}, u32[]{:S(2)}) collective-permute-start(f32[384,64]{0,1:T(8,128)} %select_n.458), channel_id=1, source_target_pairs={{0,1},{1,0},{2,3},{3,2},{4,5},{5,4},{6,7},{7,6},{8,9},{9,8},{10,11... | collective-permute-start | bytes 294920 | tf_op jit(solution)/shard_map/ppermute | solution.py:61
  179.9 17.4 %collective-permute-start.13 = (bf16[64,384]{1,0:T(8,128)(2,1)}, bf16[64,384]{1,0:T(8,128)(2,1)}, u32[]{:S(2)}, u32[]{:S(2)}) collective-permute-start(bf16[64,384]{1,0:T(8,128)(2,1)} %get-tuple-element.39), channel_id=1, source_target_pairs={{0,16},{16,32},{32,48},{48,64},{64,80},{80,96},{96,112},{112,128},... | collective-permute-start | bytes 147464 | tf_op jit(solution)/shard_map/ppermute | solution.py:15
  183.8 14.2 %collective-permute-start.14 = (bf16[64,384]{1,0:T(8,128)(2,1)}, bf16[64,384]{1,0:T(8,128)(2,1)}, u32[]{:S(2)}, u32[]{:S(2)}) collective-permute-start(bf16[64,384]{1,0:T(8,128)(2,1)} %get-tuple-element.40), channel_id=1, source_target_pairs={{16,0},{32,16},{48,32},{64,48},{80,64},{96,80},{112,96},{128,112},... | collective-permute-start | bytes 147464 | tf_op jit(solution)/shard_map/ppermute | solution.py:15
  192.2 9.2 %collective-permute-start.23 = (f32[192,64]{1,0:T(8,128)}, f32[192,64]{1,0:T(8,128)}, u32[]{:S(2)}, u32[]{:S(2)}) collective-permute-start(f32[192,64]{1,0:T(8,128)} %bitcast.347), channel_id=1, source_target_pairs={{0,2},{1,3},{2,0},{3,1},{4,6},{5,7},{6,4},{7,5},{8,10},{9,11},{10,... | collective-permute-start | bytes 147464 | tf_op jit(solution)/shard_map/ppermute | solution.py:61
  199.5 20.2 %collective-permute-start.16 = (bf16[64,384]{1,0:T(8,128)(2,1)S(1)}, bf16[64,384]{1,0:T(8,128)(2,1)S(1)}, u32[]{:S(2)}, u32[]{:S(2)}) collective-permute-start(bf16[64,384]{1,0:T(8,128)(2,1)S(1)} %pad_maximum_fusion.4), channel_id=1, source_target_pairs={{1,0},{2,1},{3,2},{4,3},{5,4},{6,5},{7,6},{8,7},{9,8},{10,9},{11,1... | collective-permute-start | bytes 147464 | tf_op jit(solution)/shard_map/ppermute | solution.py:15
  202.4 7.5 %collective-permute-start.24 = (f32[96,64]{1,0:T(8,128)S(1)}, f32[96,64]{1,0:T(8,128)S(1)}, u32[]{:S(2)}, u32[]{:S(2)}) collective-permute-start(f32[96,64]{1,0:T(8,128)S(1)} %bitcast.352), channel_id=1, source_target_pairs={{0,4},{1,5},{2,6},{3,7},{4,0},{5,1},{6,2},{7,3},{8,12},{9,13},{10,... | collective-permute-start | bytes 73736 | tf_op jit(solution)/shard_map/ppermute | solution.py:61
  207.5 11.5 %collective-permute-start.15 = (bf16[64,384]{1,0:T(8,128)(2,1)S(1)}, bf16[64,384]{1,0:T(8,128)(2,1)S(1)}, u32[]{:S(2)}, u32[]{:S(2)}) collective-permute-start(bf16[64,384]{1,0:T(8,128)(2,1)S(1)} %pad_maximum_fusion.3), channel_id=1, source_target_pairs={{0,1},{1,2},{2,3},{3,4},{4,5},{5,6},{6,7},{7,8},{8,9},{9,10},{10,1... | collective-permute-start | bytes 147464 | tf_op jit(solution)/shard_map/ppermute | solution.py:15
  210.0 26.5 %collective-permute-start.25 = (f32[48,64]{1,0:T(8,128)S(1)}, f32[48,64]{1,0:T(8,128)S(1)}, u32[]{:S(2)}, u32[]{:S(2)}) collective-permute-start(f32[48,64]{1,0:T(8,128)S(1)} %select_bitcast_fusion.3), channel_id=1, source_target_pairs={{0,8},{1,9},{2,10},{3,11},{4,12},{5,13},{6,14},{7,15},{8,0},{9,1},... | collective-permute-start | bytes 36872 | tf_op jit(solution)/shard_map/ppermute | solution.py:61
  225.9 12.2 %collective-permute-start.30 = (bf16[48,64]{1,0:T(8,128)(2,1)S(1)}, bf16[48,64]{1,0:T(8,128)(2,1)S(1)}, u32[]{:S(2)}, u32[]{:S(2)}) collective-permute-start(bf16[48,64]{1,0:T(8,128)(2,1)S(1)} %fusion.52), channel_id=1, source_target_pairs={{0,256},{16,272},{32,288},{48,304},{64,320},{80,336},{96,352},{112... | collective-permute-start | bytes 18440 | tf_op jit(solution)/shard_map/ppermute | solution.py:41
  238.2 6.8 %collective-permute-start.31 = (bf16[96,64]{1,0:T(8,128)(2,1)S(1)}, bf16[96,64]{1,0:T(8,128)(2,1)S(1)}, u32[]{:S(2)}, u32[]{:S(2)}) collective-permute-start(bf16[96,64]{1,0:T(8,128)(2,1)S(1)} %maximum_select_fusion.27), channel_id=1, source_target_pairs={{0,128},{16,144},{32,160},{48,176},{64,192},{80,208},{96,224},{112... | collective-permute-start | bytes 36872 | tf_op jit(solution)/shard_map/ppermute | solution.py:41
  245.0 6.0 %collective-permute-start.32 = (bf16[192,64]{1,0:T(8,128)(2,1)S(1)}, bf16[192,64]{1,0:T(8,128)(2,1)S(1)}, u32[]{:S(2)}, u32[]{:S(2)}) collective-permute-start(bf16[192,64]{1,0:T(8,128)(2,1)S(1)} %maximum_select_fusion.22), channel_id=1, source_target_pairs={{0,64},{16,80},{32,96},{48,112},{64,0},{80,16},{96,32},{112,48},{1... | collective-permute-start | bytes 73736 | tf_op jit(solution)/shard_map/ppermute | solution.py:41
  248.1 7.4 %collective-permute-start.26 = (bf16[64,384]{1,0:T(8,128)(2,1)S(1)}, bf16[64,384]{1,0:T(8,128)(2,1)S(1)}, u32[]{:S(2)}, u32[]{:S(2)}) collective-permute-start(bf16[64,384]{1,0:T(8,128)(2,1)S(1)} %get-tuple-element.35), channel_id=1, source_target_pairs={{0,16},{16,32},{32,48},{48,64},{64,80},{80,96},{96,112},{112,128},... | collective-permute-start | bytes 147464 | tf_op jit(solution)/shard_map/ppermute | solution.py:15
  249.4 6.1 %collective-permute-start.27 = (bf16[64,384]{1,0:T(8,128)(2,1)S(1)}, bf16[64,384]{1,0:T(8,128)(2,1)S(1)}, u32[]{:S(2)}, u32[]{:S(2)}) collective-permute-start(bf16[64,384]{1,0:T(8,128)(2,1)S(1)} %get-tuple-element.36), channel_id=1, source_target_pairs={{16,0},{32,16},{48,32},{64,48},{80,64},{96,80},{112,96},{128,112},... | collective-permute-start | bytes 147464 | tf_op jit(solution)/shard_map/ppermute | solution.py:15
  251.0 33.7 %collective-permute-start.33 = (bf16[384,64]{1,0:T(8,128)(2,1)S(1)}, bf16[384,64]{1,0:T(8,128)(2,1)S(1)}, u32[]{:S(2)}, u32[]{:S(2)}) collective-permute-start(bf16[384,64]{1,0:T(8,128)(2,1)S(1)} %maximum_select_fusion.17), channel_id=1, source_target_pairs={{0,32},{16,48},{32,0},{48,16},{64,96},{80,112},{96,64},{112,80},{1... | collective-permute-start | bytes 147464 | tf_op jit(solution)/shard_map/ppermute | solution.py:41
  257.5 16.4 %collective-permute-start.29 = (bf16[64,384]{1,0:T(8,128)(2,1)S(1)}, bf16[64,384]{1,0:T(8,128)(2,1)S(1)}, u32[]{:S(2)}, u32[]{:S(2)}) collective-permute-start(bf16[64,384]{1,0:T(8,128)(2,1)S(1)} %pad_maximum_fusion.6), channel_id=1, source_target_pairs={{1,0},{2,1},{3,2},{4,3},{5,4},{6,5},{7,6},{8,7},{9,8},{10,9},{11,1... | collective-permute-start | bytes 147464 | tf_op jit(solution)/shard_map/ppermute | solution.py:15
  274.7 12.2 %collective-permute-start.43 = (bf16[48,64]{1,0:T(8,128)(2,1)S(1)}, bf16[48,64]{1,0:T(8,128)(2,1)S(1)}, u32[]{:S(2)}, u32[]{:S(2)}) collective-permute-start(bf16[48,64]{1,0:T(8,128)(2,1)S(1)} %fusion.53), channel_id=1, source_target_pairs={{0,256},{16,272},{32,288},{48,304},{64,320},{80,336},{96,352},{112... | collective-permute-start | bytes 18440 | tf_op jit(solution)/shard_map/ppermute | solution.py:41
  284.8 12.0 %collective-permute-start.34 = (bf16[768,64]{1,0:T(8,128)(2,1)S(1)}, bf16[768,64]{1,0:T(8,128)(2,1)S(1)}, u32[]{:S(2)}, u32[]{:S(2)}) collective-permute-start(bf16[768,64]{1,0:T(8,128)(2,1)S(1)} %maximum_select_fusion.12), channel_id=1, source_target_pairs={{0,16},{16,0},{32,48},{48,32},{64,80},{80,64},{96,112},{112,96},{1... | collective-permute-start | bytes 294920 | tf_op jit(solution)/shard_map/ppermute | solution.py:41
  286.9 6.9 %collective-permute-start.44 = (bf16[96,64]{1,0:T(8,128)(2,1)S(1)}, bf16[96,64]{1,0:T(8,128)(2,1)S(1)}, u32[]{:S(2)}, u32[]{:S(2)}) collective-permute-start(bf16[96,64]{1,0:T(8,128)(2,1)S(1)} %maximum_select_fusion.28), channel_id=1, source_target_pairs={{0,128},{16,144},{32,160},{48,176},{64,192},{80,208},{96,224},{112... | collective-permute-start | bytes 36872 | tf_op jit(solution)/shard_map/ppermute | solution.py:41
  294.4 25.2 %collective-permute-start.45 = (bf16[192,64]{1,0:T(8,128)(2,1)}, bf16[192,64]{1,0:T(8,128)(2,1)}, u32[]{:S(2)}, u32[]{:S(2)}) collective-permute-start(bf16[192,64]{1,0:T(8,128)(2,1)} %maximum_select_fusion.23), channel_id=1, source_target_pairs={{0,64},{16,80},{32,96},{48,112},{64,0},{80,16},{96,32},{112,48},{1... | collective-permute-start | bytes 73736 | tf_op jit(solution)/shard_map/ppermute | solution.py:41
  305.9 23.5 %collective-permute-start.35 = (f32[384,64]{0,1:T(8,128)}, f32[384,64]{0,1:T(8,128)}, u32[]{:S(2)}, u32[]{:S(2)}) collective-permute-start(f32[384,64]{0,1:T(8,128)} %select_n.479), channel_id=1, source_target_pairs={{0,1},{1,0},{2,3},{3,2},{4,5},{5,4},{6,7},{7,6},{8,9},{9,8},{10,11... | collective-permute-start | bytes 294920 | tf_op jit(solution)/shard_map/ppermute | solution.py:61
  321.2 17.3 %collective-permute-start.46 = (bf16[384,64]{1,0:T(8,128)(2,1)}, bf16[384,64]{1,0:T(8,128)(2,1)}, u32[]{:S(2)}, u32[]{:S(2)}) collective-permute-start(bf16[384,64]{1,0:T(8,128)(2,1)} %maximum_select_fusion.18), channel_id=1, source_target_pairs={{0,32},{16,48},{32,0},{48,16},{64,96},{80,112},{96,64},{112,80},{1... | collective-permute-start | bytes 147464 | tf_op jit(solution)/shard_map/ppermute | solution.py:41
  336.6 9.1 %collective-permute-start.36 = (f32[192,64]{1,0:T(8,128)}, f32[192,64]{1,0:T(8,128)}, u32[]{:S(2)}, u32[]{:S(2)}) collective-permute-start(f32[192,64]{1,0:T(8,128)} %bitcast.350), channel_id=1, source_target_pairs={{0,2},{1,3},{2,0},{3,1},{4,6},{5,7},{6,4},{7,5},{8,10},{9,11},{10,... | collective-permute-start | bytes 147464 | tf_op jit(solution)/shard_map/ppermute | solution.py:61
  340.4 8.9 %collective-permute-start.47 = (bf16[768,64]{1,0:T(8,128)(2,1)}, bf16[768,64]{1,0:T(8,128)(2,1)}, u32[]{:S(2)}, u32[]{:S(2)}) collective-permute-start(bf16[768,64]{1,0:T(8,128)(2,1)} %maximum_select_fusion.13), channel_id=1, source_target_pairs={{0,16},{16,0},{32,48},{48,32},{64,80},{80,64},{96,112},{112,96},{1... | collective-permute-start | bytes 294920 | tf_op jit(solution)/shard_map/ppermute | solution.py:41
  347.3 7.8 %collective-permute-start.37 = (f32[96,64]{1,0:T(8,128)}, f32[96,64]{1,0:T(8,128)}, u32[]{:S(2)}, u32[]{:S(2)}) collective-permute-start(f32[96,64]{1,0:T(8,128)} %bitcast.64), channel_id=1, source_target_pairs={{0,4},{1,5},{2,6},{3,7},{4,0},{5,1},{6,2},{7,3},{8,12},{9,13},{10,... | collective-permute-start | bytes 73736 | tf_op jit(solution)/shard_map/ppermute | solution.py:61
  357.2 14.7 %collective-permute-start.38 = (f32[48,64]{1,0:T(8,128)}, f32[48,64]{1,0:T(8,128)}, u32[]{:S(2)}, u32[]{:S(2)}) collective-permute-start(f32[48,64]{1,0:T(8,128)} %select_bitcast_fusion.2), channel_id=1, source_target_pairs={{0,8},{1,9},{2,10},{3,11},{4,12},{5,13},{6,14},{7,15},{8,0},{9,1},... | collective-permute-start | bytes 36872 | tf_op jit(solution)/shard_map/ppermute | solution.py:61
  367.9 14.6 %collective-permute-start.48 = (f32[384,64]{0,1:T(8,128)}, f32[384,64]{0,1:T(8,128)}, u32[]{:S(2)}, u32[]{:S(2)}) collective-permute-start(f32[384,64]{0,1:T(8,128)} %select_n.500), channel_id=1, source_target_pairs={{0,1},{1,0},{2,3},{3,2},{4,5},{5,4},{6,7},{7,6},{8,9},{9,8},{10,11... | collective-permute-start | bytes 294920 | tf_op jit(solution)/shard_map/ppermute | solution.py:61
  377.6 17.4 %collective-permute-start.39 = (bf16[64,384]{1,0:T(8,128)(2,1)}, bf16[64,384]{1,0:T(8,128)(2,1)}, u32[]{:S(2)}, u32[]{:S(2)}) collective-permute-start(bf16[64,384]{1,0:T(8,128)(2,1)} %get-tuple-element.31), channel_id=1, source_target_pairs={{0,16},{16,32},{32,48},{48,64},{64,80},{80,96},{96,112},{112,128},... | collective-permute-start | bytes 147464 | tf_op jit(solution)/shard_map/ppermute | solution.py:15
  381.2 14.6 %collective-permute-start.40 = (bf16[64,384]{1,0:T(8,128)(2,1)}, bf16[64,384]{1,0:T(8,128)(2,1)}, u32[]{:S(2)}, u32[]{:S(2)}) collective-permute-start(bf16[64,384]{1,0:T(8,128)(2,1)} %get-tuple-element.32), channel_id=1, source_target_pairs={{16,0},{32,16},{48,32},{64,48},{80,64},{96,80},{112,96},{128,112},... | collective-permute-start | bytes 147464 | tf_op jit(solution)/shard_map/ppermute | solution.py:15
  389.6 9.5 %collective-permute-start.49 = (f32[192,64]{1,0:T(8,128)}, f32[192,64]{1,0:T(8,128)}, u32[]{:S(2)}, u32[]{:S(2)}) collective-permute-start(f32[192,64]{1,0:T(8,128)} %bitcast.348), channel_id=1, source_target_pairs={{0,2},{1,3},{2,0},{3,1},{4,6},{5,7},{6,4},{7,5},{8,10},{9,11},{10,... | collective-permute-start | bytes 147464 | tf_op jit(solution)/shard_map/ppermute | solution.py:61
  397.2 19.9 %collective-permute-start.42 = (bf16[64,384]{1,0:T(8,128)(2,1)S(1)}, bf16[64,384]{1,0:T(8,128)(2,1)S(1)}, u32[]{:S(2)}, u32[]{:S(2)}) collective-permute-start(bf16[64,384]{1,0:T(8,128)(2,1)S(1)} %pad_maximum_fusion.8), channel_id=1, source_target_pairs={{1,0},{2,1},{3,2},{4,3},{5,4},{6,5},{7,6},{8,7},{9,8},{10,9},{11,1... | collective-permute-start | bytes 147464 | tf_op jit(solution)/shard_map/ppermute | solution.py:15
  400.1 7.5 %collective-permute-start.50 = (f32[96,64]{1,0:T(8,128)S(1)}, f32[96,64]{1,0:T(8,128)S(1)}, u32[]{:S(2)}, u32[]{:S(2)}) collective-permute-start(f32[96,64]{1,0:T(8,128)S(1)} %bitcast.353), channel_id=1, source_target_pairs={{0,4},{1,5},{2,6},{3,7},{4,0},{5,1},{6,2},{7,3},{8,12},{9,13},{10,... | collective-permute-start | bytes 73736 | tf_op jit(solution)/shard_map/ppermute | solution.py:61
  404.9 11.6 %collective-permute-start.41 = (bf16[64,384]{1,0:T(8,128)(2,1)S(1)}, bf16[64,384]{1,0:T(8,128)(2,1)S(1)}, u32[]{:S(2)}, u32[]{:S(2)}) collective-permute-start(bf16[64,384]{1,0:T(8,128)(2,1)S(1)} %pad_maximum_fusion.7), channel_id=1, source_target_pairs={{0,1},{1,2},{2,3},{3,4},{4,5},{5,6},{6,7},{7,8},{8,9},{9,10},{10,1... | collective-permute-start | bytes 147464 | tf_op jit(solution)/shard_map/ppermute | solution.py:15
  407.7 25.1 %collective-permute-start.51 = (f32[48,64]{1,0:T(8,128)S(1)}, f32[48,64]{1,0:T(8,128)S(1)}, u32[]{:S(2)}, u32[]{:S(2)}) collective-permute-start(f32[48,64]{1,0:T(8,128)S(1)} %select_bitcast_fusion.1), channel_id=1, source_target_pairs={{0,8},{1,9},{2,10},{3,11},{4,12},{5,13},{6,14},{7,15},{8,0},{9,1},... | collective-permute-start | bytes 36872 | tf_op jit(solution)/shard_map/ppermute | solution.py:61
  423.4 11.2 %collective-permute-start.56 = (bf16[48,64]{1,0:T(8,128)(2,1)S(1)}, bf16[48,64]{1,0:T(8,128)(2,1)S(1)}, u32[]{:S(2)}, u32[]{:S(2)}) collective-permute-start(bf16[48,64]{1,0:T(8,128)(2,1)S(1)} %fusion.54), channel_id=1, source_target_pairs={{0,256},{16,272},{32,288},{48,304},{64,320},{80,336},{96,352},{112... | collective-permute-start | bytes 18440 | tf_op jit(solution)/shard_map/ppermute | solution.py:41
  434.6 8.7 %collective-permute-start.57 = (bf16[96,64]{1,0:T(8,128)(2,1)S(1)}, bf16[96,64]{1,0:T(8,128)(2,1)S(1)}, u32[]{:S(2)}, u32[]{:S(2)}) collective-permute-start(bf16[96,64]{1,0:T(8,128)(2,1)S(1)} %maximum_select_fusion.29), channel_id=1, source_target_pairs={{0,128},{16,144},{32,160},{48,176},{64,192},{80,208},{96,224},{112... | collective-permute-start | bytes 36872 | tf_op jit(solution)/shard_map/ppermute | solution.py:41
  443.3 6.0 %collective-permute-start.58 = (bf16[192,64]{1,0:T(8,128)(2,1)S(1)}, bf16[192,64]{1,0:T(8,128)(2,1)S(1)}, u32[]{:S(2)}, u32[]{:S(2)}) collective-permute-start(bf16[192,64]{1,0:T(8,128)(2,1)S(1)} %maximum_select_fusion.24), channel_id=1, source_target_pairs={{0,64},{16,80},{32,96},{48,112},{64,0},{80,16},{96,32},{112,48},{1... | collective-permute-start | bytes 73736 | tf_op jit(solution)/shard_map/ppermute | solution.py:41
  445.7 8.8 %collective-permute-start.52 = (bf16[64,384]{1,0:T(8,128)(2,1)S(1)}, bf16[64,384]{1,0:T(8,128)(2,1)S(1)}, u32[]{:S(2)}, u32[]{:S(2)}) collective-permute-start(bf16[64,384]{1,0:T(8,128)(2,1)S(1)} %get-tuple-element.27), channel_id=1, source_target_pairs={{0,16},{16,32},{32,48},{48,64},{64,80},{80,96},{96,112},{112,128},... | collective-permute-start | bytes 147464 | tf_op jit(solution)/shard_map/ppermute | solution.py:15
  447.0 7.5 %collective-permute-start.53 = (bf16[64,384]{1,0:T(8,128)(2,1)S(1)}, bf16[64,384]{1,0:T(8,128)(2,1)S(1)}, u32[]{:S(2)}, u32[]{:S(2)}) collective-permute-start(bf16[64,384]{1,0:T(8,128)(2,1)S(1)} %get-tuple-element.28), channel_id=1, source_target_pairs={{16,0},{32,16},{48,32},{64,48},{80,64},{96,80},{112,96},{128,112},... | collective-permute-start | bytes 147464 | tf_op jit(solution)/shard_map/ppermute | solution.py:15
  449.3 10.2 %collective-permute-start.59 = (bf16[384,64]{1,0:T(8,128)(2,1)S(1)}, bf16[384,64]{1,0:T(8,128)(2,1)S(1)}, u32[]{:S(2)}, u32[]{:S(2)}) collective-permute-start(bf16[384,64]{1,0:T(8,128)(2,1)S(1)} %maximum_select_fusion.19), channel_id=1, source_target_pairs={{0,32},{16,48},{32,0},{48,16},{64,96},{80,112},{96,64},{112,80},{1... | collective-permute-start | bytes 147464 | tf_op jit(solution)/shard_map/ppermute | solution.py:41
  455.2 35.0 %collective-permute-start.55 = (bf16[64,384]{1,0:T(8,128)(2,1)}, bf16[64,384]{1,0:T(8,128)(2,1)}, u32[]{:S(2)}, u32[]{:S(2)}) collective-permute-start(bf16[64,384]{1,0:T(8,128)(2,1)} %pad_maximum_fusion.10), channel_id=1, source_target_pairs={{1,0},{2,1},{3,2},{4,3},{5,4},{6,5},{7,6},{8,7},{9,8},{10,9},{11,1... | collective-permute-start | bytes 147464 | tf_op jit(solution)/shard_map/ppermute | solution.py:15
  457.1 6.6 %collective-permute-start.54 = (bf16[64,384]{1,0:T(8,128)(2,1)S(1)}, bf16[64,384]{1,0:T(8,128)(2,1)S(1)}, u32[]{:S(2)}, u32[]{:S(2)}) collective-permute-start(bf16[64,384]{1,0:T(8,128)(2,1)S(1)} %pad_maximum_fusion.9), channel_id=1, source_target_pairs={{0,1},{1,2},{2,3},{3,4},{4,5},{5,6},{6,7},{7,8},{8,9},{9,10},{10,1... | collective-permute-start | bytes 147464 | tf_op jit(solution)/shard_map/ppermute | solution.py:15
  459.6 7.7 %collective-permute-start.60 = (bf16[768,64]{1,0:T(8,128)(2,1)S(1)}, bf16[768,64]{1,0:T(8,128)(2,1)S(1)}, u32[]{:S(2)}, u32[]{:S(2)}) collective-permute-start(bf16[768,64]{1,0:T(8,128)(2,1)S(1)} %maximum_select_fusion.14), channel_id=1, source_target_pairs={{0,16},{16,0},{32,48},{48,32},{64,80},{80,64},{96,112},{112,96},{1... | collective-permute-start | bytes 294920 | tf_op jit(solution)/shard_map/ppermute | solution.py:41
  473.2 18.5 %collective-permute-start.61 = (f32[384,64]{0,1:T(8,128)S(1)}, f32[384,64]{0,1:T(8,128)S(1)}, u32[]{:S(2)}, u32[]{:S(2)}) collective-permute-start(f32[384,64]{0,1:T(8,128)S(1)} %select_n.521), channel_id=1, source_target_pairs={{0,1},{1,0},{2,3},{3,2},{4,5},{5,4},{6,7},{7,6},{8,9},{9,8},{10,11... | collective-permute-start | bytes 294920 | tf_op jit(solution)/shard_map/ppermute | solution.py:61
  492.5 6.6 %collective-permute-start.62 = (f32[192,64]{1,0:T(8,128)S(1)}, f32[192,64]{1,0:T(8,128)S(1)}, u32[]{:S(2)}, u32[]{:S(2)}) collective-permute-start(f32[192,64]{1,0:T(8,128)S(1)} %bitcast.351), channel_id=1, source_target_pairs={{0,2},{1,3},{2,0},{3,1},{4,6},{5,7},{6,4},{7,5},{8,10},{9,11},{10,... | collective-permute-start | bytes 147464 | tf_op jit(solution)/shard_map/ppermute | solution.py:61
  499.1 7.5 %collective-permute-start.63 = (f32[96,64]{1,0:T(8,128)S(1)}, f32[96,64]{1,0:T(8,128)S(1)}, u32[]{:S(2)}, u32[]{:S(2)}) collective-permute-start(f32[96,64]{1,0:T(8,128)S(1)} %bitcast.354), channel_id=1, source_target_pairs={{0,4},{1,5},{2,6},{3,7},{4,0},{5,1},{6,2},{7,3},{8,12},{9,13},{10,... | collective-permute-start | bytes 73736 | tf_op jit(solution)/shard_map/ppermute | solution.py:61
  506.7 14.6 %collective-permute-start.64 = (f32[48,64]{1,0:T(8,128)S(1)}, f32[48,64]{1,0:T(8,128)S(1)}, u32[]{:S(2)}, u32[]{:S(2)}) collective-permute-start(f32[48,64]{1,0:T(8,128)S(1)} %select_bitcast_fusion), channel_id=1, source_target_pairs={{0,8},{1,9},{2,10},{3,11},{4,12},{5,13},{6,14},{7,15},{8,0},{9,1},... | collective-permute-start | bytes 36872 | tf_op jit(solution)/shard_map/ppermute | solution.py:61
  (38 other events, 513.1 us)

commit v7 on v5

--- a/solution.py
+++ b/solution.py
@@ -1,4 +1,5 @@
 import jax
+import numpy as np
 import jax.numpy as jnp
 from jax import lax
 from jax.sharding import PartitionSpec as P
@@ -36,7 +37,7 @@
     index = lax.axis_index("row")
     size = lax.axis_size("row")
     current = piece
-    for bit in range(size.bit_length() - 1):
+    for bit in range(size.bit_length() - 2, -1, -1):
         route = [(i, i ^ (1 << bit)) for i in range(size)]
         other = lax.ppermute(current, "row", route)
         high = ((index >> bit) & 1) == 1
@@ -50,7 +51,7 @@
     index = lax.axis_index("col")
     size = lax.axis_size("col")
     current = partial
-    for bit in range(size.bit_length() - 2, -1, -1):
+    for bit in range(size.bit_length() - 1):
         route = [(i, i ^ (1 << bit)) for i in range(size)]
         half = current.shape[0] // 2
         high = ((index >> bit) & 1) == 1
@@ -58,6 +59,12 @@
         send = jnp.where(high, current[:half], current[half:])
         current = keep + lax.ppermute(send, "col", route)
     return current
+
+
+def reversed_blocks(count, block):
+    bits = count.bit_length() - 1
+    order = [int(format(i, f"0{bits}b")[::-1], 2) if bits else 0 for i in range(count)]
+    return np.array([order[i // block] * block + i % block for i in range(count * block)])
 
 
 def on_device(
@@ -98,7 +105,16 @@
         [operator_blocks[0, 0], placed_matrix.reshape(-1, unknowns)], 0
     )
 
-    coarse_matrix = coarse_inverse[0, :, 0, :].T
+    rows = lax.axis_size("row")
+    cols = lax.axis_size("col")
+    tile = coarse_inverse[0, :, 0, :]
+    from_rows = reversed_blocks(rows, mode_count)
+    from_cols = reversed_blocks(cols, mode_count)
+    pick_rows = (jnp.arange(rows * mode_count)[None, :] == from_rows[:, None]).astype(jnp.bfloat16)
+    pick_cols = (jnp.arange(cols * mode_count)[:, None] == from_cols[None, :]).astype(jnp.bfloat16)
+    tile = jnp.dot(pick_rows, tile, preferred_element_type=jnp.float32).astype(jnp.bfloat16)
+    tile = jnp.dot(tile, pick_cols, preferred_element_type=jnp.float32).astype(jnp.bfloat16)
+    coarse_matrix = tile.T
 
     def coarse_solve(rounded):
         restricted = lax.dot_general(

time: 433 us -> 402 us (0.928)
  waiting for transfers between devices: 135 us -> 89.9 us
  matrix products: 18.9 us -> 25.6 us
  starting transfers between devices: 253 us -> 258 us
    ppermute x25, waiting for transfers between devices: 64.1 us -> 24.1 us  [gather_rows(): other = lax.ppermute(current, 'row', route)]
    ppermute x25, starting transfers between devices: 94.9 us -> 118 us  [gather_rows(): other = lax.ppermute(current, 'row', route)]
    ppermute x20, starting transfers between devices: 87.9 us -> 76.4 us  [scatter_cols(): current = keep + lax.ppermute(send, 'col', route)]
    dot_general x0 -> x1, matrix products: none -> 7.4 us  [on_device(): jnp.dot(tile, pick_cols, preferred_element_type=jnp.float32)]
    ppermute x20, starting transfers between devices: 70.5 us -> 64.1 us  [shifted(): return lax.ppermute(block, axis, route)]
  transfers between devices with their start and end apart: 65 -> 65, of which waited for: 23 -> 25; matrix products, arithmetic and copies ran while one was open for 7% -> 8% of each run, Pallas kernels for 0% -> 0%
where the time goes in v7:
time: 402 us; the launch traced here: 395 us
  starting transfers between devices  258 us (64%)
  waiting for transfers between devices  89.9 us (22%)
  matrix products  25.6 us (6%)
  local copies, waits for them, and re-layouts  10 us (2%)
  other arithmetic  9.58 us (2%)
    ppermute x25, starting transfers between devices, gather_rows(): other = lax.ppermute(current, 'row', route)  118 us
    ppermute x20, starting transfers between devices, scatter_cols(): current = keep + lax.ppermute(send, 'col', route)  76.4 us
    ppermute x20, starting transfers between devices, shifted(): return lax.ppermute(block, axis, route)  64.1 us
    ppermute x20, waiting for transfers between devices, scatter_cols(): current = keep + lax.ppermute(send, 'col', route)  54.6 us
    ppermute x25, waiting for transfers between devices, gather_rows(): other = lax.ppermute(current, 'row', route)  24.1 us
    ppermute x20, waiting for transfers between devices, shifted(): return lax.ppermute(block, axis, route)  11.2 us
  transfers between devices with their start and end apart: 65, of which 25 were waited for; matrix products, arithmetic and copies ran while one was open for 8% of the time, Pallas kernels for 0%

profile of v7, /device:TPU:6, one launch (start us, length us, event | category | flops | bytes accessed | tf_op | source)
XLA Modules:
  0.0 395.4 jit_solution(9562066709444298195)
XLA Ops:
  2.1 2.3 constant_dynamic-update-slice_fusion.4
  8.3 5.2 %collective-permute-start = (bf16[64,384]{1,0:T(8,128)(2,1)}, bf16[64,384]{1,0:T(8,128)(2,1)}, u32[]{:S(2)}, u32[]{:S(2)}) collective-permute-start(bf16[64,384]{1,0:T(8,128)(2,1)} %get-tuple-element.27), channel_id=1, source_target_pairs={{0,16},{16,32},{32,48},{48,64},{64,80},{80,96},{96,112},{112,128},... | collective-permute-start | bytes 147464 | tf_op jit(solution)/shard_map/ppermute | solution.py:16
  13.6 9.1 %collective-permute-start.4 = (bf16[48,64]{1,0:T(8,128)(2,1)S(1)}, bf16[48,64]{1,0:T(8,128)(2,1)S(1)}, u32[]{:S(2)}, u32[]{:S(2)}) collective-permute-start(bf16[48,64]{1,0:T(8,128)(2,1)S(1)} %convolution_convert_fusion.5), channel_id=1, source_target_pairs={{0,256},{16,272},{32,288},{48,304},{64,320},{80,336},{96,352},{112... | collective-permute-start | bytes 18440 | tf_op jit(solution)/shard_map/ppermute | solution.py:42
  23.0 7.4 %convolution_convert_fusion = bf16[1536,768]{1,0:T(8,128)(2,1)} fusion(s32[768]{0:T(1024)S(1)} %copy-done.24, s32[1536]{0:T(1024)S(1)} %copy-done.23, bf16[1,1536,1,768]{3,1,2,0:T(8,128)(2,1)S(1)} %copy-done), kind=kOutput, calls=%fused_computation.5 | convolution fusion | flops 5441126400 | bytes 4727808 | tf_op jit(solution)/shard_map/dot_general | solution.py:116
  31.1 5.2 %collective-permute-start.5 = (bf16[96,64]{1,0:T(8,128)(2,1)S(1)}, bf16[96,64]{1,0:T(8,128)(2,1)S(1)}, u32[]{:S(2)}, u32[]{:S(2)}) collective-permute-start(bf16[96,64]{1,0:T(8,128)(2,1)S(1)} %maximum_select_fusion.25), channel_id=1, source_target_pairs={{0,128},{16,144},{32,160},{48,176},{64,192},{80,208},{96,224},{112... | collective-permute-start | bytes 36872 | tf_op jit(solution)/shard_map/ppermute | solution.py:42
  38.3 3.6 collective-permute-start.6
  47.3 5.2 %collective-permute-start.7 = (bf16[384,64]{1,0:T(8,128)(2,1)S(1)}, bf16[384,64]{1,0:T(8,128)(2,1)S(1)}, u32[]{:S(2)}, u32[]{:S(2)}) collective-permute-start(bf16[384,64]{1,0:T(8,128)(2,1)S(1)} %maximum_select_fusion.15), channel_id=1, source_target_pairs={{0,32},{16,48},{32,0},{48,16},{64,96},{80,112},{96,64},{112,80},{1... | collective-permute-start | bytes 147464 | tf_op jit(solution)/shard_map/ppermute | solution.py:42
  55.9 3.6 collective-permute-start.3
  59.6 6.1 %collective-permute-done.3 = bf16[64,384]{1,0:T(8,128)(2,1)S(1)} collective-permute-done((bf16[64,384]{1,0:T(8,128)(2,1)S(1)}, bf16[64,384]{1,0:T(8,128)(2,1)S(1)}, u32[]{:S(2)}, u32[]{:S(2)}) %collective-permute-start.3) | collective-permute-done | bytes 49184 | tf_op jit(solution)/shard_map/ppermute | solution.py:16
  68.2 5.6 %collective-permute-start.17 = (bf16[48,64]{1,0:T(8,128)(2,1)S(1)}, bf16[48,64]{1,0:T(8,128)(2,1)S(1)}, u32[]{:S(2)}, u32[]{:S(2)}) collective-permute-start(bf16[48,64]{1,0:T(8,128)(2,1)S(1)} %fusion.56), channel_id=1, source_target_pairs={{0,256},{16,272},{32,288},{48,304},{64,320},{80,336},{96,352},{112... | collective-permute-start | bytes 18440 | tf_op jit(solution)/shard_map/ppermute | solution.py:42
  73.9 4.7 %collective-permute-start.8 = (bf16[768,64]{1,0:T(8,128)(2,1)S(1)}, bf16[768,64]{1,0:T(8,128)(2,1)S(1)}, u32[]{:S(2)}, u32[]{:S(2)}) collective-permute-start(bf16[768,64]{1,0:T(8,128)(2,1)S(1)} %maximum_select_fusion.10), channel_id=1, source_target_pairs={{0,16},{16,0},{32,48},{48,32},{64,80},{80,64},{96,112},{112,96},{1... | collective-permute-start | bytes 294920 | tf_op jit(solution)/shard_map/ppermute | solution.py:42
  78.6 4.6 %collective-permute-start.18 = (bf16[96,64]{1,0:T(8,128)(2,1)S(1)}, bf16[96,64]{1,0:T(8,128)(2,1)S(1)}, u32[]{:S(2)}, u32[]{:S(2)}) collective-permute-start(bf16[96,64]{1,0:T(8,128)(2,1)S(1)} %maximum_select_fusion.26), channel_id=1, source_target_pairs={{0,128},{16,144},{32,160},{48,176},{64,192},{80,208},{96,224},{112... | collective-permute-start | bytes 36872 | tf_op jit(solution)/shard_map/ppermute | solution.py:42
  85.3 2.9 collective-permute-start.19
  88.8 13.8 %collective-permute-start.9 = (f32[384,64]{0,1:T(8,128)S(1)}, f32[384,64]{0,1:T(8,128)S(1)}, u32[]{:S(2)}, u32[]{:S(2)}) collective-permute-start(f32[384,64]{0,1:T(8,128)S(1)} %slice_select_fusion.4), channel_id=1, source_target_pairs={{0,1},{1,0},{2,3},{3,2},{4,5},{5,4},{6,7},{7,6},{8,9},{9,8},{10,11... | collective-permute-start | bytes 294920 | tf_op jit(solution)/shard_map/ppermute | solution.py:60
  102.7 3.7 collective-permute-start.20
  108.5 2.6 collective-permute-done.20
  111.2 2.8 collective-permute-start.21
  114.2 2.2 collective-permute-start.11
  116.4 2.9 collective-permute-done.21
  125.7 10.6 %collective-permute-done.12 = f32[48,64]{0,1:T(8,128)S(1)} collective-permute-done((f32[48,64]{0,1:T(8,128)S(1)}, f32[48,64]{0,1:T(8,128)S(1)}, u32[]{:S(2)}, u32[]{:S(2)}) %collective-permute-start.12) | collective-permute-done | bytes 12320 | tf_op jit(solution)/shard_map/ppermute | solution.py:60
  138.3 4.5 %collective-permute-start.13 = (bf16[64,384]{1,0:T(8,128)(2,1)S(1)}, bf16[64,384]{1,0:T(8,128)(2,1)S(1)}, u32[]{:S(2)}, u32[]{:S(2)}) collective-permute-start(bf16[64,384]{1,0:T(8,128)(2,1)S(1)} %get-tuple-element.19), channel_id=1, source_target_pairs={{0,16},{16,32},{32,48},{48,64},{64,80},{80,96},{96,112},{112,128},... | collective-permute-start | bytes 147464 | tf_op jit(solution)/shard_map/ppermute | solution.py:16
  146.9 2.2 collective-permute-done.23
  149.3 2.3 collective-permute-start.24
  153.5 3.1 collective-permute-done.24
  156.8 2.7 collective-permute-start.25
  160.7 8.1 %collective-permute-start.30 = (bf16[48,64]{1,0:T(8,128)(2,1)S(1)}, bf16[48,64]{1,0:T(8,128)(2,1)S(1)}, u32[]{:S(2)}, u32[]{:S(2)}) collective-permute-start(bf16[48,64]{1,0:T(8,128)(2,1)S(1)} %fusion.57), channel_id=1, source_target_pairs={{0,256},{16,272},{32,288},{48,304},{64,320},{80,336},{96,352},{112... | collective-permute-start | bytes 18440 | tf_op jit(solution)/shard_map/ppermute | solution.py:42
  168.8 3.0 collective-permute-done.25
  172.5 4.3 %collective-permute-start.31 = (bf16[96,64]{1,0:T(8,128)(2,1)S(1)}, bf16[96,64]{1,0:T(8,128)(2,1)S(1)}, u32[]{:S(2)}, u32[]{:S(2)}) collective-permute-start(bf16[96,64]{1,0:T(8,128)(2,1)S(1)} %maximum_select_fusion.27), channel_id=1, source_target_pairs={{0,128},{16,144},{32,160},{48,176},{64,192},{80,208},{96,224},{112... | collective-permute-start | bytes 36872 | tf_op jit(solution)/shard_map/ppermute | solution.py:42
  176.8 2.3 collective-permute-done.31
  179.1 3.8 collective-permute-start.32
  184.2 4.5 %collective-permute-start.26 = (bf16[64,384]{1,0:T(8,128)(2,1)S(1)}, bf16[64,384]{1,0:T(8,128)(2,1)S(1)}, u32[]{:S(2)}, u32[]{:S(2)}) collective-permute-start(bf16[64,384]{1,0:T(8,128)(2,1)S(1)} %get-tuple-element.15), channel_id=1, source_target_pairs={{0,16},{16,32},{32,48},{48,64},{64,80},{80,96},{96,112},{112,128},... | collective-permute-start | bytes 147464 | tf_op jit(solution)/shard_map/ppermute | solution.py:16
  188.8 3.9 collective-permute-start.33
  192.8 8.1 %collective-permute-start.28 = (bf16[64,384]{1,0:T(8,128)(2,1)S(1)}, bf16[64,384]{1,0:T(8,128)(2,1)S(1)}, u32[]{:S(2)}, u32[]{:S(2)}) collective-permute-start(bf16[64,384]{1,0:T(8,128)(2,1)S(1)} %pad_maximum_fusion.5), channel_id=1, source_target_pairs={{0,1},{1,2},{2,3},{3,4},{4,5},{5,6},{6,7},{7,8},{8,9},{9,10},{10,1... | collective-permute-start | bytes 147464 | tf_op jit(solution)/shard_map/ppermute | solution.py:16
  202.9 5.1 %collective-permute-done.29 = bf16[64,384]{1,0:T(8,128)(2,1)S(1)} collective-permute-done((bf16[64,384]{1,0:T(8,128)(2,1)S(1)}, bf16[64,384]{1,0:T(8,128)(2,1)S(1)}, u32[]{:S(2)}, u32[]{:S(2)}) %collective-permute-start.29) | collective-permute-done | bytes 49184 | tf_op jit(solution)/shard_map/ppermute | solution.py:16
  208.8 10.4 %collective-permute-start.43 = (bf16[48,64]{1,0:T(8,128)(2,1)S(1)}, bf16[48,64]{1,0:T(8,128)(2,1)S(1)}, u32[]{:S(2)}, u32[]{:S(2)}) collective-permute-start(bf16[48,64]{1,0:T(8,128)(2,1)S(1)} %fusion.58), channel_id=1, source_target_pairs={{0,256},{16,272},{32,288},{48,304},{64,320},{80,336},{96,352},{112... | collective-permute-start | bytes 18440 | tf_op jit(solution)/shard_map/ppermute | solution.py:42
  221.2 3.6 collective-permute-start.44
  225.1 2.7 collective-permute-done.44
  227.8 3.2 collective-permute-start.45
  231.7 13.4 %collective-permute-start.35 = (f32[384,64]{0,1:T(8,128)S(1)}, f32[384,64]{0,1:T(8,128)S(1)}, u32[]{:S(2)}, u32[]{:S(2)}) collective-permute-start(f32[384,64]{0,1:T(8,128)S(1)} %slice_select_fusion.2), channel_id=1, source_target_pairs={{0,1},{1,0},{2,3},{3,2},{4,5},{5,4},{6,7},{7,6},{8,9},{9,8},{10,11... | collective-permute-start | bytes 294920 | tf_op jit(solution)/shard_map/ppermute | solution.py:60
  245.1 3.3 collective-permute-start.46
  250.5 2.7 collective-permute-done.46
  253.3 3.7 collective-permute-start.47
  259.1 2.1 collective-permute-done.47
  261.8 2.7 collective-permute-done.37
  268.5 10.8 %collective-permute-done.38 = f32[48,64]{0,1:T(8,128)S(1)} collective-permute-done((f32[48,64]{0,1:T(8,128)S(1)}, f32[48,64]{0,1:T(8,128)S(1)}, u32[]{:S(2)}, u32[]{:S(2)}) %collective-permute-start.38) | collective-permute-done | bytes 12320 | tf_op jit(solution)/shard_map/ppermute | solution.py:60
  281.3 4.5 %collective-permute-start.39 = (bf16[64,384]{1,0:T(8,128)(2,1)S(1)}, bf16[64,384]{1,0:T(8,128)(2,1)S(1)}, u32[]{:S(2)}, u32[]{:S(2)}) collective-permute-start(bf16[64,384]{1,0:T(8,128)(2,1)S(1)} %get-tuple-element.11), channel_id=1, source_target_pairs={{0,16},{16,32},{32,48},{48,64},{64,80},{80,96},{96,112},{112,128},... | collective-permute-start | bytes 147464 | tf_op jit(solution)/shard_map/ppermute | solution.py:16
  289.9 2.2 collective-permute-done.49
  292.3 2.2 collective-permute-start.50
  296.5 3.2 collective-permute-done.50
  302.9 8.3 %collective-permute-start.56 = (bf16[48,64]{1,0:T(8,128)(2,1)S(1)}, bf16[48,64]{1,0:T(8,128)(2,1)S(1)}, u32[]{:S(2)}, u32[]{:S(2)}) collective-permute-start(bf16[48,64]{1,0:T(8,128)(2,1)S(1)} %fusion.59), channel_id=1, source_target_pairs={{0,256},{16,272},{32,288},{48,304},{64,320},{80,336},{96,352},{112... | collective-permute-start | bytes 18440 | tf_op jit(solution)/shard_map/ppermute | solution.py:42
  311.2 4.5 %collective-permute-done.51 = f32[48,64]{0,1:T(8,128)S(1)} collective-permute-done((f32[48,64]{0,1:T(8,128)S(1)}, f32[48,64]{0,1:T(8,128)S(1)}, u32[]{:S(2)}, u32[]{:S(2)}) %collective-permute-start.51) | collective-permute-done | bytes 12320 | tf_op jit(solution)/shard_map/ppermute | solution.py:60
  316.6 4.6 %collective-permute-start.57 = (bf16[96,64]{1,0:T(8,128)(2,1)S(1)}, bf16[96,64]{1,0:T(8,128)(2,1)S(1)}, u32[]{:S(2)}, u32[]{:S(2)}) collective-permute-start(bf16[96,64]{1,0:T(8,128)(2,1)S(1)} %maximum_select_fusion.29), channel_id=1, source_target_pairs={{0,128},{16,144},{32,160},{48,176},{64,192},{80,208},{96,224},{112... | collective-permute-start | bytes 36872 | tf_op jit(solution)/shard_map/ppermute | solution.py:42
  321.2 2.0 collective-permute-done.57
  323.2 2.7 collective-permute-start.58
  327.3 4.5 %collective-permute-start.52 = (bf16[64,384]{1,0:T(8,128)(2,1)S(1)}, bf16[64,384]{1,0:T(8,128)(2,1)S(1)}, u32[]{:S(2)}, u32[]{:S(2)}) collective-permute-start(bf16[64,384]{1,0:T(8,128)(2,1)S(1)} %get-tuple-element.7), channel_id=1, source_target_pairs={{0,16},{16,32},{32,48},{48,64},{64,80},{80,96},{96,112},{112,128},... | collective-permute-start | bytes 147464 | tf_op jit(solution)/shard_map/ppermute | solution.py:16
  331.9 3.5 collective-permute-start.59
  335.5 9.2 %collective-permute-start.54 = (bf16[64,384]{1,0:T(8,128)(2,1)S(1)}, bf16[64,384]{1,0:T(8,128)(2,1)S(1)}, u32[]{:S(2)}, u32[]{:S(2)}) collective-permute-start(bf16[64,384]{1,0:T(8,128)(2,1)S(1)} %pad_maximum_fusion.9), channel_id=1, source_target_pairs={{0,1},{1,2},{2,3},{3,4},{4,5},{5,6},{6,7},{7,8},{8,9},{9,10},{10,1... | collective-permute-start | bytes 147464 | tf_op jit(solution)/shard_map/ppermute | solution.py:16
  346.7 5.1 %collective-permute-start.60 = (bf16[768,64]{1,0:T(8,128)(2,1)S(1)}, bf16[768,64]{1,0:T(8,128)(2,1)S(1)}, u32[]{:S(2)}, u32[]{:S(2)}) collective-permute-start(bf16[768,64]{1,0:T(8,128)(2,1)S(1)} %maximum_select_fusion.14), channel_id=1, source_target_pairs={{0,16},{16,0},{32,48},{48,32},{64,80},{80,64},{96,112},{112,96},{1... | collective-permute-start | bytes 294920 | tf_op jit(solution)/shard_map/ppermute | solution.py:42
  351.9 3.6 collective-permute-done.60
  356.1 4.6 %collective-permute-start.61 = (f32[384,64]{0,1:T(8,128)S(1)}, f32[384,64]{0,1:T(8,128)S(1)}, u32[]{:S(2)}, u32[]{:S(2)}) collective-permute-start(f32[384,64]{0,1:T(8,128)S(1)} %slice_select_fusion), channel_id=1, source_target_pairs={{0,1},{1,0},{2,3},{3,2},{4,5},{5,4},{6,7},{7,6},{8,9},{9,8},{10,11... | collective-permute-start | bytes 294920 | tf_op jit(solution)/shard_map/ppermute | solution.py:60
  363.7 4.2 %collective-permute-done.62 = f32[192,64]{0,1:T(8,128)S(1)} collective-permute-done((f32[192,64]{0,1:T(8,128)S(1)}, f32[192,64]{0,1:T(8,128)S(1)}, u32[]{:S(2)}, u32[]{:S(2)}) %collective-permute-start.62) | collective-permute-done | bytes 49184 | tf_op jit(solution)/shard_map/ppermute | solution.py:60
  370.0 5.4 %collective-permute-done.63 = f32[96,64]{0,1:T(8,128)S(1)} collective-permute-done((f32[96,64]{0,1:T(8,128)S(1)}, f32[96,64]{0,1:T(8,128)S(1)}, u32[]{:S(2)}, u32[]{:S(2)}) %collective-permute-start.63) | collective-permute-done | bytes 24608 | tf_op jit(solution)/shard_map/ppermute | solution.py:60
  377.6 12.2 %collective-permute-start.64 = (f32[48,64]{0,1:T(8,128)}, f32[48,64]{0,1:T(8,128)}, u32[]{:S(2)}, u32[]{:S(2)}) collective-permute-start(f32[48,64]{0,1:T(8,128)} %slice_select_fusion.10), channel_id=1, source_target_pairs={{0,8},{1,9},{2,10},{3,11},{4,12},{5,13},{6,14},{7,15},{8,0},{9,1},... | collective-permute-start | bytes 36872 | tf_op jit(solution)/shard_map/ppermute | solution.py:60
  389.8 3.6 fusion.17
  (281 shorter events, 82.5 us)
Async XLA Ops:
  7.0 45.5 %collective-permute-start.1 = (bf16[64,384]{1,0:T(8,128)(2,1)}, bf16[64,384]{1,0:T(8,128)(2,1)}, u32[]{:S(2)}, u32[]{:S(2)}) collective-permute-start(bf16[64,384]{1,0:T(8,128)(2,1)} %get-tuple-element.28), channel_id=1, source_target_pairs={{16,0},{32,16},{48,32},{64,48},{80,64},{96,80},{112,96},{128,112},... | collective-permute-start | bytes 147464 | tf_op jit(solution)/shard_map/ppermute | solution.py:16
  8.3 44.9 %collective-permute-start = (bf16[64,384]{1,0:T(8,128)(2,1)}, bf16[64,384]{1,0:T(8,128)(2,1)}, u32[]{:S(2)}, u32[]{:S(2)}) collective-permute-start(bf16[64,384]{1,0:T(8,128)(2,1)} %get-tuple-element.27), channel_id=1, source_target_pairs={{0,16},{16,32},{32,48},{48,64},{64,80},{80,96},{96,112},{112,128},... | collective-permute-start | bytes 147464 | tf_op jit(solution)/shard_map/ppermute | solution.py:16
  13.6 17.4 %collective-permute-start.4 = (bf16[48,64]{1,0:T(8,128)(2,1)S(1)}, bf16[48,64]{1,0:T(8,128)(2,1)S(1)}, u32[]{:S(2)}, u32[]{:S(2)}) collective-permute-start(bf16[48,64]{1,0:T(8,128)(2,1)S(1)} %convolution_convert_fusion.5), channel_id=1, source_target_pairs={{0,256},{16,272},{32,288},{48,304},{64,320},{80,336},{96,352},{112... | collective-permute-start | bytes 18440 | tf_op jit(solution)/shard_map/ppermute | solution.py:42
  31.1 7.2 %collective-permute-start.5 = (bf16[96,64]{1,0:T(8,128)(2,1)S(1)}, bf16[96,64]{1,0:T(8,128)(2,1)S(1)}, u32[]{:S(2)}, u32[]{:S(2)}) collective-permute-start(bf16[96,64]{1,0:T(8,128)(2,1)S(1)} %maximum_select_fusion.25), channel_id=1, source_target_pairs={{0,128},{16,144},{32,160},{48,176},{64,192},{80,208},{96,224},{112... | collective-permute-start | bytes 36872 | tf_op jit(solution)/shard_map/ppermute | solution.py:42
  38.3 8.0 %collective-permute-start.6 = (bf16[192,64]{1,0:T(8,128)(2,1)S(1)}, bf16[192,64]{1,0:T(8,128)(2,1)}, u32[]{:S(2)}, u32[]{:S(2)}) collective-permute-start(bf16[192,64]{1,0:T(8,128)(2,1)S(1)} %maximum_select_fusion.20), channel_id=1, source_target_pairs={{0,64},{16,80},{32,96},{48,112},{64,0},{80,16},{96,32},{112,48},{1... | collective-permute-start | bytes 73736 | tf_op jit(solution)/shard_map/ppermute | solution.py:42
  47.3 26.5 %collective-permute-start.7 = (bf16[384,64]{1,0:T(8,128)(2,1)S(1)}, bf16[384,64]{1,0:T(8,128)(2,1)S(1)}, u32[]{:S(2)}, u32[]{:S(2)}) collective-permute-start(bf16[384,64]{1,0:T(8,128)(2,1)S(1)} %maximum_select_fusion.15), channel_id=1, source_target_pairs={{0,32},{16,48},{32,0},{48,16},{64,96},{80,112},{96,64},{112,80},{1... | collective-permute-start | bytes 147464 | tf_op jit(solution)/shard_map/ppermute | solution.py:42
  53.9 5.6 %collective-permute-start.2 = (bf16[64,384]{1,0:T(8,128)(2,1)S(1)}, bf16[64,384]{1,0:T(8,128)(2,1)S(1)}, u32[]{:S(2)}, u32[]{:S(2)}) collective-permute-start(bf16[64,384]{1,0:T(8,128)(2,1)S(1)} %pad_maximum_fusion.1), channel_id=1, source_target_pairs={{0,1},{1,2},{2,3},{3,4},{4,5},{5,6},{6,7},{7,8},{8,9},{9,10},{10,1... | collective-permute-start | bytes 147464 | tf_op jit(solution)/shard_map/ppermute | solution.py:16
  55.9 9.8 %collective-permute-start.3 = (bf16[64,384]{1,0:T(8,128)(2,1)S(1)}, bf16[64,384]{1,0:T(8,128)(2,1)S(1)}, u32[]{:S(2)}, u32[]{:S(2)}) collective-permute-start(bf16[64,384]{1,0:T(8,128)(2,1)S(1)} %pad_maximum_fusion.2), channel_id=1, source_target_pairs={{1,0},{2,1},{3,2},{4,3},{5,4},{6,5},{7,6},{8,7},{9,8},{10,9},{11,1... | collective-permute-start | bytes 147464 | tf_op jit(solution)/shard_map/ppermute | solution.py:16
  68.2 10.4 %collective-permute-start.17 = (bf16[48,64]{1,0:T(8,128)(2,1)S(1)}, bf16[48,64]{1,0:T(8,128)(2,1)S(1)}, u32[]{:S(2)}, u32[]{:S(2)}) collective-permute-start(bf16[48,64]{1,0:T(8,128)(2,1)S(1)} %fusion.56), channel_id=1, source_target_pairs={{0,256},{16,272},{32,288},{48,304},{64,320},{80,336},{96,352},{112... | collective-permute-start | bytes 18440 | tf_op jit(solution)/shard_map/ppermute | solution.py:42
  73.9 14.3 %collective-permute-start.8 = (bf16[768,64]{1,0:T(8,128)(2,1)S(1)}, bf16[768,64]{1,0:T(8,128)(2,1)S(1)}, u32[]{:S(2)}, u32[]{:S(2)}) collective-permute-start(bf16[768,64]{1,0:T(8,128)(2,1)S(1)} %maximum_select_fusion.10), channel_id=1, source_target_pairs={{0,16},{16,0},{32,48},{48,32},{64,80},{80,64},{96,112},{112,96},{1... | collective-permute-start | bytes 294920 | tf_op jit(solution)/shard_map/ppermute | solution.py:42
  78.6 6.6 %collective-permute-start.18 = (bf16[96,64]{1,0:T(8,128)(2,1)S(1)}, bf16[96,64]{1,0:T(8,128)(2,1)S(1)}, u32[]{:S(2)}, u32[]{:S(2)}) collective-permute-start(bf16[96,64]{1,0:T(8,128)(2,1)S(1)} %maximum_select_fusion.26), channel_id=1, source_target_pairs={{0,128},{16,144},{32,160},{48,176},{64,192},{80,208},{96,224},{112... | collective-permute-start | bytes 36872 | tf_op jit(solution)/shard_map/ppermute | solution.py:42
  85.3 17.3 %collective-permute-start.19 = (bf16[192,64]{1,0:T(8,128)(2,1)S(1)}, bf16[192,64]{1,0:T(8,128)(2,1)S(1)}, u32[]{:S(2)}, u32[]{:S(2)}) collective-permute-start(bf16[192,64]{1,0:T(8,128)(2,1)S(1)} %maximum_select_fusion.21), channel_id=1, source_target_pairs={{0,64},{16,80},{32,96},{48,112},{64,0},{80,16},{96,32},{112,48},{1... | collective-permute-start | bytes 73736 | tf_op jit(solution)/shard_map/ppermute | solution.py:42
  88.8 17.6 %collective-permute-start.9 = (f32[384,64]{0,1:T(8,128)S(1)}, f32[384,64]{0,1:T(8,128)S(1)}, u32[]{:S(2)}, u32[]{:S(2)}) collective-permute-start(f32[384,64]{0,1:T(8,128)S(1)} %slice_select_fusion.4), channel_id=1, source_target_pairs={{0,1},{1,0},{2,3},{3,2},{4,5},{5,4},{6,7},{7,6},{8,9},{9,8},{10,11... | collective-permute-start | bytes 294920 | tf_op jit(solution)/shard_map/ppermute | solution.py:60
  102.7 8.4 %collective-permute-start.20 = (bf16[384,64]{1,0:T(8,128)(2,1)S(1)}, bf16[384,64]{1,0:T(8,128)(2,1)S(1)}, u32[]{:S(2)}, u32[]{:S(2)}) collective-permute-start(bf16[384,64]{1,0:T(8,128)(2,1)S(1)} %maximum_select_fusion.16), channel_id=1, source_target_pairs={{0,32},{16,48},{32,0},{48,16},{64,96},{80,112},{96,64},{112,80},{1... | collective-permute-start | bytes 147464 | tf_op jit(solution)/shard_map/ppermute | solution.py:42
  106.5 7.5 %collective-permute-start.10 = (f32[192,64]{0,1:T(8,128)S(1)}, f32[192,64]{0,1:T(8,128)S(1)}, u32[]{:S(2)}, u32[]{:S(2)}) collective-permute-start(f32[192,64]{0,1:T(8,128)S(1)} %slice_select_fusion.9), channel_id=1, source_target_pairs={{0,2},{1,3},{2,0},{3,1},{4,6},{5,7},{6,4},{7,5},{8,10},{9,11},{10,... | collective-permute-start | bytes 147464 | tf_op jit(solution)/shard_map/ppermute | solution.py:60
  111.2 8.2 %collective-permute-start.21 = (bf16[768,64]{1,0:T(8,128)(2,1)S(1)}, bf16[768,64]{1,0:T(8,128)(2,1)S(1)}, u32[]{:S(2)}, u32[]{:S(2)}) collective-permute-start(bf16[768,64]{1,0:T(8,128)(2,1)S(1)} %maximum_select_fusion.11), channel_id=1, source_target_pairs={{0,16},{16,0},{32,48},{48,32},{64,80},{80,64},{96,112},{112,96},{1... | collective-permute-start | bytes 294920 | tf_op jit(solution)/shard_map/ppermute | solution.py:42
  114.2 7.4 %collective-permute-start.11 = (f32[96,64]{0,1:T(8,128)S(1)}, f32[96,64]{0,1:T(8,128)S(1)}, u32[]{:S(2)}, u32[]{:S(2)}) collective-permute-start(f32[96,64]{0,1:T(8,128)S(1)} %slice_select_fusion.19), channel_id=1, source_target_pairs={{0,4},{1,5},{2,6},{3,7},{4,0},{5,1},{6,2},{7,3},{8,12},{9,13},{10,... | collective-permute-start | bytes 73736 | tf_op jit(solution)/shard_map/ppermute | solution.py:60
  121.8 14.5 %collective-permute-start.12 = (f32[48,64]{0,1:T(8,128)S(1)}, f32[48,64]{0,1:T(8,128)S(1)}, u32[]{:S(2)}, u32[]{:S(2)}) collective-permute-start(f32[48,64]{0,1:T(8,128)S(1)} %slice_select_fusion.18), channel_id=1, source_target_pairs={{0,8},{1,9},{2,10},{3,11},{4,12},{5,13},{6,14},{7,15},{8,0},{9,1},... | collective-permute-start | bytes 36872 | tf_op jit(solution)/shard_map/ppermute | solution.py:60
  123.7 19.1 %collective-permute-start.22 = (f32[384,64]{0,1:T(8,128)S(1)}, f32[384,64]{0,1:T(8,128)S(1)}, u32[]{:S(2)}, u32[]{:S(2)}) collective-permute-start(f32[384,64]{0,1:T(8,128)S(1)} %slice_select_fusion.3), channel_id=1, source_target_pairs={{0,1},{1,0},{2,3},{3,2},{4,5},{5,4},{6,7},{7,6},{8,9},{9,8},{10,11... | collective-permute-start | bytes 294920 | tf_op jit(solution)/shard_map/ppermute | solution.py:60
  137.0 7.9 %collective-permute-start.14 = (bf16[64,384]{1,0:T(8,128)(2,1)S(1)}, bf16[64,384]{1,0:T(8,128)(2,1)S(1)}, u32[]{:S(2)}, u32[]{:S(2)}) collective-permute-start(bf16[64,384]{1,0:T(8,128)(2,1)S(1)} %get-tuple-element.20), channel_id=1, source_target_pairs={{16,0},{32,16},{48,32},{64,48},{80,64},{96,80},{112,96},{128,112},... | collective-permute-start | bytes 147464 | tf_op jit(solution)/shard_map/ppermute | solution.py:16
  138.3 6.6 %collective-permute-start.13 = (bf16[64,384]{1,0:T(8,128)(2,1)S(1)}, bf16[64,384]{1,0:T(8,128)(2,1)S(1)}, u32[]{:S(2)}, u32[]{:S(2)}) collective-permute-start(bf16[64,384]{1,0:T(8,128)(2,1)S(1)} %get-tuple-element.19), channel_id=1, source_target_pairs={{0,16},{16,32},{32,48},{48,64},{64,80},{80,96},{96,112},{112,128},... | collective-permute-start | bytes 147464 | tf_op jit(solution)/shard_map/ppermute | solution.py:16
  143.0 6.2 %collective-permute-start.23 = (f32[192,64]{0,1:T(8,128)S(1)}, f32[192,64]{0,1:T(8,128)S(1)}, u32[]{:S(2)}, u32[]{:S(2)}) collective-permute-start(f32[192,64]{0,1:T(8,128)S(1)} %slice_select_fusion.8), channel_id=1, source_target_pairs={{0,2},{1,3},{2,0},{3,1},{4,6},{5,7},{6,4},{7,5},{8,10},{9,11},{10,... | collective-permute-start | bytes 147464 | tf_op jit(solution)/shard_map/ppermute | solution.py:60
  145.0 14.5 %collective-permute-start.15 = (bf16[64,384]{1,0:T(8,128)(2,1)S(1)}, bf16[64,384]{1,0:T(8,128)(2,1)S(1)}, u32[]{:S(2)}, u32[]{:S(2)}) collective-permute-start(bf16[64,384]{1,0:T(8,128)(2,1)S(1)} %pad_maximum_fusion.3), channel_id=1, source_target_pairs={{0,1},{1,2},{2,3},{3,4},{4,5},{5,6},{6,7},{7,8},{8,9},{9,10},{10,1... | collective-permute-start | bytes 147464 | tf_op jit(solution)/shard_map/ppermute | solution.py:16
  149.3 7.3 %collective-permute-start.24 = (f32[96,64]{0,1:T(8,128)S(1)}, f32[96,64]{0,1:T(8,128)S(1)}, u32[]{:S(2)}, u32[]{:S(2)}) collective-permute-start(f32[96,64]{0,1:T(8,128)S(1)} %slice_select_fusion.17), channel_id=1, source_target_pairs={{0,4},{1,5},{2,6},{3,7},{4,0},{5,1},{6,2},{7,3},{8,12},{9,13},{10,... | collective-permute-start | bytes 73736 | tf_op jit(solution)/shard_map/ppermute | solution.py:60
  151.6 7.9 %collective-permute-start.16 = (bf16[64,384]{1,0:T(8,128)(2,1)S(1)}, bf16[64,384]{1,0:T(8,128)(2,1)S(1)}, u32[]{:S(2)}, u32[]{:S(2)}) collective-permute-start(bf16[64,384]{1,0:T(8,128)(2,1)S(1)} %pad_maximum_fusion.4), channel_id=1, source_target_pairs={{1,0},{2,1},{3,2},{4,3},{5,4},{6,5},{7,6},{8,7},{9,8},{10,9},{11,1... | collective-permute-start | bytes 147464 | tf_op jit(solution)/shard_map/ppermute | solution.py:16
  156.8 15.1 %collective-permute-start.25 = (f32[48,64]{0,1:T(8,128)S(1)}, f32[48,64]{0,1:T(8,128)S(1)}, u32[]{:S(2)}, u32[]{:S(2)}) collective-permute-start(f32[48,64]{0,1:T(8,128)S(1)} %slice_select_fusion.16), channel_id=1, source_target_pairs={{0,8},{1,9},{2,10},{3,11},{4,12},{5,13},{6,14},{7,15},{8,0},{9,1},... | collective-permute-start | bytes 36872 | tf_op jit(solution)/shard_map/ppermute | solution.py:60
  160.7 11.8 %collective-permute-start.30 = (bf16[48,64]{1,0:T(8,128)(2,1)S(1)}, bf16[48,64]{1,0:T(8,128)(2,1)S(1)}, u32[]{:S(2)}, u32[]{:S(2)}) collective-permute-start(bf16[48,64]{1,0:T(8,128)(2,1)S(1)} %fusion.57), channel_id=1, source_target_pairs={{0,256},{16,272},{32,288},{48,304},{64,320},{80,336},{96,352},{112... | collective-permute-start | bytes 18440 | tf_op jit(solution)/shard_map/ppermute | solution.py:42
  172.5 6.6 %collective-permute-start.31 = (bf16[96,64]{1,0:T(8,128)(2,1)S(1)}, bf16[96,64]{1,0:T(8,128)(2,1)S(1)}, u32[]{:S(2)}, u32[]{:S(2)}) collective-permute-start(bf16[96,64]{1,0:T(8,128)(2,1)S(1)} %maximum_select_fusion.27), channel_id=1, source_target_pairs={{0,128},{16,144},{32,160},{48,176},{64,192},{80,208},{96,224},{112... | collective-permute-start | bytes 36872 | tf_op jit(solution)/shard_map/ppermute | solution.py:42
  179.1 9.6 %collective-permute-start.32 = (bf16[192,64]{1,0:T(8,128)(2,1)S(1)}, bf16[192,64]{1,0:T(8,128)(2,1)S(1)}, u32[]{:S(2)}, u32[]{:S(2)}) collective-permute-start(bf16[192,64]{1,0:T(8,128)(2,1)S(1)} %maximum_select_fusion.22), channel_id=1, source_target_pairs={{0,64},{16,80},{32,96},{48,112},{64,0},{80,16},{96,32},{112,48},{1... | collective-permute-start | bytes 73736 | tf_op jit(solution)/shard_map/ppermute | solution.py:42
  182.9 9.8 %collective-permute-start.27 = (bf16[64,384]{1,0:T(8,128)(2,1)S(1)}, bf16[64,384]{1,0:T(8,128)(2,1)S(1)}, u32[]{:S(2)}, u32[]{:S(2)}) collective-permute-start(bf16[64,384]{1,0:T(8,128)(2,1)S(1)} %get-tuple-element.16), channel_id=1, source_target_pairs={{16,0},{32,16},{48,32},{64,48},{80,64},{96,80},{112,96},{128,112},... | collective-permute-start | bytes 147464 | tf_op jit(solution)/shard_map/ppermute | solution.py:16
  184.2 8.6 %collective-permute-start.26 = (bf16[64,384]{1,0:T(8,128)(2,1)S(1)}, bf16[64,384]{1,0:T(8,128)(2,1)S(1)}, u32[]{:S(2)}, u32[]{:S(2)}) collective-permute-start(bf16[64,384]{1,0:T(8,128)(2,1)S(1)} %get-tuple-element.15), channel_id=1, source_target_pairs={{0,16},{16,32},{32,48},{48,64},{64,80},{80,96},{96,112},{112,128},... | collective-permute-start | bytes 147464 | tf_op jit(solution)/shard_map/ppermute | solution.py:16
  188.8 30.3 %collective-permute-start.33 = (bf16[384,64]{1,0:T(8,128)(2,1)S(1)}, bf16[384,64]{1,0:T(8,128)(2,1)S(1)}, u32[]{:S(2)}, u32[]{:S(2)}) collective-permute-start(bf16[384,64]{1,0:T(8,128)(2,1)S(1)} %maximum_select_fusion.17), channel_id=1, source_target_pairs={{0,32},{16,48},{32,0},{48,16},{64,96},{80,112},{96,64},{112,80},{1... | collective-permute-start | bytes 147464 | tf_op jit(solution)/shard_map/ppermute | solution.py:42
  192.8 10.0 %collective-permute-start.28 = (bf16[64,384]{1,0:T(8,128)(2,1)S(1)}, bf16[64,384]{1,0:T(8,128)(2,1)S(1)}, u32[]{:S(2)}, u32[]{:S(2)}) collective-permute-start(bf16[64,384]{1,0:T(8,128)(2,1)S(1)} %pad_maximum_fusion.5), channel_id=1, source_target_pairs={{0,1},{1,2},{2,3},{3,4},{4,5},{5,6},{6,7},{7,8},{8,9},{9,10},{10,1... | collective-permute-start | bytes 147464 | tf_op jit(solution)/shard_map/ppermute | solution.py:16
  200.9 7.0 %collective-permute-start.29 = (bf16[64,384]{1,0:T(8,128)(2,1)S(1)}, bf16[64,384]{1,0:T(8,128)(2,1)S(1)}, u32[]{:S(2)}, u32[]{:S(2)}) collective-permute-start(bf16[64,384]{1,0:T(8,128)(2,1)S(1)} %pad_maximum_fusion.6), channel_id=1, source_target_pairs={{1,0},{2,1},{3,2},{4,3},{5,4},{6,5},{7,6},{8,7},{9,8},{10,9},{11,1... | collective-permute-start | bytes 147464 | tf_op jit(solution)/shard_map/ppermute | solution.py:16
  208.8 12.4 %collective-permute-start.43 = (bf16[48,64]{1,0:T(8,128)(2,1)S(1)}, bf16[48,64]{1,0:T(8,128)(2,1)S(1)}, u32[]{:S(2)}, u32[]{:S(2)}) collective-permute-start(bf16[48,64]{1,0:T(8,128)(2,1)S(1)} %fusion.58), channel_id=1, source_target_pairs={{0,256},{16,272},{32,288},{48,304},{64,320},{80,336},{96,352},{112... | collective-permute-start | bytes 18440 | tf_op jit(solution)/shard_map/ppermute | solution.py:42
  219.2 11.9 %collective-permute-start.34 = (bf16[768,64]{1,0:T(8,128)(2,1)S(1)}, bf16[768,64]{1,0:T(8,128)(2,1)S(1)}, u32[]{:S(2)}, u32[]{:S(2)}) collective-permute-start(bf16[768,64]{1,0:T(8,128)(2,1)S(1)} %maximum_select_fusion.12), channel_id=1, source_target_pairs={{0,16},{16,0},{32,48},{48,32},{64,80},{80,64},{96,112},{112,96},{1... | collective-permute-start | bytes 294920 | tf_op jit(solution)/shard_map/ppermute | solution.py:42
  221.2 6.6 %collective-permute-start.44 = (bf16[96,64]{1,0:T(8,128)(2,1)S(1)}, bf16[96,64]{1,0:T(8,128)(2,1)S(1)}, u32[]{:S(2)}, u32[]{:S(2)}) collective-permute-start(bf16[96,64]{1,0:T(8,128)(2,1)S(1)} %maximum_select_fusion.28), channel_id=1, source_target_pairs={{0,128},{16,144},{32,160},{48,176},{64,192},{80,208},{96,224},{112... | collective-permute-start | bytes 36872 | tf_op jit(solution)/shard_map/ppermute | solution.py:42
  227.8 17.3 %collective-permute-start.45 = (bf16[192,64]{1,0:T(8,128)(2,1)S(1)}, bf16[192,64]{1,0:T(8,128)(2,1)S(1)}, u32[]{:S(2)}, u32[]{:S(2)}) collective-permute-start(bf16[192,64]{1,0:T(8,128)(2,1)S(1)} %maximum_select_fusion.23), channel_id=1, source_target_pairs={{0,64},{16,80},{32,96},{48,112},{64,0},{80,16},{96,32},{112,48},{1... | collective-permute-start | bytes 73736 | tf_op jit(solution)/shard_map/ppermute | solution.py:42
  231.7 16.7 %collective-permute-start.35 = (f32[384,64]{0,1:T(8,128)S(1)}, f32[384,64]{0,1:T(8,128)S(1)}, u32[]{:S(2)}, u32[]{:S(2)}) collective-permute-start(f32[384,64]{0,1:T(8,128)S(1)} %slice_select_fusion.2), channel_id=1, source_target_pairs={{0,1},{1,0},{2,3},{3,2},{4,5},{5,4},{6,7},{7,6},{8,9},{9,8},{10,11... | collective-permute-start | bytes 294920 | tf_op jit(solution)/shard_map/ppermute | solution.py:60
  245.1 8.1 %collective-permute-start.46 = (bf16[384,64]{1,0:T(8,128)(2,1)S(1)}, bf16[384,64]{1,0:T(8,128)(2,1)S(1)}, u32[]{:S(2)}, u32[]{:S(2)}) collective-permute-start(bf16[384,64]{1,0:T(8,128)(2,1)S(1)} %maximum_select_fusion.18), channel_id=1, source_target_pairs={{0,32},{16,48},{32,0},{48,16},{64,96},{80,112},{96,64},{112,80},{1... | collective-permute-start | bytes 147464 | tf_op jit(solution)/shard_map/ppermute | solution.py:42
  248.6 8.5 %collective-permute-start.36 = (f32[192,64]{0,1:T(8,128)S(1)}, f32[192,64]{0,1:T(8,128)S(1)}, u32[]{:S(2)}, u32[]{:S(2)}) collective-permute-start(f32[192,64]{0,1:T(8,128)S(1)} %slice_select_fusion.7), channel_id=1, source_target_pairs={{0,2},{1,3},{2,0},{3,1},{4,6},{5,7},{6,4},{7,5},{8,10},{9,11},{10,... | collective-permute-start | bytes 147464 | tf_op jit(solution)/shard_map/ppermute | solution.py:60
  253.3 7.9 %collective-permute-start.47 = (bf16[768,64]{1,0:T(8,128)(2,1)S(1)}, bf16[768,64]{1,0:T(8,128)(2,1)S(1)}, u32[]{:S(2)}, u32[]{:S(2)}) collective-permute-start(bf16[768,64]{1,0:T(8,128)(2,1)S(1)} %maximum_select_fusion.13), channel_id=1, source_target_pairs={{0,16},{16,0},{32,48},{48,32},{64,80},{80,64},{96,112},{112,96},{1... | collective-permute-start | bytes 294920 | tf_op jit(solution)/shard_map/ppermute | solution.py:42
  257.2 7.3 %collective-permute-start.37 = (f32[96,64]{0,1:T(8,128)S(1)}, f32[96,64]{0,1:T(8,128)S(1)}, u32[]{:S(2)}, u32[]{:S(2)}) collective-permute-start(f32[96,64]{0,1:T(8,128)S(1)} %slice_select_fusion.15), channel_id=1, source_target_pairs={{0,4},{1,5},{2,6},{3,7},{4,0},{5,1},{6,2},{7,3},{8,12},{9,13},{10,... | collective-permute-start | bytes 73736 | tf_op jit(solution)/shard_map/ppermute | solution.py:60
  264.7 14.7 %collective-permute-start.38 = (f32[48,64]{0,1:T(8,128)S(1)}, f32[48,64]{0,1:T(8,128)S(1)}, u32[]{:S(2)}, u32[]{:S(2)}) collective-permute-start(f32[48,64]{0,1:T(8,128)S(1)} %slice_select_fusion.14), channel_id=1, source_target_pairs={{0,8},{1,9},{2,10},{3,11},{4,12},{5,13},{6,14},{7,15},{8,0},{9,1},... | collective-permute-start | bytes 36872 | tf_op jit(solution)/shard_map/ppermute | solution.py:60
  266.6 19.3 %collective-permute-start.48 = (f32[384,64]{0,1:T(8,128)S(1)}, f32[384,64]{0,1:T(8,128)S(1)}, u32[]{:S(2)}, u32[]{:S(2)}) collective-permute-start(f32[384,64]{0,1:T(8,128)S(1)} %slice_select_fusion.1), channel_id=1, source_target_pairs={{0,1},{1,0},{2,3},{3,2},{4,5},{5,4},{6,7},{7,6},{8,9},{9,8},{10,11... | collective-permute-start | bytes 294920 | tf_op jit(solution)/shard_map/ppermute | solution.py:60
  280.0 7.9 %collective-permute-start.40 = (bf16[64,384]{1,0:T(8,128)(2,1)S(1)}, bf16[64,384]{1,0:T(8,128)(2,1)S(1)}, u32[]{:S(2)}, u32[]{:S(2)}) collective-permute-start(bf16[64,384]{1,0:T(8,128)(2,1)S(1)} %get-tuple-element.12), channel_id=1, source_target_pairs={{16,0},{32,16},{48,32},{64,48},{80,64},{96,80},{112,96},{128,112},... | collective-permute-start | bytes 147464 | tf_op jit(solution)/shard_map/ppermute | solution.py:16
  281.3 6.6 %collective-permute-start.39 = (bf16[64,384]{1,0:T(8,128)(2,1)S(1)}, bf16[64,384]{1,0:T(8,128)(2,1)S(1)}, u32[]{:S(2)}, u32[]{:S(2)}) collective-permute-start(bf16[64,384]{1,0:T(8,128)(2,1)S(1)} %get-tuple-element.11), channel_id=1, source_target_pairs={{0,16},{16,32},{32,48},{48,64},{64,80},{80,96},{96,112},{112,128},... | collective-permute-start | bytes 147464 | tf_op jit(solution)/shard_map/ppermute | solution.py:16
  286.0 6.2 %collective-permute-start.49 = (f32[192,64]{0,1:T(8,128)S(1)}, f32[192,64]{0,1:T(8,128)S(1)}, u32[]{:S(2)}, u32[]{:S(2)}) collective-permute-start(f32[192,64]{0,1:T(8,128)S(1)} %slice_select_fusion.6), channel_id=1, source_target_pairs={{0,2},{1,3},{2,0},{3,1},{4,6},{5,7},{6,4},{7,5},{8,10},{9,11},{10,... | collective-permute-start | bytes 147464 | tf_op jit(solution)/shard_map/ppermute | solution.py:60
  288.0 13.7 %collective-permute-start.41 = (bf16[64,384]{1,0:T(8,128)(2,1)S(1)}, bf16[64,384]{1,0:T(8,128)(2,1)S(1)}, u32[]{:S(2)}, u32[]{:S(2)}) collective-permute-start(bf16[64,384]{1,0:T(8,128)(2,1)S(1)} %pad_maximum_fusion.7), channel_id=1, source_target_pairs={{0,1},{1,2},{2,3},{3,4},{4,5},{5,6},{6,7},{7,8},{8,9},{9,10},{10,1... | collective-permute-start | bytes 147464 | tf_op jit(solution)/shard_map/ppermute | solution.py:16
  292.3 7.3 %collective-permute-start.50 = (f32[96,64]{0,1:T(8,128)S(1)}, f32[96,64]{0,1:T(8,128)S(1)}, u32[]{:S(2)}, u32[]{:S(2)}) collective-permute-start(f32[96,64]{0,1:T(8,128)S(1)} %slice_select_fusion.13), channel_id=1, source_target_pairs={{0,4},{1,5},{2,6},{3,7},{4,0},{5,1},{6,2},{7,3},{8,12},{9,13},{10,... | collective-permute-start | bytes 73736 | tf_op jit(solution)/shard_map/ppermute | solution.py:60
  294.5 7.2 %collective-permute-start.42 = (bf16[64,384]{1,0:T(8,128)(2,1)S(1)}, bf16[64,384]{1,0:T(8,128)(2,1)S(1)}, u32[]{:S(2)}, u32[]{:S(2)}) collective-permute-start(bf16[64,384]{1,0:T(8,128)(2,1)S(1)} %pad_maximum_fusion.8), channel_id=1, source_target_pairs={{1,0},{2,1},{3,2},{4,3},{5,4},{6,5},{7,6},{8,7},{9,8},{10,9},{11,1... | collective-permute-start | bytes 147464 | tf_op jit(solution)/shard_map/ppermute | solution.py:16
  299.8 15.9 %collective-permute-start.51 = (f32[48,64]{0,1:T(8,128)S(1)}, f32[48,64]{0,1:T(8,128)S(1)}, u32[]{:S(2)}, u32[]{:S(2)}) collective-permute-start(f32[48,64]{0,1:T(8,128)S(1)} %slice_select_fusion.12), channel_id=1, source_target_pairs={{0,8},{1,9},{2,10},{3,11},{4,12},{5,13},{6,14},{7,15},{8,0},{9,1},... | collective-permute-start | bytes 36872 | tf_op jit(solution)/shard_map/ppermute | solution.py:60
  302.9 13.7 %collective-permute-start.56 = (bf16[48,64]{1,0:T(8,128)(2,1)S(1)}, bf16[48,64]{1,0:T(8,128)(2,1)S(1)}, u32[]{:S(2)}, u32[]{:S(2)}) collective-permute-start(bf16[48,64]{1,0:T(8,128)(2,1)S(1)} %fusion.59), channel_id=1, source_target_pairs={{0,256},{16,272},{32,288},{48,304},{64,320},{80,336},{96,352},{112... | collective-permute-start | bytes 18440 | tf_op jit(solution)/shard_map/ppermute | solution.py:42
  316.6 6.6 %collective-permute-start.57 = (bf16[96,64]{1,0:T(8,128)(2,1)S(1)}, bf16[96,64]{1,0:T(8,128)(2,1)S(1)}, u32[]{:S(2)}, u32[]{:S(2)}) collective-permute-start(bf16[96,64]{1,0:T(8,128)(2,1)S(1)} %maximum_select_fusion.29), channel_id=1, source_target_pairs={{0,128},{16,144},{32,160},{48,176},{64,192},{80,208},{96,224},{112... | collective-permute-start | bytes 36872 | tf_op jit(solution)/shard_map/ppermute | solution.py:42
  323.2 8.6 %collective-permute-start.58 = (bf16[192,64]{1,0:T(8,128)(2,1)S(1)}, bf16[192,64]{1,0:T(8,128)(2,1)S(1)}, u32[]{:S(2)}, u32[]{:S(2)}) collective-permute-start(bf16[192,64]{1,0:T(8,128)(2,1)S(1)} %maximum_select_fusion.24), channel_id=1, source_target_pairs={{0,64},{16,80},{32,96},{48,112},{64,0},{80,16},{96,32},{112,48},{1... | collective-permute-start | bytes 73736 | tf_op jit(solution)/shard_map/ppermute | solution.py:42
  326.0 9.4 %collective-permute-start.53 = (bf16[64,384]{1,0:T(8,128)(2,1)S(1)}, bf16[64,384]{1,0:T(8,128)(2,1)S(1)}, u32[]{:S(2)}, u32[]{:S(2)}) collective-permute-start(bf16[64,384]{1,0:T(8,128)(2,1)S(1)} %get-tuple-element.8), channel_id=1, source_target_pairs={{16,0},{32,16},{48,32},{64,48},{80,64},{96,80},{112,96},{128,112},... | collective-permute-start | bytes 147464 | tf_op jit(solution)/shard_map/ppermute | solution.py:16
  327.3 8.1 %collective-permute-start.52 = (bf16[64,384]{1,0:T(8,128)(2,1)S(1)}, bf16[64,384]{1,0:T(8,128)(2,1)S(1)}, u32[]{:S(2)}, u32[]{:S(2)}) collective-permute-start(bf16[64,384]{1,0:T(8,128)(2,1)S(1)} %get-tuple-element.7), channel_id=1, source_target_pairs={{0,16},{16,32},{32,48},{48,64},{64,80},{80,96},{96,112},{112,128},... | collective-permute-start | bytes 147464 | tf_op jit(solution)/shard_map/ppermute | solution.py:16
  331.9 14.7 %collective-permute-start.59 = (bf16[384,64]{1,0:T(8,128)(2,1)S(1)}, bf16[384,64]{1,0:T(8,128)(2,1)S(1)}, u32[]{:S(2)}, u32[]{:S(2)}) collective-permute-start(bf16[384,64]{1,0:T(8,128)(2,1)S(1)} %maximum_select_fusion.19), channel_id=1, source_target_pairs={{0,32},{16,48},{32,0},{48,16},{64,96},{80,112},{96,64},{112,80},{1... | collective-permute-start | bytes 147464 | tf_op jit(solution)/shard_map/ppermute | solution.py:42
  335.5 16.3 %collective-permute-start.54 = (bf16[64,384]{1,0:T(8,128)(2,1)S(1)}, bf16[64,384]{1,0:T(8,128)(2,1)S(1)}, u32[]{:S(2)}, u32[]{:S(2)}) collective-permute-start(bf16[64,384]{1,0:T(8,128)(2,1)S(1)} %pad_maximum_fusion.9), channel_id=1, source_target_pairs={{0,1},{1,2},{2,3},{3,4},{4,5},{5,6},{6,7},{7,8},{8,9},{9,10},{10,1... | collective-permute-start | bytes 147464 | tf_op jit(solution)/shard_map/ppermute | solution.py:16
  344.7 16.0 %collective-permute-start.55 = (bf16[64,384]{1,0:T(8,128)(2,1)S(1)}, bf16[64,384]{1,0:T(8,128)(2,1)S(1)}, u32[]{:S(2)}, u32[]{:S(2)}) collective-permute-start(bf16[64,384]{1,0:T(8,128)(2,1)S(1)} %pad_maximum_fusion.10), channel_id=1, source_target_pairs={{1,0},{2,1},{3,2},{4,3},{5,4},{6,5},{7,6},{8,7},{9,8},{10,9},{11,1... | collective-permute-start | bytes 147464 | tf_op jit(solution)/shard_map/ppermute | solution.py:16
  346.7 8.8 %collective-permute-start.60 = (bf16[768,64]{1,0:T(8,128)(2,1)S(1)}, bf16[768,64]{1,0:T(8,128)(2,1)S(1)}, u32[]{:S(2)}, u32[]{:S(2)}) collective-permute-start(bf16[768,64]{1,0:T(8,128)(2,1)S(1)} %maximum_select_fusion.14), channel_id=1, source_target_pairs={{0,16},{16,0},{32,48},{48,32},{64,80},{80,64},{96,112},{112,96},{1... | collective-permute-start | bytes 294920 | tf_op jit(solution)/shard_map/ppermute | solution.py:42
  361.7 6.2 %collective-permute-start.62 = (f32[192,64]{0,1:T(8,128)S(1)}, f32[192,64]{0,1:T(8,128)S(1)}, u32[]{:S(2)}, u32[]{:S(2)}) collective-permute-start(f32[192,64]{0,1:T(8,128)S(1)} %slice_select_fusion.5), channel_id=1, source_target_pairs={{0,2},{1,3},{2,0},{3,1},{4,6},{5,7},{6,4},{7,5},{8,10},{9,11},{10,... | collective-permute-start | bytes 147464 | tf_op jit(solution)/shard_map/ppermute | solution.py:60
  368.0 7.3 %collective-permute-start.63 = (f32[96,64]{0,1:T(8,128)S(1)}, f32[96,64]{0,1:T(8,128)S(1)}, u32[]{:S(2)}, u32[]{:S(2)}) collective-permute-start(f32[96,64]{0,1:T(8,128)S(1)} %slice_select_fusion.11), channel_id=1, source_target_pairs={{0,4},{1,5},{2,6},{3,7},{4,0},{5,1},{6,2},{7,3},{8,12},{9,13},{10,... | collective-permute-start | bytes 73736 | tf_op jit(solution)/shard_map/ppermute | solution.py:60
  377.6 15.8 %collective-permute-start.64 = (f32[48,64]{0,1:T(8,128)}, f32[48,64]{0,1:T(8,128)}, u32[]{:S(2)}, u32[]{:S(2)}) collective-permute-start(f32[48,64]{0,1:T(8,128)} %slice_select_fusion.10), channel_id=1, source_target_pairs={{0,8},{1,9},{2,10},{3,11},{4,12},{5,13},{6,14},{7,15},{8,0},{9,1},... | collective-permute-start | bytes 36872 | tf_op jit(solution)/shard_map/ppermute | solution.py:60
  (27 other events, 568.8 us)

commit v8 on v7

--- a/solution.py
+++ b/solution.py
@@ -16,9 +16,19 @@
     return lax.ppermute(block, axis, route)
 
 
-def neighbour_pieces(outgoing, width):
-    from_above = shifted(outgoing[:, 0 : 3 * width], "row", -1)
-    from_below = shifted(outgoing[:, 3 * width : 6 * width], "row", 1)
+def neighbour_pieces(outgoing, width, piece):
+    count = outgoing.shape[0]
+    padded = jnp.pad(piece, ((0, 0), (0, 3 * width - piece.shape[1])))
+    from_above = shifted(jnp.concatenate([outgoing[:, 0 : 3 * width], padded], 0), "row", -1)
+    from_below = shifted(jnp.concatenate([outgoing[:, 3 * width : 6 * width], padded], 0), "row", 1)
+    piece_above = from_above[count:, : piece.shape[1]]
+    piece_below = from_below[count:, : piece.shape[1]]
+    from_above = from_above[:count]
+    from_below = from_below[:count]
+    odd = (lax.axis_index("row") & 1) == 1
+    pair = jnp.where(
+        odd, jnp.concatenate([piece_above, piece], 0), jnp.concatenate([piece, piece_below], 0)
+    )
     to_right = jnp.concatenate(
         [from_above[:, :width], outgoing[:, 6 * width : 7 * width], from_below[:, :width]], 1
     )
@@ -27,17 +37,23 @@
     )
     from_left = shifted(to_right, "col", -1)
     from_right = shifted(to_left, "col", 1)
-    return jnp.concatenate(
+    incoming = jnp.concatenate(
         [from_left, from_right, from_above[:, width : 2 * width], from_below[:, width : 2 * width]],
         1,
     )
+    return incoming, pair
 
 
-def gather_rows(piece):
+def gather_order(size):
+    bits = size.bit_length() - 1
+    return [0] + list(range(bits - 1, 0, -1))
+
+
+def gather_rows(pair):
     index = lax.axis_index("row")
     size = lax.axis_size("row")
-    current = piece
-    for bit in range(size.bit_length() - 2, -1, -1):
+    current = pair
+    for bit in gather_order(size)[1:]:
         route = [(i, i ^ (1 << bit)) for i in range(size)]
         other = lax.ppermute(current, "row", route)
         high = ((index >> bit) & 1) == 1
@@ -61,10 +77,9 @@
     return current
 
 
-def reversed_blocks(count, block):
-    bits = count.bit_length() - 1
-    order = [int(format(i, f"0{bits}b")[::-1], 2) if bits else 0 for i in range(count)]
-    return np.array([order[i // block] * block + i % block for i in range(count * block)])
+def reversed_blocks(count, block, order):
+    source = [sum(((i >> t) & 1) << bit for t, bit in enumerate(order)) for i in range(count)]
+    return np.array([source[i // block] * block + i % block for i in range(count * block)])
 
 
 def on_device(
@@ -108,25 +123,28 @@
     rows = lax.axis_size("row")
     cols = lax.axis_size("col")
     tile = coarse_inverse[0, :, 0, :]
-    from_rows = reversed_blocks(rows, mode_count)
-    from_cols = reversed_blocks(cols, mode_count)
+    from_rows = reversed_blocks(rows, mode_count, gather_order(rows))
+    from_cols = reversed_blocks(cols, mode_count, list(range(cols.bit_length() - 2, -1, -1)))
     pick_rows = (jnp.arange(rows * mode_count)[None, :] == from_rows[:, None]).astype(jnp.bfloat16)
     pick_cols = (jnp.arange(cols * mode_count)[:, None] == from_cols[None, :]).astype(jnp.bfloat16)
     tile = jnp.dot(pick_rows, tile, preferred_element_type=jnp.float32).astype(jnp.bfloat16)
     tile = jnp.dot(tile, pick_cols, preferred_element_type=jnp.float32).astype(jnp.bfloat16)
     coarse_matrix = tile.T
 
-    def coarse_solve(rounded):
-        restricted = lax.dot_general(
+    def restrict(rounded):
+        return lax.dot_general(
             mode_basis, rounded, (((1,), (1,)), ((), ())), preferred_element_type=jnp.float32
         ).astype(jnp.bfloat16)
-        gathered = gather_rows(restricted)
+
+    def coarse_solve(pair):
+        gathered = gather_rows(pair)
         partial_sums = jnp.dot(coarse_matrix, gathered, preferred_element_type=jnp.float32)
         return scatter_cols(partial_sums).astype(jnp.bfloat16)
 
     solution = jnp.zeros((columns, unknowns), jnp.float32)
-    pending = None
+    carried = None
     for iteration in range(ITERS):
+        coarse = None
         if iteration == 0:
             residual = rhs_full
         else:
@@ -134,20 +152,21 @@
             outgoing = jnp.dot(field_half, select, preferred_element_type=jnp.float32).astype(
                 jnp.bfloat16
             )
-            incoming = neighbour_pieces(outgoing, block_size)
+            incoming, pair = neighbour_pieces(outgoing, block_size, carried)
+            coarse = coarse_solve(pair)
             stacked = jnp.concatenate([field_half, incoming], 1)
             residual = rhs_full - jnp.dot(
                 stacked, operator_matrix, preferred_element_type=jnp.float32
             )
         rounded = residual.astype(jnp.bfloat16)
         update = jnp.dot(rounded, solver_matrix, preferred_element_type=jnp.float32)
-        fresh = coarse_solve(rounded) if iteration + 1 < ITERS else None
-        if pending is not None:
+        if iteration + 1 < ITERS:
+            carried = restrict(rounded)
+        if coarse is not None:
             update = update + lax.dot_general(
-                pending, mode_basis, (((0,), (0,)), ((), ())), preferred_element_type=jnp.float32
+                coarse, mode_basis, (((0,), (0,)), ((), ())), preferred_element_type=jnp.float32
             )
         solution = solution + update
-        pending = fresh
     return solution[None, None]
 
 

time: 402 us -> 457 us (1.14)
  waiting for transfers between devices: 89.9 us -> 154 us
  starting transfers between devices: 258 us -> 248 us
    ppermute x20, waiting for transfers between devices: 54.6 us -> 88.8 us  [scatter_cols(): current = keep + lax.ppermute(send, 'col', route)]
    ppermute x20, starting transfers between devices: 64.1 us -> 43.1 us  [shifted(): return lax.ppermute(block, axis, route)]
    ppermute x20, starting transfers between devices: 76.4 us -> 94.3 us  [scatter_cols(): current = keep + lax.ppermute(send, 'col', route)]
    ppermute x25 -> x20, waiting for transfers between devices: 24.1 us -> 41.9 us  [gather_rows(): other = lax.ppermute(current, 'row', route)]
    ppermute x20, waiting for transfers between devices: 11.2 us -> 23 us  [shifted(): return lax.ppermute(block, axis, route)]
    ppermute x25 -> x20, starting transfers between devices: 118 us -> 110 us  [gather_rows(): other = lax.ppermute(current, 'row', route)]
  transfers between devices with their start and end apart: 65 -> 60, of which waited for: 25 -> 47; matrix products, arithmetic and copies ran while one was open for 8% -> 6% of each run, Pallas kernels for 0% -> 0%
where the time goes in v8:
time: 457 us; the launch traced here: 451 us
  starting transfers between devices  248 us (54%)
  waiting for transfers between devices  154 us (34%)
  matrix products  26.5 us (6%)
  other arithmetic  10.5 us (2%)
  local copies, waits for them, and re-layouts  10.4 us (2%)
    ppermute x20, starting transfers between devices, gather_rows(): other = lax.ppermute(current, 'row', route)  110 us
    ppermute x20, starting transfers between devices, scatter_cols(): current = keep + lax.ppermute(send, 'col', route)  94.3 us
    ppermute x20, waiting for transfers between devices, scatter_cols(): current = keep + lax.ppermute(send, 'col', route)  88.8 us
    ppermute x20, starting transfers between devices, shifted(): return lax.ppermute(block, axis, route)  43.1 us
    ppermute x20, waiting for transfers between devices, gather_rows(): other = lax.ppermute(current, 'row', route)  41.9 us
    ppermute x20, waiting for transfers between devices, shifted(): return lax.ppermute(block, axis, route)  23 us
  transfers between devices with their start and end apart: 60, of which 47 were waited for; matrix products, arithmetic and copies ran while one was open for 6% of the time, Pallas kernels for 0%

profile of v8, /device:TPU:6, one launch (start us, length us, event | category | flops | bytes accessed | tf_op | source)
XLA Modules:
  0.0 450.5 jit_solution(4942345426294581435)
XLA Ops:
  3.2 2.3 constant_dynamic-update-slice_fusion.4
  8.2 4.1 collective-permute-start
  15.8 7.4 %convolution_convert_fusion = bf16[1536,768]{1,0:T(8,128)(2,1)} fusion(s32[768]{0:T(1024)S(1)} %copy-done.18, s32[1536]{0:T(1024)S(1)} %copy-done.17, bf16[1,1536,1,768]{3,1,2,0:T(8,128)(2,1)S(1)} %copy-done), kind=kOutput, calls=%fused_computation.5 | convolution fusion | flops 5441126400 | bytes 4727808 | tf_op jit(solution)/shard_map/dot_general | solution.py:131
  29.5 12.9 %collective-permute-start.4 = (bf16[96,64]{1,0:T(8,128)(2,1)S(1)}, bf16[96,64]{1,0:T(8,128)(2,1)S(1)}, u32[]{:S(2)}, u32[]{:S(2)}) collective-permute-start(bf16[96,64]{1,0:T(8,128)(2,1)S(1)} %maximum_select_fusion.25), channel_id=1, source_target_pairs={{0,256},{16,272},{32,288},{48,304},{64,320},{80,336},{96,352},{112... | collective-permute-start | bytes 36872 | tf_op jit(solution)/shard_map/ppermute | solution.py:58
  45.8 4.0 collective-permute-start.5
  49.8 3.4 collective-permute-start.3
  53.2 3.8 collective-permute-start.6
  60.9 3.2 collective-permute-start.7
  64.8 5.1 %collective-permute-done.7 = bf16[768,64]{1,0:T(8,128)(2,1)S(1)} collective-permute-done((bf16[768,64]{1,0:T(8,128)(2,1)S(1)}, bf16[768,64]{1,0:T(8,128)(2,1)S(1)}, u32[]{:S(2)}, u32[]{:S(2)}) %collective-permute-start.7) | collective-permute-done | bytes 98336 | tf_op jit(solution)/shard_map/ppermute | solution.py:58
  70.6 13.0 %collective-permute-start.8 = (f32[384,64]{0,1:T(8,128)S(1)}, f32[384,64]{0,1:T(8,128)S(1)}, u32[]{:S(2)}, u32[]{:S(2)}) collective-permute-start(f32[384,64]{0,1:T(8,128)S(1)} %slice_select_fusion.4), channel_id=1, source_target_pairs={{0,1},{1,0},{2,3},{3,2},{4,5},{5,4},{6,7},{7,6},{8,9},{9,8},{10,11... | collective-permute-start | bytes 294920 | tf_op jit(solution)/shard_map/ppermute | solution.py:76
  87.2 3.6 collective-permute-done.9
  93.3 5.0 %collective-permute-done.10 = f32[96,64]{0,1:T(8,128)S(1)} collective-permute-done((f32[96,64]{0,1:T(8,128)S(1)}, f32[96,64]{0,1:T(8,128)S(1)}, u32[]{:S(2)}, u32[]{:S(2)}) %collective-permute-start.10) | collective-permute-done | bytes 24608 | tf_op jit(solution)/shard_map/ppermute | solution.py:76
  98.5 5.6 %collective-permute-start.11 = (f32[48,64]{0,1:T(8,128)S(1)}, f32[48,64]{0,1:T(8,128)S(1)}, u32[]{:S(2)}, u32[]{:S(2)}) collective-permute-start(f32[48,64]{0,1:T(8,128)S(1)} %slice_select_fusion.18), channel_id=1, source_target_pairs={{0,8},{1,9},{2,10},{3,11},{4,12},{5,13},{6,14},{7,15},{8,0},{9,1},... | collective-permute-start | bytes 36872 | tf_op jit(solution)/shard_map/ppermute | solution.py:76
  104.3 9.5 %collective-permute-done.11 = f32[48,64]{0,1:T(8,128)S(1)} collective-permute-done((f32[48,64]{0,1:T(8,128)S(1)}, f32[48,64]{0,1:T(8,128)S(1)}, u32[]{:S(2)}, u32[]{:S(2)}) %collective-permute-start.11) | collective-permute-done | bytes 12320 | tf_op jit(solution)/shard_map/ppermute | solution.py:76
  117.9 4.3 collective-permute-done.13
  122.2 8.6 %collective-permute-start.16 = (bf16[96,64]{1,0:T(8,128)(2,1)S(1)}, bf16[96,64]{1,0:T(8,128)(2,1)S(1)}, u32[]{:S(2)}, u32[]{:S(2)}) collective-permute-start(bf16[96,64]{1,0:T(8,128)(2,1)S(1)} %maximum_select_fusion.26), channel_id=1, source_target_pairs={{0,256},{16,272},{32,288},{48,304},{64,320},{80,336},{96,352},{112... | collective-permute-start | bytes 36872 | tf_op jit(solution)/shard_map/ppermute | solution.py:58
  133.0 5.7 %collective-permute-start.17 = (bf16[192,64]{1,0:T(8,128)(2,1)S(1)}, bf16[192,64]{1,0:T(8,128)(2,1)S(1)}, u32[]{:S(2)}, u32[]{:S(2)}) collective-permute-start(bf16[192,64]{1,0:T(8,128)(2,1)S(1)} %maximum_select_fusion.21), channel_id=1, source_target_pairs={{0,128},{16,144},{32,160},{48,176},{64,192},{80,208},{96,224},{112... | collective-permute-start | bytes 73736 | tf_op jit(solution)/shard_map/ppermute | solution.py:58
  143.6 4.1 collective-permute-done.18
  147.8 4.6 %collective-permute-start.19 = (bf16[768,64]{1,0:T(8,128)(2,1)S(1)}, bf16[768,64]{1,0:T(8,128)(2,1)S(1)}, u32[]{:S(2)}, u32[]{:S(2)}) collective-permute-start(bf16[768,64]{1,0:T(8,128)(2,1)S(1)} %maximum_select_fusion.11), channel_id=1, source_target_pairs={{0,32},{16,48},{32,0},{48,16},{64,96},{80,112},{96,64},{112,80},{1... | collective-permute-start | bytes 294920 | tf_op jit(solution)/shard_map/ppermute | solution.py:58
  152.4 4.5 collective-permute-done.19
  157.5 10.3 %collective-permute-start.20 = (f32[384,64]{0,1:T(8,128)S(1)}, f32[384,64]{0,1:T(8,128)S(1)}, u32[]{:S(2)}, u32[]{:S(2)}) collective-permute-start(f32[384,64]{0,1:T(8,128)S(1)} %slice_select_fusion.3), channel_id=1, source_target_pairs={{0,1},{1,0},{2,3},{3,2},{4,5},{5,4},{6,7},{7,6},{8,9},{9,8},{10,11... | collective-permute-start | bytes 294920 | tf_op jit(solution)/shard_map/ppermute | solution.py:76
  171.4 3.7 collective-permute-done.21
  177.5 5.1 %collective-permute-done.22 = f32[96,64]{0,1:T(8,128)S(1)} collective-permute-done((f32[96,64]{0,1:T(8,128)S(1)}, f32[96,64]{0,1:T(8,128)S(1)}, u32[]{:S(2)}, u32[]{:S(2)}) %collective-permute-start.22) | collective-permute-done | bytes 24608 | tf_op jit(solution)/shard_map/ppermute | solution.py:76
  182.7 4.8 %collective-permute-start.23 = (f32[48,64]{0,1:T(8,128)S(1)}, f32[48,64]{0,1:T(8,128)S(1)}, u32[]{:S(2)}, u32[]{:S(2)}) collective-permute-start(f32[48,64]{0,1:T(8,128)S(1)} %slice_select_fusion.16), channel_id=1, source_target_pairs={{0,8},{1,9},{2,10},{3,11},{4,12},{5,13},{6,14},{7,15},{8,0},{9,1},... | collective-permute-start | bytes 36872 | tf_op jit(solution)/shard_map/ppermute | solution.py:76
  187.7 9.8 %collective-permute-done.23 = f32[48,64]{0,1:T(8,128)S(1)} collective-permute-done((f32[48,64]{0,1:T(8,128)S(1)}, f32[48,64]{0,1:T(8,128)S(1)}, u32[]{:S(2)}, u32[]{:S(2)}) %collective-permute-start.23) | collective-permute-done | bytes 12320 | tf_op jit(solution)/shard_map/ppermute | solution.py:76
  198.1 4.1 collective-permute-start.24
  204.4 4.3 collective-permute-done.25
  208.7 5.6 %collective-permute-start.28 = (bf16[96,64]{1,0:T(8,128)(2,1)S(1)}, bf16[96,64]{1,0:T(8,128)(2,1)S(1)}, u32[]{:S(2)}, u32[]{:S(2)}) collective-permute-start(bf16[96,64]{1,0:T(8,128)(2,1)S(1)} %maximum_select_fusion.27), channel_id=1, source_target_pairs={{0,256},{16,272},{32,288},{48,304},{64,320},{80,336},{96,352},{112... | collective-permute-start | bytes 36872 | tf_op jit(solution)/shard_map/ppermute | solution.py:58
  218.3 4.3 collective-permute-start.29
  225.8 3.4 collective-permute-start.30
  229.3 3.1 collective-permute-done.30
  232.4 8.0 %collective-permute-start.31 = (bf16[768,64]{1,0:T(8,128)(2,1)S(1)}, bf16[768,64]{1,0:T(8,128)(2,1)S(1)}, u32[]{:S(2)}, u32[]{:S(2)}) collective-permute-start(bf16[768,64]{1,0:T(8,128)(2,1)S(1)} %maximum_select_fusion.12), channel_id=1, source_target_pairs={{0,32},{16,48},{32,0},{48,16},{64,96},{80,112},{96,64},{112,80},{1... | collective-permute-start | bytes 294920 | tf_op jit(solution)/shard_map/ppermute | solution.py:58
  240.5 3.6 collective-permute-done.31
  244.7 8.5 %collective-permute-start.32 = (f32[384,64]{0,1:T(8,128)S(1)}, f32[384,64]{0,1:T(8,128)S(1)}, u32[]{:S(2)}, u32[]{:S(2)}) collective-permute-start(f32[384,64]{0,1:T(8,128)S(1)} %slice_select_fusion.2), channel_id=1, source_target_pairs={{0,1},{1,0},{2,3},{3,2},{4,5},{5,4},{6,7},{7,6},{8,9},{9,8},{10,11... | collective-permute-start | bytes 294920 | tf_op jit(solution)/shard_map/ppermute | solution.py:76
  256.8 3.7 collective-permute-done.33
  262.9 5.1 %collective-permute-done.34 = f32[96,64]{0,1:T(8,128)S(1)} collective-permute-done((f32[96,64]{0,1:T(8,128)S(1)}, f32[96,64]{0,1:T(8,128)S(1)}, u32[]{:S(2)}, u32[]{:S(2)}) %collective-permute-start.34) | collective-permute-done | bytes 24608 | tf_op jit(solution)/shard_map/ppermute | solution.py:76
  268.1 5.1 %collective-permute-start.35 = (f32[48,64]{0,1:T(8,128)S(1)}, f32[48,64]{0,1:T(8,128)S(1)}, u32[]{:S(2)}, u32[]{:S(2)}) collective-permute-start(f32[48,64]{0,1:T(8,128)S(1)} %slice_select_fusion.14), channel_id=1, source_target_pairs={{0,8},{1,9},{2,10},{3,11},{4,12},{5,13},{6,14},{7,15},{8,0},{9,1},... | collective-permute-start | bytes 36872 | tf_op jit(solution)/shard_map/ppermute | solution.py:76
  273.4 9.3 %collective-permute-done.35 = f32[48,64]{0,1:T(8,128)S(1)} collective-permute-done((f32[48,64]{0,1:T(8,128)S(1)}, f32[48,64]{0,1:T(8,128)S(1)}, u32[]{:S(2)}, u32[]{:S(2)}) %collective-permute-start.35) | collective-permute-done | bytes 12320 | tf_op jit(solution)/shard_map/ppermute | solution.py:76
  283.3 2.8 collective-permute-start.36
  288.2 4.3 collective-permute-done.37
  292.5 7.1 %collective-permute-start.40 = (bf16[96,64]{1,0:T(8,128)(2,1)S(1)}, bf16[96,64]{1,0:T(8,128)(2,1)S(1)}, u32[]{:S(2)}, u32[]{:S(2)}) collective-permute-start(bf16[96,64]{1,0:T(8,128)(2,1)S(1)} %maximum_select_fusion.28), channel_id=1, source_target_pairs={{0,256},{16,272},{32,288},{48,304},{64,320},{80,336},{96,352},{112... | collective-permute-start | bytes 36872 | tf_op jit(solution)/shard_map/ppermute | solution.py:58
  302.1 5.3 %collective-permute-start.41 = (bf16[192,64]{1,0:T(8,128)(2,1)S(1)}, bf16[192,64]{1,0:T(8,128)(2,1)S(1)}, u32[]{:S(2)}, u32[]{:S(2)}) collective-permute-start(bf16[192,64]{1,0:T(8,128)(2,1)S(1)} %maximum_select_fusion.23), channel_id=1, source_target_pairs={{0,128},{16,144},{32,160},{48,176},{64,192},{80,208},{96,224},{112... | collective-permute-start | bytes 73736 | tf_op jit(solution)/shard_map/ppermute | solution.py:58
  309.6 3.3 collective-permute-start.42
  313.0 3.1 collective-permute-done.42
  316.2 7.8 %collective-permute-start.43 = (bf16[768,64]{1,0:T(8,128)(2,1)S(1)}, bf16[768,64]{1,0:T(8,128)(2,1)S(1)}, u32[]{:S(2)}, u32[]{:S(2)}) collective-permute-start(bf16[768,64]{1,0:T(8,128)(2,1)S(1)} %maximum_select_fusion.13), channel_id=1, source_target_pairs={{0,32},{16,48},{32,0},{48,16},{64,96},{80,112},{96,64},{112,80},{1... | collective-permute-start | bytes 294920 | tf_op jit(solution)/shard_map/ppermute | solution.py:58
  324.0 3.6 collective-permute-done.43
  328.2 9.1 %collective-permute-start.44 = (f32[384,64]{0,1:T(8,128)S(1)}, f32[384,64]{0,1:T(8,128)S(1)}, u32[]{:S(2)}, u32[]{:S(2)}) collective-permute-start(f32[384,64]{0,1:T(8,128)S(1)} %slice_select_fusion.1), channel_id=1, source_target_pairs={{0,1},{1,0},{2,3},{3,2},{4,5},{5,4},{6,7},{7,6},{8,9},{9,8},{10,11... | collective-permute-start | bytes 294920 | tf_op jit(solution)/shard_map/ppermute | solution.py:76
  340.9 3.7 collective-permute-done.45
  347.0 5.1 %collective-permute-done.46 = f32[96,64]{0,1:T(8,128)S(1)} collective-permute-done((f32[96,64]{0,1:T(8,128)S(1)}, f32[96,64]{0,1:T(8,128)S(1)}, u32[]{:S(2)}, u32[]{:S(2)}) %collective-permute-start.46) | collective-permute-done | bytes 24608 | tf_op jit(solution)/shard_map/ppermute | solution.py:76
  352.2 4.4 collective-permute-start.47
  356.8 9.9 %collective-permute-done.47 = f32[48,64]{0,1:T(8,128)S(1)} collective-permute-done((f32[48,64]{0,1:T(8,128)S(1)}, f32[48,64]{0,1:T(8,128)S(1)}, u32[]{:S(2)}, u32[]{:S(2)}) %collective-permute-start.47) | collective-permute-done | bytes 12320 | tf_op jit(solution)/shard_map/ppermute | solution.py:76
  367.4 3.5 collective-permute-start.48
  373.1 4.3 collective-permute-done.49
  377.4 6.6 %collective-permute-start.52 = (bf16[96,64]{1,0:T(8,128)(2,1)S(1)}, bf16[96,64]{1,0:T(8,128)(2,1)S(1)}, u32[]{:S(2)}, u32[]{:S(2)}) collective-permute-start(bf16[96,64]{1,0:T(8,128)(2,1)S(1)} %maximum_select_fusion.29), channel_id=1, source_target_pairs={{0,256},{16,272},{32,288},{48,304},{64,320},{80,336},{96,352},{112... | collective-permute-start | bytes 36872 | tf_op jit(solution)/shard_map/ppermute | solution.py:58
  384.0 3.0 collective-permute-done.52
  387.0 3.7 collective-permute-start.53
  393.9 3.5 collective-permute-start.54
  400.5 7.1 %collective-permute-start.55 = (bf16[768,64]{1,0:T(8,128)(2,1)S(1)}, bf16[768,64]{1,0:T(8,128)(2,1)S(1)}, u32[]{:S(2)}, u32[]{:S(2)}) collective-permute-start(bf16[768,64]{1,0:T(8,128)(2,1)S(1)} %maximum_select_fusion.14), channel_id=1, source_target_pairs={{0,32},{16,48},{32,0},{48,16},{64,96},{80,112},{96,64},{112,80},{1... | collective-permute-start | bytes 294920 | tf_op jit(solution)/shard_map/ppermute | solution.py:58
  407.6 3.6 collective-permute-done.55
  411.9 4.3 collective-permute-start.56
  419.1 4.8 %collective-permute-done.57 = f32[192,64]{0,1:T(8,128)S(1)} collective-permute-done((f32[192,64]{0,1:T(8,128)S(1)}, f32[192,64]{0,1:T(8,128)S(1)}, u32[]{:S(2)}, u32[]{:S(2)}) %collective-permute-start.57) | collective-permute-done | bytes 49184 | tf_op jit(solution)/shard_map/ppermute | solution.py:76
  426.1 5.4 %collective-permute-done.58 = f32[96,64]{0,1:T(8,128)S(1)} collective-permute-done((f32[96,64]{0,1:T(8,128)S(1)}, f32[96,64]{0,1:T(8,128)S(1)}, u32[]{:S(2)}, u32[]{:S(2)}) %collective-permute-start.58) | collective-permute-done | bytes 24608 | tf_op jit(solution)/shard_map/ppermute | solution.py:76
  433.7 9.9 %collective-permute-start.59 = (f32[48,64]{0,1:T(8,128)}, f32[48,64]{0,1:T(8,128)}, u32[]{:S(2)}, u32[]{:S(2)}) collective-permute-start(f32[48,64]{0,1:T(8,128)} %slice_select_fusion.10), channel_id=1, source_target_pairs={{0,8},{1,9},{2,10},{3,11},{4,12},{5,13},{6,14},{7,15},{8,0},{9,1},... | collective-permute-start | bytes 36872 | tf_op jit(solution)/shard_map/ppermute | solution.py:76
  443.6 3.6 fusion.17
  (274 shorter events, 99.6 us)
Async XLA Ops:
  8.2 19.8 %collective-permute-start = (bf16[112,384]{1,0:T(8,128)(2,1)}, bf16[112,384]{1,0:T(8,128)(2,1)}, u32[]{:S(2)}, u32[]{:S(2)}) collective-permute-start(bf16[112,384]{1,0:T(8,128)(2,1)} %get-tuple-element.57), channel_id=1, source_target_pairs={{0,16},{16,32},{32,48},{48,64},{64,80},{80,96},{96,112},{112,128},... | collective-permute-start | bytes 258056 | tf_op jit(solution)/shard_map/ppermute | solution.py:16
  12.3 16.5 %collective-permute-start.1 = (bf16[112,384]{1,0:T(8,128)(2,1)}, bf16[112,384]{1,0:T(8,128)(2,1)}, u32[]{:S(2)}, u32[]{:S(2)}) collective-permute-start(bf16[112,384]{1,0:T(8,128)(2,1)} %get-tuple-element.58), channel_id=1, source_target_pairs={{16,0},{32,16},{48,32},{64,48},{80,64},{96,80},{112,96},{128,112},... | collective-permute-start | bytes 258056 | tf_op jit(solution)/shard_map/ppermute | solution.py:16
  25.7 31.4 %copy-start.11 = (bf16[64,1792]{1,0:T(8,128)(2,1)S(1)}, bf16[64,1792]{1,0:T(8,128)(2,1)}, u32[]{:S(2)}) copy-start(bf16[64,1792]{1,0:T(8,128)(2,1)} %get-tuple-element.67) | copy-start | bytes 688132
  25.7 44.2 %copy-start.19 = (bf16[1536,768]{1,0:T(8,128)(2,1)S(1)}, bf16[1536,768]{1,0:T(8,128)(2,1)}, u32[]{:S(2)}) copy-start(bf16[1536,768]{1,0:T(8,128)(2,1)} %convolution_convert_fusion) | copy-start | bytes 7077892
  28.0 312.3 %copy-start.8 = (bf16[1024,768]{1,0:T(8,128)(2,1)}, bf16[1024,768]{1,0:T(8,128)(2,1)S(1)}, u32[]{:S(2)}) copy-start(bf16[1024,768]{1,0:T(8,128)(2,1)S(1)} %fusion.14) | copy-start | bytes 4718596
  29.5 16.3 %collective-permute-start.4 = (bf16[96,64]{1,0:T(8,128)(2,1)S(1)}, bf16[96,64]{1,0:T(8,128)(2,1)S(1)}, u32[]{:S(2)}, u32[]{:S(2)}) collective-permute-start(bf16[96,64]{1,0:T(8,128)(2,1)S(1)} %maximum_select_fusion.25), channel_id=1, source_target_pairs={{0,256},{16,272},{32,288},{48,304},{64,320},{80,336},{96,352},{112... | collective-permute-start | bytes 36872 | tf_op jit(solution)/shard_map/ppermute | solution.py:58
  43.8 13.2 %collective-permute-start.2 = (bf16[64,384]{1,0:T(8,128)(2,1)S(1)}, bf16[64,384]{1,0:T(8,128)(2,1)S(1)}, u32[]{:S(2)}, u32[]{:S(2)}) collective-permute-start(bf16[64,384]{1,0:T(8,128)(2,1)S(1)} %pad_maximum_fusion.1), channel_id=1, source_target_pairs={{0,1},{1,2},{2,3},{3,4},{4,5},{5,6},{6,7},{7,8},{8,9},{9,10},{10,1... | collective-permute-start | bytes 147464 | tf_op jit(solution)/shard_map/ppermute | solution.py:16
  45.8 7.4 %collective-permute-start.5 = (bf16[192,64]{1,0:T(8,128)(2,1)S(1)}, bf16[192,64]{1,0:T(8,128)(2,1)S(1)}, u32[]{:S(2)}, u32[]{:S(2)}) collective-permute-start(bf16[192,64]{1,0:T(8,128)(2,1)S(1)} %maximum_select_fusion.20), channel_id=1, source_target_pairs={{0,128},{16,144},{32,160},{48,176},{64,192},{80,208},{96,224},{112... | collective-permute-start | bytes 73736 | tf_op jit(solution)/shard_map/ppermute | solution.py:58
  49.8 9.6 %collective-permute-start.3 = (bf16[64,384]{1,0:T(8,128)(2,1)S(1)}, bf16[64,384]{1,0:T(8,128)(2,1)S(1)}, u32[]{:S(2)}, u32[]{:S(2)}) collective-permute-start(bf16[64,384]{1,0:T(8,128)(2,1)S(1)} %pad_maximum_fusion.2), channel_id=1, source_target_pairs={{1,0},{2,1},{3,2},{4,3},{5,4},{6,5},{7,6},{8,7},{9,8},{10,9},{11,1... | collective-permute-start | bytes 147464 | tf_op jit(solution)/shard_map/ppermute | solution.py:16
  53.2 7.6 %collective-permute-start.6 = (bf16[384,64]{1,0:T(8,128)(2,1)S(1)}, bf16[384,64]{1,0:T(8,128)(2,1)S(1)}, u32[]{:S(2)}, u32[]{:S(2)}) collective-permute-start(bf16[384,64]{1,0:T(8,128)(2,1)S(1)} %maximum_select_fusion.15), channel_id=1, source_target_pairs={{0,64},{16,80},{32,96},{48,112},{64,0},{80,16},{96,32},{112,48},{1... | collective-permute-start | bytes 147464 | tf_op jit(solution)/shard_map/ppermute | solution.py:58
  60.9 9.1 %collective-permute-start.7 = (bf16[768,64]{1,0:T(8,128)(2,1)S(1)}, bf16[768,64]{1,0:T(8,128)(2,1)S(1)}, u32[]{:S(2)}, u32[]{:S(2)}) collective-permute-start(bf16[768,64]{1,0:T(8,128)(2,1)S(1)} %maximum_select_fusion.10), channel_id=1, source_target_pairs={{0,32},{16,48},{32,0},{48,16},{64,96},{80,112},{96,64},{112,80},{1... | collective-permute-start | bytes 294920 | tf_op jit(solution)/shard_map/ppermute | solution.py:58
  70.6 14.0 %collective-permute-start.8 = (f32[384,64]{0,1:T(8,128)S(1)}, f32[384,64]{0,1:T(8,128)S(1)}, u32[]{:S(2)}, u32[]{:S(2)}) collective-permute-start(f32[384,64]{0,1:T(8,128)S(1)} %slice_select_fusion.4), channel_id=1, source_target_pairs={{0,1},{1,0},{2,3},{3,2},{4,5},{5,4},{6,7},{7,6},{8,9},{9,8},{10,11... | collective-permute-start | bytes 294920 | tf_op jit(solution)/shard_map/ppermute | solution.py:76
  84.6 6.2 %collective-permute-start.9 = (f32[192,64]{0,1:T(8,128)S(1)}, f32[192,64]{0,1:T(8,128)S(1)}, u32[]{:S(2)}, u32[]{:S(2)}) collective-permute-start(f32[192,64]{0,1:T(8,128)S(1)} %slice_select_fusion.9), channel_id=1, source_target_pairs={{0,2},{1,3},{2,0},{3,1},{4,6},{5,7},{6,4},{7,5},{8,10},{9,11},{10,... | collective-permute-start | bytes 147464 | tf_op jit(solution)/shard_map/ppermute | solution.py:76
  91.0 7.3 %collective-permute-start.10 = (f32[96,64]{0,1:T(8,128)S(1)}, f32[96,64]{0,1:T(8,128)S(1)}, u32[]{:S(2)}, u32[]{:S(2)}) collective-permute-start(f32[96,64]{0,1:T(8,128)S(1)} %slice_select_fusion.19), channel_id=1, source_target_pairs={{0,4},{1,5},{2,6},{3,7},{4,0},{5,1},{6,2},{7,3},{8,12},{9,13},{10,... | collective-permute-start | bytes 73736 | tf_op jit(solution)/shard_map/ppermute | solution.py:76
  98.5 15.3 %collective-permute-start.11 = (f32[48,64]{0,1:T(8,128)S(1)}, f32[48,64]{0,1:T(8,128)S(1)}, u32[]{:S(2)}, u32[]{:S(2)}) collective-permute-start(f32[48,64]{0,1:T(8,128)S(1)} %slice_select_fusion.18), channel_id=1, source_target_pairs={{0,8},{1,9},{2,10},{3,11},{4,12},{5,13},{6,14},{7,15},{8,0},{9,1},... | collective-permute-start | bytes 36872 | tf_op jit(solution)/shard_map/ppermute | solution.py:76
  114.5 3.4 collective-permute-start.12
  115.8 6.4 %collective-permute-start.13 = (bf16[112,384]{1,0:T(8,128)(2,1)S(1)}, bf16[112,384]{1,0:T(8,128)(2,1)S(1)}, u32[]{:S(2)}, u32[]{:S(2)}) collective-permute-start(bf16[112,384]{1,0:T(8,128)(2,1)S(1)} %get-tuple-element.56), channel_id=1, source_target_pairs={{16,0},{32,16},{48,32},{64,48},{80,64},{96,80},{112,96},{128,112},... | collective-permute-start | bytes 258056 | tf_op jit(solution)/shard_map/ppermute | solution.py:16
  122.2 10.7 %collective-permute-start.16 = (bf16[96,64]{1,0:T(8,128)(2,1)S(1)}, bf16[96,64]{1,0:T(8,128)(2,1)S(1)}, u32[]{:S(2)}, u32[]{:S(2)}) collective-permute-start(bf16[96,64]{1,0:T(8,128)(2,1)S(1)} %maximum_select_fusion.26), channel_id=1, source_target_pairs={{0,256},{16,272},{32,288},{48,304},{64,320},{80,336},{96,352},{112... | collective-permute-start | bytes 36872 | tf_op jit(solution)/shard_map/ppermute | solution.py:58
  130.8 12.4 %collective-permute-start.14 = (bf16[64,384]{1,0:T(8,128)(2,1)S(1)}, bf16[64,384]{1,0:T(8,128)(2,1)S(1)}, u32[]{:S(2)}, u32[]{:S(2)}) collective-permute-start(bf16[64,384]{1,0:T(8,128)(2,1)S(1)} %pad_maximum_fusion.3), channel_id=1, source_target_pairs={{0,1},{1,2},{2,3},{3,4},{4,5},{5,6},{6,7},{7,8},{8,9},{9,10},{10,1... | collective-permute-start | bytes 147464 | tf_op jit(solution)/shard_map/ppermute | solution.py:16
  133.0 8.2 %collective-permute-start.17 = (bf16[192,64]{1,0:T(8,128)(2,1)S(1)}, bf16[192,64]{1,0:T(8,128)(2,1)S(1)}, u32[]{:S(2)}, u32[]{:S(2)}) collective-permute-start(bf16[192,64]{1,0:T(8,128)(2,1)S(1)} %maximum_select_fusion.21), channel_id=1, source_target_pairs={{0,128},{16,144},{32,160},{48,176},{64,192},{80,208},{96,224},{112... | collective-permute-start | bytes 73736 | tf_op jit(solution)/shard_map/ppermute | solution.py:58
  138.7 4.9 %collective-permute-start.15 = (bf16[64,384]{1,0:T(8,128)(2,1)S(1)}, bf16[64,384]{1,0:T(8,128)(2,1)S(1)}, u32[]{:S(2)}, u32[]{:S(2)}) collective-permute-start(bf16[64,384]{1,0:T(8,128)(2,1)S(1)} %pad_maximum_fusion.4), channel_id=1, source_target_pairs={{1,0},{2,1},{3,2},{4,3},{5,4},{6,5},{7,6},{8,7},{9,8},{10,9},{11,1... | collective-permute-start | bytes 147464 | tf_op jit(solution)/shard_map/ppermute | solution.py:16
  141.2 6.5 %collective-permute-start.18 = (bf16[384,64]{1,0:T(8,128)(2,1)S(1)}, bf16[384,64]{1,0:T(8,128)(2,1)S(1)}, u32[]{:S(2)}, u32[]{:S(2)}) collective-permute-start(bf16[384,64]{1,0:T(8,128)(2,1)S(1)} %maximum_select_fusion.16), channel_id=1, source_target_pairs={{0,64},{16,80},{32,96},{48,112},{64,0},{80,16},{96,32},{112,48},{1... | collective-permute-start | bytes 147464 | tf_op jit(solution)/shard_map/ppermute | solution.py:58
  147.8 9.1 %collective-permute-start.19 = (bf16[768,64]{1,0:T(8,128)(2,1)S(1)}, bf16[768,64]{1,0:T(8,128)(2,1)S(1)}, u32[]{:S(2)}, u32[]{:S(2)}) collective-permute-start(bf16[768,64]{1,0:T(8,128)(2,1)S(1)} %maximum_select_fusion.11), channel_id=1, source_target_pairs={{0,32},{16,48},{32,0},{48,16},{64,96},{80,112},{96,64},{112,80},{1... | collective-permute-start | bytes 294920 | tf_op jit(solution)/shard_map/ppermute | solution.py:58
  157.5 11.3 %collective-permute-start.20 = (f32[384,64]{0,1:T(8,128)S(1)}, f32[384,64]{0,1:T(8,128)S(1)}, u32[]{:S(2)}, u32[]{:S(2)}) collective-permute-start(f32[384,64]{0,1:T(8,128)S(1)} %slice_select_fusion.3), channel_id=1, source_target_pairs={{0,1},{1,0},{2,3},{3,2},{4,5},{5,4},{6,7},{7,6},{8,9},{9,8},{10,11... | collective-permute-start | bytes 294920 | tf_op jit(solution)/shard_map/ppermute | solution.py:76
  168.9 6.2 %collective-permute-start.21 = (f32[192,64]{0,1:T(8,128)S(1)}, f32[192,64]{0,1:T(8,128)S(1)}, u32[]{:S(2)}, u32[]{:S(2)}) collective-permute-start(f32[192,64]{0,1:T(8,128)S(1)} %slice_select_fusion.8), channel_id=1, source_target_pairs={{0,2},{1,3},{2,0},{3,1},{4,6},{5,7},{6,4},{7,5},{8,10},{9,11},{10,... | collective-permute-start | bytes 147464 | tf_op jit(solution)/shard_map/ppermute | solution.py:76
  175.3 7.3 %collective-permute-start.22 = (f32[96,64]{0,1:T(8,128)S(1)}, f32[96,64]{0,1:T(8,128)S(1)}, u32[]{:S(2)}, u32[]{:S(2)}) collective-permute-start(f32[96,64]{0,1:T(8,128)S(1)} %slice_select_fusion.17), channel_id=1, source_target_pairs={{0,4},{1,5},{2,6},{3,7},{4,0},{5,1},{6,2},{7,3},{8,12},{9,13},{10,... | collective-permute-start | bytes 73736 | tf_op jit(solution)/shard_map/ppermute | solution.py:76
  182.7 14.7 %collective-permute-start.23 = (f32[48,64]{0,1:T(8,128)S(1)}, f32[48,64]{0,1:T(8,128)S(1)}, u32[]{:S(2)}, u32[]{:S(2)}) collective-permute-start(f32[48,64]{0,1:T(8,128)S(1)} %slice_select_fusion.16), channel_id=1, source_target_pairs={{0,8},{1,9},{2,10},{3,11},{4,12},{5,13},{6,14},{7,15},{8,0},{9,1},... | collective-permute-start | bytes 36872 | tf_op jit(solution)/shard_map/ppermute | solution.py:76
  198.1 6.2 %collective-permute-start.24 = (bf16[112,384]{1,0:T(8,128)(2,1)S(1)}, bf16[112,384]{1,0:T(8,128)(2,1)S(1)}, u32[]{:S(2)}, u32[]{:S(2)}) collective-permute-start(bf16[112,384]{1,0:T(8,128)(2,1)S(1)} %get-tuple-element.53), channel_id=1, source_target_pairs={{0,16},{16,32},{32,48},{48,64},{64,80},{80,96},{96,112},{112,128},... | collective-permute-start | bytes 258056 | tf_op jit(solution)/shard_map/ppermute | solution.py:16
  202.3 6.4 %collective-permute-start.25 = (bf16[112,384]{1,0:T(8,128)(2,1)S(1)}, bf16[112,384]{1,0:T(8,128)(2,1)S(1)}, u32[]{:S(2)}, u32[]{:S(2)}) collective-permute-start(bf16[112,384]{1,0:T(8,128)(2,1)S(1)} %get-tuple-element.54), channel_id=1, source_target_pairs={{16,0},{32,16},{48,32},{64,48},{80,64},{96,80},{112,96},{128,112},... | collective-permute-start | bytes 258056 | tf_op jit(solution)/shard_map/ppermute | solution.py:16
  208.7 9.6 %collective-permute-start.28 = (bf16[96,64]{1,0:T(8,128)(2,1)S(1)}, bf16[96,64]{1,0:T(8,128)(2,1)S(1)}, u32[]{:S(2)}, u32[]{:S(2)}) collective-permute-start(bf16[96,64]{1,0:T(8,128)(2,1)S(1)} %maximum_select_fusion.27), channel_id=1, source_target_pairs={{0,256},{16,272},{32,288},{48,304},{64,320},{80,336},{96,352},{112... | collective-permute-start | bytes 36872 | tf_op jit(solution)/shard_map/ppermute | solution.py:58
  214.4 14.8 %collective-permute-start.26 = (bf16[64,384]{1,0:T(8,128)(2,1)S(1)}, bf16[64,384]{1,0:T(8,128)(2,1)S(1)}, u32[]{:S(2)}, u32[]{:S(2)}) collective-permute-start(bf16[64,384]{1,0:T(8,128)(2,1)S(1)} %pad_maximum_fusion.5), channel_id=1, source_target_pairs={{0,1},{1,2},{2,3},{3,4},{4,5},{5,6},{6,7},{7,8},{8,9},{9,10},{10,1... | collective-permute-start | bytes 147464 | tf_op jit(solution)/shard_map/ppermute | solution.py:16
  218.3 7.5 %collective-permute-start.29 = (bf16[192,64]{1,0:T(8,128)(2,1)S(1)}, bf16[192,64]{1,0:T(8,128)(2,1)S(1)}, u32[]{:S(2)}, u32[]{:S(2)}) collective-permute-start(bf16[192,64]{1,0:T(8,128)(2,1)S(1)} %maximum_select_fusion.22), channel_id=1, source_target_pairs={{0,128},{16,144},{32,160},{48,176},{64,192},{80,208},{96,224},{112... | collective-permute-start | bytes 73736 | tf_op jit(solution)/shard_map/ppermute | solution.py:58
  222.7 6.6 %collective-permute-start.27 = (bf16[64,384]{1,0:T(8,128)(2,1)S(1)}, bf16[64,384]{1,0:T(8,128)(2,1)S(1)}, u32[]{:S(2)}, u32[]{:S(2)}) collective-permute-start(bf16[64,384]{1,0:T(8,128)(2,1)S(1)} %pad_maximum_fusion.6), channel_id=1, source_target_pairs={{1,0},{2,1},{3,2},{4,3},{5,4},{6,5},{7,6},{8,7},{9,8},{10,9},{11,1... | collective-permute-start | bytes 147464 | tf_op jit(solution)/shard_map/ppermute | solution.py:16
  225.8 6.5 %collective-permute-start.30 = (bf16[384,64]{1,0:T(8,128)(2,1)S(1)}, bf16[384,64]{1,0:T(8,128)(2,1)S(1)}, u32[]{:S(2)}, u32[]{:S(2)}) collective-permute-start(bf16[384,64]{1,0:T(8,128)(2,1)S(1)} %maximum_select_fusion.17), channel_id=1, source_target_pairs={{0,64},{16,80},{32,96},{48,112},{64,0},{80,16},{96,32},{112,48},{1... | collective-permute-start | bytes 147464 | tf_op jit(solution)/shard_map/ppermute | solution.py:58
  232.4 11.7 %collective-permute-start.31 = (bf16[768,64]{1,0:T(8,128)(2,1)S(1)}, bf16[768,64]{1,0:T(8,128)(2,1)S(1)}, u32[]{:S(2)}, u32[]{:S(2)}) collective-permute-start(bf16[768,64]{1,0:T(8,128)(2,1)S(1)} %maximum_select_fusion.12), channel_id=1, source_target_pairs={{0,32},{16,48},{32,0},{48,16},{64,96},{80,112},{96,64},{112,80},{1... | collective-permute-start | bytes 294920 | tf_op jit(solution)/shard_map/ppermute | solution.py:58
  244.7 9.5 %collective-permute-start.32 = (f32[384,64]{0,1:T(8,128)S(1)}, f32[384,64]{0,1:T(8,128)S(1)}, u32[]{:S(2)}, u32[]{:S(2)}) collective-permute-start(f32[384,64]{0,1:T(8,128)S(1)} %slice_select_fusion.2), channel_id=1, source_target_pairs={{0,1},{1,0},{2,3},{3,2},{4,5},{5,4},{6,7},{7,6},{8,9},{9,8},{10,11... | collective-permute-start | bytes 294920 | tf_op jit(solution)/shard_map/ppermute | solution.py:76
  254.3 6.2 %collective-permute-start.33 = (f32[192,64]{0,1:T(8,128)S(1)}, f32[192,64]{0,1:T(8,128)S(1)}, u32[]{:S(2)}, u32[]{:S(2)}) collective-permute-start(f32[192,64]{0,1:T(8,128)S(1)} %slice_select_fusion.7), channel_id=1, source_target_pairs={{0,2},{1,3},{2,0},{3,1},{4,6},{5,7},{6,4},{7,5},{8,10},{9,11},{10,... | collective-permute-start | bytes 147464 | tf_op jit(solution)/shard_map/ppermute | solution.py:76
  260.7 7.3 %collective-permute-start.34 = (f32[96,64]{0,1:T(8,128)S(1)}, f32[96,64]{0,1:T(8,128)S(1)}, u32[]{:S(2)}, u32[]{:S(2)}) collective-permute-start(f32[96,64]{0,1:T(8,128)S(1)} %slice_select_fusion.15), channel_id=1, source_target_pairs={{0,4},{1,5},{2,6},{3,7},{4,0},{5,1},{6,2},{7,3},{8,12},{9,13},{10,... | collective-permute-start | bytes 73736 | tf_op jit(solution)/shard_map/ppermute | solution.py:76
  268.1 14.5 %collective-permute-start.35 = (f32[48,64]{0,1:T(8,128)S(1)}, f32[48,64]{0,1:T(8,128)S(1)}, u32[]{:S(2)}, u32[]{:S(2)}) collective-permute-start(f32[48,64]{0,1:T(8,128)S(1)} %slice_select_fusion.14), channel_id=1, source_target_pairs={{0,8},{1,9},{2,10},{3,11},{4,12},{5,13},{6,14},{7,15},{8,0},{9,1},... | collective-permute-start | bytes 36872 | tf_op jit(solution)/shard_map/ppermute | solution.py:76
  283.3 4.8 %collective-permute-start.36 = (bf16[112,384]{1,0:T(8,128)(2,1)S(1)}, bf16[112,384]{1,0:T(8,128)(2,1)S(1)}, u32[]{:S(2)}, u32[]{:S(2)}) collective-permute-start(bf16[112,384]{1,0:T(8,128)(2,1)S(1)} %get-tuple-element.51), channel_id=1, source_target_pairs={{0,16},{16,32},{32,48},{48,64},{64,80},{80,96},{96,112},{112,128},... | collective-permute-start | bytes 258056 | tf_op jit(solution)/shard_map/ppermute | solution.py:16
  286.1 6.4 %collective-permute-start.37 = (bf16[112,384]{1,0:T(8,128)(2,1)S(1)}, bf16[112,384]{1,0:T(8,128)(2,1)S(1)}, u32[]{:S(2)}, u32[]{:S(2)}) collective-permute-start(bf16[112,384]{1,0:T(8,128)(2,1)S(1)} %get-tuple-element.52), channel_id=1, source_target_pairs={{16,0},{32,16},{48,32},{64,48},{80,64},{96,80},{112,96},{128,112},... | collective-permute-start | bytes 258056 | tf_op jit(solution)/shard_map/ppermute | solution.py:16
  292.5 9.6 %collective-permute-start.40 = (bf16[96,64]{1,0:T(8,128)(2,1)S(1)}, bf16[96,64]{1,0:T(8,128)(2,1)S(1)}, u32[]{:S(2)}, u32[]{:S(2)}) collective-permute-start(bf16[96,64]{1,0:T(8,128)(2,1)S(1)} %maximum_select_fusion.28), channel_id=1, source_target_pairs={{0,256},{16,272},{32,288},{48,304},{64,320},{80,336},{96,352},{112... | collective-permute-start | bytes 36872 | tf_op jit(solution)/shard_map/ppermute | solution.py:58
  299.7 13.3 %collective-permute-start.38 = (bf16[64,384]{1,0:T(8,128)(2,1)S(1)}, bf16[64,384]{1,0:T(8,128)(2,1)S(1)}, u32[]{:S(2)}, u32[]{:S(2)}) collective-permute-start(bf16[64,384]{1,0:T(8,128)(2,1)S(1)} %pad_maximum_fusion.7), channel_id=1, source_target_pairs={{0,1},{1,2},{2,3},{3,4},{4,5},{5,6},{6,7},{7,8},{8,9},{9,10},{10,1... | collective-permute-start | bytes 147464 | tf_op jit(solution)/shard_map/ppermute | solution.py:16
  302.1 7.4 %collective-permute-start.41 = (bf16[192,64]{1,0:T(8,128)(2,1)S(1)}, bf16[192,64]{1,0:T(8,128)(2,1)S(1)}, u32[]{:S(2)}, u32[]{:S(2)}) collective-permute-start(bf16[192,64]{1,0:T(8,128)(2,1)S(1)} %maximum_select_fusion.23), channel_id=1, source_target_pairs={{0,128},{16,144},{32,160},{48,176},{64,192},{80,208},{96,224},{112... | collective-permute-start | bytes 73736 | tf_op jit(solution)/shard_map/ppermute | solution.py:58
  307.4 5.5 %collective-permute-start.39 = (bf16[64,384]{1,0:T(8,128)(2,1)S(1)}, bf16[64,384]{1,0:T(8,128)(2,1)S(1)}, u32[]{:S(2)}, u32[]{:S(2)}) collective-permute-start(bf16[64,384]{1,0:T(8,128)(2,1)S(1)} %pad_maximum_fusion.8), channel_id=1, source_target_pairs={{1,0},{2,1},{3,2},{4,3},{5,4},{6,5},{7,6},{8,7},{9,8},{10,9},{11,1... | collective-permute-start | bytes 147464 | tf_op jit(solution)/shard_map/ppermute | solution.py:16
  309.6 6.5 %collective-permute-start.42 = (bf16[384,64]{1,0:T(8,128)(2,1)S(1)}, bf16[384,64]{1,0:T(8,128)(2,1)S(1)}, u32[]{:S(2)}, u32[]{:S(2)}) collective-permute-start(bf16[384,64]{1,0:T(8,128)(2,1)S(1)} %maximum_select_fusion.18), channel_id=1, source_target_pairs={{0,64},{16,80},{32,96},{48,112},{64,0},{80,16},{96,32},{112,48},{1... | collective-permute-start | bytes 147464 | tf_op jit(solution)/shard_map/ppermute | solution.py:58
  316.2 11.4 %collective-permute-start.43 = (bf16[768,64]{1,0:T(8,128)(2,1)S(1)}, bf16[768,64]{1,0:T(8,128)(2,1)S(1)}, u32[]{:S(2)}, u32[]{:S(2)}) collective-permute-start(bf16[768,64]{1,0:T(8,128)(2,1)S(1)} %maximum_select_fusion.13), channel_id=1, source_target_pairs={{0,32},{16,48},{32,0},{48,16},{64,96},{80,112},{96,64},{112,80},{1... | collective-permute-start | bytes 294920 | tf_op jit(solution)/shard_map/ppermute | solution.py:58
  328.2 10.0 %collective-permute-start.44 = (f32[384,64]{0,1:T(8,128)S(1)}, f32[384,64]{0,1:T(8,128)S(1)}, u32[]{:S(2)}, u32[]{:S(2)}) collective-permute-start(f32[384,64]{0,1:T(8,128)S(1)} %slice_select_fusion.1), channel_id=1, source_target_pairs={{0,1},{1,0},{2,3},{3,2},{4,5},{5,4},{6,7},{7,6},{8,9},{9,8},{10,11... | collective-permute-start | bytes 294920 | tf_op jit(solution)/shard_map/ppermute | solution.py:76
  338.3 6.2 %collective-permute-start.45 = (f32[192,64]{0,1:T(8,128)S(1)}, f32[192,64]{0,1:T(8,128)S(1)}, u32[]{:S(2)}, u32[]{:S(2)}) collective-permute-start(f32[192,64]{0,1:T(8,128)S(1)} %slice_select_fusion.6), channel_id=1, source_target_pairs={{0,2},{1,3},{2,0},{3,1},{4,6},{5,7},{6,4},{7,5},{8,10},{9,11},{10,... | collective-permute-start | bytes 147464 | tf_op jit(solution)/shard_map/ppermute | solution.py:76
  344.8 7.3 %collective-permute-start.46 = (f32[96,64]{0,1:T(8,128)S(1)}, f32[96,64]{0,1:T(8,128)S(1)}, u32[]{:S(2)}, u32[]{:S(2)}) collective-permute-start(f32[96,64]{0,1:T(8,128)S(1)} %slice_select_fusion.13), channel_id=1, source_target_pairs={{0,4},{1,5},{2,6},{3,7},{4,0},{5,1},{6,2},{7,3},{8,12},{9,13},{10,... | collective-permute-start | bytes 73736 | tf_op jit(solution)/shard_map/ppermute | solution.py:76
  352.2 14.5 %collective-permute-start.47 = (f32[48,64]{0,1:T(8,128)S(1)}, f32[48,64]{0,1:T(8,128)S(1)}, u32[]{:S(2)}, u32[]{:S(2)}) collective-permute-start(f32[48,64]{0,1:T(8,128)S(1)} %slice_select_fusion.12), channel_id=1, source_target_pairs={{0,8},{1,9},{2,10},{3,11},{4,12},{5,13},{6,14},{7,15},{8,0},{9,1},... | collective-permute-start | bytes 36872 | tf_op jit(solution)/shard_map/ppermute | solution.py:76
  367.0 30.5 %copy-start.7 = (f32[64,768]{1,0:T(8,128)}, f32[64,768]{1,0:T(8,128)S(1)}, u32[]{:S(2)}) copy-start(f32[64,768]{1,0:T(8,128)S(1)} %get-tuple-element.76) | copy-start | bytes 589828
  367.4 5.6 %collective-permute-start.48 = (bf16[112,384]{1,0:T(8,128)(2,1)S(1)}, bf16[112,384]{1,0:T(8,128)(2,1)S(1)}, u32[]{:S(2)}, u32[]{:S(2)}) collective-permute-start(bf16[112,384]{1,0:T(8,128)(2,1)S(1)} %get-tuple-element.49), channel_id=1, source_target_pairs={{0,16},{16,32},{32,48},{48,64},{64,80},{80,96},{96,112},{112,128},... | collective-permute-start | bytes 258056 | tf_op jit(solution)/shard_map/ppermute | solution.py:16
  371.0 6.4 %collective-permute-start.49 = (bf16[112,384]{1,0:T(8,128)(2,1)S(1)}, bf16[112,384]{1,0:T(8,128)(2,1)S(1)}, u32[]{:S(2)}, u32[]{:S(2)}) collective-permute-start(bf16[112,384]{1,0:T(8,128)(2,1)S(1)} %get-tuple-element.50), channel_id=1, source_target_pairs={{16,0},{32,16},{48,32},{64,48},{80,64},{96,80},{112,96},{128,112},... | collective-permute-start | bytes 258056 | tf_op jit(solution)/shard_map/ppermute | solution.py:16
  377.4 9.6 %collective-permute-start.52 = (bf16[96,64]{1,0:T(8,128)(2,1)S(1)}, bf16[96,64]{1,0:T(8,128)(2,1)S(1)}, u32[]{:S(2)}, u32[]{:S(2)}) collective-permute-start(bf16[96,64]{1,0:T(8,128)(2,1)S(1)} %maximum_select_fusion.29), channel_id=1, source_target_pairs={{0,256},{16,272},{32,288},{48,304},{64,320},{80,336},{96,352},{112... | collective-permute-start | bytes 36872 | tf_op jit(solution)/shard_map/ppermute | solution.py:58
  387.0 6.9 %collective-permute-start.53 = (bf16[192,64]{1,0:T(8,128)(2,1)S(1)}, bf16[192,64]{1,0:T(8,128)(2,1)S(1)}, u32[]{:S(2)}, u32[]{:S(2)}) collective-permute-start(bf16[192,64]{1,0:T(8,128)(2,1)S(1)} %maximum_select_fusion.24), channel_id=1, source_target_pairs={{0,128},{16,144},{32,160},{48,176},{64,192},{80,208},{96,224},{112... | collective-permute-start | bytes 73736 | tf_op jit(solution)/shard_map/ppermute | solution.py:58
  390.7 16.9 %collective-permute-start.50 = (bf16[64,384]{1,0:T(8,128)(2,1)S(1)}, bf16[64,384]{1,0:T(8,128)(2,1)S(1)}, u32[]{:S(2)}, u32[]{:S(2)}) collective-permute-start(bf16[64,384]{1,0:T(8,128)(2,1)S(1)} %pad_maximum_fusion.9), channel_id=1, source_target_pairs={{0,1},{1,2},{2,3},{3,4},{4,5},{5,6},{6,7},{7,8},{8,9},{9,10},{10,1... | collective-permute-start | bytes 147464 | tf_op jit(solution)/shard_map/ppermute | solution.py:16
  393.9 6.5 %collective-permute-start.54 = (bf16[384,64]{1,0:T(8,128)(2,1)S(1)}, bf16[384,64]{1,0:T(8,128)(2,1)S(1)}, u32[]{:S(2)}, u32[]{:S(2)}) collective-permute-start(bf16[384,64]{1,0:T(8,128)(2,1)S(1)} %maximum_select_fusion.19), channel_id=1, source_target_pairs={{0,64},{16,80},{32,96},{48,112},{64,0},{80,16},{96,32},{112,48},{1... | collective-permute-start | bytes 147464 | tf_op jit(solution)/shard_map/ppermute | solution.py:58
  397.5 18.7 %collective-permute-start.51 = (bf16[64,384]{1,0:T(8,128)(2,1)S(1)}, bf16[64,384]{1,0:T(8,128)(2,1)S(1)}, u32[]{:S(2)}, u32[]{:S(2)}) collective-permute-start(bf16[64,384]{1,0:T(8,128)(2,1)S(1)} %pad_maximum_fusion.10), channel_id=1, source_target_pairs={{1,0},{2,1},{3,2},{4,3},{5,4},{6,5},{7,6},{8,7},{9,8},{10,9},{11,1... | collective-permute-start | bytes 147464 | tf_op jit(solution)/shard_map/ppermute | solution.py:16
  400.5 10.7 %collective-permute-start.55 = (bf16[768,64]{1,0:T(8,128)(2,1)S(1)}, bf16[768,64]{1,0:T(8,128)(2,1)S(1)}, u32[]{:S(2)}, u32[]{:S(2)}) collective-permute-start(bf16[768,64]{1,0:T(8,128)(2,1)S(1)} %maximum_select_fusion.14), channel_id=1, source_target_pairs={{0,32},{16,48},{32,0},{48,16},{64,96},{80,112},{96,64},{112,80},{1... | collective-permute-start | bytes 294920 | tf_op jit(solution)/shard_map/ppermute | solution.py:58
  411.9 5.2 %collective-permute-start.56 = (f32[384,64]{0,1:T(8,128)S(1)}, f32[384,64]{0,1:T(8,128)S(1)}, u32[]{:S(2)}, u32[]{:S(2)}) collective-permute-start(f32[384,64]{0,1:T(8,128)S(1)} %slice_select_fusion), channel_id=1, source_target_pairs={{0,1},{1,0},{2,3},{3,2},{4,5},{5,4},{6,7},{7,6},{8,9},{9,8},{10,11... | collective-permute-start | bytes 294920 | tf_op jit(solution)/shard_map/ppermute | solution.py:76
  417.2 6.8 %collective-permute-start.57 = (f32[192,64]{0,1:T(8,128)S(1)}, f32[192,64]{0,1:T(8,128)S(1)}, u32[]{:S(2)}, u32[]{:S(2)}) collective-permute-start(f32[192,64]{0,1:T(8,128)S(1)} %slice_select_fusion.5), channel_id=1, source_target_pairs={{0,2},{1,3},{2,0},{3,1},{4,6},{5,7},{6,4},{7,5},{8,10},{9,11},{10,... | collective-permute-start | bytes 147464 | tf_op jit(solution)/shard_map/ppermute | solution.py:76
  424.2 7.3 %collective-permute-start.58 = (f32[96,64]{0,1:T(8,128)S(1)}, f32[96,64]{0,1:T(8,128)S(1)}, u32[]{:S(2)}, u32[]{:S(2)}) collective-permute-start(f32[96,64]{0,1:T(8,128)S(1)} %slice_select_fusion.11), channel_id=1, source_target_pairs={{0,4},{1,5},{2,6},{3,7},{4,0},{5,1},{6,2},{7,3},{8,12},{9,13},{10,... | collective-permute-start | bytes 73736 | tf_op jit(solution)/shard_map/ppermute | solution.py:76
  433.7 14.8 %collective-permute-start.59 = (f32[48,64]{0,1:T(8,128)}, f32[48,64]{0,1:T(8,128)}, u32[]{:S(2)}, u32[]{:S(2)}) collective-permute-start(f32[48,64]{0,1:T(8,128)} %slice_select_fusion.10), channel_id=1, source_target_pairs={{0,8},{1,9},{2,10},{3,11},{4,12},{5,13},{6,14},{7,15},{8,0},{9,1},... | collective-permute-start | bytes 36872 | tf_op jit(solution)/shard_map/ppermute | solution.py:76
  (16 other events, 195.9 us)

commit v9 on v7

--- a/solution.py
+++ b/solution.py
@@ -110,9 +110,13 @@
     tile = coarse_inverse[0, :, 0, :]
     from_rows = reversed_blocks(rows, mode_count)
     from_cols = reversed_blocks(cols, mode_count)
-    pick_rows = (jnp.arange(rows * mode_count)[None, :] == from_rows[:, None]).astype(jnp.bfloat16)
+    from_row_blocks = from_rows[::mode_count] // mode_count
+    pick_rows = (jnp.arange(rows)[None, :] == from_row_blocks[:, None]).astype(jnp.bfloat16)
     pick_cols = (jnp.arange(cols * mode_count)[:, None] == from_cols[None, :]).astype(jnp.bfloat16)
-    tile = jnp.dot(pick_rows, tile, preferred_element_type=jnp.float32).astype(jnp.bfloat16)
+    tile = jnp.einsum(
+        "ij,jmn->imn", pick_rows, tile.reshape(rows, mode_count, -1),
+        preferred_element_type=jnp.float32,
+    ).astype(jnp.bfloat16).reshape(rows * mode_count, -1)
     tile = jnp.dot(tile, pick_cols, preferred_element_type=jnp.float32).astype(jnp.bfloat16)
     coarse_matrix = tile.T
 

time: 402 us -> 403 us (level)
  waiting for transfers between devices: 89.9 us -> 99.6 us
    ppermute x20, starting transfers between devices: 64.1 us -> 44.2 us  [shifted(): return lax.ppermute(block, axis, route)]
    ppermute x20, waiting for transfers between devices: 11.2 us -> 24.3 us  [shifted(): return lax.ppermute(block, axis, route)]
    ppermute x25, starting transfers between devices: 118 us -> 128 us  [gather_rows(): other = lax.ppermute(current, 'row', route)]
    ppermute x20, waiting for transfers between devices: 54.6 us -> 49 us  [scatter_cols(): current = keep + lax.ppermute(send, 'col', route)]
    ppermute x20, starting transfers between devices: 76.4 us -> 81.8 us  [scatter_cols(): current = keep + lax.ppermute(send, 'col', route)]
  transfers between devices with their start and end apart: 65 -> 65, of which waited for: 25 -> 31; matrix products, arithmetic and copies ran while one was open for 8% -> 9% of each run, Pallas kernels for 0% -> 0%
where the time goes in v9:
time: 403 us; the launch traced here: 400 us
  starting transfers between devices  254 us (63%)
  waiting for transfers between devices  99.6 us (25%)
  matrix products  23.7 us (6%)
  local copies, waits for them, and re-layouts  11.4 us (3%)
  other arithmetic  9.42 us (2%)
    ppermute x25, starting transfers between devices, gather_rows(): other = lax.ppermute(current, 'row', route)  128 us
    ppermute x20, starting transfers between devices, scatter_cols(): current = keep + lax.ppermute(send, 'col', route)  81.8 us
    ppermute x20, waiting for transfers between devices, scatter_cols(): current = keep + lax.ppermute(send, 'col', route)  49 us
    ppermute x20, starting transfers between devices, shifted(): return lax.ppermute(block, axis, route)  44.2 us
    ppermute x25, waiting for transfers between devices, gather_rows(): other = lax.ppermute(current, 'row', route)  26.3 us
    ppermute x20, waiting for transfers between devices, shifted(): return lax.ppermute(block, axis, route)  24.3 us
  transfers between devices with their start and end apart: 65, of which 31 were waited for; matrix products, arithmetic and copies ran while one was open for 9% of the time, Pallas kernels for 0%

profile of v9, /device:TPU:6, one launch (start us, length us, event | category | flops | bytes accessed | tf_op | source)
XLA Modules:
  0.0 400.4 jit_solution(838099050942681684)
XLA Ops:
  1.2 9.1 %collective-permute-start.4 = (bf16[48,64]{1,0:T(8,128)(2,1)S(1)}, bf16[48,64]{1,0:T(8,128)(2,1)S(1)}, u32[]{:S(2)}, u32[]{:S(2)}) collective-permute-start(bf16[48,64]{1,0:T(8,128)(2,1)S(1)} %convolution_convert_fusion.5), channel_id=1, source_target_pairs={{0,256},{16,272},{32,288},{48,304},{64,320},{80,336},{96,352},{112... | collective-permute-start | bytes 18440 | tf_op jit(solution)/shard_map/ppermute | solution.py:42
  12.3 2.3 constant_dynamic-update-slice_fusion.4
  17.2 4.1 %collective-permute-start = (bf16[64,384]{1,0:T(8,128)(2,1)}, bf16[64,384]{1,0:T(8,128)(2,1)}, u32[]{:S(2)}, u32[]{:S(2)}) collective-permute-start(bf16[64,384]{1,0:T(8,128)(2,1)} %get-tuple-element.27), channel_id=1, source_target_pairs={{0,16},{16,32},{32,48},{48,64},{64,80},{80,96},{96,112},{112,128},... | collective-permute-start | bytes 147464 | tf_op jit(solution)/shard_map/ppermute | solution.py:16
  25.0 3.5 convolution_convert_fusion
  29.3 7.8 %collective-permute-start.5 = (bf16[96,64]{1,0:T(8,128)(2,1)S(1)}, bf16[96,64]{1,0:T(8,128)(2,1)S(1)}, u32[]{:S(2)}, u32[]{:S(2)}) collective-permute-start(bf16[96,64]{1,0:T(8,128)(2,1)S(1)} %maximum_select_fusion.25), channel_id=1, source_target_pairs={{0,128},{16,144},{32,160},{48,176},{64,192},{80,208},{96,224},{112... | collective-permute-start | bytes 36872 | tf_op jit(solution)/shard_map/ppermute | solution.py:42
  38.9 3.8 collective-permute-start.6
  48.1 3.0 collective-permute-start.7
  54.6 3.6 collective-permute-start.3
  58.3 6.7 %collective-permute-done.3 = bf16[64,384]{1,0:T(8,128)(2,1)S(1)} collective-permute-done((bf16[64,384]{1,0:T(8,128)(2,1)S(1)}, bf16[64,384]{1,0:T(8,128)(2,1)S(1)}, u32[]{:S(2)}, u32[]{:S(2)}) %collective-permute-start.3) | collective-permute-done | bytes 49184 | tf_op jit(solution)/shard_map/ppermute | solution.py:16
  67.5 5.6 %collective-permute-start.17 = (bf16[48,64]{1,0:T(8,128)(2,1)S(1)}, bf16[48,64]{1,0:T(8,128)(2,1)S(1)}, u32[]{:S(2)}, u32[]{:S(2)}) collective-permute-start(bf16[48,64]{1,0:T(8,128)(2,1)S(1)} %fusion.57), channel_id=1, source_target_pairs={{0,256},{16,272},{32,288},{48,304},{64,320},{80,336},{96,352},{112... | collective-permute-start | bytes 18440 | tf_op jit(solution)/shard_map/ppermute | solution.py:42
  73.1 2.6 collective-permute-start.8
  77.1 3.4 collective-permute-start.18
  80.8 2.9 collective-permute-done.18
  83.8 2.9 collective-permute-start.19
  87.3 13.0 %collective-permute-start.9 = (f32[384,64]{0,1:T(8,128)S(1)}, f32[384,64]{0,1:T(8,128)S(1)}, u32[]{:S(2)}, u32[]{:S(2)}) collective-permute-start(f32[384,64]{0,1:T(8,128)S(1)} %slice_select_fusion.4), channel_id=1, source_target_pairs={{0,1},{1,0},{2,3},{3,2},{4,5},{5,4},{6,7},{7,6},{8,9},{9,8},{10,11... | collective-permute-start | bytes 294920 | tf_op jit(solution)/shard_map/ppermute | solution.py:60
  100.3 4.6 %collective-permute-start.20 = (bf16[384,64]{1,0:T(8,128)(2,1)S(1)}, bf16[384,64]{1,0:T(8,128)(2,1)S(1)}, u32[]{:S(2)}, u32[]{:S(2)}) collective-permute-start(bf16[384,64]{1,0:T(8,128)(2,1)S(1)} %maximum_select_fusion.16), channel_id=1, source_target_pairs={{0,32},{16,48},{32,0},{48,16},{64,96},{80,112},{96,64},{112,80},{1... | collective-permute-start | bytes 147464 | tf_op jit(solution)/shard_map/ppermute | solution.py:42
  108.5 2.6 collective-permute-start.21
  111.4 2.1 collective-permute-start.11
  113.5 2.9 collective-permute-done.21
  122.9 10.6 %collective-permute-done.12 = f32[48,64]{0,1:T(8,128)S(1)} collective-permute-done((f32[48,64]{0,1:T(8,128)S(1)}, f32[48,64]{0,1:T(8,128)S(1)}, u32[]{:S(2)}, u32[]{:S(2)}) %collective-permute-start.12) | collective-permute-done | bytes 12320 | tf_op jit(solution)/shard_map/ppermute | solution.py:60
  134.2 3.1 collective-permute-start.13
  138.8 2.5 collective-permute-start.23
  141.3 2.4 collective-permute-done.14
  145.8 2.2 collective-permute-start.24
  148.0 2.1 collective-permute-start.15
  150.2 3.0 collective-permute-done.24
  153.3 2.2 collective-permute-start.25
  156.7 11.6 %collective-permute-start.30 = (bf16[48,64]{1,0:T(8,128)(2,1)S(1)}, bf16[48,64]{1,0:T(8,128)(2,1)S(1)}, u32[]{:S(2)}, u32[]{:S(2)}) collective-permute-start(bf16[48,64]{1,0:T(8,128)(2,1)S(1)} %fusion.58), channel_id=1, source_target_pairs={{0,256},{16,272},{32,288},{48,304},{64,320},{80,336},{96,352},{112... | collective-permute-start | bytes 18440 | tf_op jit(solution)/shard_map/ppermute | solution.py:42
  170.0 5.2 %collective-permute-start.31 = (bf16[96,64]{1,0:T(8,128)(2,1)S(1)}, bf16[96,64]{1,0:T(8,128)(2,1)S(1)}, u32[]{:S(2)}, u32[]{:S(2)}) collective-permute-start(bf16[96,64]{1,0:T(8,128)(2,1)S(1)} %maximum_select_fusion.27), channel_id=1, source_target_pairs={{0,128},{16,144},{32,160},{48,176},{64,192},{80,208},{96,224},{112... | collective-permute-start | bytes 36872 | tf_op jit(solution)/shard_map/ppermute | solution.py:42
  177.1 3.8 collective-permute-start.32
  184.0 8.7 %collective-permute-start.33 = (bf16[384,64]{1,0:T(8,128)(2,1)S(1)}, bf16[384,64]{1,0:T(8,128)(2,1)S(1)}, u32[]{:S(2)}, u32[]{:S(2)}) collective-permute-start(bf16[384,64]{1,0:T(8,128)(2,1)S(1)} %maximum_select_fusion.17), channel_id=1, source_target_pairs={{0,32},{16,48},{32,0},{48,16},{64,96},{80,112},{96,64},{112,80},{1... | collective-permute-start | bytes 147464 | tf_op jit(solution)/shard_map/ppermute | solution.py:42
  192.8 2.4 collective-permute-start.28
  195.2 3.2 collective-permute-start.29
  198.4 12.5 %collective-permute-done.29 = bf16[64,384]{1,0:T(8,128)(2,1)S(1)} collective-permute-done((bf16[64,384]{1,0:T(8,128)(2,1)S(1)}, bf16[64,384]{1,0:T(8,128)(2,1)S(1)}, u32[]{:S(2)}, u32[]{:S(2)}) %collective-permute-start.29) | collective-permute-done | bytes 49184 | tf_op jit(solution)/shard_map/ppermute | solution.py:16
  211.7 5.8 %collective-permute-start.43 = (bf16[48,64]{1,0:T(8,128)(2,1)S(1)}, bf16[48,64]{1,0:T(8,128)(2,1)S(1)}, u32[]{:S(2)}, u32[]{:S(2)}) collective-permute-start(bf16[48,64]{1,0:T(8,128)(2,1)S(1)} %fusion.59), channel_id=1, source_target_pairs={{0,256},{16,272},{32,288},{48,304},{64,320},{80,336},{96,352},{112... | collective-permute-start | bytes 18440 | tf_op jit(solution)/shard_map/ppermute | solution.py:42
  217.6 2.1 collective-permute-start.34
  221.2 4.8 %collective-permute-start.44 = (bf16[96,64]{1,0:T(8,128)(2,1)S(1)}, bf16[96,64]{1,0:T(8,128)(2,1)S(1)}, u32[]{:S(2)}, u32[]{:S(2)}) collective-permute-start(bf16[96,64]{1,0:T(8,128)(2,1)S(1)} %maximum_select_fusion.28), channel_id=1, source_target_pairs={{0,128},{16,144},{32,160},{48,176},{64,192},{80,208},{96,224},{112... | collective-permute-start | bytes 36872 | tf_op jit(solution)/shard_map/ppermute | solution.py:42
  227.8 2.0 collective-permute-start.45
  230.5 13.9 %collective-permute-start.35 = (f32[384,64]{0,1:T(8,128)S(1)}, f32[384,64]{0,1:T(8,128)S(1)}, u32[]{:S(2)}, u32[]{:S(2)}) collective-permute-start(f32[384,64]{0,1:T(8,128)S(1)} %slice_select_fusion.2), channel_id=1, source_target_pairs={{0,1},{1,0},{2,3},{3,2},{4,5},{5,4},{6,7},{7,6},{8,9},{9,8},{10,11... | collective-permute-start | bytes 294920 | tf_op jit(solution)/shard_map/ppermute | solution.py:60
  244.4 6.4 %collective-permute-start.46 = (bf16[384,64]{1,0:T(8,128)(2,1)S(1)}, bf16[384,64]{1,0:T(8,128)(2,1)S(1)}, u32[]{:S(2)}, u32[]{:S(2)}) collective-permute-start(bf16[384,64]{1,0:T(8,128)(2,1)S(1)} %maximum_select_fusion.18), channel_id=1, source_target_pairs={{0,32},{16,48},{32,0},{48,16},{64,96},{80,112},{96,64},{112,80},{1... | collective-permute-start | bytes 147464 | tf_op jit(solution)/shard_map/ppermute | solution.py:42
  254.2 2.8 collective-permute-start.47
  259.2 3.5 collective-permute-done.47
  268.6 10.9 %collective-permute-done.38 = f32[48,64]{0,1:T(8,128)S(1)} collective-permute-done((f32[48,64]{0,1:T(8,128)S(1)}, f32[48,64]{0,1:T(8,128)S(1)}, u32[]{:S(2)}, u32[]{:S(2)}) %collective-permute-start.38) | collective-permute-done | bytes 12320 | tf_op jit(solution)/shard_map/ppermute | solution.py:60
  280.2 3.0 collective-permute-start.39
  284.6 2.4 collective-permute-start.49
  287.0 2.6 collective-permute-done.40
  291.7 2.1 collective-permute-start.50
  293.9 2.2 collective-permute-start.41
  296.1 3.0 collective-permute-done.50
  302.3 9.5 %collective-permute-start.56 = (bf16[48,64]{1,0:T(8,128)(2,1)S(1)}, bf16[48,64]{1,0:T(8,128)(2,1)S(1)}, u32[]{:S(2)}, u32[]{:S(2)}) collective-permute-start(bf16[48,64]{1,0:T(8,128)(2,1)S(1)} %fusion.60), channel_id=1, source_target_pairs={{0,256},{16,272},{32,288},{48,304},{64,320},{80,336},{96,352},{112... | collective-permute-start | bytes 18440 | tf_op jit(solution)/shard_map/ppermute | solution.py:42
  311.8 2.7 collective-permute-done.51
  315.4 7.3 %collective-permute-start.57 = (bf16[96,64]{1,0:T(8,128)(2,1)S(1)}, bf16[96,64]{1,0:T(8,128)(2,1)S(1)}, u32[]{:S(2)}, u32[]{:S(2)}) collective-permute-start(bf16[96,64]{1,0:T(8,128)(2,1)S(1)} %maximum_select_fusion.29), channel_id=1, source_target_pairs={{0,128},{16,144},{32,160},{48,176},{64,192},{80,208},{96,224},{112... | collective-permute-start | bytes 36872 | tf_op jit(solution)/shard_map/ppermute | solution.py:42
  324.5 3.6 collective-permute-start.58
  330.8 6.5 %collective-permute-start.59 = (bf16[384,64]{1,0:T(8,128)(2,1)S(1)}, bf16[384,64]{1,0:T(8,128)(2,1)S(1)}, u32[]{:S(2)}, u32[]{:S(2)}) collective-permute-start(bf16[384,64]{1,0:T(8,128)(2,1)S(1)} %maximum_select_fusion.19), channel_id=1, source_target_pairs={{0,32},{16,48},{32,0},{48,16},{64,96},{80,112},{96,64},{112,80},{1... | collective-permute-start | bytes 147464 | tf_op jit(solution)/shard_map/ppermute | solution.py:42
  339.3 3.2 collective-permute-start.54
  342.6 3.0 collective-permute-start.60
  345.8 4.4 %collective-permute-done.60 = bf16[768,64]{1,0:T(8,128)(2,1)S(1)} collective-permute-done((bf16[768,64]{1,0:T(8,128)(2,1)S(1)}, bf16[768,64]{1,0:T(8,128)(2,1)S(1)}, u32[]{:S(2)}, u32[]{:S(2)}) %collective-permute-start.60) | collective-permute-done | bytes 98336 | tf_op jit(solution)/shard_map/ppermute | solution.py:42
  350.8 15.7 %collective-permute-start.61 = (f32[384,64]{0,1:T(8,128)S(1)}, f32[384,64]{0,1:T(8,128)S(1)}, u32[]{:S(2)}, u32[]{:S(2)}) collective-permute-start(f32[384,64]{0,1:T(8,128)S(1)} %slice_select_fusion), channel_id=1, source_target_pairs={{0,1},{1,0},{2,3},{3,2},{4,5},{5,4},{6,7},{7,6},{8,9},{9,8},{10,11... | collective-permute-start | bytes 294920 | tf_op jit(solution)/shard_map/ppermute | solution.py:60
  369.5 4.3 %collective-permute-done.62 = f32[192,64]{0,1:T(8,128)S(1)} collective-permute-done((f32[192,64]{0,1:T(8,128)S(1)}, f32[192,64]{0,1:T(8,128)S(1)}, u32[]{:S(2)}, u32[]{:S(2)}) %collective-permute-start.62) | collective-permute-done | bytes 49184 | tf_op jit(solution)/shard_map/ppermute | solution.py:60
  375.9 5.4 %collective-permute-done.63 = f32[96,64]{0,1:T(8,128)S(1)} collective-permute-done((f32[96,64]{0,1:T(8,128)S(1)}, f32[96,64]{0,1:T(8,128)S(1)}, u32[]{:S(2)}, u32[]{:S(2)}) %collective-permute-start.63) | collective-permute-done | bytes 24608 | tf_op jit(solution)/shard_map/ppermute | solution.py:60
  383.5 6.6 %collective-permute-start.64 = (f32[48,64]{0,1:T(8,128)}, f32[48,64]{0,1:T(8,128)}, u32[]{:S(2)}, u32[]{:S(2)}) collective-permute-start(f32[48,64]{0,1:T(8,128)} %slice_select_fusion.10), channel_id=1, source_target_pairs={{0,8},{1,9},{2,10},{3,11},{4,12},{5,13},{6,14},{7,15},{8,0},{9,1},... | collective-permute-start | bytes 36872 | tf_op jit(solution)/shard_map/ppermute | solution.py:60
  390.0 3.6 fusion.18
  393.6 4.7 %collective-permute-done.64 = f32[48,64]{0,1:T(8,128)} collective-permute-done((f32[48,64]{0,1:T(8,128)}, f32[48,64]{0,1:T(8,128)}, u32[]{:S(2)}, u32[]{:S(2)}) %collective-permute-start.64) | collective-permute-done | bytes 12320 | tf_op jit(solution)/shard_map/ppermute | solution.py:60
  398.4 2.0 fusion.32
  (279 shorter events, 86.8 us)
Async XLA Ops:
  1.2 28.1 %collective-permute-start.4 = (bf16[48,64]{1,0:T(8,128)(2,1)S(1)}, bf16[48,64]{1,0:T(8,128)(2,1)S(1)}, u32[]{:S(2)}, u32[]{:S(2)}) collective-permute-start(bf16[48,64]{1,0:T(8,128)(2,1)S(1)} %convolution_convert_fusion.5), channel_id=1, source_target_pairs={{0,256},{16,272},{32,288},{48,304},{64,320},{80,336},{96,352},{112... | collective-permute-start | bytes 18440 | tf_op jit(solution)/shard_map/ppermute | solution.py:42
  17.2 33.9 %collective-permute-start = (bf16[64,384]{1,0:T(8,128)(2,1)}, bf16[64,384]{1,0:T(8,128)(2,1)}, u32[]{:S(2)}, u32[]{:S(2)}) collective-permute-start(bf16[64,384]{1,0:T(8,128)(2,1)} %get-tuple-element.27), channel_id=1, source_target_pairs={{0,16},{16,32},{32,48},{48,64},{64,80},{80,96},{96,112},{112,128},... | collective-permute-start | bytes 147464 | tf_op jit(solution)/shard_map/ppermute | solution.py:16
  21.3 30.6 %collective-permute-start.1 = (bf16[64,384]{1,0:T(8,128)(2,1)}, bf16[64,384]{1,0:T(8,128)(2,1)}, u32[]{:S(2)}, u32[]{:S(2)}) collective-permute-start(bf16[64,384]{1,0:T(8,128)(2,1)} %get-tuple-element.28), channel_id=1, source_target_pairs={{16,0},{32,16},{48,32},{64,48},{80,64},{96,80},{112,96},{128,112},... | collective-permute-start | bytes 147464 | tf_op jit(solution)/shard_map/ppermute | solution.py:16
  29.3 9.6 %collective-permute-start.5 = (bf16[96,64]{1,0:T(8,128)(2,1)S(1)}, bf16[96,64]{1,0:T(8,128)(2,1)S(1)}, u32[]{:S(2)}, u32[]{:S(2)}) collective-permute-start(bf16[96,64]{1,0:T(8,128)(2,1)S(1)} %maximum_select_fusion.25), channel_id=1, source_target_pairs={{0,128},{16,144},{32,160},{48,176},{64,192},{80,208},{96,224},{112... | collective-permute-start | bytes 36872 | tf_op jit(solution)/shard_map/ppermute | solution.py:42
  38.9 8.2 %collective-permute-start.6 = (bf16[192,64]{1,0:T(8,128)(2,1)S(1)}, bf16[192,64]{1,0:T(8,128)(2,1)}, u32[]{:S(2)}, u32[]{:S(2)}) collective-permute-start(bf16[192,64]{1,0:T(8,128)(2,1)S(1)} %maximum_select_fusion.20), channel_id=1, source_target_pairs={{0,64},{16,80},{32,96},{48,112},{64,0},{80,16},{96,32},{112,48},{1... | collective-permute-start | bytes 73736 | tf_op jit(solution)/shard_map/ppermute | solution.py:42
  48.1 25.0 %collective-permute-start.7 = (bf16[384,64]{1,0:T(8,128)(2,1)S(1)}, bf16[384,64]{1,0:T(8,128)(2,1)S(1)}, u32[]{:S(2)}, u32[]{:S(2)}) collective-permute-start(bf16[384,64]{1,0:T(8,128)(2,1)S(1)} %maximum_select_fusion.15), channel_id=1, source_target_pairs={{0,32},{16,48},{32,0},{48,16},{64,96},{80,112},{96,64},{112,80},{1... | collective-permute-start | bytes 147464 | tf_op jit(solution)/shard_map/ppermute | solution.py:42
  52.6 5.6 %collective-permute-start.2 = (bf16[64,384]{1,0:T(8,128)(2,1)S(1)}, bf16[64,384]{1,0:T(8,128)(2,1)S(1)}, u32[]{:S(2)}, u32[]{:S(2)}) collective-permute-start(bf16[64,384]{1,0:T(8,128)(2,1)S(1)} %pad_maximum_fusion.1), channel_id=1, source_target_pairs={{0,1},{1,2},{2,3},{3,4},{4,5},{5,6},{6,7},{7,8},{8,9},{9,10},{10,1... | collective-permute-start | bytes 147464 | tf_op jit(solution)/shard_map/ppermute | solution.py:16
  54.6 10.4 %collective-permute-start.3 = (bf16[64,384]{1,0:T(8,128)(2,1)S(1)}, bf16[64,384]{1,0:T(8,128)(2,1)S(1)}, u32[]{:S(2)}, u32[]{:S(2)}) collective-permute-start(bf16[64,384]{1,0:T(8,128)(2,1)S(1)} %pad_maximum_fusion.2), channel_id=1, source_target_pairs={{1,0},{2,1},{3,2},{4,3},{5,4},{6,5},{7,6},{8,7},{9,8},{10,9},{11,1... | collective-permute-start | bytes 147464 | tf_op jit(solution)/shard_map/ppermute | solution.py:16
  67.5 9.6 %collective-permute-start.17 = (bf16[48,64]{1,0:T(8,128)(2,1)S(1)}, bf16[48,64]{1,0:T(8,128)(2,1)S(1)}, u32[]{:S(2)}, u32[]{:S(2)}) collective-permute-start(bf16[48,64]{1,0:T(8,128)(2,1)S(1)} %fusion.57), channel_id=1, source_target_pairs={{0,256},{16,272},{32,288},{48,304},{64,320},{80,336},{96,352},{112... | collective-permute-start | bytes 18440 | tf_op jit(solution)/shard_map/ppermute | solution.py:42
  73.1 13.5 %collective-permute-start.8 = (bf16[768,64]{1,0:T(8,128)(2,1)S(1)}, bf16[768,64]{1,0:T(8,128)(2,1)S(1)}, u32[]{:S(2)}, u32[]{:S(2)}) collective-permute-start(bf16[768,64]{1,0:T(8,128)(2,1)S(1)} %maximum_select_fusion.10), channel_id=1, source_target_pairs={{0,16},{16,0},{32,48},{48,32},{64,80},{80,64},{96,112},{112,96},{1... | collective-permute-start | bytes 294920 | tf_op jit(solution)/shard_map/ppermute | solution.py:42
  77.1 6.6 %collective-permute-start.18 = (bf16[96,64]{1,0:T(8,128)(2,1)S(1)}, bf16[96,64]{1,0:T(8,128)(2,1)S(1)}, u32[]{:S(2)}, u32[]{:S(2)}) collective-permute-start(bf16[96,64]{1,0:T(8,128)(2,1)S(1)} %maximum_select_fusion.26), channel_id=1, source_target_pairs={{0,128},{16,144},{32,160},{48,176},{64,192},{80,208},{96,224},{112... | collective-permute-start | bytes 36872 | tf_op jit(solution)/shard_map/ppermute | solution.py:42
  83.8 16.5 %collective-permute-start.19 = (bf16[192,64]{1,0:T(8,128)(2,1)S(1)}, bf16[192,64]{1,0:T(8,128)(2,1)S(1)}, u32[]{:S(2)}, u32[]{:S(2)}) collective-permute-start(bf16[192,64]{1,0:T(8,128)(2,1)S(1)} %maximum_select_fusion.21), channel_id=1, source_target_pairs={{0,64},{16,80},{32,96},{48,112},{64,0},{80,16},{96,32},{112,48},{1... | collective-permute-start | bytes 73736 | tf_op jit(solution)/shard_map/ppermute | solution.py:42
  87.3 17.6 %collective-permute-start.9 = (f32[384,64]{0,1:T(8,128)S(1)}, f32[384,64]{0,1:T(8,128)S(1)}, u32[]{:S(2)}, u32[]{:S(2)}) collective-permute-start(f32[384,64]{0,1:T(8,128)S(1)} %slice_select_fusion.4), channel_id=1, source_target_pairs={{0,1},{1,0},{2,3},{3,2},{4,5},{5,4},{6,7},{7,6},{8,9},{9,8},{10,11... | collective-permute-start | bytes 294920 | tf_op jit(solution)/shard_map/ppermute | solution.py:60
  100.3 8.1 %collective-permute-start.20 = (bf16[384,64]{1,0:T(8,128)(2,1)S(1)}, bf16[384,64]{1,0:T(8,128)(2,1)S(1)}, u32[]{:S(2)}, u32[]{:S(2)}) collective-permute-start(bf16[384,64]{1,0:T(8,128)(2,1)S(1)} %maximum_select_fusion.16), channel_id=1, source_target_pairs={{0,32},{16,48},{32,0},{48,16},{64,96},{80,112},{96,64},{112,80},{1... | collective-permute-start | bytes 147464 | tf_op jit(solution)/shard_map/ppermute | solution.py:42
  105.1 6.2 %collective-permute-start.10 = (f32[192,64]{0,1:T(8,128)S(1)}, f32[192,64]{0,1:T(8,128)S(1)}, u32[]{:S(2)}, u32[]{:S(2)}) collective-permute-start(f32[192,64]{0,1:T(8,128)S(1)} %slice_select_fusion.9), channel_id=1, source_target_pairs={{0,2},{1,3},{2,0},{3,1},{4,6},{5,7},{6,4},{7,5},{8,10},{9,11},{10,... | collective-permute-start | bytes 147464 | tf_op jit(solution)/shard_map/ppermute | solution.py:60
  108.5 7.9 %collective-permute-start.21 = (bf16[768,64]{1,0:T(8,128)(2,1)S(1)}, bf16[768,64]{1,0:T(8,128)(2,1)S(1)}, u32[]{:S(2)}, u32[]{:S(2)}) collective-permute-start(bf16[768,64]{1,0:T(8,128)(2,1)S(1)} %maximum_select_fusion.11), channel_id=1, source_target_pairs={{0,16},{16,0},{32,48},{48,32},{64,80},{80,64},{96,112},{112,96},{1... | collective-permute-start | bytes 294920 | tf_op jit(solution)/shard_map/ppermute | solution.py:42
  111.4 7.4 %collective-permute-start.11 = (f32[96,64]{0,1:T(8,128)S(1)}, f32[96,64]{0,1:T(8,128)S(1)}, u32[]{:S(2)}, u32[]{:S(2)}) collective-permute-start(f32[96,64]{0,1:T(8,128)S(1)} %slice_select_fusion.19), channel_id=1, source_target_pairs={{0,4},{1,5},{2,6},{3,7},{4,0},{5,1},{6,2},{7,3},{8,12},{9,13},{10,... | collective-permute-start | bytes 73736 | tf_op jit(solution)/shard_map/ppermute | solution.py:60
  119.0 14.5 %collective-permute-start.12 = (f32[48,64]{0,1:T(8,128)S(1)}, f32[48,64]{0,1:T(8,128)S(1)}, u32[]{:S(2)}, u32[]{:S(2)}) collective-permute-start(f32[48,64]{0,1:T(8,128)S(1)} %slice_select_fusion.18), channel_id=1, source_target_pairs={{0,8},{1,9},{2,10},{3,11},{4,12},{5,13},{6,14},{7,15},{8,0},{9,1},... | collective-permute-start | bytes 36872 | tf_op jit(solution)/shard_map/ppermute | solution.py:60
  121.0 17.7 %collective-permute-start.22 = (f32[384,64]{0,1:T(8,128)S(1)}, f32[384,64]{0,1:T(8,128)S(1)}, u32[]{:S(2)}, u32[]{:S(2)}) collective-permute-start(f32[384,64]{0,1:T(8,128)S(1)} %slice_select_fusion.3), channel_id=1, source_target_pairs={{0,1},{1,0},{2,3},{3,2},{4,5},{5,4},{6,7},{7,6},{8,9},{9,8},{10,11... | collective-permute-start | bytes 294920 | tf_op jit(solution)/shard_map/ppermute | solution.py:60
  134.2 7.1 %collective-permute-start.13 = (bf16[64,384]{1,0:T(8,128)(2,1)S(1)}, bf16[64,384]{1,0:T(8,128)(2,1)S(1)}, u32[]{:S(2)}, u32[]{:S(2)}) collective-permute-start(bf16[64,384]{1,0:T(8,128)(2,1)S(1)} %get-tuple-element.19), channel_id=1, source_target_pairs={{0,16},{16,32},{32,48},{48,64},{64,80},{80,96},{96,112},{112,128},... | collective-permute-start | bytes 147464 | tf_op jit(solution)/shard_map/ppermute | solution.py:16
  137.3 6.4 %collective-permute-start.14 = (bf16[64,384]{1,0:T(8,128)(2,1)S(1)}, bf16[64,384]{1,0:T(8,128)(2,1)S(1)}, u32[]{:S(2)}, u32[]{:S(2)}) collective-permute-start(bf16[64,384]{1,0:T(8,128)(2,1)S(1)} %get-tuple-element.20), channel_id=1, source_target_pairs={{16,0},{32,16},{48,32},{64,48},{80,64},{96,80},{112,96},{128,112},... | collective-permute-start | bytes 147464 | tf_op jit(solution)/shard_map/ppermute | solution.py:16
  138.8 6.9 %collective-permute-start.23 = (f32[192,64]{0,1:T(8,128)S(1)}, f32[192,64]{0,1:T(8,128)S(1)}, u32[]{:S(2)}, u32[]{:S(2)}) collective-permute-start(f32[192,64]{0,1:T(8,128)S(1)} %slice_select_fusion.8), channel_id=1, source_target_pairs={{0,2},{1,3},{2,0},{3,1},{4,6},{5,7},{6,4},{7,5},{8,10},{9,11},{10,... | collective-permute-start | bytes 147464 | tf_op jit(solution)/shard_map/ppermute | solution.py:60
  143.7 11.8 %collective-permute-start.16 = (bf16[64,384]{1,0:T(8,128)(2,1)S(1)}, bf16[64,384]{1,0:T(8,128)(2,1)S(1)}, u32[]{:S(2)}, u32[]{:S(2)}) collective-permute-start(bf16[64,384]{1,0:T(8,128)(2,1)S(1)} %pad_maximum_fusion.4), channel_id=1, source_target_pairs={{1,0},{2,1},{3,2},{4,3},{5,4},{6,5},{7,6},{8,7},{9,8},{10,9},{11,1... | collective-permute-start | bytes 147464 | tf_op jit(solution)/shard_map/ppermute | solution.py:16
  145.8 7.3 %collective-permute-start.24 = (f32[96,64]{0,1:T(8,128)S(1)}, f32[96,64]{0,1:T(8,128)S(1)}, u32[]{:S(2)}, u32[]{:S(2)}) collective-permute-start(f32[96,64]{0,1:T(8,128)S(1)} %slice_select_fusion.17), channel_id=1, source_target_pairs={{0,4},{1,5},{2,6},{3,7},{4,0},{5,1},{6,2},{7,3},{8,12},{9,13},{10,... | collective-permute-start | bytes 73736 | tf_op jit(solution)/shard_map/ppermute | solution.py:60
  148.0 7.5 %collective-permute-start.15 = (bf16[64,384]{1,0:T(8,128)(2,1)S(1)}, bf16[64,384]{1,0:T(8,128)(2,1)S(1)}, u32[]{:S(2)}, u32[]{:S(2)}) collective-permute-start(bf16[64,384]{1,0:T(8,128)(2,1)S(1)} %pad_maximum_fusion.3), channel_id=1, source_target_pairs={{0,1},{1,2},{2,3},{3,4},{4,5},{5,6},{6,7},{7,8},{8,9},{9,10},{10,1... | collective-permute-start | bytes 147464 | tf_op jit(solution)/shard_map/ppermute | solution.py:16
  153.3 15.1 %collective-permute-start.25 = (f32[48,64]{0,1:T(8,128)S(1)}, f32[48,64]{0,1:T(8,128)S(1)}, u32[]{:S(2)}, u32[]{:S(2)}) collective-permute-start(f32[48,64]{0,1:T(8,128)S(1)} %slice_select_fusion.16), channel_id=1, source_target_pairs={{0,8},{1,9},{2,10},{3,11},{4,12},{5,13},{6,14},{7,15},{8,0},{9,1},... | collective-permute-start | bytes 36872 | tf_op jit(solution)/shard_map/ppermute | solution.py:60
  156.7 13.3 %collective-permute-start.30 = (bf16[48,64]{1,0:T(8,128)(2,1)S(1)}, bf16[48,64]{1,0:T(8,128)(2,1)S(1)}, u32[]{:S(2)}, u32[]{:S(2)}) collective-permute-start(bf16[48,64]{1,0:T(8,128)(2,1)S(1)} %fusion.58), channel_id=1, source_target_pairs={{0,256},{16,272},{32,288},{48,304},{64,320},{80,336},{96,352},{112... | collective-permute-start | bytes 18440 | tf_op jit(solution)/shard_map/ppermute | solution.py:42
  170.0 7.0 %collective-permute-start.31 = (bf16[96,64]{1,0:T(8,128)(2,1)S(1)}, bf16[96,64]{1,0:T(8,128)(2,1)S(1)}, u32[]{:S(2)}, u32[]{:S(2)}) collective-permute-start(bf16[96,64]{1,0:T(8,128)(2,1)S(1)} %maximum_select_fusion.27), channel_id=1, source_target_pairs={{0,128},{16,144},{32,160},{48,176},{64,192},{80,208},{96,224},{112... | collective-permute-start | bytes 36872 | tf_op jit(solution)/shard_map/ppermute | solution.py:42
  177.1 6.9 %collective-permute-start.32 = (bf16[192,64]{1,0:T(8,128)(2,1)S(1)}, bf16[192,64]{1,0:T(8,128)(2,1)S(1)}, u32[]{:S(2)}, u32[]{:S(2)}) collective-permute-start(bf16[192,64]{1,0:T(8,128)(2,1)S(1)} %maximum_select_fusion.22), channel_id=1, source_target_pairs={{0,64},{16,80},{32,96},{48,112},{64,0},{80,16},{96,32},{112,48},{1... | collective-permute-start | bytes 73736 | tf_op jit(solution)/shard_map/ppermute | solution.py:42
  180.9 11.8 %collective-permute-start.26 = (bf16[64,384]{1,0:T(8,128)(2,1)S(1)}, bf16[64,384]{1,0:T(8,128)(2,1)S(1)}, u32[]{:S(2)}, u32[]{:S(2)}) collective-permute-start(bf16[64,384]{1,0:T(8,128)(2,1)S(1)} %get-tuple-element.15), channel_id=1, source_target_pairs={{0,16},{16,32},{32,48},{48,64},{64,80},{80,96},{96,112},{112,128},... | collective-permute-start | bytes 147464 | tf_op jit(solution)/shard_map/ppermute | solution.py:16
  182.7 10.1 %collective-permute-start.27 = (bf16[64,384]{1,0:T(8,128)(2,1)S(1)}, bf16[64,384]{1,0:T(8,128)(2,1)S(1)}, u32[]{:S(2)}, u32[]{:S(2)}) collective-permute-start(bf16[64,384]{1,0:T(8,128)(2,1)S(1)} %get-tuple-element.16), channel_id=1, source_target_pairs={{16,0},{32,16},{48,32},{64,48},{80,64},{96,80},{112,96},{128,112},... | collective-permute-start | bytes 147464 | tf_op jit(solution)/shard_map/ppermute | solution.py:16
  184.0 33.5 %collective-permute-start.33 = (bf16[384,64]{1,0:T(8,128)(2,1)S(1)}, bf16[384,64]{1,0:T(8,128)(2,1)S(1)}, u32[]{:S(2)}, u32[]{:S(2)}) collective-permute-start(bf16[384,64]{1,0:T(8,128)(2,1)S(1)} %maximum_select_fusion.17), channel_id=1, source_target_pairs={{0,32},{16,48},{32,0},{48,16},{64,96},{80,112},{96,64},{112,80},{1... | collective-permute-start | bytes 147464 | tf_op jit(solution)/shard_map/ppermute | solution.py:42
  195.2 15.7 %collective-permute-start.29 = (bf16[64,384]{1,0:T(8,128)(2,1)S(1)}, bf16[64,384]{1,0:T(8,128)(2,1)S(1)}, u32[]{:S(2)}, u32[]{:S(2)}) collective-permute-start(bf16[64,384]{1,0:T(8,128)(2,1)S(1)} %pad_maximum_fusion.6), channel_id=1, source_target_pairs={{1,0},{2,1},{3,2},{4,3},{5,4},{6,5},{7,6},{8,7},{9,8},{10,9},{11,1... | collective-permute-start | bytes 147464 | tf_op jit(solution)/shard_map/ppermute | solution.py:16
  211.7 9.5 %collective-permute-start.43 = (bf16[48,64]{1,0:T(8,128)(2,1)S(1)}, bf16[48,64]{1,0:T(8,128)(2,1)S(1)}, u32[]{:S(2)}, u32[]{:S(2)}) collective-permute-start(bf16[48,64]{1,0:T(8,128)(2,1)S(1)} %fusion.59), channel_id=1, source_target_pairs={{0,256},{16,272},{32,288},{48,304},{64,320},{80,336},{96,352},{112... | collective-permute-start | bytes 18440 | tf_op jit(solution)/shard_map/ppermute | solution.py:42
  217.6 12.3 %collective-permute-start.34 = (bf16[768,64]{1,0:T(8,128)(2,1)S(1)}, bf16[768,64]{1,0:T(8,128)(2,1)S(1)}, u32[]{:S(2)}, u32[]{:S(2)}) collective-permute-start(bf16[768,64]{1,0:T(8,128)(2,1)S(1)} %maximum_select_fusion.12), channel_id=1, source_target_pairs={{0,16},{16,0},{32,48},{48,32},{64,80},{80,64},{96,112},{112,96},{1... | collective-permute-start | bytes 294920 | tf_op jit(solution)/shard_map/ppermute | solution.py:42
  221.2 6.6 %collective-permute-start.44 = (bf16[96,64]{1,0:T(8,128)(2,1)S(1)}, bf16[96,64]{1,0:T(8,128)(2,1)S(1)}, u32[]{:S(2)}, u32[]{:S(2)}) collective-permute-start(bf16[96,64]{1,0:T(8,128)(2,1)S(1)} %maximum_select_fusion.28), channel_id=1, source_target_pairs={{0,128},{16,144},{32,160},{48,176},{64,192},{80,208},{96,224},{112... | collective-permute-start | bytes 36872 | tf_op jit(solution)/shard_map/ppermute | solution.py:42
  227.8 16.6 %collective-permute-start.45 = (bf16[192,64]{1,0:T(8,128)(2,1)S(1)}, bf16[192,64]{1,0:T(8,128)(2,1)S(1)}, u32[]{:S(2)}, u32[]{:S(2)}) collective-permute-start(bf16[192,64]{1,0:T(8,128)(2,1)S(1)} %maximum_select_fusion.23), channel_id=1, source_target_pairs={{0,64},{16,80},{32,96},{48,112},{64,0},{80,16},{96,32},{112,48},{1... | collective-permute-start | bytes 73736 | tf_op jit(solution)/shard_map/ppermute | solution.py:42
  230.5 20.4 %collective-permute-start.35 = (f32[384,64]{0,1:T(8,128)S(1)}, f32[384,64]{0,1:T(8,128)S(1)}, u32[]{:S(2)}, u32[]{:S(2)}) collective-permute-start(f32[384,64]{0,1:T(8,128)S(1)} %slice_select_fusion.2), channel_id=1, source_target_pairs={{0,1},{1,0},{2,3},{3,2},{4,5},{5,4},{6,7},{7,6},{8,9},{9,8},{10,11... | collective-permute-start | bytes 294920 | tf_op jit(solution)/shard_map/ppermute | solution.py:60
  244.4 9.7 %collective-permute-start.46 = (bf16[384,64]{1,0:T(8,128)(2,1)S(1)}, bf16[384,64]{1,0:T(8,128)(2,1)S(1)}, u32[]{:S(2)}, u32[]{:S(2)}) collective-permute-start(bf16[384,64]{1,0:T(8,128)(2,1)S(1)} %maximum_select_fusion.18), channel_id=1, source_target_pairs={{0,32},{16,48},{32,0},{48,16},{64,96},{80,112},{96,64},{112,80},{1... | collective-permute-start | bytes 147464 | tf_op jit(solution)/shard_map/ppermute | solution.py:42
  250.9 6.2 %collective-permute-start.36 = (f32[192,64]{0,1:T(8,128)S(1)}, f32[192,64]{0,1:T(8,128)S(1)}, u32[]{:S(2)}, u32[]{:S(2)}) collective-permute-start(f32[192,64]{0,1:T(8,128)S(1)} %slice_select_fusion.7), channel_id=1, source_target_pairs={{0,2},{1,3},{2,0},{3,1},{4,6},{5,7},{6,4},{7,5},{8,10},{9,11},{10,... | collective-permute-start | bytes 147464 | tf_op jit(solution)/shard_map/ppermute | solution.py:60
  254.2 8.5 %collective-permute-start.47 = (bf16[768,64]{1,0:T(8,128)(2,1)S(1)}, bf16[768,64]{1,0:T(8,128)(2,1)S(1)}, u32[]{:S(2)}, u32[]{:S(2)}) collective-permute-start(bf16[768,64]{1,0:T(8,128)(2,1)S(1)} %maximum_select_fusion.13), channel_id=1, source_target_pairs={{0,16},{16,0},{32,48},{48,32},{64,80},{80,64},{96,112},{112,96},{1... | collective-permute-start | bytes 294920 | tf_op jit(solution)/shard_map/ppermute | solution.py:42
  257.3 7.3 %collective-permute-start.37 = (f32[96,64]{0,1:T(8,128)S(1)}, f32[96,64]{0,1:T(8,128)S(1)}, u32[]{:S(2)}, u32[]{:S(2)}) collective-permute-start(f32[96,64]{0,1:T(8,128)S(1)} %slice_select_fusion.15), channel_id=1, source_target_pairs={{0,4},{1,5},{2,6},{3,7},{4,0},{5,1},{6,2},{7,3},{8,12},{9,13},{10,... | collective-permute-start | bytes 73736 | tf_op jit(solution)/shard_map/ppermute | solution.py:60
  264.7 14.8 %collective-permute-start.38 = (f32[48,64]{0,1:T(8,128)S(1)}, f32[48,64]{0,1:T(8,128)S(1)}, u32[]{:S(2)}, u32[]{:S(2)}) collective-permute-start(f32[48,64]{0,1:T(8,128)S(1)} %slice_select_fusion.14), channel_id=1, source_target_pairs={{0,8},{1,9},{2,10},{3,11},{4,12},{5,13},{6,14},{7,15},{8,0},{9,1},... | collective-permute-start | bytes 36872 | tf_op jit(solution)/shard_map/ppermute | solution.py:60
  266.7 17.8 %collective-permute-start.48 = (f32[384,64]{0,1:T(8,128)S(1)}, f32[384,64]{0,1:T(8,128)S(1)}, u32[]{:S(2)}, u32[]{:S(2)}) collective-permute-start(f32[384,64]{0,1:T(8,128)S(1)} %slice_select_fusion.1), channel_id=1, source_target_pairs={{0,1},{1,0},{2,3},{3,2},{4,5},{5,4},{6,7},{7,6},{8,9},{9,8},{10,11... | collective-permute-start | bytes 294920 | tf_op jit(solution)/shard_map/ppermute | solution.py:60
  280.2 6.8 %collective-permute-start.39 = (bf16[64,384]{1,0:T(8,128)(2,1)S(1)}, bf16[64,384]{1,0:T(8,128)(2,1)S(1)}, u32[]{:S(2)}, u32[]{:S(2)}) collective-permute-start(bf16[64,384]{1,0:T(8,128)(2,1)S(1)} %get-tuple-element.11), channel_id=1, source_target_pairs={{0,16},{16,32},{32,48},{48,64},{64,80},{80,96},{96,112},{112,128},... | collective-permute-start | bytes 147464 | tf_op jit(solution)/shard_map/ppermute | solution.py:16
  283.2 6.4 %collective-permute-start.40 = (bf16[64,384]{1,0:T(8,128)(2,1)S(1)}, bf16[64,384]{1,0:T(8,128)(2,1)S(1)}, u32[]{:S(2)}, u32[]{:S(2)}) collective-permute-start(bf16[64,384]{1,0:T(8,128)(2,1)S(1)} %get-tuple-element.12), channel_id=1, source_target_pairs={{16,0},{32,16},{48,32},{64,48},{80,64},{96,80},{112,96},{128,112},... | collective-permute-start | bytes 147464 | tf_op jit(solution)/shard_map/ppermute | solution.py:16
  284.6 7.0 %collective-permute-start.49 = (f32[192,64]{0,1:T(8,128)S(1)}, f32[192,64]{0,1:T(8,128)S(1)}, u32[]{:S(2)}, u32[]{:S(2)}) collective-permute-start(f32[192,64]{0,1:T(8,128)S(1)} %slice_select_fusion.6), channel_id=1, source_target_pairs={{0,2},{1,3},{2,0},{3,1},{4,6},{5,7},{6,4},{7,5},{8,10},{9,11},{10,... | collective-permute-start | bytes 147464 | tf_op jit(solution)/shard_map/ppermute | solution.py:60
  289.6 11.5 %collective-permute-start.42 = (bf16[64,384]{1,0:T(8,128)(2,1)S(1)}, bf16[64,384]{1,0:T(8,128)(2,1)S(1)}, u32[]{:S(2)}, u32[]{:S(2)}) collective-permute-start(bf16[64,384]{1,0:T(8,128)(2,1)S(1)} %pad_maximum_fusion.8), channel_id=1, source_target_pairs={{1,0},{2,1},{3,2},{4,3},{5,4},{6,5},{7,6},{8,7},{9,8},{10,9},{11,1... | collective-permute-start | bytes 147464 | tf_op jit(solution)/shard_map/ppermute | solution.py:16
  291.7 7.3 %collective-permute-start.50 = (f32[96,64]{0,1:T(8,128)S(1)}, f32[96,64]{0,1:T(8,128)S(1)}, u32[]{:S(2)}, u32[]{:S(2)}) collective-permute-start(f32[96,64]{0,1:T(8,128)S(1)} %slice_select_fusion.13), channel_id=1, source_target_pairs={{0,4},{1,5},{2,6},{3,7},{4,0},{5,1},{6,2},{7,3},{8,12},{9,13},{10,... | collective-permute-start | bytes 73736 | tf_op jit(solution)/shard_map/ppermute | solution.py:60
  293.9 7.3 %collective-permute-start.41 = (bf16[64,384]{1,0:T(8,128)(2,1)S(1)}, bf16[64,384]{1,0:T(8,128)(2,1)S(1)}, u32[]{:S(2)}, u32[]{:S(2)}) collective-permute-start(bf16[64,384]{1,0:T(8,128)(2,1)S(1)} %pad_maximum_fusion.7), channel_id=1, source_target_pairs={{0,1},{1,2},{2,3},{3,4},{4,5},{5,6},{6,7},{7,8},{8,9},{9,10},{10,1... | collective-permute-start | bytes 147464 | tf_op jit(solution)/shard_map/ppermute | solution.py:16
  299.2 15.3 %collective-permute-start.51 = (f32[48,64]{0,1:T(8,128)S(1)}, f32[48,64]{0,1:T(8,128)S(1)}, u32[]{:S(2)}, u32[]{:S(2)}) collective-permute-start(f32[48,64]{0,1:T(8,128)S(1)} %slice_select_fusion.12), channel_id=1, source_target_pairs={{0,8},{1,9},{2,10},{3,11},{4,12},{5,13},{6,14},{7,15},{8,0},{9,1},... | collective-permute-start | bytes 36872 | tf_op jit(solution)/shard_map/ppermute | solution.py:60
  302.3 13.1 %collective-permute-start.56 = (bf16[48,64]{1,0:T(8,128)(2,1)S(1)}, bf16[48,64]{1,0:T(8,128)(2,1)S(1)}, u32[]{:S(2)}, u32[]{:S(2)}) collective-permute-start(bf16[48,64]{1,0:T(8,128)(2,1)S(1)} %fusion.60), channel_id=1, source_target_pairs={{0,256},{16,272},{32,288},{48,304},{64,320},{80,336},{96,352},{112... | collective-permute-start | bytes 18440 | tf_op jit(solution)/shard_map/ppermute | solution.py:42
  315.4 9.1 %collective-permute-start.57 = (bf16[96,64]{1,0:T(8,128)(2,1)S(1)}, bf16[96,64]{1,0:T(8,128)(2,1)S(1)}, u32[]{:S(2)}, u32[]{:S(2)}) collective-permute-start(bf16[96,64]{1,0:T(8,128)(2,1)S(1)} %maximum_select_fusion.29), channel_id=1, source_target_pairs={{0,128},{16,144},{32,160},{48,176},{64,192},{80,208},{96,224},{112... | collective-permute-start | bytes 36872 | tf_op jit(solution)/shard_map/ppermute | solution.py:42
  324.5 6.2 %collective-permute-start.58 = (bf16[192,64]{1,0:T(8,128)(2,1)S(1)}, bf16[192,64]{1,0:T(8,128)(2,1)S(1)}, u32[]{:S(2)}, u32[]{:S(2)}) collective-permute-start(bf16[192,64]{1,0:T(8,128)(2,1)S(1)} %maximum_select_fusion.24), channel_id=1, source_target_pairs={{0,64},{16,80},{32,96},{48,112},{64,0},{80,16},{96,32},{112,48},{1... | collective-permute-start | bytes 73736 | tf_op jit(solution)/shard_map/ppermute | solution.py:42
  328.1 9.2 %collective-permute-start.52 = (bf16[64,384]{1,0:T(8,128)(2,1)S(1)}, bf16[64,384]{1,0:T(8,128)(2,1)S(1)}, u32[]{:S(2)}, u32[]{:S(2)}) collective-permute-start(bf16[64,384]{1,0:T(8,128)(2,1)S(1)} %get-tuple-element.7), channel_id=1, source_target_pairs={{0,16},{16,32},{32,48},{48,64},{64,80},{80,96},{96,112},{112,128},... | collective-permute-start | bytes 147464 | tf_op jit(solution)/shard_map/ppermute | solution.py:16
  329.4 7.9 %collective-permute-start.53 = (bf16[64,384]{1,0:T(8,128)(2,1)S(1)}, bf16[64,384]{1,0:T(8,128)(2,1)S(1)}, u32[]{:S(2)}, u32[]{:S(2)}) collective-permute-start(bf16[64,384]{1,0:T(8,128)(2,1)S(1)} %get-tuple-element.8), channel_id=1, source_target_pairs={{16,0},{32,16},{48,32},{64,48},{80,64},{96,80},{112,96},{128,112},... | collective-permute-start | bytes 147464 | tf_op jit(solution)/shard_map/ppermute | solution.py:16
  330.8 11.8 %collective-permute-start.59 = (bf16[384,64]{1,0:T(8,128)(2,1)S(1)}, bf16[384,64]{1,0:T(8,128)(2,1)S(1)}, u32[]{:S(2)}, u32[]{:S(2)}) collective-permute-start(bf16[384,64]{1,0:T(8,128)(2,1)S(1)} %maximum_select_fusion.19), channel_id=1, source_target_pairs={{0,32},{16,48},{32,0},{48,16},{64,96},{80,112},{96,64},{112,80},{1... | collective-permute-start | bytes 147464 | tf_op jit(solution)/shard_map/ppermute | solution.py:42
  337.3 29.2 %collective-permute-start.55 = (bf16[64,384]{1,0:T(8,128)(2,1)S(1)}, bf16[64,384]{1,0:T(8,128)(2,1)S(1)}, u32[]{:S(2)}, u32[]{:S(2)}) collective-permute-start(bf16[64,384]{1,0:T(8,128)(2,1)S(1)} %pad_maximum_fusion.10), channel_id=1, source_target_pairs={{1,0},{2,1},{3,2},{4,3},{5,4},{6,5},{7,6},{8,7},{9,8},{10,9},{11,1... | collective-permute-start | bytes 147464 | tf_op jit(solution)/shard_map/ppermute | solution.py:16
  339.3 6.5 %collective-permute-start.54 = (bf16[64,384]{1,0:T(8,128)(2,1)S(1)}, bf16[64,384]{1,0:T(8,128)(2,1)S(1)}, u32[]{:S(2)}, u32[]{:S(2)}) collective-permute-start(bf16[64,384]{1,0:T(8,128)(2,1)S(1)} %pad_maximum_fusion.9), channel_id=1, source_target_pairs={{0,1},{1,2},{2,3},{3,4},{4,5},{5,6},{6,7},{7,8},{8,9},{9,10},{10,1... | collective-permute-start | bytes 147464 | tf_op jit(solution)/shard_map/ppermute | solution.py:16
  342.6 7.6 %collective-permute-start.60 = (bf16[768,64]{1,0:T(8,128)(2,1)S(1)}, bf16[768,64]{1,0:T(8,128)(2,1)S(1)}, u32[]{:S(2)}, u32[]{:S(2)}) collective-permute-start(bf16[768,64]{1,0:T(8,128)(2,1)S(1)} %maximum_select_fusion.14), channel_id=1, source_target_pairs={{0,16},{16,0},{32,48},{48,32},{64,80},{80,64},{96,112},{112,96},{1... | collective-permute-start | bytes 294920 | tf_op jit(solution)/shard_map/ppermute | solution.py:42
  350.8 16.6 %collective-permute-start.61 = (f32[384,64]{0,1:T(8,128)S(1)}, f32[384,64]{0,1:T(8,128)S(1)}, u32[]{:S(2)}, u32[]{:S(2)}) collective-permute-start(f32[384,64]{0,1:T(8,128)S(1)} %slice_select_fusion), channel_id=1, source_target_pairs={{0,1},{1,0},{2,3},{3,2},{4,5},{5,4},{6,7},{7,6},{8,9},{9,8},{10,11... | collective-permute-start | bytes 294920 | tf_op jit(solution)/shard_map/ppermute | solution.py:60
  367.5 6.2 %collective-permute-start.62 = (f32[192,64]{0,1:T(8,128)S(1)}, f32[192,64]{0,1:T(8,128)S(1)}, u32[]{:S(2)}, u32[]{:S(2)}) collective-permute-start(f32[192,64]{0,1:T(8,128)S(1)} %slice_select_fusion.5), channel_id=1, source_target_pairs={{0,2},{1,3},{2,0},{3,1},{4,6},{5,7},{6,4},{7,5},{8,10},{9,11},{10,... | collective-permute-start | bytes 147464 | tf_op jit(solution)/shard_map/ppermute | solution.py:60
  374.0 7.3 %collective-permute-start.63 = (f32[96,64]{0,1:T(8,128)S(1)}, f32[96,64]{0,1:T(8,128)S(1)}, u32[]{:S(2)}, u32[]{:S(2)}) collective-permute-start(f32[96,64]{0,1:T(8,128)S(1)} %slice_select_fusion.11), channel_id=1, source_target_pairs={{0,4},{1,5},{2,6},{3,7},{4,0},{5,1},{6,2},{7,3},{8,12},{9,13},{10,... | collective-permute-start | bytes 73736 | tf_op jit(solution)/shard_map/ppermute | solution.py:60
  383.5 14.9 %collective-permute-start.64 = (f32[48,64]{0,1:T(8,128)}, f32[48,64]{0,1:T(8,128)}, u32[]{:S(2)}, u32[]{:S(2)}) collective-permute-start(f32[48,64]{0,1:T(8,128)} %slice_select_fusion.10), channel_id=1, source_target_pairs={{0,8},{1,9},{2,10},{3,11},{4,12},{5,13},{6,14},{7,15},{8,0},{9,1},... | collective-permute-start | bytes 36872 | tf_op jit(solution)/shard_map/ppermute | solution.py:60
  (25 other events, 453.4 us)

commit v10 on v7

--- a/solution.py
+++ b/solution.py
@@ -57,7 +57,8 @@
         high = ((index >> bit) & 1) == 1
         keep = jnp.where(high, current[half:], current[:half])
         send = jnp.where(high, current[:half], current[half:])
-        current = keep + lax.ppermute(send, "col", route)
+        received = lax.ppermute(send.astype(jnp.bfloat16), "col", route)
+        current = keep + received.astype(jnp.float32)
     return current
 
 

time: 402 us -> 384 us (0.955)
  waiting for transfers between devices: 89.9 us -> 60.8 us
  starting transfers between devices: 258 us -> 270 us
    ppermute x20, waiting for transfers between devices: 54.6 us -> 37.5 us  [scatter_cols(): received = lax.ppermute(send.astype(jnp.bfloat16), 'col', route)]
    ppermute x20, starting transfers between devices: 76.4 us -> 88 us  [scatter_cols(): received = lax.ppermute(send.astype(jnp.bfloat16), 'col', route)]
    ppermute x20, waiting for transfers between devices: 11.2 us -> 3.58 us  [shifted(): return lax.ppermute(block, axis, route)]
    ppermute x25, waiting for transfers between devices: 24.1 us -> 19.8 us  [gather_rows(): other = lax.ppermute(current, 'row', route)]
  transfers between devices with their start and end apart: 65 -> 65, of which waited for: 25 -> 27; matrix products, arithmetic and copies ran while one was open for 8% -> 9% of each run, Pallas kernels for 0% -> 0%
where the time goes in v10:
time: 384 us; the launch traced here: 377 us
  starting transfers between devices  270 us (70%)
  waiting for transfers between devices  60.8 us (16%)
  matrix products  25.5 us (7%)
  local copies, waits for them, and re-layouts  10.8 us (3%)
  other arithmetic  8.14 us (2%)
    ppermute x25, starting transfers between devices, gather_rows(): other = lax.ppermute(current, 'row', route)  117 us
    ppermute x20, starting transfers between devices, scatter_cols(): received = lax.ppermute(send.astype(jnp.bfloat16), 'col', route)  88 us
    ppermute x20, starting transfers between devices, shifted(): return lax.ppermute(block, axis, route)  65.2 us
    ppermute x20, waiting for transfers between devices, scatter_cols(): received = lax.ppermute(send.astype(jnp.bfloat16), 'col', route)  37.5 us
    ppermute x25, waiting for transfers between devices, gather_rows(): other = lax.ppermute(current, 'row', route)  19.8 us
  transfers between devices with their start and end apart: 65, of which 27 were waited for; matrix products, arithmetic and copies ran while one was open for 9% of the time, Pallas kernels for 0%

profile of v10, /device:TPU:6, one launch (start us, length us, event | category | flops | bytes accessed | tf_op | source)
XLA Modules:
  0.0 377.2 jit_solution(6907964777508071914)
XLA Ops:
  2.1 2.3 constant_dynamic-update-slice_fusion.4
  8.3 5.2 %collective-permute-start = (bf16[64,384]{1,0:T(8,128)(2,1)}, bf16[64,384]{1,0:T(8,128)(2,1)}, u32[]{:S(2)}, u32[]{:S(2)}) collective-permute-start(bf16[64,384]{1,0:T(8,128)(2,1)} %get-tuple-element.27), channel_id=1, source_target_pairs={{0,16},{16,32},{32,48},{48,64},{64,80},{80,96},{96,112},{112,128},... | collective-permute-start | bytes 147464 | tf_op jit(solution)/shard_map/ppermute | solution.py:16
  13.6 9.0 %collective-permute-start.4 = (bf16[48,64]{1,0:T(8,128)(2,1)S(1)}, bf16[48,64]{1,0:T(8,128)(2,1)S(1)}, u32[]{:S(2)}, u32[]{:S(2)}) collective-permute-start(bf16[48,64]{1,0:T(8,128)(2,1)S(1)} %convolution_convert_fusion.5), channel_id=1, source_target_pairs={{0,256},{16,272},{32,288},{48,304},{64,320},{80,336},{96,352},{112... | collective-permute-start | bytes 18440 | tf_op jit(solution)/shard_map/ppermute | solution.py:42
  23.0 7.4 %convolution_convert_fusion = bf16[1536,768]{1,0:T(8,128)(2,1)} fusion(s32[768]{0:T(1024)S(1)} %copy-done.25, s32[1536]{0:T(1024)S(1)} %copy-done.24, bf16[1,1536,1,768]{3,1,2,0:T(8,128)(2,1)S(1)} %copy-done), kind=kOutput, calls=%fused_computation.5 | convolution fusion | flops 5441126400 | bytes 4727808 | tf_op jit(solution)/shard_map/dot_general | solution.py:117
  31.1 5.2 %collective-permute-start.5 = (bf16[96,64]{1,0:T(8,128)(2,1)S(1)}, bf16[96,64]{1,0:T(8,128)(2,1)S(1)}, u32[]{:S(2)}, u32[]{:S(2)}) collective-permute-start(bf16[96,64]{1,0:T(8,128)(2,1)S(1)} %maximum_select_fusion.25), channel_id=1, source_target_pairs={{0,128},{16,144},{32,160},{48,176},{64,192},{80,208},{96,224},{112... | collective-permute-start | bytes 36872 | tf_op jit(solution)/shard_map/ppermute | solution.py:42
  38.3 3.6 collective-permute-start.6
  47.3 5.1 %collective-permute-start.7 = (bf16[384,64]{1,0:T(8,128)(2,1)S(1)}, bf16[384,64]{1,0:T(8,128)(2,1)S(1)}, u32[]{:S(2)}, u32[]{:S(2)}) collective-permute-start(bf16[384,64]{1,0:T(8,128)(2,1)S(1)} %maximum_select_fusion.15), channel_id=1, source_target_pairs={{0,32},{16,48},{32,0},{48,16},{64,96},{80,112},{96,64},{112,80},{1... | collective-permute-start | bytes 147464 | tf_op jit(solution)/shard_map/ppermute | solution.py:42
  53.9 1.9 collective-permute-start.2
  55.9 3.6 collective-permute-start.3
  59.6 3.8 collective-permute-start.8
  63.4 2.3 collective-permute-done.3
  68.9 5.5 %collective-permute-start.17 = (bf16[48,64]{1,0:T(8,128)(2,1)S(1)}, bf16[48,64]{1,0:T(8,128)(2,1)S(1)}, u32[]{:S(2)}, u32[]{:S(2)}) collective-permute-start(bf16[48,64]{1,0:T(8,128)(2,1)S(1)} %fusion.56), channel_id=1, source_target_pairs={{0,256},{16,272},{32,288},{48,304},{64,320},{80,336},{96,352},{112... | collective-permute-start | bytes 18440 | tf_op jit(solution)/shard_map/ppermute | solution.py:42
  75.1 15.4 %collective-permute-start.9 = (bf16[384,64]{0,1:T(8,128)(2,1)S(1)}, bf16[384,64]{0,1:T(8,128)(2,1)S(1)}, u32[]{:S(2)}, u32[]{:S(2)}) collective-permute-start(bf16[384,64]{0,1:T(8,128)(2,1)S(1)} %select_convert_fusion.4), channel_id=1, source_target_pairs={{0,1},{1,0},{2,3},{3,2},{4,5},{5,4},{6,7},{7,6},{8,9},{9,8},{10,11... | collective-permute-start | bytes 147464 | tf_op jit(solution)/shard_map/ppermute | solution.py:60
  90.5 3.5 collective-permute-start.18
  94.0 1.9 collective-permute-start.10
  97.4 2.9 collective-permute-start.19
  103.4 3.8 %collective-permute-start.20 = (bf16[384,64]{1,0:T(8,128)(2,1)S(1)}, bf16[384,64]{1,0:T(8,128)(2,1)S(1)}, u32[]{:S(2)}, u32[]{:S(2)}) collective-permute-start(bf16[384,64]{1,0:T(8,128)(2,1)S(1)} %maximum_select_fusion.16), channel_id=1, source_target_pairs={{0,32},{16,48},{32,0},{48,16},{64,96},{80,112},{96,64},{112,80},{1... | collective-permute-start | bytes 147464 | tf_op jit(solution)/shard_map/ppermute | solution.py:42
  107.7 4.4 %collective-permute-start.12 = (bf16[48,64]{0,1:T(8,128)(2,1)S(1)}, bf16[48,64]{0,1:T(8,128)(2,1)S(1)}, u32[]{:S(2)}, u32[]{:S(2)}) collective-permute-start(bf16[48,64]{0,1:T(8,128)(2,1)S(1)} %select_convert_fusion.18), channel_id=1, source_target_pairs={{0,8},{1,9},{2,10},{3,11},{4,12},{5,13},{6,14},{7,15},{8,0},{9,1},... | collective-permute-start | bytes 18440 | tf_op jit(solution)/shard_map/ppermute | solution.py:60
  112.3 4.7 %collective-permute-start.21 = (bf16[768,64]{1,0:T(8,128)(2,1)S(1)}, bf16[768,64]{1,0:T(8,128)(2,1)S(1)}, u32[]{:S(2)}, u32[]{:S(2)}) collective-permute-start(bf16[768,64]{1,0:T(8,128)(2,1)S(1)} %maximum_select_fusion.11), channel_id=1, source_target_pairs={{0,16},{16,0},{32,48},{48,32},{64,80},{80,64},{96,112},{112,96},{1... | collective-permute-start | bytes 294920 | tf_op jit(solution)/shard_map/ppermute | solution.py:42
  117.0 5.1 %collective-permute-done.12 = bf16[48,64]{0,1:T(8,128)(2,1)S(1)} collective-permute-done((bf16[48,64]{0,1:T(8,128)(2,1)S(1)}, bf16[48,64]{0,1:T(8,128)(2,1)S(1)}, u32[]{:S(2)}, u32[]{:S(2)}) %collective-permute-start.12) | collective-permute-done | bytes 6176 | tf_op jit(solution)/shard_map/ppermute | solution.py:60
  124.1 6.9 %collective-permute-start.13 = (bf16[64,384]{1,0:T(8,128)(2,1)S(1)}, bf16[64,384]{1,0:T(8,128)(2,1)S(1)}, u32[]{:S(2)}, u32[]{:S(2)}) collective-permute-start(bf16[64,384]{1,0:T(8,128)(2,1)S(1)} %get-tuple-element.19), channel_id=1, source_target_pairs={{0,16},{16,32},{32,48},{48,64},{64,80},{80,96},{96,112},{112,128},... | collective-permute-start | bytes 147464 | tf_op jit(solution)/shard_map/ppermute | solution.py:16
  131.6 1.9 collective-permute-start.22
  134.8 2.0 collective-permute-start.23
  136.9 2.0 collective-permute-start.15
  140.8 2.3 collective-permute-start.24
  143.1 1.9 collective-permute-start.16
  145.0 3.0 collective-permute-done.24
  148.2 4.3 %collective-permute-start.25 = (bf16[48,64]{0,1:T(8,128)(2,1)S(1)}, bf16[48,64]{0,1:T(8,128)(2,1)S(1)}, u32[]{:S(2)}, u32[]{:S(2)}) collective-permute-start(bf16[48,64]{0,1:T(8,128)(2,1)S(1)} %select_convert_fusion.16), channel_id=1, source_target_pairs={{0,8},{1,9},{2,10},{3,11},{4,12},{5,13},{6,14},{7,15},{8,0},{9,1},... | collective-permute-start | bytes 18440 | tf_op jit(solution)/shard_map/ppermute | solution.py:60
  153.7 7.5 %collective-permute-start.30 = (bf16[48,64]{1,0:T(8,128)(2,1)S(1)}, bf16[48,64]{1,0:T(8,128)(2,1)S(1)}, u32[]{:S(2)}, u32[]{:S(2)}) collective-permute-start(bf16[48,64]{1,0:T(8,128)(2,1)S(1)} %fusion.57), channel_id=1, source_target_pairs={{0,256},{16,272},{32,288},{48,304},{64,320},{80,336},{96,352},{112... | collective-permute-start | bytes 18440 | tf_op jit(solution)/shard_map/ppermute | solution.py:42
  163.2 6.5 %collective-permute-start.31 = (bf16[96,64]{1,0:T(8,128)(2,1)S(1)}, bf16[96,64]{1,0:T(8,128)(2,1)S(1)}, u32[]{:S(2)}, u32[]{:S(2)}) collective-permute-start(bf16[96,64]{1,0:T(8,128)(2,1)S(1)} %maximum_select_fusion.27), channel_id=1, source_target_pairs={{0,128},{16,144},{32,160},{48,176},{64,192},{80,208},{96,224},{112... | collective-permute-start | bytes 36872 | tf_op jit(solution)/shard_map/ppermute | solution.py:42
  171.6 3.8 %collective-permute-start.32 = (bf16[192,64]{1,0:T(8,128)(2,1)S(1)}, bf16[192,64]{1,0:T(8,128)(2,1)S(1)}, u32[]{:S(2)}, u32[]{:S(2)}) collective-permute-start(bf16[192,64]{1,0:T(8,128)(2,1)S(1)} %maximum_select_fusion.22), channel_id=1, source_target_pairs={{0,64},{16,80},{32,96},{48,112},{64,0},{80,16},{96,32},{112,48},{1... | collective-permute-start | bytes 73736 | tf_op jit(solution)/shard_map/ppermute | solution.py:42
  176.7 4.5 %collective-permute-start.26 = (bf16[64,384]{1,0:T(8,128)(2,1)S(1)}, bf16[64,384]{1,0:T(8,128)(2,1)S(1)}, u32[]{:S(2)}, u32[]{:S(2)}) collective-permute-start(bf16[64,384]{1,0:T(8,128)(2,1)S(1)} %get-tuple-element.15), channel_id=1, source_target_pairs={{0,16},{16,32},{32,48},{48,64},{64,80},{80,96},{96,112},{112,128},... | collective-permute-start | bytes 147464 | tf_op jit(solution)/shard_map/ppermute | solution.py:16
  181.3 3.1 collective-permute-start.33
  184.5 7.5 %collective-permute-start.28 = (bf16[64,384]{1,0:T(8,128)(2,1)S(1)}, bf16[64,384]{1,0:T(8,128)(2,1)S(1)}, u32[]{:S(2)}, u32[]{:S(2)}) collective-permute-start(bf16[64,384]{1,0:T(8,128)(2,1)S(1)} %pad_maximum_fusion.5), channel_id=1, source_target_pairs={{0,1},{1,2},{2,3},{3,4},{4,5},{5,6},{6,7},{7,8},{8,9},{9,10},{10,1... | collective-permute-start | bytes 147464 | tf_op jit(solution)/shard_map/ppermute | solution.py:16
  192.0 1.9 collective-permute-start.29
  194.0 5.0 %collective-permute-start.34 = (bf16[768,64]{1,0:T(8,128)(2,1)S(1)}, bf16[768,64]{1,0:T(8,128)(2,1)S(1)}, u32[]{:S(2)}, u32[]{:S(2)}) collective-permute-start(bf16[768,64]{1,0:T(8,128)(2,1)S(1)} %maximum_select_fusion.12), channel_id=1, source_target_pairs={{0,16},{16,0},{32,48},{48,32},{64,80},{80,64},{96,112},{112,96},{1... | collective-permute-start | bytes 294920 | tf_op jit(solution)/shard_map/ppermute | solution.py:42
  201.5 10.7 %collective-permute-start.43 = (bf16[48,64]{1,0:T(8,128)(2,1)S(1)}, bf16[48,64]{1,0:T(8,128)(2,1)S(1)}, u32[]{:S(2)}, u32[]{:S(2)}) collective-permute-start(bf16[48,64]{1,0:T(8,128)(2,1)S(1)} %fusion.58), channel_id=1, source_target_pairs={{0,256},{16,272},{32,288},{48,304},{64,320},{80,336},{96,352},{112... | collective-permute-start | bytes 18440 | tf_op jit(solution)/shard_map/ppermute | solution.py:42
  212.8 15.2 %collective-permute-start.35 = (bf16[384,64]{0,1:T(8,128)(2,1)S(1)}, bf16[384,64]{0,1:T(8,128)(2,1)S(1)}, u32[]{:S(2)}, u32[]{:S(2)}) collective-permute-start(bf16[384,64]{0,1:T(8,128)(2,1)S(1)} %select_convert_fusion.2), channel_id=1, source_target_pairs={{0,1},{1,0},{2,3},{3,2},{4,5},{5,4},{6,7},{7,6},{8,9},{9,8},{10,11... | collective-permute-start | bytes 147464 | tf_op jit(solution)/shard_map/ppermute | solution.py:60
  230.2 1.9 collective-permute-start.36
  232.1 2.6 collective-permute-done.44
  238.8 2.0 collective-permute-done.45
  244.1 3.0 collective-permute-start.38
  248.8 1.9 collective-permute-start.47
  250.8 7.7 %collective-permute-done.38 = bf16[48,64]{0,1:T(8,128)(2,1)S(1)} collective-permute-done((bf16[48,64]{0,1:T(8,128)(2,1)S(1)}, bf16[48,64]{0,1:T(8,128)(2,1)S(1)}, u32[]{:S(2)}, u32[]{:S(2)}) %collective-permute-start.38) | collective-permute-done | bytes 6176 | tf_op jit(solution)/shard_map/ppermute | solution.py:60
  260.4 4.5 %collective-permute-start.39 = (bf16[64,384]{1,0:T(8,128)(2,1)S(1)}, bf16[64,384]{1,0:T(8,128)(2,1)S(1)}, u32[]{:S(2)}, u32[]{:S(2)}) collective-permute-start(bf16[64,384]{1,0:T(8,128)(2,1)S(1)} %get-tuple-element.11), channel_id=1, source_target_pairs={{0,16},{16,32},{32,48},{48,64},{64,80},{80,96},{96,112},{112,128},... | collective-permute-start | bytes 147464 | tf_op jit(solution)/shard_map/ppermute | solution.py:16
  270.8 2.1 collective-permute-start.41
  274.8 2.2 collective-permute-start.50
  279.0 3.0 collective-permute-done.50
  282.1 3.0 collective-permute-start.51
  286.4 10.2 %collective-permute-start.56 = (bf16[48,64]{1,0:T(8,128)(2,1)S(1)}, bf16[48,64]{1,0:T(8,128)(2,1)S(1)}, u32[]{:S(2)}, u32[]{:S(2)}) collective-permute-start(bf16[48,64]{1,0:T(8,128)(2,1)S(1)} %fusion.59), channel_id=1, source_target_pairs={{0,256},{16,272},{32,288},{48,304},{64,320},{80,336},{96,352},{112... | collective-permute-start | bytes 18440 | tf_op jit(solution)/shard_map/ppermute | solution.py:42
  298.6 3.6 collective-permute-start.57
  302.2 3.0 collective-permute-done.57
  305.3 4.4 %collective-permute-start.58 = (bf16[192,64]{1,0:T(8,128)(2,1)S(1)}, bf16[192,64]{1,0:T(8,128)(2,1)S(1)}, u32[]{:S(2)}, u32[]{:S(2)}) collective-permute-start(bf16[192,64]{1,0:T(8,128)(2,1)S(1)} %maximum_select_fusion.24), channel_id=1, source_target_pairs={{0,64},{16,80},{32,96},{48,112},{64,0},{80,16},{96,32},{112,48},{1... | collective-permute-start | bytes 73736 | tf_op jit(solution)/shard_map/ppermute | solution.py:42
  311.0 4.5 %collective-permute-start.52 = (bf16[64,384]{1,0:T(8,128)(2,1)S(1)}, bf16[64,384]{1,0:T(8,128)(2,1)S(1)}, u32[]{:S(2)}, u32[]{:S(2)}) collective-permute-start(bf16[64,384]{1,0:T(8,128)(2,1)S(1)} %get-tuple-element.7), channel_id=1, source_target_pairs={{0,16},{16,32},{32,48},{48,64},{64,80},{80,96},{96,112},{112,128},... | collective-permute-start | bytes 147464 | tf_op jit(solution)/shard_map/ppermute | solution.py:16
  317.6 8.2 %collective-permute-start.54 = (bf16[64,384]{1,0:T(8,128)(2,1)S(1)}, bf16[64,384]{1,0:T(8,128)(2,1)S(1)}, u32[]{:S(2)}, u32[]{:S(2)}) collective-permute-start(bf16[64,384]{1,0:T(8,128)(2,1)S(1)} %pad_maximum_fusion.9), channel_id=1, source_target_pairs={{0,1},{1,2},{2,3},{3,4},{4,5},{5,6},{6,7},{7,8},{8,9},{9,10},{10,1... | collective-permute-start | bytes 147464 | tf_op jit(solution)/shard_map/ppermute | solution.py:16
  325.9 1.9 collective-permute-start.55
  327.9 5.1 %collective-permute-start.60 = (bf16[768,64]{1,0:T(8,128)(2,1)S(1)}, bf16[768,64]{1,0:T(8,128)(2,1)S(1)}, u32[]{:S(2)}, u32[]{:S(2)}) collective-permute-start(bf16[768,64]{1,0:T(8,128)(2,1)S(1)} %maximum_select_fusion.14), channel_id=1, source_target_pairs={{0,16},{16,0},{32,48},{48,32},{64,80},{80,64},{96,112},{112,96},{1... | collective-permute-start | bytes 294920 | tf_op jit(solution)/shard_map/ppermute | solution.py:42
  333.1 3.6 collective-permute-done.60
  337.3 6.8 %collective-permute-start.61 = (bf16[384,64]{0,1:T(8,128)(2,1)S(1)}, bf16[384,64]{0,1:T(8,128)(2,1)S(1)}, u32[]{:S(2)}, u32[]{:S(2)}) collective-permute-start(bf16[384,64]{0,1:T(8,128)(2,1)S(1)} %select_convert_fusion), channel_id=1, source_target_pairs={{0,1},{1,0},{2,3},{3,2},{4,5},{5,4},{6,7},{7,6},{8,9},{9,8},{10,11... | collective-permute-start | bytes 147464 | tf_op jit(solution)/shard_map/ppermute | solution.py:60
  347.0 3.9 %collective-permute-done.62 = bf16[192,64]{0,1:T(8,128)(2,1)S(1)} collective-permute-done((bf16[192,64]{0,1:T(8,128)(2,1)S(1)}, bf16[192,64]{0,1:T(8,128)(2,1)S(1)}, u32[]{:S(2)}, u32[]{:S(2)}) %collective-permute-start.62) | collective-permute-done | bytes 24608 | tf_op jit(solution)/shard_map/ppermute | solution.py:60
  353.0 5.2 %collective-permute-done.63 = bf16[96,64]{0,1:T(8,128)(2,1)S(1)} collective-permute-done((bf16[96,64]{0,1:T(8,128)(2,1)S(1)}, bf16[96,64]{0,1:T(8,128)(2,1)S(1)}, u32[]{:S(2)}, u32[]{:S(2)}) %collective-permute-start.63) | collective-permute-done | bytes 12320 | tf_op jit(solution)/shard_map/ppermute | solution.py:60
  359.5 12.0 %collective-permute-start.64 = (bf16[48,64]{0,1:T(8,128)(2,1)}, bf16[48,64]{0,1:T(8,128)(2,1)S(1)}, u32[]{:S(2)}, u32[]{:S(2)}) collective-permute-start(bf16[48,64]{0,1:T(8,128)(2,1)} %select_convert_fusion.10), channel_id=1, source_target_pairs={{0,8},{1,9},{2,10},{3,11},{4,12},{5,13},{6,14},{7,15},{8,0},{9,1},... | collective-permute-start | bytes 18440 | tf_op jit(solution)/shard_map/ppermute | solution.py:60
  371.6 3.6 fusion.17
  375.2 2.0 fusion.31
  (283 shorter events, 76.2 us)
Async XLA Ops:
  7.0 45.4 %collective-permute-start.1 = (bf16[64,384]{1,0:T(8,128)(2,1)}, bf16[64,384]{1,0:T(8,128)(2,1)}, u32[]{:S(2)}, u32[]{:S(2)}) collective-permute-start(bf16[64,384]{1,0:T(8,128)(2,1)} %get-tuple-element.28), channel_id=1, source_target_pairs={{16,0},{32,16},{48,32},{64,48},{80,64},{96,80},{112,96},{128,112},... | collective-permute-start | bytes 147464 | tf_op jit(solution)/shard_map/ppermute | solution.py:16
  8.3 44.9 %collective-permute-start = (bf16[64,384]{1,0:T(8,128)(2,1)}, bf16[64,384]{1,0:T(8,128)(2,1)}, u32[]{:S(2)}, u32[]{:S(2)}) collective-permute-start(bf16[64,384]{1,0:T(8,128)(2,1)} %get-tuple-element.27), channel_id=1, source_target_pairs={{0,16},{16,32},{32,48},{48,64},{64,80},{80,96},{96,112},{112,128},... | collective-permute-start | bytes 147464 | tf_op jit(solution)/shard_map/ppermute | solution.py:16
  13.6 17.4 %collective-permute-start.4 = (bf16[48,64]{1,0:T(8,128)(2,1)S(1)}, bf16[48,64]{1,0:T(8,128)(2,1)S(1)}, u32[]{:S(2)}, u32[]{:S(2)}) collective-permute-start(bf16[48,64]{1,0:T(8,128)(2,1)S(1)} %convolution_convert_fusion.5), channel_id=1, source_target_pairs={{0,256},{16,272},{32,288},{48,304},{64,320},{80,336},{96,352},{112... | collective-permute-start | bytes 18440 | tf_op jit(solution)/shard_map/ppermute | solution.py:42
  31.1 7.2 %collective-permute-start.5 = (bf16[96,64]{1,0:T(8,128)(2,1)S(1)}, bf16[96,64]{1,0:T(8,128)(2,1)S(1)}, u32[]{:S(2)}, u32[]{:S(2)}) collective-permute-start(bf16[96,64]{1,0:T(8,128)(2,1)S(1)} %maximum_select_fusion.25), channel_id=1, source_target_pairs={{0,128},{16,144},{32,160},{48,176},{64,192},{80,208},{96,224},{112... | collective-permute-start | bytes 36872 | tf_op jit(solution)/shard_map/ppermute | solution.py:42
  38.3 8.0 %collective-permute-start.6 = (bf16[192,64]{1,0:T(8,128)(2,1)S(1)}, bf16[192,64]{1,0:T(8,128)(2,1)}, u32[]{:S(2)}, u32[]{:S(2)}) collective-permute-start(bf16[192,64]{1,0:T(8,128)(2,1)S(1)} %maximum_select_fusion.20), channel_id=1, source_target_pairs={{0,64},{16,80},{32,96},{48,112},{64,0},{80,16},{96,32},{112,48},{1... | collective-permute-start | bytes 73736 | tf_op jit(solution)/shard_map/ppermute | solution.py:42
  47.3 12.3 %collective-permute-start.7 = (bf16[384,64]{1,0:T(8,128)(2,1)S(1)}, bf16[384,64]{1,0:T(8,128)(2,1)S(1)}, u32[]{:S(2)}, u32[]{:S(2)}) collective-permute-start(bf16[384,64]{1,0:T(8,128)(2,1)S(1)} %maximum_select_fusion.15), channel_id=1, source_target_pairs={{0,32},{16,48},{32,0},{48,16},{64,96},{80,112},{96,64},{112,80},{1... | collective-permute-start | bytes 147464 | tf_op jit(solution)/shard_map/ppermute | solution.py:42
  53.9 9.4 %collective-permute-start.2 = (bf16[64,384]{1,0:T(8,128)(2,1)S(1)}, bf16[64,384]{1,0:T(8,128)(2,1)S(1)}, u32[]{:S(2)}, u32[]{:S(2)}) collective-permute-start(bf16[64,384]{1,0:T(8,128)(2,1)S(1)} %pad_maximum_fusion.1), channel_id=1, source_target_pairs={{0,1},{1,2},{2,3},{3,4},{4,5},{5,6},{6,7},{7,8},{8,9},{9,10},{10,1... | collective-permute-start | bytes 147464 | tf_op jit(solution)/shard_map/ppermute | solution.py:16
  55.9 9.8 %collective-permute-start.3 = (bf16[64,384]{1,0:T(8,128)(2,1)S(1)}, bf16[64,384]{1,0:T(8,128)(2,1)S(1)}, u32[]{:S(2)}, u32[]{:S(2)}) collective-permute-start(bf16[64,384]{1,0:T(8,128)(2,1)S(1)} %pad_maximum_fusion.2), channel_id=1, source_target_pairs={{1,0},{2,1},{3,2},{4,3},{5,4},{6,5},{7,6},{8,7},{9,8},{10,9},{11,1... | collective-permute-start | bytes 147464 | tf_op jit(solution)/shard_map/ppermute | solution.py:16
  59.6 14.8 %collective-permute-start.8 = (bf16[768,64]{1,0:T(8,128)(2,1)S(1)}, bf16[768,64]{1,0:T(8,128)(2,1)S(1)}, u32[]{:S(2)}, u32[]{:S(2)}) collective-permute-start(bf16[768,64]{1,0:T(8,128)(2,1)S(1)} %maximum_select_fusion.10), channel_id=1, source_target_pairs={{0,16},{16,0},{32,48},{48,32},{64,80},{80,64},{96,112},{112,96},{1... | collective-permute-start | bytes 294920 | tf_op jit(solution)/shard_map/ppermute | solution.py:42
  68.9 21.5 %collective-permute-start.17 = (bf16[48,64]{1,0:T(8,128)(2,1)S(1)}, bf16[48,64]{1,0:T(8,128)(2,1)S(1)}, u32[]{:S(2)}, u32[]{:S(2)}) collective-permute-start(bf16[48,64]{1,0:T(8,128)(2,1)S(1)} %fusion.56), channel_id=1, source_target_pairs={{0,256},{16,272},{32,288},{48,304},{64,320},{80,336},{96,352},{112... | collective-permute-start | bytes 18440 | tf_op jit(solution)/shard_map/ppermute | solution.py:42
  75.1 18.9 %collective-permute-start.9 = (bf16[384,64]{0,1:T(8,128)(2,1)S(1)}, bf16[384,64]{0,1:T(8,128)(2,1)S(1)}, u32[]{:S(2)}, u32[]{:S(2)}) collective-permute-start(bf16[384,64]{0,1:T(8,128)(2,1)S(1)} %select_convert_fusion.4), channel_id=1, source_target_pairs={{0,1},{1,0},{2,3},{3,2},{4,5},{5,4},{6,7},{7,6},{8,9},{9,8},{10,11... | collective-permute-start | bytes 147464 | tf_op jit(solution)/shard_map/ppermute | solution.py:60
  90.5 6.9 %collective-permute-start.18 = (bf16[96,64]{1,0:T(8,128)(2,1)S(1)}, bf16[96,64]{1,0:T(8,128)(2,1)S(1)}, u32[]{:S(2)}, u32[]{:S(2)}) collective-permute-start(bf16[96,64]{1,0:T(8,128)(2,1)S(1)} %maximum_select_fusion.26), channel_id=1, source_target_pairs={{0,128},{16,144},{32,160},{48,176},{64,192},{80,208},{96,224},{112... | collective-permute-start | bytes 36872 | tf_op jit(solution)/shard_map/ppermute | solution.py:42
  94.0 6.2 %collective-permute-start.10 = (bf16[192,64]{0,1:T(8,128)(2,1)S(1)}, bf16[192,64]{0,1:T(8,128)(2,1)S(1)}, u32[]{:S(2)}, u32[]{:S(2)}) collective-permute-start(bf16[192,64]{0,1:T(8,128)(2,1)S(1)} %select_convert_fusion.9), channel_id=1, source_target_pairs={{0,2},{1,3},{2,0},{3,1},{4,6},{5,7},{6,4},{7,5},{8,10},{9,11},{10,... | collective-permute-start | bytes 73736 | tf_op jit(solution)/shard_map/ppermute | solution.py:60
  97.4 6.0 %collective-permute-start.19 = (bf16[192,64]{1,0:T(8,128)(2,1)S(1)}, bf16[192,64]{1,0:T(8,128)(2,1)S(1)}, u32[]{:S(2)}, u32[]{:S(2)}) collective-permute-start(bf16[192,64]{1,0:T(8,128)(2,1)S(1)} %maximum_select_fusion.21), channel_id=1, source_target_pairs={{0,64},{16,80},{32,96},{48,112},{64,0},{80,16},{96,32},{112,48},{1... | collective-permute-start | bytes 73736 | tf_op jit(solution)/shard_map/ppermute | solution.py:42
  100.5 7.1 %collective-permute-start.11 = (bf16[96,64]{0,1:T(8,128)(2,1)S(1)}, bf16[96,64]{0,1:T(8,128)(2,1)S(1)}, u32[]{:S(2)}, u32[]{:S(2)}) collective-permute-start(bf16[96,64]{0,1:T(8,128)(2,1)S(1)} %select_convert_fusion.19), channel_id=1, source_target_pairs={{0,4},{1,5},{2,6},{3,7},{4,0},{5,1},{6,2},{7,3},{8,12},{9,13},{10,... | collective-permute-start | bytes 36872 | tf_op jit(solution)/shard_map/ppermute | solution.py:60
  103.4 8.8 %collective-permute-start.20 = (bf16[384,64]{1,0:T(8,128)(2,1)S(1)}, bf16[384,64]{1,0:T(8,128)(2,1)S(1)}, u32[]{:S(2)}, u32[]{:S(2)}) collective-permute-start(bf16[384,64]{1,0:T(8,128)(2,1)S(1)} %maximum_select_fusion.16), channel_id=1, source_target_pairs={{0,32},{16,48},{32,0},{48,16},{64,96},{80,112},{96,64},{112,80},{1... | collective-permute-start | bytes 147464 | tf_op jit(solution)/shard_map/ppermute | solution.py:42
  107.7 14.3 %collective-permute-start.12 = (bf16[48,64]{0,1:T(8,128)(2,1)S(1)}, bf16[48,64]{0,1:T(8,128)(2,1)S(1)}, u32[]{:S(2)}, u32[]{:S(2)}) collective-permute-start(bf16[48,64]{0,1:T(8,128)(2,1)S(1)} %select_convert_fusion.18), channel_id=1, source_target_pairs={{0,8},{1,9},{2,10},{3,11},{4,12},{5,13},{6,14},{7,15},{8,0},{9,1},... | collective-permute-start | bytes 18440 | tf_op jit(solution)/shard_map/ppermute | solution.py:60
  112.3 18.7 %collective-permute-start.21 = (bf16[768,64]{1,0:T(8,128)(2,1)S(1)}, bf16[768,64]{1,0:T(8,128)(2,1)S(1)}, u32[]{:S(2)}, u32[]{:S(2)}) collective-permute-start(bf16[768,64]{1,0:T(8,128)(2,1)S(1)} %maximum_select_fusion.11), channel_id=1, source_target_pairs={{0,16},{16,0},{32,48},{48,32},{64,80},{80,64},{96,112},{112,96},{1... | collective-permute-start | bytes 294920 | tf_op jit(solution)/shard_map/ppermute | solution.py:42
  122.8 10.8 %collective-permute-start.14 = (bf16[64,384]{1,0:T(8,128)(2,1)S(1)}, bf16[64,384]{1,0:T(8,128)(2,1)S(1)}, u32[]{:S(2)}, u32[]{:S(2)}) collective-permute-start(bf16[64,384]{1,0:T(8,128)(2,1)S(1)} %get-tuple-element.20), channel_id=1, source_target_pairs={{16,0},{32,16},{48,32},{64,48},{80,64},{96,80},{112,96},{128,112},... | collective-permute-start | bytes 147464 | tf_op jit(solution)/shard_map/ppermute | solution.py:16
  124.1 9.5 %collective-permute-start.13 = (bf16[64,384]{1,0:T(8,128)(2,1)S(1)}, bf16[64,384]{1,0:T(8,128)(2,1)S(1)}, u32[]{:S(2)}, u32[]{:S(2)}) collective-permute-start(bf16[64,384]{1,0:T(8,128)(2,1)S(1)} %get-tuple-element.19), channel_id=1, source_target_pairs={{0,16},{16,32},{32,48},{48,64},{64,80},{80,96},{96,112},{112,128},... | collective-permute-start | bytes 147464 | tf_op jit(solution)/shard_map/ppermute | solution.py:16
  131.6 3.1 collective-permute-start.22
  134.8 5.8 %collective-permute-start.23 = (bf16[192,64]{0,1:T(8,128)(2,1)S(1)}, bf16[192,64]{0,1:T(8,128)(2,1)S(1)}, u32[]{:S(2)}, u32[]{:S(2)}) collective-permute-start(bf16[192,64]{0,1:T(8,128)(2,1)S(1)} %select_convert_fusion.8), channel_id=1, source_target_pairs={{0,2},{1,3},{2,0},{3,1},{4,6},{5,7},{6,4},{7,5},{8,10},{9,11},{10,... | collective-permute-start | bytes 73736 | tf_op jit(solution)/shard_map/ppermute | solution.py:60
  136.9 15.6 %collective-permute-start.15 = (bf16[64,384]{1,0:T(8,128)(2,1)S(1)}, bf16[64,384]{1,0:T(8,128)(2,1)S(1)}, u32[]{:S(2)}, u32[]{:S(2)}) collective-permute-start(bf16[64,384]{1,0:T(8,128)(2,1)S(1)} %pad_maximum_fusion.3), channel_id=1, source_target_pairs={{0,1},{1,2},{2,3},{3,4},{4,5},{5,6},{6,7},{7,8},{8,9},{9,10},{10,1... | collective-permute-start | bytes 147464 | tf_op jit(solution)/shard_map/ppermute | solution.py:16
  140.8 7.2 %collective-permute-start.24 = (bf16[96,64]{0,1:T(8,128)(2,1)S(1)}, bf16[96,64]{0,1:T(8,128)(2,1)S(1)}, u32[]{:S(2)}, u32[]{:S(2)}) collective-permute-start(bf16[96,64]{0,1:T(8,128)(2,1)S(1)} %select_convert_fusion.17), channel_id=1, source_target_pairs={{0,4},{1,5},{2,6},{3,7},{4,0},{5,1},{6,2},{7,3},{8,12},{9,13},{10,... | collective-permute-start | bytes 36872 | tf_op jit(solution)/shard_map/ppermute | solution.py:60
  143.1 9.4 %collective-permute-start.16 = (bf16[64,384]{1,0:T(8,128)(2,1)S(1)}, bf16[64,384]{1,0:T(8,128)(2,1)S(1)}, u32[]{:S(2)}, u32[]{:S(2)}) collective-permute-start(bf16[64,384]{1,0:T(8,128)(2,1)S(1)} %pad_maximum_fusion.4), channel_id=1, source_target_pairs={{1,0},{2,1},{3,2},{4,3},{5,4},{6,5},{7,6},{8,7},{9,8},{10,9},{11,1... | collective-permute-start | bytes 147464 | tf_op jit(solution)/shard_map/ppermute | solution.py:16
  148.2 14.3 %collective-permute-start.25 = (bf16[48,64]{0,1:T(8,128)(2,1)S(1)}, bf16[48,64]{0,1:T(8,128)(2,1)S(1)}, u32[]{:S(2)}, u32[]{:S(2)}) collective-permute-start(bf16[48,64]{0,1:T(8,128)(2,1)S(1)} %select_convert_fusion.16), channel_id=1, source_target_pairs={{0,8},{1,9},{2,10},{3,11},{4,12},{5,13},{6,14},{7,15},{8,0},{9,1},... | collective-permute-start | bytes 18440 | tf_op jit(solution)/shard_map/ppermute | solution.py:60
  153.7 9.5 %collective-permute-start.30 = (bf16[48,64]{1,0:T(8,128)(2,1)S(1)}, bf16[48,64]{1,0:T(8,128)(2,1)S(1)}, u32[]{:S(2)}, u32[]{:S(2)}) collective-permute-start(bf16[48,64]{1,0:T(8,128)(2,1)S(1)} %fusion.57), channel_id=1, source_target_pairs={{0,256},{16,272},{32,288},{48,304},{64,320},{80,336},{96,352},{112... | collective-permute-start | bytes 18440 | tf_op jit(solution)/shard_map/ppermute | solution.py:42
  163.2 8.3 %collective-permute-start.31 = (bf16[96,64]{1,0:T(8,128)(2,1)S(1)}, bf16[96,64]{1,0:T(8,128)(2,1)S(1)}, u32[]{:S(2)}, u32[]{:S(2)}) collective-permute-start(bf16[96,64]{1,0:T(8,128)(2,1)S(1)} %maximum_select_fusion.27), channel_id=1, source_target_pairs={{0,128},{16,144},{32,160},{48,176},{64,192},{80,208},{96,224},{112... | collective-permute-start | bytes 36872 | tf_op jit(solution)/shard_map/ppermute | solution.py:42
  171.6 9.7 %collective-permute-start.32 = (bf16[192,64]{1,0:T(8,128)(2,1)S(1)}, bf16[192,64]{1,0:T(8,128)(2,1)S(1)}, u32[]{:S(2)}, u32[]{:S(2)}) collective-permute-start(bf16[192,64]{1,0:T(8,128)(2,1)S(1)} %maximum_select_fusion.22), channel_id=1, source_target_pairs={{0,64},{16,80},{32,96},{48,112},{64,0},{80,16},{96,32},{112,48},{1... | collective-permute-start | bytes 73736 | tf_op jit(solution)/shard_map/ppermute | solution.py:42
  175.4 9.0 %collective-permute-start.27 = (bf16[64,384]{1,0:T(8,128)(2,1)S(1)}, bf16[64,384]{1,0:T(8,128)(2,1)S(1)}, u32[]{:S(2)}, u32[]{:S(2)}) collective-permute-start(bf16[64,384]{1,0:T(8,128)(2,1)S(1)} %get-tuple-element.16), channel_id=1, source_target_pairs={{16,0},{32,16},{48,32},{64,48},{80,64},{96,80},{112,96},{128,112},... | collective-permute-start | bytes 147464 | tf_op jit(solution)/shard_map/ppermute | solution.py:16
  176.7 7.7 %collective-permute-start.26 = (bf16[64,384]{1,0:T(8,128)(2,1)S(1)}, bf16[64,384]{1,0:T(8,128)(2,1)S(1)}, u32[]{:S(2)}, u32[]{:S(2)}) collective-permute-start(bf16[64,384]{1,0:T(8,128)(2,1)S(1)} %get-tuple-element.15), channel_id=1, source_target_pairs={{0,16},{16,32},{32,48},{48,64},{64,80},{80,96},{96,112},{112,128},... | collective-permute-start | bytes 147464 | tf_op jit(solution)/shard_map/ppermute | solution.py:16
  181.3 12.6 %collective-permute-start.33 = (bf16[384,64]{1,0:T(8,128)(2,1)S(1)}, bf16[384,64]{1,0:T(8,128)(2,1)S(1)}, u32[]{:S(2)}, u32[]{:S(2)}) collective-permute-start(bf16[384,64]{1,0:T(8,128)(2,1)S(1)} %maximum_select_fusion.17), channel_id=1, source_target_pairs={{0,32},{16,48},{32,0},{48,16},{64,96},{80,112},{96,64},{112,80},{1... | collective-permute-start | bytes 147464 | tf_op jit(solution)/shard_map/ppermute | solution.py:42
  184.5 14.6 %collective-permute-start.28 = (bf16[64,384]{1,0:T(8,128)(2,1)S(1)}, bf16[64,384]{1,0:T(8,128)(2,1)S(1)}, u32[]{:S(2)}, u32[]{:S(2)}) collective-permute-start(bf16[64,384]{1,0:T(8,128)(2,1)S(1)} %pad_maximum_fusion.5), channel_id=1, source_target_pairs={{0,1},{1,2},{2,3},{3,4},{4,5},{5,6},{6,7},{7,8},{8,9},{9,10},{10,1... | collective-permute-start | bytes 147464 | tf_op jit(solution)/shard_map/ppermute | solution.py:16
  192.0 8.3 %collective-permute-start.29 = (bf16[64,384]{1,0:T(8,128)(2,1)S(1)}, bf16[64,384]{1,0:T(8,128)(2,1)S(1)}, u32[]{:S(2)}, u32[]{:S(2)}) collective-permute-start(bf16[64,384]{1,0:T(8,128)(2,1)S(1)} %pad_maximum_fusion.6), channel_id=1, source_target_pairs={{1,0},{2,1},{3,2},{4,3},{5,4},{6,5},{7,6},{8,7},{9,8},{10,9},{11,1... | collective-permute-start | bytes 147464 | tf_op jit(solution)/shard_map/ppermute | solution.py:16
  194.0 18.2 %collective-permute-start.34 = (bf16[768,64]{1,0:T(8,128)(2,1)S(1)}, bf16[768,64]{1,0:T(8,128)(2,1)S(1)}, u32[]{:S(2)}, u32[]{:S(2)}) collective-permute-start(bf16[768,64]{1,0:T(8,128)(2,1)S(1)} %maximum_select_fusion.12), channel_id=1, source_target_pairs={{0,16},{16,0},{32,48},{48,32},{64,80},{80,64},{96,112},{112,96},{1... | collective-permute-start | bytes 294920 | tf_op jit(solution)/shard_map/ppermute | solution.py:42
  201.5 26.6 %collective-permute-start.43 = (bf16[48,64]{1,0:T(8,128)(2,1)S(1)}, bf16[48,64]{1,0:T(8,128)(2,1)S(1)}, u32[]{:S(2)}, u32[]{:S(2)}) collective-permute-start(bf16[48,64]{1,0:T(8,128)(2,1)S(1)} %fusion.58), channel_id=1, source_target_pairs={{0,256},{16,272},{32,288},{48,304},{64,320},{80,336},{96,352},{112... | collective-permute-start | bytes 18440 | tf_op jit(solution)/shard_map/ppermute | solution.py:42
  212.8 17.2 %collective-permute-start.35 = (bf16[384,64]{0,1:T(8,128)(2,1)S(1)}, bf16[384,64]{0,1:T(8,128)(2,1)S(1)}, u32[]{:S(2)}, u32[]{:S(2)}) collective-permute-start(bf16[384,64]{0,1:T(8,128)(2,1)S(1)} %select_convert_fusion.2), channel_id=1, source_target_pairs={{0,1},{1,0},{2,3},{3,2},{4,5},{5,4},{6,7},{7,6},{8,9},{9,8},{10,11... | collective-permute-start | bytes 147464 | tf_op jit(solution)/shard_map/ppermute | solution.py:60
  228.1 6.6 %collective-permute-start.44 = (bf16[96,64]{1,0:T(8,128)(2,1)S(1)}, bf16[96,64]{1,0:T(8,128)(2,1)S(1)}, u32[]{:S(2)}, u32[]{:S(2)}) collective-permute-start(bf16[96,64]{1,0:T(8,128)(2,1)S(1)} %maximum_select_fusion.28), channel_id=1, source_target_pairs={{0,128},{16,144},{32,160},{48,176},{64,192},{80,208},{96,224},{112... | collective-permute-start | bytes 36872 | tf_op jit(solution)/shard_map/ppermute | solution.py:42
  230.2 6.5 %collective-permute-start.36 = (bf16[192,64]{0,1:T(8,128)(2,1)S(1)}, bf16[192,64]{0,1:T(8,128)(2,1)S(1)}, u32[]{:S(2)}, u32[]{:S(2)}) collective-permute-start(bf16[192,64]{0,1:T(8,128)(2,1)S(1)} %select_convert_fusion.7), channel_id=1, source_target_pairs={{0,2},{1,3},{2,0},{3,1},{4,6},{5,7},{6,4},{7,5},{8,10},{9,11},{10,... | collective-permute-start | bytes 73736 | tf_op jit(solution)/shard_map/ppermute | solution.py:60
  234.7 6.0 %collective-permute-start.45 = (bf16[192,64]{1,0:T(8,128)(2,1)S(1)}, bf16[192,64]{1,0:T(8,128)(2,1)S(1)}, u32[]{:S(2)}, u32[]{:S(2)}) collective-permute-start(bf16[192,64]{1,0:T(8,128)(2,1)S(1)} %maximum_select_fusion.23), channel_id=1, source_target_pairs={{0,64},{16,80},{32,96},{48,112},{64,0},{80,16},{96,32},{112,48},{1... | collective-permute-start | bytes 73736 | tf_op jit(solution)/shard_map/ppermute | solution.py:42
  236.9 7.1 %collective-permute-start.37 = (bf16[96,64]{0,1:T(8,128)(2,1)S(1)}, bf16[96,64]{0,1:T(8,128)(2,1)S(1)}, u32[]{:S(2)}, u32[]{:S(2)}) collective-permute-start(bf16[96,64]{0,1:T(8,128)(2,1)S(1)} %select_convert_fusion.15), channel_id=1, source_target_pairs={{0,4},{1,5},{2,6},{3,7},{4,0},{5,1},{6,2},{7,3},{8,12},{9,13},{10,... | collective-permute-start | bytes 36872 | tf_op jit(solution)/shard_map/ppermute | solution.py:60
  240.8 8.0 %collective-permute-start.46 = (bf16[384,64]{1,0:T(8,128)(2,1)S(1)}, bf16[384,64]{1,0:T(8,128)(2,1)S(1)}, u32[]{:S(2)}, u32[]{:S(2)}) collective-permute-start(bf16[384,64]{1,0:T(8,128)(2,1)S(1)} %maximum_select_fusion.18), channel_id=1, source_target_pairs={{0,32},{16,48},{32,0},{48,16},{64,96},{80,112},{96,64},{112,80},{1... | collective-permute-start | bytes 147464 | tf_op jit(solution)/shard_map/ppermute | solution.py:42
  244.1 14.3 %collective-permute-start.38 = (bf16[48,64]{0,1:T(8,128)(2,1)S(1)}, bf16[48,64]{0,1:T(8,128)(2,1)S(1)}, u32[]{:S(2)}, u32[]{:S(2)}) collective-permute-start(bf16[48,64]{0,1:T(8,128)(2,1)S(1)} %select_convert_fusion.14), channel_id=1, source_target_pairs={{0,8},{1,9},{2,10},{3,11},{4,12},{5,13},{6,14},{7,15},{8,0},{9,1},... | collective-permute-start | bytes 18440 | tf_op jit(solution)/shard_map/ppermute | solution.py:60
  248.8 16.2 %collective-permute-start.47 = (bf16[768,64]{1,0:T(8,128)(2,1)S(1)}, bf16[768,64]{1,0:T(8,128)(2,1)S(1)}, u32[]{:S(2)}, u32[]{:S(2)}) collective-permute-start(bf16[768,64]{1,0:T(8,128)(2,1)S(1)} %maximum_select_fusion.13), channel_id=1, source_target_pairs={{0,16},{16,0},{32,48},{48,32},{64,80},{80,64},{96,112},{112,96},{1... | collective-permute-start | bytes 294920 | tf_op jit(solution)/shard_map/ppermute | solution.py:42
  259.1 8.4 %collective-permute-start.40 = (bf16[64,384]{1,0:T(8,128)(2,1)S(1)}, bf16[64,384]{1,0:T(8,128)(2,1)S(1)}, u32[]{:S(2)}, u32[]{:S(2)}) collective-permute-start(bf16[64,384]{1,0:T(8,128)(2,1)S(1)} %get-tuple-element.12), channel_id=1, source_target_pairs={{16,0},{32,16},{48,32},{64,48},{80,64},{96,80},{112,96},{128,112},... | collective-permute-start | bytes 147464 | tf_op jit(solution)/shard_map/ppermute | solution.py:16
  260.4 7.1 %collective-permute-start.39 = (bf16[64,384]{1,0:T(8,128)(2,1)S(1)}, bf16[64,384]{1,0:T(8,128)(2,1)S(1)}, u32[]{:S(2)}, u32[]{:S(2)}) collective-permute-start(bf16[64,384]{1,0:T(8,128)(2,1)S(1)} %get-tuple-element.11), channel_id=1, source_target_pairs={{0,16},{16,32},{32,48},{48,64},{64,80},{80,96},{96,112},{112,128},... | collective-permute-start | bytes 147464 | tf_op jit(solution)/shard_map/ppermute | solution.py:16
  268.9 5.8 %collective-permute-start.49 = (bf16[192,64]{0,1:T(8,128)(2,1)S(1)}, bf16[192,64]{0,1:T(8,128)(2,1)S(1)}, u32[]{:S(2)}, u32[]{:S(2)}) collective-permute-start(bf16[192,64]{0,1:T(8,128)(2,1)S(1)} %select_convert_fusion.6), channel_id=1, source_target_pairs={{0,2},{1,3},{2,0},{3,1},{4,6},{5,7},{6,4},{7,5},{8,10},{9,11},{10,... | collective-permute-start | bytes 73736 | tf_op jit(solution)/shard_map/ppermute | solution.py:60
  270.8 14.4 %collective-permute-start.41 = (bf16[64,384]{1,0:T(8,128)(2,1)S(1)}, bf16[64,384]{1,0:T(8,128)(2,1)S(1)}, u32[]{:S(2)}, u32[]{:S(2)}) collective-permute-start(bf16[64,384]{1,0:T(8,128)(2,1)S(1)} %pad_maximum_fusion.7), channel_id=1, source_target_pairs={{0,1},{1,2},{2,3},{3,4},{4,5},{5,6},{6,7},{7,8},{8,9},{9,10},{10,1... | collective-permute-start | bytes 147464 | tf_op jit(solution)/shard_map/ppermute | solution.py:16
  274.8 7.1 %collective-permute-start.50 = (bf16[96,64]{0,1:T(8,128)(2,1)S(1)}, bf16[96,64]{0,1:T(8,128)(2,1)S(1)}, u32[]{:S(2)}, u32[]{:S(2)}) collective-permute-start(bf16[96,64]{0,1:T(8,128)(2,1)S(1)} %select_convert_fusion.13), channel_id=1, source_target_pairs={{0,4},{1,5},{2,6},{3,7},{4,0},{5,1},{6,2},{7,3},{8,12},{9,13},{10,... | collective-permute-start | bytes 36872 | tf_op jit(solution)/shard_map/ppermute | solution.py:60
  277.1 8.1 %collective-permute-start.42 = (bf16[64,384]{1,0:T(8,128)(2,1)S(1)}, bf16[64,384]{1,0:T(8,128)(2,1)S(1)}, u32[]{:S(2)}, u32[]{:S(2)}) collective-permute-start(bf16[64,384]{1,0:T(8,128)(2,1)S(1)} %pad_maximum_fusion.8), channel_id=1, source_target_pairs={{1,0},{2,1},{3,2},{4,3},{5,4},{6,5},{7,6},{8,7},{9,8},{10,9},{11,1... | collective-permute-start | bytes 147464 | tf_op jit(solution)/shard_map/ppermute | solution.py:16
  282.1 14.4 %collective-permute-start.51 = (bf16[48,64]{0,1:T(8,128)(2,1)S(1)}, bf16[48,64]{0,1:T(8,128)(2,1)S(1)}, u32[]{:S(2)}, u32[]{:S(2)}) collective-permute-start(bf16[48,64]{0,1:T(8,128)(2,1)S(1)} %select_convert_fusion.12), channel_id=1, source_target_pairs={{0,8},{1,9},{2,10},{3,11},{4,12},{5,13},{6,14},{7,15},{8,0},{9,1},... | collective-permute-start | bytes 18440 | tf_op jit(solution)/shard_map/ppermute | solution.py:60
  286.4 12.2 %collective-permute-start.56 = (bf16[48,64]{1,0:T(8,128)(2,1)S(1)}, bf16[48,64]{1,0:T(8,128)(2,1)S(1)}, u32[]{:S(2)}, u32[]{:S(2)}) collective-permute-start(bf16[48,64]{1,0:T(8,128)(2,1)S(1)} %fusion.59), channel_id=1, source_target_pairs={{0,256},{16,272},{32,288},{48,304},{64,320},{80,336},{96,352},{112... | collective-permute-start | bytes 18440 | tf_op jit(solution)/shard_map/ppermute | solution.py:42
  298.6 6.6 %collective-permute-start.57 = (bf16[96,64]{1,0:T(8,128)(2,1)S(1)}, bf16[96,64]{1,0:T(8,128)(2,1)S(1)}, u32[]{:S(2)}, u32[]{:S(2)}) collective-permute-start(bf16[96,64]{1,0:T(8,128)(2,1)S(1)} %maximum_select_fusion.29), channel_id=1, source_target_pairs={{0,128},{16,144},{32,160},{48,176},{64,192},{80,208},{96,224},{112... | collective-permute-start | bytes 36872 | tf_op jit(solution)/shard_map/ppermute | solution.py:42
  305.3 10.3 %collective-permute-start.58 = (bf16[192,64]{1,0:T(8,128)(2,1)S(1)}, bf16[192,64]{1,0:T(8,128)(2,1)S(1)}, u32[]{:S(2)}, u32[]{:S(2)}) collective-permute-start(bf16[192,64]{1,0:T(8,128)(2,1)S(1)} %maximum_select_fusion.24), channel_id=1, source_target_pairs={{0,64},{16,80},{32,96},{48,112},{64,0},{80,16},{96,32},{112,48},{1... | collective-permute-start | bytes 73736 | tf_op jit(solution)/shard_map/ppermute | solution.py:42
  309.7 7.8 %collective-permute-start.53 = (bf16[64,384]{1,0:T(8,128)(2,1)S(1)}, bf16[64,384]{1,0:T(8,128)(2,1)S(1)}, u32[]{:S(2)}, u32[]{:S(2)}) collective-permute-start(bf16[64,384]{1,0:T(8,128)(2,1)S(1)} %get-tuple-element.8), channel_id=1, source_target_pairs={{16,0},{32,16},{48,32},{64,48},{80,64},{96,80},{112,96},{128,112},... | collective-permute-start | bytes 147464 | tf_op jit(solution)/shard_map/ppermute | solution.py:16
  311.0 6.6 %collective-permute-start.52 = (bf16[64,384]{1,0:T(8,128)(2,1)S(1)}, bf16[64,384]{1,0:T(8,128)(2,1)S(1)}, u32[]{:S(2)}, u32[]{:S(2)}) collective-permute-start(bf16[64,384]{1,0:T(8,128)(2,1)S(1)} %get-tuple-element.7), channel_id=1, source_target_pairs={{0,16},{16,32},{32,48},{48,64},{64,80},{80,96},{96,112},{112,128},... | collective-permute-start | bytes 147464 | tf_op jit(solution)/shard_map/ppermute | solution.py:16
  315.6 12.2 %collective-permute-start.59 = (bf16[384,64]{1,0:T(8,128)(2,1)S(1)}, bf16[384,64]{1,0:T(8,128)(2,1)S(1)}, u32[]{:S(2)}, u32[]{:S(2)}) collective-permute-start(bf16[384,64]{1,0:T(8,128)(2,1)S(1)} %maximum_select_fusion.19), channel_id=1, source_target_pairs={{0,32},{16,48},{32,0},{48,16},{64,96},{80,112},{96,64},{112,80},{1... | collective-permute-start | bytes 147464 | tf_op jit(solution)/shard_map/ppermute | solution.py:42
  317.6 15.4 %collective-permute-start.54 = (bf16[64,384]{1,0:T(8,128)(2,1)S(1)}, bf16[64,384]{1,0:T(8,128)(2,1)S(1)}, u32[]{:S(2)}, u32[]{:S(2)}) collective-permute-start(bf16[64,384]{1,0:T(8,128)(2,1)S(1)} %pad_maximum_fusion.9), channel_id=1, source_target_pairs={{0,1},{1,2},{2,3},{3,4},{4,5},{5,6},{6,7},{7,8},{8,9},{9,10},{10,1... | collective-permute-start | bytes 147464 | tf_op jit(solution)/shard_map/ppermute | solution.py:16
  325.9 18.2 %collective-permute-start.55 = (bf16[64,384]{1,0:T(8,128)(2,1)S(1)}, bf16[64,384]{1,0:T(8,128)(2,1)S(1)}, u32[]{:S(2)}, u32[]{:S(2)}) collective-permute-start(bf16[64,384]{1,0:T(8,128)(2,1)S(1)} %pad_maximum_fusion.10), channel_id=1, source_target_pairs={{1,0},{2,1},{3,2},{4,3},{5,4},{6,5},{7,6},{8,7},{9,8},{10,9},{11,1... | collective-permute-start | bytes 147464 | tf_op jit(solution)/shard_map/ppermute | solution.py:16
  327.9 8.8 %collective-permute-start.60 = (bf16[768,64]{1,0:T(8,128)(2,1)S(1)}, bf16[768,64]{1,0:T(8,128)(2,1)S(1)}, u32[]{:S(2)}, u32[]{:S(2)}) collective-permute-start(bf16[768,64]{1,0:T(8,128)(2,1)S(1)} %maximum_select_fusion.14), channel_id=1, source_target_pairs={{0,16},{16,0},{32,48},{48,32},{64,80},{80,64},{96,112},{112,96},{1... | collective-permute-start | bytes 294920 | tf_op jit(solution)/shard_map/ppermute | solution.py:42
  337.3 7.7 %collective-permute-start.61 = (bf16[384,64]{0,1:T(8,128)(2,1)S(1)}, bf16[384,64]{0,1:T(8,128)(2,1)S(1)}, u32[]{:S(2)}, u32[]{:S(2)}) collective-permute-start(bf16[384,64]{0,1:T(8,128)(2,1)S(1)} %select_convert_fusion), channel_id=1, source_target_pairs={{0,1},{1,0},{2,3},{3,2},{4,5},{5,4},{6,7},{7,6},{8,9},{9,8},{10,11... | collective-permute-start | bytes 147464 | tf_op jit(solution)/shard_map/ppermute | solution.py:60
  345.1 5.8 %collective-permute-start.62 = (bf16[192,64]{0,1:T(8,128)(2,1)S(1)}, bf16[192,64]{0,1:T(8,128)(2,1)S(1)}, u32[]{:S(2)}, u32[]{:S(2)}) collective-permute-start(bf16[192,64]{0,1:T(8,128)(2,1)S(1)} %select_convert_fusion.5), channel_id=1, source_target_pairs={{0,2},{1,3},{2,0},{3,1},{4,6},{5,7},{6,4},{7,5},{8,10},{9,11},{10,... | collective-permute-start | bytes 73736 | tf_op jit(solution)/shard_map/ppermute | solution.py:60
  351.1 7.1 %collective-permute-start.63 = (bf16[96,64]{0,1:T(8,128)(2,1)S(1)}, bf16[96,64]{0,1:T(8,128)(2,1)S(1)}, u32[]{:S(2)}, u32[]{:S(2)}) collective-permute-start(bf16[96,64]{0,1:T(8,128)(2,1)S(1)} %select_convert_fusion.11), channel_id=1, source_target_pairs={{0,4},{1,5},{2,6},{3,7},{4,0},{5,1},{6,2},{7,3},{8,12},{9,13},{10,... | collective-permute-start | bytes 36872 | tf_op jit(solution)/shard_map/ppermute | solution.py:60
  359.5 15.6 %collective-permute-start.64 = (bf16[48,64]{0,1:T(8,128)(2,1)}, bf16[48,64]{0,1:T(8,128)(2,1)S(1)}, u32[]{:S(2)}, u32[]{:S(2)}) collective-permute-start(bf16[48,64]{0,1:T(8,128)(2,1)} %select_convert_fusion.10), channel_id=1, source_target_pairs={{0,8},{1,9},{2,10},{3,11},{4,12},{5,13},{6,14},{7,15},{8,0},{9,1},... | collective-permute-start | bytes 18440 | tf_op jit(solution)/shard_map/ppermute | solution.py:60
  (28 other events, 607.2 us)
